TPU v7x, 32 devices: a whole 2x2x4 slice. The times are simulated.
32 devices in a mesh: region: 4 (over y, x), col: 8 (over z, core).
Axes of the slice: x: 2, y: 2, z: 4, core: 2. Of those that a mesh axis runs over, the one named last changes fastest.
Arguments:
- tiles: float32 [1536, 128, 128], P(('region', 'col')), may hold values from -0.109375 to 0.109375
- tile_rows: int32 [1536], P(('region', 'col')), may hold values from 0 to 1
- tile_cols: int32 [1536], P(('region', 'col')), may hold values from 0 to 15
- tile_count: int32 [32], P(('region', 'col')), may hold values from 12 to 48, as said below
- rhs: float32 [64, 128], P(('region', 'col')), may hold values from -6 to 6
- base_cost: float32 [64, 128], P(('region', 'col')), may hold values from 0.1 to 1
- upper: float32 [64, 128], P(('region', 'col')), may hold values from 0.5 to 4
- primal: float32 [64, 16, 128], P(('region', 'col')), may hold values from 0 to 1
- dual: float32 [64, 16, 128], P(('region', 'col')), may hold values from 0 to 1
- price_levels: float32 [32, 128], replicated, may hold values from 0.5 to 2
- scenario_ids: int32 [16], replicated, may hold values from 0 to 31
Outputs:
- primal_out: float32 [64, 16, 128], P(('region', 'col'))
- dual_out: float32 [64, 16, 128], P(('region', 'col'))
- weight_out: float32 [16], replicated
Inputs may be any that keep to these rules, and one draw needn't show every extreme that they name: `tile_count`: slots at or past a device's count are padding and hold no part of the matrix; in every draw some device has all 48 slots live.
All inputs are finite; a program needn't handle non-finite values.
Results may differ from a plain program's by a relative error of at most 0.0001.
Values sent between devices are 32-bit elements; how exact they have to be, the bound alone decides.
No kernel may reach another device: no remote copies, remote signals or barrier semaphores. Data moves between devices by JAX's collectives and lax.ppermute only.
A program may use at most 64 MiB of HBM per device.

v0:
```python
import jax
import jax.numpy as jnp
from jax import lax
from jax.sharding import PartitionSpec as P

ITERS = 2


def local(
    tiles,
    tile_rows,
    tile_cols,
    tile_count,
    rhs,
    base_cost,
    upper,
    primal,
    dual,
    price_levels,
    scenario_ids,
):
    hp = lax.Precision.HIGHEST
    ntiles = tiles.shape[0]
    row_blocks = rhs.shape[0]
    own_blocks = base_cost.shape[0]
    scenarios = primal.shape[1]
    lanes = primal.shape[2]
    region_blocks = own_blocks * lax.axis_size("col")
    devices = lax.axis_size(("region", "col"))
    live = (jnp.arange(ntiles, dtype=jnp.int32) < tile_count[0]).astype(jnp.float32)
    row_select = (tile_rows[:, None] == jnp.arange(row_blocks, dtype=jnp.int32)[None, :]).astype(
        jnp.float32
    )
    row_live = row_select * live[:, None]
    col_select = (tile_cols[:, None] == jnp.arange(region_blocks, dtype=jnp.int32)[None, :]).astype(
        jnp.float32
    )
    col_live = col_select * live[:, None]
    choose = (
        scenario_ids[:, None] == jnp.arange(price_levels.shape[0], dtype=jnp.int32)[None, :]
    ).astype(jnp.float32)
    factor = jnp.dot(choose, price_levels, precision=hp)
    cost = base_cost[:, None, :] * factor[None, :, :]
    local_a = jnp.sum(jnp.sum(tiles * tiles, axis=(1, 2)) * live)
    local_c = jnp.sum(cost * cost, axis=(0, 2))
    local_b = jnp.sum(rhs * rhs)
    sq_a, sq_c, sq_b = lax.psum((local_a, local_c, local_b), ("region", "col"))
    eta = 0.5 / jnp.sqrt(sq_a / (lanes * row_blocks * devices))
    weight = jnp.sqrt(sq_c) / jnp.sqrt(sq_b)
    width = scenarios * lanes
    for step in range(ITERS):
        tau = (eta / weight)[None, :, None]
        sigma = (eta * weight)[None, :, None]
        dual_rows = jnp.dot(row_select, dual.reshape(row_blocks, width), precision=hp).reshape(
            ntiles, scenarios, lanes
        )
        contrib = jnp.einsum("tij,tsi->tsj", tiles, dual_rows, precision=hp)
        flat_terms = contrib.reshape(ntiles, width)
        partial_value = jnp.dot(col_live.T, flat_terms, precision=hp).reshape(
            region_blocks, scenarios, lanes
        )
        grad = lax.psum_scatter(partial_value, "col", scatter_dimension=0, tiled=True)
        new_primal = jnp.clip(primal - tau * (cost - grad), 0.0, upper[:, None, :])
        point = 2.0 * new_primal - primal
        region_point = lax.all_gather(point, "col", axis=0, tiled=True)
        selected = jnp.dot(
            col_select, region_point.reshape(region_blocks, width), precision=hp
        ).reshape(ntiles, scenarios, lanes)
        image = jnp.einsum("tij,tsj->tsi", tiles, selected, precision=hp)
        product = jnp.dot(row_live.T, image.reshape(ntiles, width), precision=hp).reshape(
            row_blocks, scenarios, lanes
        )
        new_dual = jnp.maximum(dual + sigma * (rhs[:, None, :] - product), 0.0)
        local_x = jnp.sum((new_primal - primal) ** 2, axis=(0, 2))
        local_y = jnp.sum((new_dual - dual) ** 2, axis=(0, 2))
        step_x = lax.psum(local_x, ("region", "col"))
        step_y = lax.psum(local_y, ("region", "col"))
        weight = jnp.sqrt(weight * jnp.sqrt((step_x + 1e-06) / (step_y + 1e-06)))
        primal, dual = (new_primal, new_dual)
    return (primal, dual, weight)


def solution(mesh):
    placed = (
        P(("region", "col"), None, None),
        P(("region", "col")),
        P(("region", "col")),
        P(("region", "col")),
        P(("region", "col"), None),
        P(("region", "col"), None),
        P(("region", "col"), None),
        P(("region", "col"), None, None),
        P(("region", "col"), None, None),
        P(),
        P(),
    )
    return jax.shard_map(
        local,
        mesh=mesh,
        in_specs=placed,
        out_specs=(P(("region", "col"), None, None), P(("region", "col"), None, None), P()),
        check_vma=False,
    )
```

profile of v0, /device:TPU:0, one launch (start us, length us, event | category | flops | bytes accessed | tf_op | source)
XLA Modules:
  0.0 194.0 jit_solution(15329960555821616585)
XLA Ops:
  7.2 0.0 copy-start
  7.2 0.0 copy-start.1
  7.2 0.0 copy-start.7
  7.2 0.0 reduce-scatter.3.cloned.1.call-start
  8.1 1.2 fusion.37
  9.3 0.0 copy-start.10
  9.3 0.0 copy-start.5
  9.3 0.0 copy-start.9
  9.3 0.0 copy-start.3
  9.3 0.0 copy-start.8
  9.3 4.7 %fusion.18 = f32[48,16,128]{2,1,0:T(8,128)S(1)} fusion(f32[48,128,128]{2,1,0:T(8,128)} %param.11, f32[48,16,128]{2,0,1:T(8,128)S(1)} %fusion.37), kind=kOutput, calls=%fused_computation.23 | convolution fusion | flops 150994944 | bytes 3932160 | tf_op jit(solution)/shard_map/tij,tsi->tsj/dot_general | solution.py:57
  14.1 0.0 copy-done.7
  14.1 0.4 fusion.9
  14.5 0.7 copy.80
  15.2 0.0 reduce-scatter.3.cloned.1.call-update
  15.2 0.0 reduce-scatter.5.cloned.1.call-start
  15.2 0.0 copy-done.1
  15.3 0.5 multiply_reduce_fusion
  15.7 0.0 copy-start.6
  15.7 0.0 copy-start.2
  15.7 0.6 fusion.68
  16.3 0.0 copy-done
  16.3 0.0 copy-done.10
  16.3 0.2 fusion.52
  16.5 0.0 copy-done.5
  16.5 0.1 fusion.26
  16.6 0.0 copy-done.9
  16.6 0.6 multiply_reduce_fusion.5
  17.2 42.3 %all-reduce.2 = (f32[16]{0:T(128)S(1)}, f32[]{:T(128)}, f32[]{:T(128)}) all-reduce(f32[16]{0:T(128)S(1)} %fusion.26, f32[]{:T(128)} %fusion.68, f32[]{:T(128)} %multiply_reduce_fusion.5), channel_id=1, replica_groups=mesh['region'=4,'col'=8] {'region','col'}, use_global_device_ids=true, to_apply=%region_6.0 | all-reduce | flops 18 | bytes 144 | tf_op jit(solution)/shard_map/psum | solution.py:47
  60.9 0.0 reduce-scatter.3.cloned.1.call-done
  60.9 0.0 copy-done.3
  60.9 0.0 copy-done.8
  61.0 0.9 multiply_reduce_fusion.4
  61.9 14.1 %all_gather.6 = f32[16,16,128]{2,1,0:T(8,128)S(1)} all-gather(f32[2,16,128]{2,1,0:T(8,128)S(1)} %multiply_subtract_fusion.3), channel_id=1, replica_groups=mesh['region'=4,'col'=8] {'col'}, dimensions={0}, use_global_device_ids=true | all-gather | bytes 147456 | tf_op jit(solution)/shard_map/all_gather | solution.py:65
  76.0 0.4 fusion.23
  76.4 5.0 %fusion.16 = f32[48,16,128]{2,1,0:T(8,128)S(1)} fusion(f32[48,128,128]{2,1,0:T(8,128)S(1)} %copy-done.1, f32[48,16,128]{2,0,1:T(8,128)S(1)} %fusion.23), kind=kOutput, calls=%fused_computation.21 | convolution fusion | flops 150994944 | bytes 3932160 | tf_op jit(solution)/shard_map/tij,tsj->tsi/dot_general | solution.py:69
  81.4 0.0 copy-done.6
  81.4 0.4 fusion.6
  81.8 0.0 copy-done.2
  81.8 0.2 multiply_reduce_fusion.3
  82.0 0.4 fusion.35
  82.4 2.9 %fusion.14 = f32[48,16,128]{2,1,0:T(8,128)S(1)} fusion(f32[48,128,128]{2,1,0:T(8,128)S(1)} %copy-done.1, f32[48,16,128]{2,0,1:T(8,128)S(1)} %fusion.35), kind=kOutput, calls=%fused_computation.19 | convolution fusion | flops 150994944 | bytes 3932160 | tf_op jit(solution)/shard_map/tij,tsi->tsj/dot_general | solution.py:57
  85.3 0.4 fusion.3
  85.7 0.7 copy.87
  86.4 0.0 reduce-scatter.5.cloned.1.call-update
  86.4 39.3 %all-reduce.1 = (f32[16]{0:T(128)S(1)}, f32[16]{0:T(128)S(1)}) all-reduce(f32[16]{0:T(128)S(1)} %get-tuple-element.30, f32[16]{0:T(128)S(1)} %get-tuple-element.28), channel_id=1, replica_groups=mesh['region'=4,'col'=8] {'region','col'}, use_global_device_ids=true, to_apply=%region_11.12 | all-reduce | flops 32 | bytes 256 | tf_op jit(solution)/shard_map/psum | solution.py:77
  125.7 0.0 reduce-scatter.5.cloned.1.call-done
  125.8 0.9 multiply_reduce_fusion.2
  126.7 0.0 copy-start.4
  126.7 14.2 %all_gather.7 = f32[16,16,128]{2,1,0:T(8,128)S(1)} all-gather(f32[2,16,128]{2,1,0:T(8,128)S(1)} %multiply_subtract_fusion.2), channel_id=1, replica_groups=mesh['region'=4,'col'=8] {'col'}, dimensions={0}, use_global_device_ids=true | all-gather | bytes 147456 | tf_op jit(solution)/shard_map/all_gather | solution.py:65
  140.9 0.4 fusion.20
  141.2 5.0 %fusion.12 = f32[48,16,128]{2,1,0:T(8,128)S(1)} fusion(f32[48,128,128]{2,1,0:T(8,128)S(1)} %copy-done.1, f32[48,16,128]{2,0,1:T(8,128)S(1)} %fusion.20), kind=kOutput, calls=%fused_computation.17 | convolution fusion | flops 150994944 | bytes 3932160 | tf_op jit(solution)/shard_map/tij,tsj->tsi/dot_general | solution.py:69
  146.2 0.4 fusion
  146.7 0.8 multiply_reduce_fusion.1
  147.4 39.2 %all-reduce = (f32[16]{0:T(128)S(1)}, f32[16]{0:T(128)S(1)}) all-reduce(f32[16]{0:T(128)S(1)} %get-tuple-element.24, f32[16]{0:T(128)S(1)} %get-tuple-element.22), channel_id=1, replica_groups=mesh['region'=4,'col'=8] {'region','col'}, use_global_device_ids=true, to_apply=%region_16.17 | all-reduce | flops 32 | bytes 256 | tf_op jit(solution)/shard_map/psum | solution.py:77
  186.6 0.5 multiply_sqrt_fusion
  187.2 0.0 copy-done.4
  (6 shorter events, 0.0 us)
Async XLA Ops:
  7.2 9.2 %copy-start = (f32[32,128]{1,0:T(8,128)S(1)}, f32[32,128]{1,0:T(8,128)}, u32[]{:S(2)}) copy-start(f32[32,128]{1,0:T(8,128)} %param.20) | copy-start | bytes 49156
  7.2 8.1 %copy-start.1 = (f32[48,128,128]{2,1,0:T(8,128)S(1)}, f32[48,128,128]{2,1,0:T(8,128)}, u32[]{:S(2)}) copy-start(f32[48,128,128]{2,1,0:T(8,128)} %param.11) | copy-start | bytes 9437188
  7.2 6.9 %copy-start.7 = (s32[48]{0:T(128)S(1)}, s32[48]{0:T(128)}, u32[]{:S(2)}) copy-start(s32[48]{0:T(128)} %param.13) | copy-start | bytes 580
  7.2 53.7 %reduce-scatter.3.cloned.1.call-start = ((), (), s32[]{:S(2)}) async-start(), calls=%async_computation.2 | async-start | bytes 147456 | tf_op jit(solution)/shard_map/reduce_scatter | solution.py:62
  9.3 7.0 %copy-start.10 = (s32[16]{0:T(128)S(1)}, s32[16]{0:T(128)}, u32[]{:S(2)}) copy-start(s32[16]{0:T(128)} %param.21) | copy-start | bytes 196
  9.3 7.2 %copy-start.5 = (f32[2,128]{1,0:T(2,128)S(1)}, f32[2,128]{1,0:T(2,128)}, u32[]{:S(2)}) copy-start(f32[2,128]{1,0:T(2,128)} %param.16) | copy-start | bytes 3076
  9.3 7.3 %copy-start.9 = (f32[2,128]{1,0:T(2,128)S(1)}, f32[2,128]{1,0:T(2,128)}, u32[]{:S(2)}) copy-start(f32[2,128]{1,0:T(2,128)} %param.15) | copy-start | bytes 3076
  9.3 51.6 %copy-start.3 = (f32[2,16,128]{2,1,0:T(8,128)S(1)}, f32[2,16,128]{2,1,0:T(8,128)}, u32[]{:S(2)}) copy-start(f32[2,16,128]{2,1,0:T(8,128)} %param.18) | copy-start | bytes 49156
  9.3 51.6 %copy-start.8 = (f32[2,128]{1,0:T(2,128)S(1)}, f32[2,128]{1,0:T(2,128)}, u32[]{:S(2)}) copy-start(f32[2,128]{1,0:T(2,128)} %param.17) | copy-start | bytes 3076
  15.2 110.6 %reduce-scatter.5.cloned.1.call-start = ((), (), s32[]{:S(2)}) async-start(), calls=%async_computation.3 | async-start | bytes 147456 | tf_op jit(solution)/shard_map/reduce_scatter | solution.py:62
  15.7 65.7 %copy-start.6 = (s32[48]{0:T(128)S(1)}, s32[48]{0:T(128)}, u32[]{:S(2)}) copy-start(s32[48]{0:T(128)} %param.12) | copy-start | bytes 580
  15.7 66.1 %copy-start.2 = (f32[2,16,128]{2,1,0:T(8,128)S(1)}, f32[2,16,128]{2,1,0:T(8,128)}, u32[]{:S(2)}) copy-start(f32[2,16,128]{2,1,0:T(8,128)} %param.19) | copy-start | bytes 49156
  126.7 60.5 %copy-start.4 = (f32[2,16,128]{2,1,0:T(8,128)}, f32[2,16,128]{2,1,0:T(8,128)S(1)}, u32[]{:S(2)}) copy-start(f32[2,16,128]{2,1,0:T(8,128)S(1)} %get-tuple-element.23) | copy-start | bytes 49156
Sparse Core Ops, SparseCore 0:
  15.3 32.9 reduce-scatter.2
  86.5 30.1 reduce-scatter.4
where the time goes:
time: 195 us; the launch traced here: 194 us
  blocking collectives  149 us (76%)
  matrix products  21.7 us (11%)
  between operations  16.4 us (8%)
  other arithmetic  5.15 us (3%)
    psum x2, blocking collectives, local(): step_y = lax.psum(local_y, ('region', 'col'))  78.5 us
    psum x1, blocking collectives, local(): sq_a, sq_c, sq_b = lax.psum((local_a, local_c, local_b), ('region', 'col'))  42.3 us
    all_gather x2, blocking collectives, local(): region_point = lax.all_gather(point, 'col', axis=0, tiled=True)  28.3 us
    dot_general x2, matrix products, local(): image = jnp.einsum('tij,tsj->tsi', tiles, selected, precision=hp)  9.98 us
    dot_general x2, matrix products, local(): contrib = jnp.einsum('tij,tsi->tsj', tiles, dual_rows, precision=hp)  7.59 us
  transfers between devices with their start and end apart: 2, of which 0 were waited for; matrix products, arithmetic and copies ran while one was open for 1% of the time, Pallas kernels for 0%

commit v1 on v0

v1 whole, which is shorter than its diff:
```python
import jax
import jax.numpy as jnp
from jax import lax
from jax.sharding import PartitionSpec as P

ITERS = 2


def _pow2(n):
    return n >= 1 and (n & (n - 1)) == 0


def _exchange(x, axis, n, bit):
    return lax.ppermute(x, axis, [(i, i ^ (1 << bit)) for i in range(n)])


def _rounds(axis, sums, chunk=None):
    n = lax.axis_size(axis)
    if not _pow2(n):
        sums = [lax.psum(s, axis) for s in sums]
        if chunk is not None:
            chunk = lax.all_gather(chunk, axis, axis=0, tiled=False)
        return sums, chunk
    shapes = [s.shape for s in sums]
    sizes = [s.size for s in sums]
    me = lax.axis_index(axis)
    if chunk is not None:
        chunk = chunk[None]
    bits = n.bit_length() - 1
    for bit in range(bits):
        parts = [s.reshape(-1) for s in sums]
        if chunk is not None:
            parts.append(chunk.reshape(-1))
        flat = jnp.concatenate(parts) if len(parts) > 1 else parts[0]
        got = _exchange(flat, axis, n, bit)
        off = 0
        new_sums = []
        for shape, size, s in zip(shapes, sizes, sums):
            new_sums.append(s + got[off : off + size].reshape(shape))
            off += size
        sums = new_sums
        if chunk is not None:
            theirs = got[off:].reshape(chunk.shape)
            low = ((me >> bit) & 1) == 0
            chunk = jnp.where(
                low,
                jnp.concatenate([chunk, theirs], axis=0),
                jnp.concatenate([theirs, chunk], axis=0),
            )
    return sums, chunk


def local(
    tiles,
    tile_rows,
    tile_cols,
    tile_count,
    rhs,
    base_cost,
    upper,
    primal,
    dual,
    price_levels,
    scenario_ids,
):
    hp = lax.Precision.HIGHEST
    ntiles = tiles.shape[0]
    row_blocks = rhs.shape[0]
    own_blocks = base_cost.shape[0]
    scenarios = primal.shape[1]
    lanes = primal.shape[2]
    ncol = lax.axis_size("col")
    region_blocks = own_blocks * ncol
    devices = lax.axis_size(("region", "col"))
    me = lax.axis_index("col")
    live = (jnp.arange(ntiles, dtype=jnp.int32) < tile_count[0]).astype(jnp.float32)
    row_select = (tile_rows[:, None] == jnp.arange(row_blocks, dtype=jnp.int32)[None, :]).astype(
        jnp.float32
    )
    row_live = row_select * live[:, None]
    col_select = (tile_cols[:, None] == jnp.arange(region_blocks, dtype=jnp.int32)[None, :]).astype(
        jnp.float32
    )
    col_live = col_select * live[:, None]
    choose = (
        scenario_ids[:, None] == jnp.arange(price_levels.shape[0], dtype=jnp.int32)[None, :]
    ).astype(jnp.float32)
    factor = jnp.dot(choose, price_levels, precision=hp)
    cost = base_cost[:, None, :] * factor[None, :, :]
    local_a = jnp.sum(jnp.sum(tiles * tiles, axis=(1, 2)) * live)
    local_c = jnp.sum(cost * cost, axis=(0, 2))
    local_b = jnp.sum(rhs * rhs)
    width = scenarios * lanes

    def transposed_product(dual):
        dual_rows = jnp.dot(row_select, dual.reshape(row_blocks, width), precision=hp).reshape(
            ntiles, scenarios, lanes
        )
        contrib = jnp.einsum("tij,tsi->tsj", tiles, dual_rows, precision=hp)
        return jnp.dot(col_live.T, contrib.reshape(ntiles, width), precision=hp).reshape(
            region_blocks, scenarios, lanes
        )

    (local_a, local_c, local_b), _ = _rounds(
        "region", [local_a.reshape(1), local_c, local_b.reshape(1)]
    )
    own = jnp.concatenate([primal, base_cost[:, None, :], upper[:, None, :]], axis=1)
    partial_value = transposed_product(dual)
    (grad, sq_a, sq_c, sq_b), gathered = _rounds(
        "col", [partial_value, local_a, local_c, local_b], own
    )
    gathered = gathered.reshape(region_blocks, scenarios + 2, lanes)
    primal_reg = gathered[:, :scenarios, :]
    cost_reg = gathered[:, scenarios, :][:, None, :] * factor[None, :, :]
    upper_reg = gathered[:, scenarios + 1, :][:, None, :]
    eta = 0.5 / jnp.sqrt(sq_a[0] / (lanes * row_blocks * devices))
    weight = jnp.sqrt(sq_c) / jnp.sqrt(sq_b[0])
    for step in range(ITERS):
        if step > 0:
            (step_x, part_y), _ = _rounds("region", [local_x, local_y])
            partial_value = transposed_product(dual)
            (grad, step_y), _ = _rounds("col", [partial_value, part_y])
            weight = jnp.sqrt(weight * jnp.sqrt((step_x + 1e-06) / (step_y + 1e-06)))
        tau = (eta / weight)[None, :, None]
        sigma = (eta * weight)[None, :, None]
        new_primal = jnp.clip(primal_reg - tau * (cost_reg - grad), 0.0, upper_reg)
        point = 2.0 * new_primal - primal_reg
        selected = jnp.dot(col_select, point.reshape(region_blocks, width), precision=hp).reshape(
            ntiles, scenarios, lanes
        )
        image = jnp.einsum("tij,tsj->tsi", tiles, selected, precision=hp)
        product = jnp.dot(row_live.T, image.reshape(ntiles, width), precision=hp).reshape(
            row_blocks, scenarios, lanes
        )
        new_dual = jnp.maximum(dual + sigma * (rhs[:, None, :] - product), 0.0)
        local_x = jnp.sum((new_primal - primal_reg) ** 2, axis=(0, 2))
        local_y = jnp.sum((new_dual - dual) ** 2, axis=(0, 2))
        primal_reg, dual = (new_primal, new_dual)
    (step_x, part_y), _ = _rounds("region", [local_x, local_y])
    (step_y,), _ = _rounds("col", [part_y])
    weight = jnp.sqrt(weight * jnp.sqrt((step_x + 1e-06) / (step_y + 1e-06)))
    primal_out = lax.dynamic_slice_in_dim(primal_reg, me * own_blocks, own_blocks, axis=0)
    return (primal_out, dual, weight)


def solution(mesh):
    placed = (
        P(("region", "col"), None, None),
        P(("region", "col")),
        P(("region", "col")),
        P(("region", "col")),
        P(("region", "col"), None),
        P(("region", "col"), None),
        P(("region", "col"), None),
        P(("region", "col"), None, None),
        P(("region", "col"), None, None),
        P(),
        P(),
    )
    return jax.shard_map(
        local,
        mesh=mesh,
        in_specs=placed,
        out_specs=(P(("region", "col"), None, None), P(("region", "col"), None, None), P()),
        check_vma=False,
    )
```

time: 195 us -> 130 us (0.67)
  blocking collectives: 149 us -> 0 us
  waiting for transfers between devices: 0.07 us -> 43.2 us
  local copies, waits for them, and re-layouts: 1.42 us -> 20.1 us
  starting transfers between devices: 0.08 us -> 18.7 us
  other arithmetic: 5.15 us -> 17 us
  between operations: 16.4 us -> 9.58 us
    psum x3 -> x0, blocking collectives: 121 us -> none  [the longest x2 78.5 us: local(): step_y = lax.psum(local_y, ('region', 'col'))]
    ppermute x0 -> x15, waiting for transfers between devices: none -> 43.2 us  [_exchange(): return lax.ppermute(x, axis, [(i, i ^ 1 << bit) for i in range(n)])]
    all_gather x2 -> x0, blocking collectives: 28.3 us -> none  [local(): region_point = lax.all_gather(point, 'col', axis=0, tiled=True)]
    ppermute x0 -> x15, starting transfers between devices: none -> 18.7 us  [_exchange(): return lax.ppermute(x, axis, [(i, i ^ 1 << bit) for i in range(n)])]
    slice x0 -> x11, local copies, waits for them, and re-layouts: none -> 8.72 us  [the longest x7 6.09 us: _rounds(): new_sums.append(s + got[off:off + size].reshape(shape))]
    concatenate x0 -> x3, local copies, waits for them, and re-layouts: none -> 7.39 us  [_rounds(): flat = jnp.concatenate(parts) if len(parts) > 1 else parts[0]]
    slice x0 -> x4, other arithmetic: none -> 3.24 us  [_rounds(): new_sums.append(s + got[off:off + size].reshape(shape))]
    add x0 -> x12, other arithmetic: none -> 2.47 us  [_rounds(): new_sums.append(s + got[off:off + size].reshape(shape))]
  transfers between devices with their start and end apart: 2 -> 15, of which waited for: 0 -> 13; matrix products, arithmetic and copies ran while one was open for 1% -> 7% of each run, Pallas kernels for 0% -> 0%
where the time goes in v1:
time: 130 us; the launch traced here: 129 us
  waiting for transfers between devices  43.2 us (33%)
  local copies, waits for them, and re-layouts  20.1 us (15%)
  matrix products  20.1 us (15%)
  starting transfers between devices  18.7 us (14%)
  other arithmetic  17 us (13%)
  between operations  9.58 us (7%)
    ppermute x15, waiting for transfers between devices, _exchange(): return lax.ppermute(x, axis, [(i, i ^ 1 << bit) for i in range(n)])  43.2 us
    ppermute x15, starting transfers between devices, _exchange(): return lax.ppermute(x, axis, [(i, i ^ 1 << bit) for i in range(n)])  18.7 us
    dot_general x2, matrix products, local(): image = jnp.einsum('tij,tsj->tsi', tiles, selected, precision=hp)  10 us
    concatenate x3, local copies, waits for them, and re-layouts, _rounds(): flat = jnp.concatenate(parts) if len(parts) > 1 else parts[0]  7.39 us
    slice x7, local copies, waits for them, and re-layouts, _rounds(): new_sums.append(s + got[off:off + size].reshape(shape))  6.09 us
    dot_general x2, matrix products, transposed_product(): contrib = jnp.einsum('tij,tsi->tsj', tiles, dual_rows, precision=hp)  5.75 us
    slice x4, other arithmetic, _rounds(): new_sums.append(s + got[off:off + size].reshape(shape))  3.24 us
    reduce_sum x2, other arithmetic, local(): local_a = jnp.sum(jnp.sum(tiles * tiles, axis=(1, 2)) * live)  2.98 us
  transfers between devices with their start and end apart: 15, of which 13 were waited for; matrix products, arithmetic and copies ran while one was open for 7% of the time, Pallas kernels for 0%

profile of v1, /device:TPU:0, one launch (start us, length us, event | category | flops | bytes accessed | tf_op | source)
XLA Modules:
  0.0 128.7 jit_solution(10598872442955021088)
XLA Ops:
  1.5 1.5 %multiply_reduce_fusion.6 = f32[]{:T(128)} fusion(f32[2,128]{1,0:T(2,128)} %param.15), kind=kLoop, calls=%fused_computation.95 | loop fusion | flops 511 | bytes 1028 | tf_op jit(solution)/shard_map/reduce_sum | solution.py:92
  3.0 2.4 %multiply_reduce_fusion = f32[48]{0:T(128)S(1)} fusion(f32[48,128,128]{2,1,0:T(8,128)} %param.11), kind=kLoop, calls=%fused_computation | loop fusion | flops 1572816 | bytes 3145920 | tf_op jit(solution)/shard_map/reduce_sum | solution.py:90
  5.4 0.6 fusion.67
  6.3 1.4 %pad_maximum_fusion.4 = f32[18]{0:T(128)S(1)} fusion(f32[1]{0:T(128)} %bitcast.8, f32[16]{0:T(128)S(1)} %multiply_reduce_fusion.5, f32[1]{0:T(128)} %bitcast.7), kind=kLoop, calls=%fused_computation.107 | loop fusion | flops 36 | bytes 144 | tf_op jit(solution)/shard_map/concatenate | solution.py:34
  7.8 2.9 %collective-permute-start = (f32[18]{0:T(128)S(1)}, f32[18]{0:T(128)S(1)}, u32[]{:S(2)}, u32[]{:S(2)}) collective-permute-start(f32[18]{0:T(128)S(1)} %pad_maximum_fusion.4), channel_id=1, source_target_pairs={{0,8},{8,0},{16,24},{24,16},{1,9},{9,1},{17,25},{25,17},{2,10},{10... | collective-permute-start | bytes 224 | tf_op jit(solution)/shard_map/ppermute | solution.py:14
  11.1 2.9 %fusion.22 = f32[48,16,128]{2,1,0:T(8,128)S(1)} fusion(f32[48,128,128]{2,1,0:T(8,128)S(1)} %copy-done.1, f32[48,16,128]{2,0,1:T(8,128)S(1)} %fusion.42), kind=kOutput, calls=%fused_computation.27 | convolution fusion | flops 150994944 | bytes 3932160 | tf_op jit(solution)/shard_map/tij,tsi->tsj/dot_general | solution.py:99
  14.5 0.6 fusion.95
  17.8 1.5 %collective-permute-start.1 = (f32[18]{0:T(128)S(1)}, f32[18]{0:T(128)S(1)}, u32[]{:S(2)}, u32[]{:S(2)}) collective-permute-start(f32[18]{0:T(128)S(1)} %pad_maximum_fusion.5), channel_id=1, source_target_pairs={{0,16},{8,24},{16,0},{24,8},{1,17},{9,25},{17,1},{25,9},{2,18},{10... | collective-permute-start | bytes 224 | tf_op jit(solution)/shard_map/ppermute | solution.py:14
  19.3 2.0 %collective-permute-done.1 = f32[18]{0:T(128)S(1)} collective-permute-done((f32[18]{0:T(128)S(1)}, f32[18]{0:T(128)S(1)}, u32[]{:S(2)}, u32[]{:S(2)}) %collective-permute-start.1) | collective-permute-done | bytes 104 | tf_op jit(solution)/shard_map/ppermute | solution.py:14
  21.3 0.6 fusion.94
  23.3 0.8 concatenate.60
  24.0 1.7 %collective-permute-done.2 = f32[37394]{0:T(1024)} collective-permute-done((f32[37394]{0:T(1024)}, f32[37394]{0:T(1024)}, u32[]{:S(2)}, u32[]{:S(2)}) %collective-permute-start.2) | collective-permute-done | bytes 149608 | tf_op jit(solution)/shard_map/ppermute | solution.py:14
  25.7 1.3 %fusion.91 = (f32[1]{0:T(128)}, f32[1]{0:T(128)}) fusion(f32[37394]{0:T(1024)} %collective-permute-done.2), kind=kLoop, calls=%fused_computation.152 | loop fusion | bytes 16 | tf_op jit(solution)/shard_map/slice | solution.py:39
  28.4 0.8 slice.152
  29.2 0.6 select_n.43
  29.8 1.3 slice_add_fusion.5
  31.1 1.6 %fusion.90 = (f32[32768]{0:T(1024)}, f32[32768]{0:T(1024)S(1)}) fusion(f32[37394]{0:T(1024)} %collective-permute-done.2, f32[32768]{0:T(1024)S(1)} %bitcast.156), kind=kLoop, calls=%fused_computation.151 | loop fusion | flops 32768 | bytes 524288 | tf_op jit(solution)/shard_map/slice | solution.py:39
  32.7 1.5 %concatenate.63 = f32[42002]{0:T(1024)} concatenate(f32[32768]{0:T(1024)S(1)} %get-tuple-element.36, f32[1]{0:T(128)S(6)} %add.147, f32[16]{0:T(128)} %slice_add_fusion.5, f32[1]{0:T(128)S(6)} %add.149, f32[9216]{0:T(1024)} %select_n.43), dimensions={0} | concatenate | bytes 336016 | tf_op jit(solution)/shard_map/concatenate | solution.py:34
  34.2 1.6 %collective-permute-start.3 = (f32[42002]{0:T(1024)}, f32[42002]{0:T(1024)}, u32[]{:S(2)}, u32[]{:S(2)}) collective-permute-start(f32[42002]{0:T(1024)} %concatenate.63), channel_id=1, source_target_pairs={{0,2},{1,3},{2,0},{3,1},{4,6},{5,7},{6,4},{7,5},{8,10},{9,11},{10,... | collective-permute-start | bytes 504032 | tf_op jit(solution)/shard_map/ppermute | solution.py:14
  35.8 5.2 %collective-permute-done.3 = f32[42002]{0:T(1024)} collective-permute-done((f32[42002]{0:T(1024)}, f32[42002]{0:T(1024)}, u32[]{:S(2)}, u32[]{:S(2)}) %collective-permute-start.3) | collective-permute-done | bytes 168040 | tf_op jit(solution)/shard_map/ppermute | solution.py:14
  40.9 1.3 %fusion.89 = (f32[1]{0:T(128)}, f32[1]{0:T(128)}) fusion(f32[42002]{0:T(1024)} %collective-permute-done.3), kind=kLoop, calls=%fused_computation.150 | loop fusion | bytes 16 | tf_op jit(solution)/shard_map/slice | solution.py:39
  43.5 0.9 slice.157
  44.4 0.6 reshape.130
  45.0 0.9 maximum_select_fusion.1
  45.9 0.7 select_n.45
  46.6 0.8 slice_add_fusion.4
  47.3 1.6 %fusion.88 = (f32[32768]{0:T(1024)}, f32[32768]{0:T(1024)}) fusion(f32[42002]{0:T(1024)} %collective-permute-done.3, f32[32768]{0:T(1024)S(1)} %get-tuple-element.36), kind=kLoop, calls=%fused_computation.149 | loop fusion | flops 32768 | bytes 524288 | tf_op jit(solution)/shard_map/slice | solution.py:39
  49.0 5.1 %concatenate.66 = f32[51218]{0:T(1024)} concatenate(f32[32768]{0:T(1024)} %get-tuple-element.32, f32[1]{0:T(128)S(6)} %add.151, f32[16]{0:T(128)S(1)} %slice_add_fusion.4, f32[1]{0:T(128)S(6)} %add.153, f32[18432]{0:T(1024)} %select_n.45), dimensions={0} | concatenate | bytes 409744 | tf_op jit(solution)/shard_map/concatenate | solution.py:34
  54.1 2.6 %collective-permute-start.4 = (f32[51218]{0:T(1024)}, f32[51218]{0:T(1024)}, u32[]{:S(2)}, u32[]{:S(2)}) collective-permute-start(f32[51218]{0:T(1024)} %concatenate.66), channel_id=1, source_target_pairs={{0,4},{1,5},{2,6},{3,7},{4,0},{5,1},{6,2},{7,3},{8,12},{9,13},{10,... | collective-permute-start | bytes 614624 | tf_op jit(solution)/shard_map/ppermute | solution.py:14
  56.7 9.5 %collective-permute-done.4 = f32[51218]{0:T(1024)} collective-permute-done((f32[51218]{0:T(1024)}, f32[51218]{0:T(1024)}, u32[]{:S(2)}, u32[]{:S(2)}) %collective-permute-start.4) | collective-permute-done | bytes 204904 | tf_op jit(solution)/shard_map/ppermute | solution.py:14
  66.1 1.3 %fusion.86 = (f32[1]{0:T(128)}, f32[1]{0:T(128)}) fusion(f32[51218]{0:T(1024)} %collective-permute-done.4), kind=kLoop, calls=%fused_computation.147 | loop fusion | bytes 16 | tf_op jit(solution)/shard_map/slice | solution.py:39
  68.8 1.0 slice.162
  69.8 0.6 reshape.131
  70.5 1.1 maximum_select_fusion
  71.6 0.9 slice.169
  72.5 0.8 broadcast_multiply_fusion.1
  73.3 1.2 multiply_reduce_fusion.2
  74.5 1.0 fusion.39
  75.5 5.0 %fusion.20 = f32[48,16,128]{2,1,0:T(8,128)S(1)} fusion(f32[48,128,128]{2,1,0:T(8,128)S(1)} %copy-done.1, f32[48,16,128]{2,0,1:T(8,128)S(1)} %fusion.39), kind=kOutput, calls=%fused_computation.25 | convolution fusion | flops 150994944 | bytes 3932160 | tf_op jit(solution)/shard_map/tij,tsj->tsi/dot_general | solution.py:131
  80.6 0.6 multiply_reduce_fusion.4
  81.3 0.7 collective-permute-start.5
  82.3 2.9 %fusion.18 = f32[48,16,128]{2,1,0:T(8,128)S(1)} fusion(f32[48,128,128]{2,1,0:T(8,128)S(1)} %copy-done.1, f32[48,16,128]{2,0,1:T(8,128)S(1)} %fusion.44), kind=kOutput, calls=%fused_computation.23 | convolution fusion | flops 150994944 | bytes 3932160 | tf_op jit(solution)/shard_map/tij,tsi->tsj/dot_general | solution.py:99
  85.2 0.4 fusion.6
  85.8 1.4 %collective-permute-start.6 = (f32[32]{0:T(128)S(1)}, f32[32]{0:T(128)S(1)}, u32[]{:S(2)}, u32[]{:S(2)}) collective-permute-start(f32[32]{0:T(128)S(1)} %pad_maximum_fusion.7), channel_id=1, source_target_pairs={{0,16},{8,24},{16,0},{24,8},{1,17},{9,25},{17,1},{25,9},{2,18},{10... | collective-permute-start | bytes 392 | tf_op jit(solution)/shard_map/ppermute | solution.py:14
  87.2 2.1 %collective-permute-done.6 = f32[32]{0:T(128)S(1)} collective-permute-done((f32[32]{0:T(128)S(1)}, f32[32]{0:T(128)S(1)}, u32[]{:S(2)}, u32[]{:S(2)}) %collective-permute-start.6) | collective-permute-done | bytes 160 | tf_op jit(solution)/shard_map/ppermute | solution.py:14
  89.5 1.3 %collective-permute-done.7 = f32[32784]{0:T(1024)S(1)} collective-permute-done((f32[32784]{0:T(1024)S(1)}, f32[32784]{0:T(1024)S(1)}, u32[]{:S(2)}, u32[]{:S(2)}) %collective-permute-start.7) | collective-permute-done | bytes 131168 | tf_op jit(solution)/shard_map/ppermute | solution.py:14
  90.9 0.6 collective-permute-start.8
  91.5 5.1 %collective-permute-done.8 = f32[32784]{0:T(1024)S(1)} collective-permute-done((f32[32784]{0:T(1024)S(1)}, f32[32784]{0:T(1024)S(1)}, u32[]{:S(2)}, u32[]{:S(2)}) %collective-permute-start.8) | collective-permute-done | bytes 131168 | tf_op jit(solution)/shard_map/ppermute | solution.py:14
  96.7 2.2 %collective-permute-start.9 = (f32[32784]{0:T(1024)S(1)}, f32[32784]{0:T(1024)S(1)}, u32[]{:S(2)}, u32[]{:S(2)}) collective-permute-start(f32[32784]{0:T(1024)S(1)} %pad_maximum_fusion.2), channel_id=1, source_target_pairs={{0,4},{1,5},{2,6},{3,7},{4,0},{5,1},{6,2},{7,3},{8,12},{9,13},{10,... | collective-permute-start | bytes 393416 | tf_op jit(solution)/shard_map/ppermute | solution.py:14
  98.9 6.4 %collective-permute-done.9 = f32[32784]{0:T(1024)S(1)} collective-permute-done((f32[32784]{0:T(1024)S(1)}, f32[32784]{0:T(1024)S(1)}, u32[]{:S(2)}, u32[]{:S(2)}) %collective-permute-start.9) | collective-permute-done | bytes 131168 | tf_op jit(solution)/shard_map/ppermute | solution.py:14
  106.0 5.0 %fusion.16 = f32[48,16,128]{2,1,0:T(8,128)S(1)} fusion(f32[48,128,128]{2,1,0:T(8,128)S(1)} %copy-done.1, f32[48,16,128]{2,0,1:T(8,128)S(1)} %fusion.36), kind=kOutput, calls=%fused_computation.21 | convolution fusion | flops 150994944 | bytes 3932160 | tf_op jit(solution)/shard_map/tij,tsj->tsi/dot_general | solution.py:131
  111.0 0.6 multiply_reduce_fusion.3
  111.7 1.4 %collective-permute-start.10 = (f32[32]{0:T(128)S(1)}, f32[32]{0:T(128)S(1)}, u32[]{:S(2)}, u32[]{:S(2)}) collective-permute-start(f32[32]{0:T(128)S(1)} %pad_maximum_fusion.8), channel_id=1, source_target_pairs={{0,8},{8,0},{16,24},{24,16},{1,9},{9,1},{17,25},{25,17},{2,10},{10... | collective-permute-start | bytes 392 | tf_op jit(solution)/shard_map/ppermute | solution.py:14
  113.1 2.2 %collective-permute-done.10 = f32[32]{0:T(128)S(1)} collective-permute-done((f32[32]{0:T(128)S(1)}, f32[32]{0:T(128)S(1)}, u32[]{:S(2)}, u32[]{:S(2)}) %collective-permute-start.10) | collective-permute-done | bytes 160 | tf_op jit(solution)/shard_map/ppermute | solution.py:14
  115.4 1.4 %collective-permute-start.11 = (f32[32]{0:T(128)S(1)}, f32[32]{0:T(128)S(1)}, u32[]{:S(2)}, u32[]{:S(2)}) collective-permute-start(f32[32]{0:T(128)S(1)} %pad_maximum_fusion.9), channel_id=1, source_target_pairs={{0,16},{8,24},{16,0},{24,8},{1,17},{9,25},{17,1},{25,9},{2,18},{10... | collective-permute-start | bytes 392 | tf_op jit(solution)/shard_map/ppermute | solution.py:14
  116.8 2.2 %collective-permute-done.11 = f32[32]{0:T(128)S(1)} collective-permute-done((f32[32]{0:T(128)S(1)}, f32[32]{0:T(128)S(1)}, u32[]{:S(2)}, u32[]{:S(2)}) %collective-permute-start.11) | collective-permute-done | bytes 160 | tf_op jit(solution)/shard_map/ppermute | solution.py:14
  119.0 1.1 collective-permute-done.12
  120.2 0.5 collective-permute-start.13
  120.7 0.6 constant_dynamic-slice_fusion
  121.3 2.4 %collective-permute-done.13 = f32[16]{0:T(128)S(1)} collective-permute-done((f32[16]{0:T(128)S(1)}, f32[16]{0:T(128)S(1)}, u32[]{:S(2)}, u32[]{:S(2)}) %collective-permute-start.13) | collective-permute-done | bytes 96 | tf_op jit(solution)/shard_map/ppermute | solution.py:14
  123.7 1.9 %collective-permute-start.14 = (f32[16]{0:T(128)S(1)}, f32[16]{0:T(128)S(1)}, u32[]{:S(2)}, u32[]{:S(2)}) collective-permute-start(f32[16]{0:T(128)S(1)} %add.183), channel_id=1, source_target_pairs={{0,4},{1,5},{2,6},{3,7},{4,0},{5,1},{6,2},{7,3},{8,12},{9,13},{10,... | collective-permute-start | bytes 200 | tf_op jit(solution)/shard_map/ppermute | solution.py:14
  125.6 0.6 copy.52
  126.2 2.0 %collective-permute-done.14 = f32[16]{0:T(128)S(1)} collective-permute-done((f32[16]{0:T(128)S(1)}, f32[16]{0:T(128)S(1)}, u32[]{:S(2)}, u32[]{:S(2)}) %collective-permute-start.14) | collective-permute-done | bytes 96 | tf_op jit(solution)/shard_map/ppermute | solution.py:14
  128.1 0.5 multiply_sqrt_fusion
  (87 shorter events, 3.4 us)
Async XLA Ops:
  0.6 5.4 %copy-start = (f32[32,128]{1,0:T(8,128)S(1)}, f32[32,128]{1,0:T(8,128)}, u32[]{:S(2)}) copy-start(f32[32,128]{1,0:T(8,128)} %param.20) | copy-start | bytes 49156
  0.6 10.5 %copy-start.1 = (f32[48,128,128]{2,1,0:T(8,128)S(1)}, f32[48,128,128]{2,1,0:T(8,128)}, u32[]{:S(2)}) copy-start(f32[48,128,128]{2,1,0:T(8,128)} %param.11) | copy-start | bytes 9437188
  0.7 5.4 %copy-start.19 = (s32[16]{0:T(128)S(1)}, s32[16]{0:T(128)}, u32[]{:S(2)}) copy-start(s32[16]{0:T(128)} %param.21) | copy-start | bytes 196
  0.7 5.5 %copy-start.16 = (f32[2,128]{1,0:T(2,128)S(1)}, f32[2,128]{1,0:T(2,128)}, u32[]{:S(2)}) copy-start(f32[2,128]{1,0:T(2,128)} %param.16) | copy-start | bytes 3076
  0.7 10.0 %copy-start.9 = (s32[48]{0:T(128)S(1)}, s32[48]{0:T(128)}, u32[]{:S(2)}) copy-start(s32[48]{0:T(128)} %param.12) | copy-start | bytes 580
  0.7 10.0 %copy-start.6 = (f32[2,16,128]{2,1,0:T(8,128)S(1)}, f32[2,16,128]{2,1,0:T(8,128)}, u32[]{:S(2)}) copy-start(f32[2,16,128]{2,1,0:T(8,128)} %param.19) | copy-start | bytes 49156
  3.0 11.0 %copy-start.8 = (f32[2,16,128]{2,1,0:T(8,128)S(1)}, f32[2,16,128]{2,1,0:T(8,128)}, u32[]{:S(2)}) copy-start(f32[2,16,128]{2,1,0:T(8,128)} %param.18) | copy-start | bytes 49156
  3.0 11.0 %copy-start.18 = (f32[2,128]{1,0:T(2,128)S(1)}, f32[2,128]{1,0:T(2,128)}, u32[]{:S(2)}) copy-start(f32[2,128]{1,0:T(2,128)} %param.17) | copy-start | bytes 3076
  3.0 11.0 %copy-start.11 = (s32[48]{0:T(128)S(1)}, s32[48]{0:T(128)}, u32[]{:S(2)}) copy-start(s32[48]{0:T(128)} %param.13) | copy-start | bytes 580
  6.2 4.5 %copy-start.4 = (f32[16,128]{1,0:T(8,128)}, f32[16,128]{1,0:T(8,128)S(1)}, u32[]{:S(2)}) copy-start(f32[16,128]{1,0:T(8,128)S(1)} %fusion.51) | copy-start | bytes 24580
  7.8 6.7 %collective-permute-start = (f32[18]{0:T(128)S(1)}, f32[18]{0:T(128)S(1)}, u32[]{:S(2)}, u32[]{:S(2)}) collective-permute-start(f32[18]{0:T(128)S(1)} %pad_maximum_fusion.4), channel_id=1, source_target_pairs={{0,8},{8,0},{16,24},{24,16},{1,9},{9,1},{17,25},{25,17},{2,10},{10... | collective-permute-start | bytes 224 | tf_op jit(solution)/shard_map/ppermute | solution.py:14
  10.7 8.6 %copy-start.13 = (f32[48]{0:T(128)}, f32[48]{0:T(128)S(1)}, u32[]{:S(2)}) copy-start(f32[48]{0:T(128)S(1)} %compare_convert_fusion) | copy-start | bytes 580
  17.8 3.5 %collective-permute-start.1 = (f32[18]{0:T(128)S(1)}, f32[18]{0:T(128)S(1)}, u32[]{:S(2)}, u32[]{:S(2)}) collective-permute-start(f32[18]{0:T(128)S(1)} %pad_maximum_fusion.5), channel_id=1, source_target_pairs={{0,16},{8,24},{16,0},{24,8},{1,17},{9,25},{17,1},{25,9},{2,18},{10... | collective-permute-start | bytes 224 | tf_op jit(solution)/shard_map/ppermute | solution.py:14
  24.0 1.7 %collective-permute-start.2 = (f32[37394]{0:T(1024)}, f32[37394]{0:T(1024)}, u32[]{:S(2)}, u32[]{:S(2)}) collective-permute-start(f32[37394]{0:T(1024)} %concatenate.60), channel_id=1, source_target_pairs={{0,1},{1,0},{2,3},{3,2},{4,5},{5,4},{6,7},{7,6},{8,9},{9,8},{10,11... | collective-permute-start | bytes 448736 | tf_op jit(solution)/shard_map/ppermute | solution.py:14
  29.2 0.6 copy-start.3
  34.2 6.7 %collective-permute-start.3 = (f32[42002]{0:T(1024)}, f32[42002]{0:T(1024)}, u32[]{:S(2)}, u32[]{:S(2)}) collective-permute-start(f32[42002]{0:T(1024)} %concatenate.63), channel_id=1, source_target_pairs={{0,2},{1,3},{2,0},{3,1},{4,6},{5,7},{6,4},{7,5},{8,10},{9,11},{10,... | collective-permute-start | bytes 504032 | tf_op jit(solution)/shard_map/ppermute | solution.py:14
  45.9 23.9 %copy-start.2 = (f32[4,2,18,128]{3,2,1,0:T(8,128)}, f32[4,2,18,128]{3,2,1,0:T(8,128)S(1)}, u32[]{:S(2)}) copy-start(f32[4,2,18,128]{3,2,1,0:T(8,128)S(1)} %maximum_select_fusion.1) | copy-start | bytes 221188
  47.3 9.3 %copy-start.17 = (f32[16]{0:T(128)}, f32[16]{0:T(128)S(1)}, u32[]{:S(2)}) copy-start(f32[16]{0:T(128)S(1)} %slice_add_fusion.4) | copy-start | bytes 196
  54.1 12.1 %collective-permute-start.4 = (f32[51218]{0:T(1024)}, f32[51218]{0:T(1024)}, u32[]{:S(2)}, u32[]{:S(2)}) collective-permute-start(f32[51218]{0:T(1024)} %concatenate.66), channel_id=1, source_target_pairs={{0,4},{1,5},{2,6},{3,7},{4,0},{5,1},{6,2},{7,3},{8,12},{9,13},{10,... | collective-permute-start | bytes 614624 | tf_op jit(solution)/shard_map/ppermute | solution.py:14
  70.5 10.1 %copy-start.7 = (f32[2,16,128]{2,1,0:T(8,128)S(1)}, f32[2,16,128]{2,1,0:T(8,128)}, u32[]{:S(2)}) copy-start(f32[2,16,128]{2,1,0:T(8,128)} %param.19) | copy-start | bytes 49156
  70.5 10.1 %copy-start.10 = (s32[48]{0:T(128)S(1)}, s32[48]{0:T(128)}, u32[]{:S(2)}) copy-start(s32[48]{0:T(128)} %param.12) | copy-start | bytes 580
  70.5 10.1 %copy-start.14 = (f32[48]{0:T(128)S(1)}, f32[48]{0:T(128)}, u32[]{:S(2)}) copy-start(f32[48]{0:T(128)} %copy-done.13) | copy-start | bytes 580
  70.5 10.1 %copy-start.15 = (f32[2,128]{1,0:T(2,128)S(1)}, f32[2,128]{1,0:T(2,128)}, u32[]{:S(2)}) copy-start(f32[2,128]{1,0:T(2,128)} %param.15) | copy-start | bytes 3076
  80.5 4.7 %copy-start.12 = (s32[48]{0:T(128)S(1)}, s32[48]{0:T(128)}, u32[]{:S(2)}) copy-start(s32[48]{0:T(128)} %param.13) | copy-start | bytes 580
  81.3 4.4 %collective-permute-start.5 = (f32[32]{0:T(128)S(1)}, f32[32]{0:T(128)S(1)}, u32[]{:S(2)}, u32[]{:S(2)}) collective-permute-start(f32[32]{0:T(128)S(1)} %pad_maximum_fusion.6), channel_id=1, source_target_pairs={{0,8},{8,0},{16,24},{24,16},{1,9},{9,1},{17,25},{25,17},{2,10},{10... | collective-permute-start | bytes 392 | tf_op jit(solution)/shard_map/ppermute | solution.py:14
  82.3 23.1 %copy-start.5 = (f32[16,128]{1,0:T(8,128)S(1)}, f32[16,128]{1,0:T(8,128)}, u32[]{:S(2)}) copy-start(f32[16,128]{1,0:T(8,128)} %copy-done.4) | copy-start | bytes 24580
  85.8 3.5 %collective-permute-start.6 = (f32[32]{0:T(128)S(1)}, f32[32]{0:T(128)S(1)}, u32[]{:S(2)}, u32[]{:S(2)}) collective-permute-start(f32[32]{0:T(128)S(1)} %pad_maximum_fusion.7), channel_id=1, source_target_pairs={{0,16},{8,24},{16,0},{24,8},{1,17},{9,25},{17,1},{25,9},{2,18},{10... | collective-permute-start | bytes 392 | tf_op jit(solution)/shard_map/ppermute | solution.py:14
  89.4 1.4 %collective-permute-start.7 = (f32[32784]{0:T(1024)S(1)}, f32[32784]{0:T(1024)S(1)}, u32[]{:S(2)}, u32[]{:S(2)}) collective-permute-start(f32[32784]{0:T(1024)S(1)} %pad_maximum_fusion), channel_id=1, source_target_pairs={{0,1},{1,0},{2,3},{3,2},{4,5},{5,4},{6,7},{7,6},{8,9},{9,8},{10,11... | collective-permute-start | bytes 393416 | tf_op jit(solution)/shard_map/ppermute | solution.py:14
  90.9 5.7 %collective-permute-start.8 = (f32[32784]{0:T(1024)S(1)}, f32[32784]{0:T(1024)S(1)}, u32[]{:S(2)}, u32[]{:S(2)}) collective-permute-start(f32[32784]{0:T(1024)S(1)} %pad_maximum_fusion.1), channel_id=1, source_target_pairs={{0,2},{1,3},{2,0},{3,1},{4,6},{5,7},{6,4},{7,5},{8,10},{9,11},{10,... | collective-permute-start | bytes 393416 | tf_op jit(solution)/shard_map/ppermute | solution.py:14
  96.7 8.7 %collective-permute-start.9 = (f32[32784]{0:T(1024)S(1)}, f32[32784]{0:T(1024)S(1)}, u32[]{:S(2)}, u32[]{:S(2)}) collective-permute-start(f32[32784]{0:T(1024)S(1)} %pad_maximum_fusion.2), channel_id=1, source_target_pairs={{0,4},{1,5},{2,6},{3,7},{4,0},{5,1},{6,2},{7,3},{8,12},{9,13},{10,... | collective-permute-start | bytes 393416 | tf_op jit(solution)/shard_map/ppermute | solution.py:14
  111.7 3.5 %collective-permute-start.10 = (f32[32]{0:T(128)S(1)}, f32[32]{0:T(128)S(1)}, u32[]{:S(2)}, u32[]{:S(2)}) collective-permute-start(f32[32]{0:T(128)S(1)} %pad_maximum_fusion.8), channel_id=1, source_target_pairs={{0,8},{8,0},{16,24},{24,16},{1,9},{9,1},{17,25},{25,17},{2,10},{10... | collective-permute-start | bytes 392 | tf_op jit(solution)/shard_map/ppermute | solution.py:14
  115.4 3.5 %collective-permute-start.11 = (f32[32]{0:T(128)S(1)}, f32[32]{0:T(128)S(1)}, u32[]{:S(2)}, u32[]{:S(2)}) collective-permute-start(f32[32]{0:T(128)S(1)} %pad_maximum_fusion.9), channel_id=1, source_target_pairs={{0,16},{8,24},{16,0},{24,8},{1,17},{9,25},{17,1},{25,9},{2,18},{10... | collective-permute-start | bytes 392 | tf_op jit(solution)/shard_map/ppermute | solution.py:14
  119.0 1.1 collective-permute-start.12
  120.2 3.5 %collective-permute-start.13 = (f32[16]{0:T(128)S(1)}, f32[16]{0:T(128)S(1)}, u32[]{:S(2)}, u32[]{:S(2)}) collective-permute-start(f32[16]{0:T(128)S(1)} %add.182), channel_id=1, source_target_pairs={{0,2},{1,3},{2,0},{3,1},{4,6},{5,7},{6,4},{7,5},{8,10},{9,11},{10,... | collective-permute-start | bytes 200 | tf_op jit(solution)/shard_map/ppermute | solution.py:14
  123.7 4.4 %collective-permute-start.14 = (f32[16]{0:T(128)S(1)}, f32[16]{0:T(128)S(1)}, u32[]{:S(2)}, u32[]{:S(2)}) collective-permute-start(f32[16]{0:T(128)S(1)} %add.183), channel_id=1, source_target_pairs={{0,4},{1,5},{2,6},{3,7},{4,0},{5,1},{6,2},{7,3},{8,12},{9,13},{10,... | collective-permute-start | bytes 200 | tf_op jit(solution)/shard_map/ppermute | solution.py:14

commit v2 on v1

--- a/solution.py
+++ b/solution.py
@@ -14,40 +14,40 @@
     return lax.ppermute(x, axis, [(i, i ^ (1 << bit)) for i in range(n)])
 
 
-def _rounds(axis, sums, chunk=None):
+def _rounds(axis, total, own=None):
     n = lax.axis_size(axis)
     if not _pow2(n):
-        sums = [lax.psum(s, axis) for s in sums]
-        if chunk is not None:
-            chunk = lax.all_gather(chunk, axis, axis=0, tiled=False)
-        return sums, chunk
-    shapes = [s.shape for s in sums]
-    sizes = [s.size for s in sums]
+        total = lax.psum(total, axis)
+        if own is not None:
+            own = lax.all_gather(own, axis, axis=0, tiled=True)
+        return total, own
     me = lax.axis_index(axis)
-    if chunk is not None:
-        chunk = chunk[None]
-    bits = n.bit_length() - 1
-    for bit in range(bits):
-        parts = [s.reshape(-1) for s in sums]
-        if chunk is not None:
-            parts.append(chunk.reshape(-1))
-        flat = jnp.concatenate(parts) if len(parts) > 1 else parts[0]
-        got = _exchange(flat, axis, n, bit)
-        off = 0
-        new_sums = []
-        for shape, size, s in zip(shapes, sizes, sums):
-            new_sums.append(s + got[off : off + size].reshape(shape))
-            off += size
-        sums = new_sums
-        if chunk is not None:
-            theirs = got[off:].reshape(chunk.shape)
-            low = ((me >> bit) & 1) == 0
-            chunk = jnp.where(
-                low,
-                jnp.concatenate([chunk, theirs], axis=0),
-                jnp.concatenate([theirs, chunk], axis=0),
-            )
-    return sums, chunk
+    rows = total.shape[0]
+    buf = None
+    if own is not None:
+        g = own.shape[0]
+        buf = jnp.zeros((n * g, own.shape[1]), own.dtype)
+        buf = lax.dynamic_update_slice_in_dim(buf, own, me * g, axis=0)
+    for bit in range(n.bit_length() - 1):
+        if buf is None:
+            got = _exchange(total, axis, n, bit)
+            total = total + got
+            continue
+        span = (1 << bit) * g
+        mine = lax.dynamic_slice_in_dim(buf, ((me >> bit) << bit) * g, span, axis=0)
+        got = _exchange(jnp.concatenate([total, mine], axis=0), axis, n, bit)
+        total = total + got[:rows]
+        theirs = ((me ^ (1 << bit)) >> bit) << bit
+        buf = lax.dynamic_update_slice_in_dim(buf, got[rows:], theirs * g, axis=0)
+    return total, buf
+
+
+def _pack(lanes, *vectors):
+    small = jnp.zeros((8, lanes), jnp.float32)
+    for row, v in enumerate(vectors):
+        v = jnp.reshape(v, (-1,))
+        small = small.at[row, : v.shape[0]].set(v)
+    return small
 
 
 def local(
@@ -101,25 +101,45 @@
             region_blocks, scenarios, lanes
         )
 
-    (local_a, local_c, local_b), _ = _rounds(
-        "region", [local_a.reshape(1), local_c, local_b.reshape(1)]
+    small, _ = _rounds("region", _pack(lanes, local_c, local_a, local_b))
+    own_rows = own_blocks * (scenarios + 2)
+    pad = -own_rows % 8
+    own = jnp.concatenate(
+        [
+            primal.reshape(own_blocks * scenarios, lanes),
+            base_cost,
+            upper,
+            jnp.zeros((pad, lanes), jnp.float32),
+        ],
+        axis=0,
     )
-    own = jnp.concatenate([primal, base_cost[:, None, :], upper[:, None, :]], axis=1)
-    partial_value = transposed_product(dual)
-    (grad, sq_a, sq_c, sq_b), gathered = _rounds(
-        "col", [partial_value, local_a, local_c, local_b], own
+    grad_rows = region_blocks * scenarios
+    partial_value = transposed_product(dual).reshape(grad_rows, lanes)
+    summed, gathered = _rounds("col", jnp.concatenate([partial_value, small], axis=0), own)
+    grad = summed[:grad_rows].reshape(region_blocks, scenarios, lanes)
+    sq_c = summed[grad_rows, :scenarios]
+    sq_a = summed[grad_rows + 1, 0]
+    sq_b = summed[grad_rows + 2, 0]
+    gathered = gathered.reshape(ncol, own_rows + pad, lanes)
+    primal_reg = gathered[:, : own_blocks * scenarios].reshape(region_blocks, scenarios, lanes)
+    base_reg = gathered[:, own_blocks * scenarios : own_blocks * (scenarios + 1)].reshape(
+        region_blocks, lanes
     )
-    gathered = gathered.reshape(region_blocks, scenarios + 2, lanes)
-    primal_reg = gathered[:, :scenarios, :]
-    cost_reg = gathered[:, scenarios, :][:, None, :] * factor[None, :, :]
-    upper_reg = gathered[:, scenarios + 1, :][:, None, :]
-    eta = 0.5 / jnp.sqrt(sq_a[0] / (lanes * row_blocks * devices))
-    weight = jnp.sqrt(sq_c) / jnp.sqrt(sq_b[0])
+    upper_reg = gathered[:, own_blocks * (scenarios + 1) : own_rows].reshape(region_blocks, lanes)
+    cost_reg = base_reg[:, None, :] * factor[None, :, :]
+    upper_reg = upper_reg[:, None, :]
+    eta = 0.5 / jnp.sqrt(sq_a / (lanes * row_blocks * devices))
+    weight = jnp.sqrt(sq_c) / jnp.sqrt(sq_b)
     for step in range(ITERS):
         if step > 0:
-            (step_x, part_y), _ = _rounds("region", [local_x, local_y])
-            partial_value = transposed_product(dual)
-            (grad, step_y), _ = _rounds("col", [partial_value, part_y])
+            steps, _ = _rounds("region", _pack(lanes, local_x, local_y))
+            partial_value = transposed_product(dual).reshape(grad_rows, lanes)
+            summed, _ = _rounds(
+                "col", jnp.concatenate([partial_value, _pack(lanes, steps[1, :scenarios])], axis=0)
+            )
+            grad = summed[:grad_rows].reshape(region_blocks, scenarios, lanes)
+            step_x = steps[0, :scenarios]
+            step_y = summed[grad_rows, :scenarios]
             weight = jnp.sqrt(weight * jnp.sqrt((step_x + 1e-06) / (step_y + 1e-06)))
         tau = (eta / weight)[None, :, None]
         sigma = (eta * weight)[None, :, None]
@@ -136,8 +156,10 @@
         local_x = jnp.sum((new_primal - primal_reg) ** 2, axis=(0, 2))
         local_y = jnp.sum((new_dual - dual) ** 2, axis=(0, 2))
         primal_reg, dual = (new_primal, new_dual)
-    (step_x, part_y), _ = _rounds("region", [local_x, local_y])
-    (step_y,), _ = _rounds("col", [part_y])
+    steps, _ = _rounds("region", _pack(lanes, local_x, local_y))
+    summed, _ = _rounds("col", _pack(lanes, steps[1, :scenarios]))
+    step_x = steps[0, :scenarios]
+    step_y = summed[0, :scenarios]
     weight = jnp.sqrt(weight * jnp.sqrt((step_x + 1e-06) / (step_y + 1e-06)))
     primal_out = lax.dynamic_slice_in_dim(primal_reg, me * own_blocks, own_blocks, axis=0)
     return (primal_out, dual, weight)

time: 130 us -> 136 us (1.046)
  other arithmetic: 17 us -> 24.7 us
  between operations: 9.58 us -> 3.19 us
  matrix products: 20.1 us -> 25.3 us
  waiting for transfers between devices: 43.2 us -> 40 us
  local copies, waits for them, and re-layouts: 20.1 us -> 22.7 us
    slice x11 -> x6, local copies, waits for them, and re-layouts: 8.72 us -> 0.59 us  [the longest x1 0.55 us: local(): sq_b = summed[grad_rows + 2, 0]]
    concatenate x3 -> x1, local copies, waits for them, and re-layouts: 7.39 us -> 0.08 us  [local(): jnp.concatenate([primal.reshape(own_blocks * scenarios, lanes), base_cost...]
    scatter x0 -> x8, local copies, waits for them, and re-layouts: none -> 6.52 us  [_pack(): small = small.at[row, :v.shape[0]].set(v)]
    mul x0 -> x7, local copies, waits for them, and re-layouts: none -> 4.09 us  [the longest x6 3.33 us: local(): new_primal = jnp.clip(primal_reg - tau * (cost_reg - grad), 0.0, upper_reg)]
    add x12 -> x15, other arithmetic: 2.47 us -> 6.26 us  [the longest x3 4.2 us: _rounds(): total = total + got[:rows]]
    ppermute x15, waiting for transfers between devices: 43.2 us -> 40 us  [_exchange(): return lax.ppermute(x, axis, [(i, i ^ 1 << bit) for i in range(n)])]
    unnamed x45 -> x67, local copies, waits for them, and re-layouts: 0.82 us -> 3.32 us
    dynamic_update_slice x0 -> x3, local copies, waits for them, and re-layouts: none -> 2.41 us  [_rounds(): buf = lax.dynamic_update_slice_in_dim(buf, got[rows:], theirs * g, axis=0)]
  transfers between devices with their start and end apart: 15 -> 15, of which waited for: 13 -> 13; matrix products, arithmetic and copies ran while one was open for 7% -> 12% of each run, Pallas kernels for 0% -> 0%
where the time goes in v2:
time: 136 us; the launch traced here: 135 us
  waiting for transfers between devices  40 us (29%)
  matrix products  25.3 us (19%)
  other arithmetic  24.7 us (18%)
  local copies, waits for them, and re-layouts  22.7 us (17%)
  starting transfers between devices  18.9 us (14%)
  between operations  3.19 us (2%)
    ppermute x15, waiting for transfers between devices, _exchange(): return lax.ppermute(x, axis, [(i, i ^ 1 << bit) for i in range(n)])  40 us
    ppermute x15, starting transfers between devices, _exchange(): return lax.ppermute(x, axis, [(i, i ^ 1 << bit) for i in range(n)])  18.9 us
    dot_general x2, matrix products, local(): image = jnp.einsum('tij,tsj->tsi', tiles, selected, precision=hp)  10 us
    scatter x8, local copies, waits for them, and re-layouts, _pack(): small = small.at[row, :v.shape[0]].set(v)  6.52 us
    dot_general x2, matrix products, transposed_product(): contrib = jnp.einsum('tij,tsi->tsj', tiles, dual_rows, precision=hp)  5.74 us
    add x3, other arithmetic, _rounds(): total = total + got[:rows]  4.2 us
    concatenate x3, other arithmetic, _rounds(): got = _exchange(jnp.concatenate([total, mine], axis=0), axis, n, bit)  3.86 us
    mul x6, local copies, waits for them, and re-layouts, local(): new_primal = jnp.clip(primal_reg - tau * (cost_reg - grad), 0.0, upper_reg)  3.33 us
  transfers between devices with their start and end apart: 15, of which 13 were waited for; matrix products, arithmetic and copies ran while one was open for 12% of the time, Pallas kernels for 0%

profile of v2, /device:TPU:0, one launch (start us, length us, event | category | flops | bytes accessed | tf_op | source)
XLA Modules:
  0.0 134.8 jit_solution(14193023964615895112)
XLA Ops:
  1.5 1.4 %multiply_reduce_fusion.5 = f32[]{:T(128)} fusion(f32[2,128]{1,0:T(2,128)} %param.33), kind=kLoop, calls=%fused_computation.116 | loop fusion | flops 511 | bytes 1028 | tf_op jit(solution)/shard_map/reduce_sum | solution.py:92
  2.9 2.3 %multiply_reduce_fusion = f32[48]{0:T(128)S(1)} fusion(f32[48,128,128]{2,1,0:T(8,128)} %param.29), kind=kLoop, calls=%fused_computation | loop fusion | flops 1572816 | bytes 3145920 | tf_op jit(solution)/shard_map/reduce_sum | solution.py:90
  7.5 2.0 %scatter.31 = f32[8,128]{1,0:T(8,128)} dynamic-update-slice(f32[8,128]{1,0:T(8,128)} %scatter.30, f32[1,1]{1,0:T(1,128)} %bitcast.6, s32[]{:T(128)} %constant.222.clone.1, s32[]{:T(128)} %constant.220.clone.1) | dynamic-update-slice | bytes 12 | tf_op jit(solution)/shard_map/scatter | solution.py:49
  9.4 1.9 %scatter.34 = f32[8,128]{1,0:T(8,128)} dynamic-update-slice(f32[8,128]{1,0:T(8,128)} %scatter.31, f32[1,1]{1,0:T(1,128)} %bitcast.7, s32[]{:T(128)} %constant.223.clone.1, s32[]{:T(128)} %constant.220.clone.1) | dynamic-update-slice | bytes 12 | tf_op jit(solution)/shard_map/scatter | solution.py:49
  11.3 2.9 %collective-permute-start = (f32[8,128]{1,0:T(8,128)}, f32[8,128]{1,0:T(8,128)}, u32[]{:S(2)}, u32[]{:S(2)}) collective-permute-start(f32[8,128]{1,0:T(8,128)} %scatter.34), channel_id=1, source_target_pairs={{0,8},{8,0},{16,24},{24,16},{1,9},{9,1},{17,25},{25,17},{2,10},{10... | collective-permute-start | bytes 12296 | tf_op jit(solution)/shard_map/ppermute | solution.py:14
  15.2 2.9 %fusion.22 = f32[48,16,128]{2,1,0:T(8,128)S(1)} fusion(f32[48,128,128]{2,1,0:T(8,128)S(1)} %copy-done.1, f32[48,16,128]{2,0,1:T(8,128)S(1)} %fusion.42), kind=kOutput, calls=%fused_computation.27 | convolution fusion | flops 150994944 | bytes 3932160 | tf_op jit(solution)/shard_map/tij,tsi->tsj/dot_general | solution.py:99
  18.2 1.8 %fusion.9 = f32[16,2048]{1,0:T(8,128)} fusion(f32[6,8,16,128]{3,2,1,0:T(8,128)S(1)} %bitcast.211, f32[48]{0:T(128)} %compare_convert_fusion, s32[48]{0:T(128)} %param.31), kind=kOutput, calls=%fused_computation.14 | convolution fusion | flops 18875904 | bytes 524672 | tf_op jit(solution)/shard_map/dot_general | solution.py:100
  19.9 0.8 maximum_dynamic-update-slice_fusion
  20.8 0.7 add.134
  21.5 1.5 %collective-permute-start.1 = (f32[8,128]{1,0:T(8,128)S(1)}, f32[8,128]{1,0:T(8,128)S(1)}, u32[]{:S(2)}, u32[]{:S(2)}) collective-permute-start(f32[8,128]{1,0:T(8,128)S(1)} %add.134), channel_id=1, source_target_pairs={{0,16},{8,24},{16,0},{24,8},{1,17},{9,25},{17,1},{25,9},{2,18},{10... | collective-permute-start | bytes 12296 | tf_op jit(solution)/shard_map/ppermute | solution.py:14
  23.0 0.9 reshape_reshape.6
  23.9 1.2 collective-permute-done.1
  25.1 0.7 pad_maximum_fusion.2
  25.8 1.7 %collective-permute-done.2 = f32[304,128]{1,0:T(8,128)} collective-permute-done((f32[304,128]{1,0:T(8,128)}, f32[304,128]{1,0:T(8,128)}, u32[]{:S(2)}, u32[]{:S(2)}) %collective-permute-start.2) | collective-permute-done | bytes 155680 | tf_op jit(solution)/shard_map/ppermute | solution.py:14
  27.5 0.7 slice_dynamic-update-slice_fusion.2
  28.2 1.6 %slice_add_fusion.2 = f32[264,128]{1,0:T(8,128)} fusion(f32[304,128]{1,0:T(8,128)} %collective-permute-done.2, f32[8,128]{1,0:T(8,128)S(1)} %add.135, f32[256,128]{1,0:T(8,128)S(1)} %reshape_reshape.6), kind=kLoop, calls=%fused_computation.38 | loop fusion | flops 67584 | bytes 405504 | tf_op jit(solution)/shard_map/add | solution.py:39
  29.8 1.6 %pad_maximum_fusion.1 = f32[344,128]{1,0:T(8,128)} fusion(f32[80,128]{1,0:T(8,128)S(1)} %constant_dynamic-slice_fusion.2, f32[264,128]{1,0:T(8,128)} %slice_add_fusion.2), kind=kLoop, calls=%fused_computation.32 | loop fusion | flops 44032 | bytes 352256 | tf_op jit(solution)/shard_map/concatenate | solution.py:38
  31.4 1.6 %collective-permute-start.3 = (f32[344,128]{1,0:T(8,128)}, f32[344,128]{1,0:T(8,128)}, u32[]{:S(2)}, u32[]{:S(2)}) collective-permute-start(f32[344,128]{1,0:T(8,128)} %pad_maximum_fusion.1), channel_id=1, source_target_pairs={{0,2},{1,3},{2,0},{3,1},{4,6},{5,7},{6,4},{7,5},{8,10},{9,11},{10,... | collective-permute-start | bytes 528392 | tf_op jit(solution)/shard_map/ppermute | solution.py:14
  32.9 5.3 %collective-permute-done.3 = f32[344,128]{1,0:T(8,128)} collective-permute-done((f32[344,128]{1,0:T(8,128)}, f32[344,128]{1,0:T(8,128)}, u32[]{:S(2)}, u32[]{:S(2)}) %collective-permute-start.3) | collective-permute-done | bytes 176160 | tf_op jit(solution)/shard_map/ppermute | solution.py:14
  38.2 0.8 slice_dynamic-update-slice_fusion.1
  39.0 1.6 %slice_add_fusion.1 = f32[264,128]{1,0:T(8,128)} fusion(f32[264,128]{1,0:T(8,128)} %slice_add_fusion.2, f32[344,128]{1,0:T(8,128)} %collective-permute-done.3), kind=kLoop, calls=%fused_computation.37 | loop fusion | flops 33792 | bytes 405504 | tf_op jit(solution)/shard_map/add | solution.py:39
  40.6 1.6 %pad_maximum_fusion = f32[424,128]{1,0:T(8,128)} fusion(f32[160,128]{1,0:T(8,128)S(1)} %constant_dynamic-slice_fusion.1, f32[264,128]{1,0:T(8,128)} %slice_add_fusion.1), kind=kLoop, calls=%fused_computation.29 | loop fusion | flops 54272 | bytes 434176 | tf_op jit(solution)/shard_map/concatenate | solution.py:38
  42.2 2.6 %collective-permute-start.4 = (f32[424,128]{1,0:T(8,128)}, f32[424,128]{1,0:T(8,128)}, u32[]{:S(2)}, u32[]{:S(2)}) collective-permute-start(f32[424,128]{1,0:T(8,128)} %pad_maximum_fusion), channel_id=1, source_target_pairs={{0,4},{1,5},{2,6},{3,7},{4,0},{5,1},{6,2},{7,3},{8,12},{9,13},{10,... | collective-permute-start | bytes 651272 | tf_op jit(solution)/shard_map/ppermute | solution.py:14
  44.8 9.8 %collective-permute-done.4 = f32[424,128]{1,0:T(8,128)} collective-permute-done((f32[424,128]{1,0:T(8,128)}, f32[424,128]{1,0:T(8,128)}, u32[]{:S(2)}, u32[]{:S(2)}) %collective-permute-start.4) | collective-permute-done | bytes 217120 | tf_op jit(solution)/shard_map/ppermute | solution.py:14
  54.7 1.0 slice_add_fusion
  57.7 1.3 multiply_bitcast_fusion.2
  59.7 0.9 slice_dynamic-update-slice_fusion
  60.6 0.7 reshape.435
  61.3 0.7 subtract_multiply_fusion
  62.7 1.7 %fusion.88 = (f32[8,32,128]{2,1,0:T(8,128)}, f32[8,32]{1,0:T(8,128)S(1)}) fusion(f32[8,40,128]{2,1,0:T(8,128)} %bitcast.208, f32[8,32,128]{2,1,0:T(8,128)S(1)} %bitcast.201, f32[32]{0:T(128)S(1)} %mul.231, f32[8,32,128]{2,1,0:T(8,128)S(1)} %bitcast.216, f32[8,32,128]{2,1,0:T(8,128)S(1)} %bitcast.203), kind=kLoop, calls=%fused_computation.142 | loop fusion | flops 261888 | bytes 656512 | tf_op jit(solution)/shard_map/slice | solution.py:124
  65.1 0.9 reshape.434
  66.1 0.8 mul.226
  67.5 1.3 fusion.33
  68.8 5.0 %fusion.20 = f32[48,16,128]{2,1,0:T(8,128)S(1)} fusion(f32[48,128,128]{2,1,0:T(8,128)S(1)} %copy-done.1, f32[48,16,128]{2,0,1:T(8,128)S(1)} %fusion.33), kind=kOutput, calls=%fused_computation.25 | convolution fusion | flops 150994944 | bytes 3932160 | tf_op jit(solution)/shard_map/tij,tsj->tsi/dot_general | solution.py:151
  73.8 1.6 %multiply_reduce_fusion.3 = (f32[16]{0:T(128)}, f32[2,16,128]{2,0,1:T(2,128)}) fusion(f32[2,16,128]{2,1,0:T(8,128)S(1)} %copy-done.12, f32[48]{0:T(128)S(1)} %copy-done.19, s32[48]{0:T(128)S(1)} %copy-done.16, f32[2,128]{1,0:T(2,128)S(1)} %copy-done.22, f32[16]{0:T(128)S(1)} %copy-done.27, f32[6,8,16,128]{3,2,1,0:T(8,128)S(1)} %bitcast.213), kind=kOutput, calls=%fused_computation.84 | convolution fusion | flops 2388144 | bytes 427520 | tf_op jit(solution)/shard_map/dot_general | solution.py:152
  75.5 1.3 scatter.36
  76.8 0.8 collective-permute-start.5
  77.5 1.1 fusion.50
  78.6 2.9 %fusion.18 = f32[48,16,128]{2,1,0:T(8,128)S(1)} fusion(f32[48,128,128]{2,1,0:T(8,128)S(1)} %copy-done.1, f32[48,16,128]{2,0,1:T(8,128)S(1)} %fusion.50), kind=kOutput, calls=%fused_computation.23 | convolution fusion | flops 150994944 | bytes 3932160 | tf_op jit(solution)/shard_map/tij,tsi->tsj/dot_general | solution.py:99
  82.1 1.4 %collective-permute-start.6 = (f32[8,128]{1,0:T(8,128)}, f32[8,128]{1,0:T(8,128)}, u32[]{:S(2)}, u32[]{:S(2)}) collective-permute-start(f32[8,128]{1,0:T(8,128)} %add.146), channel_id=1, source_target_pairs={{0,16},{8,24},{16,0},{24,8},{1,17},{9,25},{17,1},{25,9},{2,18},{10... | collective-permute-start | bytes 12296 | tf_op jit(solution)/shard_map/ppermute | solution.py:14
  83.5 1.1 fusion.6
  84.6 0.9 reshape_reshape.7
  86.1 0.7 add.147
  86.8 1.3 collective-permute-done.7
  88.8 5.1 %collective-permute-done.8 = f32[264,128]{1,0:T(8,128)S(1)} collective-permute-done((f32[264,128]{1,0:T(8,128)S(1)}, f32[264,128]{1,0:T(8,128)S(1)}, u32[]{:S(2)}, u32[]{:S(2)}) %collective-permute-start.8) | collective-permute-done | bytes 135200 | tf_op jit(solution)/shard_map/ppermute | solution.py:14
  93.9 2.2 %collective-permute-start.9 = (f32[264,128]{1,0:T(8,128)S(1)}, f32[264,128]{1,0:T(8,128)S(1)}, u32[]{:S(2)}, u32[]{:S(2)}) collective-permute-start(f32[264,128]{1,0:T(8,128)S(1)} %add.150), channel_id=1, source_target_pairs={{0,4},{1,5},{2,6},{3,7},{4,0},{5,1},{6,2},{7,3},{8,12},{9,13},{10,... | collective-permute-start | bytes 405512 | tf_op jit(solution)/shard_map/ppermute | solution.py:14
  96.2 6.4 %collective-permute-done.9 = f32[264,128]{1,0:T(8,128)S(1)} collective-permute-done((f32[264,128]{1,0:T(8,128)S(1)}, f32[264,128]{1,0:T(8,128)S(1)}, u32[]{:S(2)}, u32[]{:S(2)}) %collective-permute-start.9) | collective-permute-done | bytes 135200 | tf_op jit(solution)/shard_map/ppermute | solution.py:14
  102.6 1.2 multiply_bitcast_fusion
  104.4 0.7 broadcast_bitcast_fusion
  105.6 1.3 mul.264
  107.0 0.7 reshape.441
  107.7 1.8 %fusion.26 = f32[8,32]{1,0:T(8,128)} fusion(f32[8,32,128]{2,1,0:T(8,128)S(1)} %bitcast.214, f32[8,32,128]{2,1,0:T(8,128)S(1)} %bitcast.202, f32[32]{0:T(128)} %mul.264, f32[32]{0:T(128)} %copy-done.31, f32[8,40,128]{2,1,0:T(8,128)} %bitcast.209, f32[8,32,128]{2,1,0:T(8,128)S(1)} %bitcast.205, f32[8,32,128]{2,1,0:T(8,128)} %bitcast.217), kind=kLoop, calls=%fused_computation.41 | loop fusion | flops 425728 | bytes 656640 | tf_op jit(solution)/shard_map/reduce_sum | solution.py:156
  109.5 0.8 reduce_sum.95
  110.3 1.5 %fusion.30 = f32[48,16,128]{2,0,1:T(8,128)S(1)} fusion(s32[48]{0:T(128)} %param.31, f32[16,2048]{1,0:T(8,128)} %reshape.441, f32[2,8,16,128]{3,2,1,0:T(8,128)S(1)} %bitcast.206, f32[2,8,16,128]{3,2,1,0:T(8,128)} %bitcast.219, f32[16,2048]{1,0:T(8,128)} %copy-done.4, f32[16,2048]{1,0:T(8,128)} %reshape.435, f32[2048]{0:T(1024)} %broadcast_bitcast_fusion, ...), kind=kOutput, calls=%fused_computation.48 | convolution fusion | flops 19301120 | bytes 1073344 | tf_op jit(solution)/shard_map/dot_general | solution.py:148
  111.8 5.0 %fusion.16 = f32[48,16,128]{2,1,0:T(8,128)S(1)} fusion(f32[48,128,128]{2,1,0:T(8,128)S(1)} %copy-done.1, f32[48,16,128]{2,0,1:T(8,128)S(1)} %fusion.30), kind=kOutput, calls=%fused_computation.21 | convolution fusion | flops 150994944 | bytes 3932160 | tf_op jit(solution)/shard_map/tij,tsj->tsi/dot_general | solution.py:151
  117.6 1.4 %collective-permute-start.10 = (f32[8,128]{1,0:T(8,128)S(1)}, f32[8,128]{1,0:T(8,128)S(1)}, u32[]{:S(2)}, u32[]{:S(2)}) collective-permute-start(f32[8,128]{1,0:T(8,128)S(1)} %scatter.41), channel_id=1, source_target_pairs={{0,8},{8,0},{16,24},{24,16},{1,9},{9,1},{17,25},{25,17},{2,10},{10... | collective-permute-start | bytes 12296 | tf_op jit(solution)/shard_map/ppermute | solution.py:14
  119.1 2.3 %collective-permute-done.10 = f32[8,128]{1,0:T(8,128)S(1)} collective-permute-done((f32[8,128]{1,0:T(8,128)S(1)}, f32[8,128]{1,0:T(8,128)S(1)}, u32[]{:S(2)}, u32[]{:S(2)}) %collective-permute-start.10) | collective-permute-done | bytes 4128 | tf_op jit(solution)/shard_map/ppermute | solution.py:14
  121.3 1.4 %collective-permute-start.11 = (f32[8,128]{1,0:T(8,128)S(1)}, f32[8,128]{1,0:T(8,128)S(1)}, u32[]{:S(2)}, u32[]{:S(2)}) collective-permute-start(f32[8,128]{1,0:T(8,128)S(1)} %add.155), channel_id=1, source_target_pairs={{0,16},{8,24},{16,0},{24,8},{1,17},{9,25},{17,1},{25,9},{2,18},{10... | collective-permute-start | bytes 12296 | tf_op jit(solution)/shard_map/ppermute | solution.py:14
  122.7 2.2 %collective-permute-done.11 = f32[8,128]{1,0:T(8,128)S(1)} collective-permute-done((f32[8,128]{1,0:T(8,128)S(1)}, f32[8,128]{1,0:T(8,128)S(1)}, u32[]{:S(2)}, u32[]{:S(2)}) %collective-permute-start.11) | collective-permute-done | bytes 4128 | tf_op jit(solution)/shard_map/ppermute | solution.py:14
  125.0 1.2 collective-permute-done.12
  126.7 0.7 constant_dynamic-slice_fusion
  127.4 2.4 %collective-permute-done.13 = f32[8,128]{1,0:T(8,128)S(1)} collective-permute-done((f32[8,128]{1,0:T(8,128)S(1)}, f32[8,128]{1,0:T(8,128)S(1)}, u32[]{:S(2)}, u32[]{:S(2)}) %collective-permute-start.13) | collective-permute-done | bytes 4128 | tf_op jit(solution)/shard_map/ppermute | solution.py:14
  129.8 1.9 %collective-permute-start.14 = (f32[8,128]{1,0:T(8,128)S(1)}, f32[8,128]{1,0:T(8,128)S(1)}, u32[]{:S(2)}, u32[]{:S(2)}) collective-permute-start(f32[8,128]{1,0:T(8,128)S(1)} %fusion.96), channel_id=1, source_target_pairs={{0,4},{1,5},{2,6},{3,7},{4,0},{5,1},{6,2},{7,3},{8,12},{9,13},{10,... | collective-permute-start | bytes 12296 | tf_op jit(solution)/shard_map/ppermute | solution.py:14
  131.7 1.4 %fusion.47 = f32[2,16,128]{2,1,0:T(8,128)} fusion(f32[16,16,128]{2,1,0:T(8,128)S(1)} %bitcast.215, s32[]{:T(128)S(6)} %select_n.31, f32[16,16,128]{2,1,0:T(8,128)} %copy-done.3, f32[16,16,128]{2,1,0:T(8,128)} %get-tuple-element.134, f32[16,16,128]{2,1,0:T(8,128)} %bitcast.220, f32[16]{0:T(128)S(1)} %copy-done.26, f32[2,128]{1,0:T(2,128)S(1)} %constant_dynamic-slice_fusion), kind=kLoop, calls=%fused_computation.77 | loop fusion | flops 32768 | bytes 83012 | tf_op jit(solution)/shard_map/jit(clip)/min | solution.py:146
  (120 shorter events, 13.0 us)
Async XLA Ops:
  0.6 5.3 %copy-start = (f32[32,128]{1,0:T(8,128)S(1)}, f32[32,128]{1,0:T(8,128)}, u32[]{:S(2)}) copy-start(f32[32,128]{1,0:T(8,128)} %param.38) | copy-start | bytes 49156
  0.6 14.6 %copy-start.1 = (f32[48,128,128]{2,1,0:T(8,128)S(1)}, f32[48,128,128]{2,1,0:T(8,128)}, u32[]{:S(2)}) copy-start(f32[48,128,128]{2,1,0:T(8,128)} %param.29) | copy-start | bytes 9437188
  0.7 5.3 %copy-start.32 = (s32[16]{0:T(128)S(1)}, s32[16]{0:T(128)}, u32[]{:S(2)}) copy-start(s32[16]{0:T(128)} %param.39) | copy-start | bytes 196
  0.7 6.1 %copy-start.24 = (f32[2,128]{1,0:T(2,128)S(1)}, f32[2,128]{1,0:T(2,128)}, u32[]{:S(2)}) copy-start(f32[2,128]{1,0:T(2,128)} %param.34) | copy-start | bytes 3076
  0.7 14.2 %copy-start.15 = (s32[48]{0:T(128)S(1)}, s32[48]{0:T(128)}, u32[]{:S(2)}) copy-start(s32[48]{0:T(128)} %param.30) | copy-start | bytes 580
  0.7 14.1 %copy-start.11 = (f32[2,16,128]{2,1,0:T(8,128)S(1)}, f32[2,16,128]{2,1,0:T(8,128)}, u32[]{:S(2)}) copy-start(f32[2,16,128]{2,1,0:T(8,128)} %param.37) | copy-start | bytes 49156
  6.1 0.6 copy-start.8
  11.3 9.5 %collective-permute-start = (f32[8,128]{1,0:T(8,128)}, f32[8,128]{1,0:T(8,128)}, u32[]{:S(2)}, u32[]{:S(2)}) collective-permute-start(f32[8,128]{1,0:T(8,128)} %scatter.34), channel_id=1, source_target_pairs={{0,8},{8,0},{16,24},{24,16},{1,9},{9,1},{17,25},{25,17},{2,10},{10... | collective-permute-start | bytes 12296 | tf_op jit(solution)/shard_map/ppermute | solution.py:14
  19.9 41.4 %copy-start.9 = (f32[16,128]{1,0:T(8,128)S(1)}, f32[16,128]{1,0:T(8,128)}, u32[]{:S(2)}) copy-start(f32[16,128]{1,0:T(8,128)} %copy-done.8) | copy-start | bytes 24580
  21.5 3.6 %collective-permute-start.1 = (f32[8,128]{1,0:T(8,128)S(1)}, f32[8,128]{1,0:T(8,128)S(1)}, u32[]{:S(2)}, u32[]{:S(2)}) collective-permute-start(f32[8,128]{1,0:T(8,128)S(1)} %add.134), channel_id=1, source_target_pairs={{0,16},{8,24},{16,0},{24,8},{1,17},{9,25},{17,1},{25,9},{2,18},{10... | collective-permute-start | bytes 12296 | tf_op jit(solution)/shard_map/ppermute | solution.py:14
  25.7 1.7 %collective-permute-start.2 = (f32[304,128]{1,0:T(8,128)}, f32[304,128]{1,0:T(8,128)}, u32[]{:S(2)}, u32[]{:S(2)}) collective-permute-start(f32[304,128]{1,0:T(8,128)} %pad_maximum_fusion.2), channel_id=1, source_target_pairs={{0,1},{1,0},{2,3},{3,2},{4,5},{5,4},{6,7},{7,6},{8,9},{9,8},{10,11... | collective-permute-start | bytes 466952 | tf_op jit(solution)/shard_map/ppermute | solution.py:14
  31.4 6.8 %collective-permute-start.3 = (f32[344,128]{1,0:T(8,128)}, f32[344,128]{1,0:T(8,128)}, u32[]{:S(2)}, u32[]{:S(2)}) collective-permute-start(f32[344,128]{1,0:T(8,128)} %pad_maximum_fusion.1), channel_id=1, source_target_pairs={{0,2},{1,3},{2,0},{3,1},{4,6},{5,7},{6,4},{7,5},{8,10},{9,11},{10,... | collective-permute-start | bytes 528392 | tf_op jit(solution)/shard_map/ppermute | solution.py:14
  42.2 12.4 %collective-permute-start.4 = (f32[424,128]{1,0:T(8,128)}, f32[424,128]{1,0:T(8,128)}, u32[]{:S(2)}, u32[]{:S(2)}) collective-permute-start(f32[424,128]{1,0:T(8,128)} %pad_maximum_fusion), channel_id=1, source_target_pairs={{0,4},{1,5},{2,6},{3,7},{4,0},{5,1},{6,2},{7,3},{8,12},{9,13},{10,... | collective-permute-start | bytes 651272 | tf_op jit(solution)/shard_map/ppermute | solution.py:14
  55.7 0.7 copy-start.6
  59.7 5.4 %copy-start.31 = (f32[32]{0:T(128)}, f32[32]{0:T(128)S(1)}, u32[]{:S(2)}) copy-start(f32[32]{0:T(128)S(1)} %mul.231) | copy-start | bytes 388
  60.6 1.5 %copy-start.2 = (f32[320,128]{1,0:T(8,128)}, f32[320,128]{1,0:T(8,128)S(1)}, u32[]{:S(2)}) copy-start(f32[320,128]{1,0:T(8,128)S(1)} %slice_dynamic-update-slice_fusion) | copy-start | bytes 491524
  60.6 4.4 %copy-start.10 = (f32[8,2,128]{2,1,0:T(2,128)}, f32[8,2,128]{2,1,0:T(2,128)S(1)}, u32[]{:S(2)}) copy-start(f32[8,2,128]{2,1,0:T(2,128)S(1)} %get-tuple-element.130) | copy-start | bytes 24580
  60.6 4.4 %copy-start.13 = (f32[8,2,128]{2,1,0:T(2,128)}, f32[8,2,128]{2,1,0:T(2,128)S(1)}, u32[]{:S(2)}) copy-start(f32[8,2,128]{2,1,0:T(2,128)S(1)} %get-tuple-element.129) | copy-start | bytes 24580
  62.1 0.6 copy-start.3
  66.0 15.5 %copy-start.4 = (f32[16,2048]{1,0:T(8,128)}, f32[16,2048]{1,0:T(8,128)S(1)}, u32[]{:S(2)}) copy-start(f32[16,2048]{1,0:T(8,128)S(1)} %reshape.434) | copy-start | bytes 393220
  66.0 7.8 %copy-start.12 = (f32[2,16,128]{2,1,0:T(8,128)S(1)}, f32[2,16,128]{2,1,0:T(8,128)}, u32[]{:S(2)}) copy-start(f32[2,16,128]{2,1,0:T(8,128)} %param.37) | copy-start | bytes 49156
  66.0 7.8 %copy-start.16 = (s32[48]{0:T(128)S(1)}, s32[48]{0:T(128)}, u32[]{:S(2)}) copy-start(s32[48]{0:T(128)} %param.30) | copy-start | bytes 580
  66.0 7.8 %copy-start.19 = (f32[48]{0:T(128)S(1)}, f32[48]{0:T(128)}, u32[]{:S(2)}) copy-start(f32[48]{0:T(128)} %compare_convert_fusion) | copy-start | bytes 580
  66.1 7.8 %copy-start.22 = (f32[2,128]{1,0:T(2,128)S(1)}, f32[2,128]{1,0:T(2,128)}, u32[]{:S(2)}) copy-start(f32[2,128]{1,0:T(2,128)} %param.33) | copy-start | bytes 3076
  66.1 7.8 %copy-start.27 = (f32[16]{0:T(128)S(1)}, f32[16]{0:T(128)}, u32[]{:S(2)}) copy-start(f32[16]{0:T(128)} %get-tuple-element.125) | copy-start | bytes 196
  66.8 0.6 copy-start.5
  76.8 4.8 %copy-start.14 = (f32[8,128]{1,0:T(8,128)S(1)}, f32[8,128]{1,0:T(8,128)}, u32[]{:S(2)}) copy-start(f32[8,128]{1,0:T(8,128)} %scatter.36) | copy-start | bytes 12292
  76.8 6.7 %copy-start.18 = (s32[48]{0:T(128)S(1)}, s32[48]{0:T(128)}, u32[]{:S(2)}) copy-start(s32[48]{0:T(128)} %param.31) | copy-start | bytes 580
  76.8 6.7 %copy-start.20 = (f32[48]{0:T(128)S(1)}, f32[48]{0:T(128)}, u32[]{:S(2)}) copy-start(f32[48]{0:T(128)} %compare_convert_fusion) | copy-start | bytes 580
  76.8 4.7 %collective-permute-start.5 = (f32[8,128]{1,0:T(8,128)}, f32[8,128]{1,0:T(8,128)S(1)}, u32[]{:S(2)}, u32[]{:S(2)}) collective-permute-start(f32[8,128]{1,0:T(8,128)} %scatter.36), channel_id=1, source_target_pairs={{0,8},{8,0},{16,24},{24,16},{1,9},{9,1},{17,25},{25,17},{2,10},{10... | collective-permute-start | bytes 12296 | tf_op jit(solution)/shard_map/ppermute | solution.py:14
  82.1 3.9 %collective-permute-start.6 = (f32[8,128]{1,0:T(8,128)}, f32[8,128]{1,0:T(8,128)}, u32[]{:S(2)}, u32[]{:S(2)}) collective-permute-start(f32[8,128]{1,0:T(8,128)} %add.146), channel_id=1, source_target_pairs={{0,16},{8,24},{16,0},{24,8},{1,17},{9,25},{17,1},{25,9},{2,18},{10... | collective-permute-start | bytes 12296 | tf_op jit(solution)/shard_map/ppermute | solution.py:14
  86.8 1.4 %collective-permute-start.7 = (f32[264,128]{1,0:T(8,128)S(1)}, f32[264,128]{1,0:T(8,128)S(1)}, u32[]{:S(2)}, u32[]{:S(2)}) collective-permute-start(f32[264,128]{1,0:T(8,128)S(1)} %select_maximum_fusion), channel_id=1, source_target_pairs={{0,1},{1,0},{2,3},{3,2},{4,5},{5,4},{6,7},{7,6},{8,9},{9,8},{10,11... | collective-permute-start | bytes 405512 | tf_op jit(solution)/shard_map/ppermute | solution.py:14
  88.2 5.7 %collective-permute-start.8 = (f32[264,128]{1,0:T(8,128)S(1)}, f32[264,128]{1,0:T(8,128)S(1)}, u32[]{:S(2)}, u32[]{:S(2)}) collective-permute-start(f32[264,128]{1,0:T(8,128)S(1)} %fusion.87), channel_id=1, source_target_pairs={{0,2},{1,3},{2,0},{3,1},{4,6},{5,7},{6,4},{7,5},{8,10},{9,11},{10,... | collective-permute-start | bytes 405512 | tf_op jit(solution)/shard_map/ppermute | solution.py:14
  93.9 8.7 %collective-permute-start.9 = (f32[264,128]{1,0:T(8,128)S(1)}, f32[264,128]{1,0:T(8,128)S(1)}, u32[]{:S(2)}, u32[]{:S(2)}) collective-permute-start(f32[264,128]{1,0:T(8,128)S(1)} %add.150), channel_id=1, source_target_pairs={{0,4},{1,5},{2,6},{3,7},{4,0},{5,1},{6,2},{7,3},{8,12},{9,13},{10,... | collective-permute-start | bytes 405512 | tf_op jit(solution)/shard_map/ppermute | solution.py:14
  103.8 0.6 copy-start.29
  104.4 0.7 copy-start.25
  109.4 7.4 %copy-start.7 = (f32[2,16,128]{2,0,1:T(2,128)S(1)}, f32[2,16,128]{2,0,1:T(2,128)}, u32[]{:S(2)}) copy-start(f32[2,16,128]{2,0,1:T(2,128)} %get-tuple-element.137) | copy-start | bytes 49156
  109.4 7.4 %copy-start.17 = (s32[48]{0:T(128)S(1)}, s32[48]{0:T(128)}, u32[]{:S(2)}) copy-start(s32[48]{0:T(128)} %param.30) | copy-start | bytes 580
  109.4 7.4 %copy-start.21 = (f32[48]{0:T(128)S(1)}, f32[48]{0:T(128)}, u32[]{:S(2)}) copy-start(f32[48]{0:T(128)} %compare_convert_fusion) | copy-start | bytes 580
  109.4 7.4 %copy-start.23 = (f32[2,128]{1,0:T(2,128)S(1)}, f32[2,128]{1,0:T(2,128)}, u32[]{:S(2)}) copy-start(f32[2,128]{1,0:T(2,128)} %param.33) | copy-start | bytes 3076
  109.4 7.4 %copy-start.28 = (f32[16]{0:T(128)S(1)}, f32[16]{0:T(128)}, u32[]{:S(2)}) copy-start(f32[16]{0:T(128)} %get-tuple-element.123) | copy-start | bytes 196
  109.4 22.2 %copy-start.26 = (f32[16]{0:T(128)S(1)}, f32[16]{0:T(128)}, u32[]{:S(2)}) copy-start(f32[16]{0:T(128)} %copy-done.25) | copy-start | bytes 196
  109.5 24.8 %copy-start.30 = (f32[1,16]{1,0:T(1,128)S(1)}, f32[1,16]{1,0:T(1,128)}, u32[]{:S(2)}) copy-start(f32[1,16]{1,0:T(1,128)} %copy-done.29) | copy-start | bytes 196
  117.6 3.7 %collective-permute-start.10 = (f32[8,128]{1,0:T(8,128)S(1)}, f32[8,128]{1,0:T(8,128)S(1)}, u32[]{:S(2)}, u32[]{:S(2)}) collective-permute-start(f32[8,128]{1,0:T(8,128)S(1)} %scatter.41), channel_id=1, source_target_pairs={{0,8},{8,0},{16,24},{24,16},{1,9},{9,1},{17,25},{25,17},{2,10},{10... | collective-permute-start | bytes 12296 | tf_op jit(solution)/shard_map/ppermute | solution.py:14
  121.3 3.6 %collective-permute-start.11 = (f32[8,128]{1,0:T(8,128)S(1)}, f32[8,128]{1,0:T(8,128)S(1)}, u32[]{:S(2)}, u32[]{:S(2)}) collective-permute-start(f32[8,128]{1,0:T(8,128)S(1)} %add.155), channel_id=1, source_target_pairs={{0,16},{8,24},{16,0},{24,8},{1,17},{9,25},{17,1},{25,9},{2,18},{10... | collective-permute-start | bytes 12296 | tf_op jit(solution)/shard_map/ppermute | solution.py:14
  124.9 1.2 collective-permute-start.12
  126.2 3.6 %collective-permute-start.13 = (f32[8,128]{1,0:T(8,128)S(1)}, f32[8,128]{1,0:T(8,128)S(1)}, u32[]{:S(2)}, u32[]{:S(2)}) collective-permute-start(f32[8,128]{1,0:T(8,128)S(1)} %pad_add_fusion), channel_id=1, source_target_pairs={{0,2},{1,3},{2,0},{3,1},{4,6},{5,7},{6,4},{7,5},{8,10},{9,11},{10,... | collective-permute-start | bytes 12296 | tf_op jit(solution)/shard_map/ppermute | solution.py:14
  129.8 4.5 %collective-permute-start.14 = (f32[8,128]{1,0:T(8,128)S(1)}, f32[8,128]{1,0:T(8,128)S(1)}, u32[]{:S(2)}, u32[]{:S(2)}) collective-permute-start(f32[8,128]{1,0:T(8,128)S(1)} %fusion.96), channel_id=1, source_target_pairs={{0,4},{1,5},{2,6},{3,7},{4,0},{5,1},{6,2},{7,3},{8,12},{9,13},{10,... | collective-permute-start | bytes 12296 | tf_op jit(solution)/shard_map/ppermute | solution.py:14

commit v3 on v2

--- a/solution.py
+++ b/solution.py
@@ -14,40 +14,54 @@
     return lax.ppermute(x, axis, [(i, i ^ (1 << bit)) for i in range(n)])
 
 
-def _rounds(axis, total, own=None):
+def _rounds(axis, total, owns=()):
     n = lax.axis_size(axis)
     if not _pow2(n):
         total = lax.psum(total, axis)
-        if own is not None:
-            own = lax.all_gather(own, axis, axis=0, tiled=True)
-        return total, own
+        owns = [lax.all_gather(o, axis, axis=0, tiled=True) for o in owns]
+        return total, owns
     me = lax.axis_index(axis)
     rows = total.shape[0]
-    buf = None
-    if own is not None:
-        g = own.shape[0]
-        buf = jnp.zeros((n * g, own.shape[1]), own.dtype)
-        buf = lax.dynamic_update_slice_in_dim(buf, own, me * g, axis=0)
+    bufs = []
+    for o in owns:
+        buf = jnp.zeros((n * o.shape[0],) + o.shape[1:], o.dtype)
+        bufs.append(lax.dynamic_update_slice_in_dim(buf, o, me * o.shape[0], axis=0))
     for bit in range(n.bit_length() - 1):
-        if buf is None:
-            got = _exchange(total, axis, n, bit)
-            total = total + got
+        if not bufs:
+            total = total + _exchange(total, axis, n, bit)
             continue
-        span = (1 << bit) * g
-        mine = lax.dynamic_slice_in_dim(buf, ((me >> bit) << bit) * g, span, axis=0)
-        got = _exchange(jnp.concatenate([total, mine], axis=0), axis, n, bit)
+        start = (me >> bit) << bit
+        theirs = ((me ^ (1 << bit)) >> bit) << bit
+        parts = [total]
+        for o, buf in zip(owns, bufs):
+            g = o.shape[0]
+            parts.append(lax.dynamic_slice_in_dim(buf, start * g, (1 << bit) * g, axis=0))
+        got = _exchange(jnp.concatenate(parts, axis=0), axis, n, bit)
         total = total + got[:rows]
-        theirs = ((me ^ (1 << bit)) >> bit) << bit
-        buf = lax.dynamic_update_slice_in_dim(buf, got[rows:], theirs * g, axis=0)
-    return total, buf
+        off = rows
+        for i, o in enumerate(owns):
+            span = (1 << bit) * o.shape[0]
+            bufs[i] = lax.dynamic_update_slice_in_dim(
+                bufs[i], got[off : off + span], theirs * o.shape[0], axis=0
+            )
+            off += span
+    return total, bufs
 
 
 def _pack(lanes, *vectors):
-    small = jnp.zeros((8, lanes), jnp.float32)
-    for row, v in enumerate(vectors):
-        v = jnp.reshape(v, (-1,))
-        small = small.at[row, : v.shape[0]].set(v)
-    return small
+    flat = jnp.concatenate([jnp.reshape(v, (-1,)) for v in vectors])
+    size = 8 * lanes
+    flat = jnp.concatenate([flat, jnp.zeros((size - flat.shape[0],), flat.dtype)])
+    return flat.reshape(8, lanes)
+
+
+def _unpack(small, *sizes):
+    flat = small.reshape(-1)
+    out, off = [], 0
+    for s in sizes:
+        out.append(flat[off : off + s])
+        off += s
+    return out
 
 
 def local(
@@ -101,45 +115,40 @@
             region_blocks, scenarios, lanes
         )
 
-    small, _ = _rounds("region", _pack(lanes, local_c, local_a, local_b))
-    own_rows = own_blocks * (scenarios + 2)
-    pad = -own_rows % 8
-    own = jnp.concatenate(
-        [
-            primal.reshape(own_blocks * scenarios, lanes),
-            base_cost,
-            upper,
-            jnp.zeros((pad, lanes), jnp.float32),
-        ],
-        axis=0,
+    norms = jnp.concatenate([local_a.reshape(1), local_c, local_b.reshape(1)])
+    norms, _ = _rounds("region", norms)
+    own_misc = jnp.concatenate(
+        [base_cost, upper, jnp.zeros((-2 * own_blocks % 8, lanes), jnp.float32)], axis=0
     )
+    misc_rows = own_misc.shape[0]
     grad_rows = region_blocks * scenarios
     partial_value = transposed_product(dual).reshape(grad_rows, lanes)
-    summed, gathered = _rounds("col", jnp.concatenate([partial_value, small], axis=0), own)
+    summed, (primal_reg, misc) = _rounds(
+        "col",
+        jnp.concatenate([partial_value, _pack(lanes, norms)], axis=0),
+        (primal.reshape(own_blocks * scenarios, lanes), own_misc),
+    )
     grad = summed[:grad_rows].reshape(region_blocks, scenarios, lanes)
-    sq_c = summed[grad_rows, :scenarios]
-    sq_a = summed[grad_rows + 1, 0]
-    sq_b = summed[grad_rows + 2, 0]
-    gathered = gathered.reshape(ncol, own_rows + pad, lanes)
-    primal_reg = gathered[:, : own_blocks * scenarios].reshape(region_blocks, scenarios, lanes)
-    base_reg = gathered[:, own_blocks * scenarios : own_blocks * (scenarios + 1)].reshape(
-        region_blocks, lanes
-    )
-    upper_reg = gathered[:, own_blocks * (scenarios + 1) : own_rows].reshape(region_blocks, lanes)
+    (norms,) = _unpack(summed[grad_rows:], scenarios + 2)
+    sq_a, sq_c, sq_b = norms[0], norms[1 : scenarios + 1], norms[scenarios + 1]
+    primal_reg = primal_reg.reshape(region_blocks, scenarios, lanes)
+    misc = misc.reshape(ncol, misc_rows, lanes)
+    base_reg = misc[:, :own_blocks].reshape(region_blocks, lanes)
+    upper_reg = misc[:, own_blocks : 2 * own_blocks].reshape(region_blocks, lanes)
     cost_reg = base_reg[:, None, :] * factor[None, :, :]
     upper_reg = upper_reg[:, None, :]
     eta = 0.5 / jnp.sqrt(sq_a / (lanes * row_blocks * devices))
     weight = jnp.sqrt(sq_c) / jnp.sqrt(sq_b)
     for step in range(ITERS):
         if step > 0:
-            steps, _ = _rounds("region", _pack(lanes, local_x, local_y))
+            steps, _ = _rounds("region", jnp.concatenate([local_x, local_y]))
             partial_value = transposed_product(dual).reshape(grad_rows, lanes)
             summed, _ = _rounds(
-                "col", jnp.concatenate([partial_value, _pack(lanes, steps[1, :scenarios])], axis=0)
+                "col", jnp.concatenate([partial_value, _pack(lanes, steps[scenarios:])], axis=0)
             )
             grad = summed[:grad_rows].reshape(region_blocks, scenarios, lanes)
-            step_x = steps[0, :scenarios]
-            step_y = summed[grad_rows, :scenarios]
+            step_x = steps[:scenarios]
+            (step_y,) = _unpack(summed[grad_rows:], scenarios)
             weight = jnp.sqrt(weight * jnp.sqrt((step_x + 1e-06) / (step_y + 1e-06)))
         tau = (eta / weight)[None, :, None]
         sigma = (eta * weight)[None, :, None]
@@ -156,10 +165,9 @@
         local_x = jnp.sum((new_primal - primal_reg) ** 2, axis=(0, 2))
         local_y = jnp.sum((new_dual - dual) ** 2, axis=(0, 2))
         primal_reg, dual = (new_primal, new_dual)
-    steps, _ = _rounds("region", _pack(lanes, local_x, local_y))
-    summed, _ = _rounds("col", _pack(lanes, steps[1, :scenarios]))
-    step_x = steps[0, :scenarios]
-    step_y = summed[0, :scenarios]
+    steps, _ = _rounds("region", jnp.concatenate([local_x, local_y]))
+    step_y, _ = _rounds("col", steps[scenarios:])
+    step_x = steps[:scenarios]
     weight = jnp.sqrt(weight * jnp.sqrt((step_x + 1e-06) / (step_y + 1e-06)))
     primal_out = lax.dynamic_slice_in_dim(primal_reg, me * own_blocks, own_blocks, axis=0)
     return (primal_out, dual, weight)

time: 136 us -> 145 us (1.066)
  other arithmetic: 24.7 us -> 30.8 us
  local copies, waits for them, and re-layouts: 22.7 us -> 26.2 us
    scatter x8 -> x0, local copies, waits for them, and re-layouts: 6.52 us -> none  [_pack(): small = small.at[row, :v.shape[0]].set(v)]
    reduce_sum x3 -> x4, other arithmetic: 1.81 us -> 6.56 us  [local(): local_x = jnp.sum((new_primal - primal_reg) ** 2, axis=(0, 2))]
    add x12 -> x11, other arithmetic: 2.06 us -> 6.36 us  [_rounds(): total = total + _exchange(total, axis, n, bit)]
    dynamic_update_slice x3 -> x7, local copies, waits for them, and re-layouts: 2.41 us -> 5.53 us  [the longest x6 5.52 us: _rounds(): lax.dynamic_update_slice_in_dim(bufs[i], got[off:off + span], theirs * o....]
    dynamic_slice x3 -> x6, local copies, waits for them, and re-layouts: 0.01 us -> 2.65 us  [_rounds(): lax.dynamic_slice_in_dim(buf, start * g, (1 << bit) * g, axis=0)]
    reduce_sum x2, local copies, waits for them, and re-layouts: 0.85 us -> 2.66 us  [local(): local_x = jnp.sum((new_primal - primal_reg) ** 2, axis=(0, 2))]
    slice x1 -> x0, other arithmetic: 1.65 us -> none  [local(): gathered[:, :own_blocks * scenarios]]
    slice x6 -> x4, local copies, waits for them, and re-layouts: 0.59 us -> 2.16 us  [the longest x1 1.43 us: local(): upper_reg = misc[:, own_blocks:2 * own_blocks].reshape(region_blocks, lanes)]
  transfers between devices with their start and end apart: 15 -> 15, of which waited for: 13 -> 13; matrix products, arithmetic and copies ran while one was open for 12% -> 11% of each run, Pallas kernels for 0% -> 0%
where the time goes in v3:
time: 145 us; the launch traced here: 143 us
  waiting for transfers between devices  39.8 us (27%)
  other arithmetic  30.8 us (21%)
  local copies, waits for them, and re-layouts  26.2 us (18%)
  matrix products  24.3 us (17%)
  starting transfers between devices  18.8 us (13%)
  between operations  3.23 us (2%)
    ppermute x15, waiting for transfers between devices, _exchange(): return lax.ppermute(x, axis, [(i, i ^ 1 << bit) for i in range(n)])  39.8 us
    ppermute x15, starting transfers between devices, _exchange(): return lax.ppermute(x, axis, [(i, i ^ 1 << bit) for i in range(n)])  18.8 us
    dot_general x2, matrix products, local(): image = jnp.einsum('tij,tsj->tsi', tiles, selected, precision=hp)  10 us
    dot_general x2, matrix products, transposed_product(): contrib = jnp.einsum('tij,tsi->tsj', tiles, dual_rows, precision=hp)  6.68 us
    reduce_sum x4, other arithmetic, local(): local_x = jnp.sum((new_primal - primal_reg) ** 2, axis=(0, 2))  6.56 us
    add x11, other arithmetic, _rounds(): total = total + _exchange(total, axis, n, bit)  6.36 us
    dynamic_update_slice x6, local copies, waits for them, and re-layouts, _rounds(): lax.dynamic_update_slice_in_dim(bufs[i], got[off:off + span], theirs * o....  5.52 us
    unnamed x81, local copies, waits for them, and re-layouts  4.43 us
  transfers between devices with their start and end apart: 15, of which 13 were waited for; matrix products, arithmetic and copies ran while one was open for 11% of the time, Pallas kernels for 0%

profile of v3, /device:TPU:0, one launch (start us, length us, event | category | flops | bytes accessed | tf_op | source)
XLA Modules:
  0.0 143.2 jit_solution(3617548898210457683)
XLA Ops:
  1.5 1.4 %multiply_reduce_fusion.5 = f32[]{:T(128)} fusion(f32[2,128]{1,0:T(2,128)} %param.15), kind=kLoop, calls=%fused_computation.125 | loop fusion | flops 511 | bytes 1028 | tf_op jit(solution)/shard_map/reduce_sum | solution.py:106
  2.9 2.4 %multiply_reduce_fusion = f32[48]{0:T(128)S(1)} fusion(f32[48,128,128]{2,1,0:T(8,128)} %param.11), kind=kLoop, calls=%fused_computation | loop fusion | flops 1572816 | bytes 3145920 | tf_op jit(solution)/shard_map/reduce_sum | solution.py:104
  6.3 1.4 pad_maximum_fusion.4
  7.7 2.9 %collective-permute-start = (f32[18]{0:T(128)S(1)}, f32[18]{0:T(128)S(1)}, u32[]{:S(2)}, u32[]{:S(2)}) collective-permute-start(f32[18]{0:T(128)S(1)} %pad_maximum_fusion.4), channel_id=1, source_target_pairs={{0,8},{8,0},{16,24},{24,16},{1,9},{9,1},{17,25},{25,17},{2,10},{10... | collective-permute-start | bytes 224 | tf_op jit(solution)/shard_map/ppermute | solution.py:14
  11.1 3.6 %fusion.22 = f32[48,16,128]{2,1,0:T(8,128)} fusion(f32[48,128,128]{2,1,0:T(8,128)S(1)} %copy-done.1, f32[48,16,128]{2,0,1:T(8,128)S(1)} %fusion.42), kind=kOutput, calls=%fused_computation.27 | convolution fusion | flops 150994944 | bytes 3932160 | tf_op jit(solution)/shard_map/tij,tsi->tsj/dot_general | solution.py:113
  15.4 1.4 fusion.9
  17.6 2.0 %fusion.96 = f32[18]{0:T(128)} fusion(f32[18]{0:T(128)S(1)} %collective-permute-done, f32[1]{0:T(128)} %bitcast.5, f32[16]{0:T(128)S(1)} %multiply_reduce_fusion.4, f32[1]{0:T(128)} %bitcast.4), kind=kLoop, calls=%fused_computation.159 | loop fusion | flops 54 | bytes 216 | tf_op jit(solution)/shard_map/add | solution.py:31
  19.5 1.5 %collective-permute-start.1 = (f32[18]{0:T(128)}, f32[18]{0:T(128)}, u32[]{:S(2)}, u32[]{:S(2)}) collective-permute-start(f32[18]{0:T(128)} %fusion.96), channel_id=1, source_target_pairs={{0,16},{8,24},{16,0},{24,8},{1,17},{9,25},{17,1},{25,9},{2,18},{10... | collective-permute-start | bytes 224 | tf_op jit(solution)/shard_map/ppermute | solution.py:14
  21.1 2.1 %collective-permute-done.1 = f32[18]{0:T(128)} collective-permute-done((f32[18]{0:T(128)}, f32[18]{0:T(128)}, u32[]{:S(2)}, u32[]{:S(2)}) %collective-permute-start.1) | collective-permute-done | bytes 104 | tf_op jit(solution)/shard_map/ppermute | solution.py:14
  23.9 1.4 pad_maximum_fusion.2
  25.3 1.7 %collective-permute-done.2 = f32[304,128]{1,0:T(8,128)} collective-permute-done((f32[304,128]{1,0:T(8,128)}, f32[304,128]{1,0:T(8,128)}, u32[]{:S(2)}, u32[]{:S(2)}) %collective-permute-start.2) | collective-permute-done | bytes 155680 | tf_op jit(solution)/shard_map/ppermute | solution.py:14
  27.0 1.3 constant_dynamic-update-slice_fusion
  28.3 0.7 constant_dynamic-slice_fusion.3
  29.0 0.7 slice_dynamic-update-slice_fusion.3
  29.7 1.0 slice_add_fusion.2
  31.4 1.6 %collective-permute-start.3 = (f32[344,128]{1,0:T(8,128)}, f32[344,128]{1,0:T(8,128)}, u32[]{:S(2)}, u32[]{:S(2)}) collective-permute-start(f32[344,128]{1,0:T(8,128)} %pad_maximum_fusion.1), channel_id=1, source_target_pairs={{0,2},{1,3},{2,0},{3,1},{4,6},{5,7},{6,4},{7,5},{8,10},{9,11},{10,... | collective-permute-start | bytes 528392 | tf_op jit(solution)/shard_map/ppermute | solution.py:14
  33.0 5.3 %collective-permute-done.3 = f32[344,128]{1,0:T(8,128)} collective-permute-done((f32[344,128]{1,0:T(8,128)}, f32[344,128]{1,0:T(8,128)}, u32[]{:S(2)}, u32[]{:S(2)}) %collective-permute-start.3) | collective-permute-done | bytes 176160 | tf_op jit(solution)/shard_map/ppermute | solution.py:14
  38.2 1.3 slice_dynamic-update-slice_fusion.4
  39.5 0.7 constant_dynamic-slice_fusion.1
  40.2 0.8 slice_dynamic-update-slice_fusion.1
  41.0 0.9 slice_add_fusion.1
  42.6 0.7 pad_maximum_fusion
  43.3 2.6 %collective-permute-start.4 = (f32[424,128]{1,0:T(8,128)}, f32[424,128]{1,0:T(8,128)S(1)}, u32[]{:S(2)}, u32[]{:S(2)}) collective-permute-start(f32[424,128]{1,0:T(8,128)} %pad_maximum_fusion), channel_id=1, source_target_pairs={{0,4},{1,5},{2,6},{3,7},{4,0},{5,1},{6,2},{7,3},{8,12},{9,13},{10,... | collective-permute-start | bytes 651272 | tf_op jit(solution)/shard_map/ppermute | solution.py:14
  45.9 9.7 %collective-permute-done.4 = f32[424,128]{1,0:T(8,128)S(1)} collective-permute-done((f32[424,128]{1,0:T(8,128)}, f32[424,128]{1,0:T(8,128)S(1)}, u32[]{:S(2)}, u32[]{:S(2)}) %collective-permute-start.4) | collective-permute-done | bytes 217120 | tf_op jit(solution)/shard_map/ppermute | solution.py:14
  56.3 1.4 fusion.87
  57.7 0.9 slice_add_fusion
  63.2 0.7 broadcast_multiply_fusion
  63.9 0.9 slice_dynamic-update-slice_fusion
  65.5 1.7 %multiply_reduce_fusion.1 = (f32[256]{0:T(256)}, f32[256,128]{1,0:T(8,128)S(1)}) fusion(f32[256,128]{1,0:T(8,128)S(1)} %slice_dynamic-update-slice_fusion, f32[16,16,128]{2,1,0:T(8,128)S(1)} %broadcast_multiply_fusion, f32[256]{0:T(256)} %mul.238, f32[16,128]{1,0:T(8,128)} %bitcast.203, f32[264,128]{1,0:T(8,128)} %copy-done.3), kind=kLoop, calls=%fused_computation.62 | loop fusion | flops 261888 | bytes 534528 | tf_op jit(solution)/shard_map/reduce_sum | solution.py:165
  67.2 1.4 reduce_sum.91
  68.5 1.3 reduce_sum.92
  70.5 0.7 mul.233
  71.3 0.7 min.39
  72.6 1.4 fusion.33
  74.1 5.0 %fusion.20 = f32[48,16,128]{2,1,0:T(8,128)S(1)} fusion(f32[48,128,128]{2,1,0:T(8,128)S(1)} %copy-done.1, f32[48,16,128]{2,0,1:T(8,128)S(1)} %fusion.33), kind=kOutput, calls=%fused_computation.25 | convolution fusion | flops 150994944 | bytes 3932160 | tf_op jit(solution)/shard_map/tij,tsj->tsi/dot_general | solution.py:160
  80.9 3.0 %fusion.18 = f32[48,16,128]{2,1,0:T(8,128)S(1)} fusion(f32[48,128,128]{2,1,0:T(8,128)S(1)} %copy-done.1, f32[48,16,128]{2,0,1:T(8,128)S(1)} %fusion.50), kind=kOutput, calls=%fused_computation.23 | convolution fusion | flops 150994944 | bytes 3932160 | tf_op jit(solution)/shard_map/tij,tsi->tsj/dot_general | solution.py:113
  84.5 1.4 collective-permute-start.6
  85.9 1.1 fusion.6
  87.0 0.9 reshape_reshape.7
  89.6 1.3 collective-permute-done.7
  90.9 0.7 collective-permute-start.8
  91.6 5.0 %collective-permute-done.8 = f32[264,128]{1,0:T(8,128)S(1)} collective-permute-done((f32[264,128]{1,0:T(8,128)S(1)}, f32[264,128]{1,0:T(8,128)S(1)}, u32[]{:S(2)}, u32[]{:S(2)}) %collective-permute-start.8) | collective-permute-done | bytes 135200 | tf_op jit(solution)/shard_map/ppermute | solution.py:14
  97.3 2.2 %collective-permute-start.9 = (f32[264,128]{1,0:T(8,128)}, f32[264,128]{1,0:T(8,128)}, u32[]{:S(2)}, u32[]{:S(2)}) collective-permute-start(f32[264,128]{1,0:T(8,128)} %add.136), channel_id=1, source_target_pairs={{0,4},{1,5},{2,6},{3,7},{4,0},{5,1},{6,2},{7,3},{8,12},{9,13},{10,... | collective-permute-start | bytes 405512 | tf_op jit(solution)/shard_map/ppermute | solution.py:14
  99.5 6.8 %collective-permute-done.9 = f32[264,128]{1,0:T(8,128)} collective-permute-done((f32[264,128]{1,0:T(8,128)}, f32[264,128]{1,0:T(8,128)}, u32[]{:S(2)}, u32[]{:S(2)}) %collective-permute-start.9) | collective-permute-done | bytes 135200 | tf_op jit(solution)/shard_map/ppermute | solution.py:14
  106.2 1.0 add.137
  107.9 1.2 broadcast_multiply_fusion.1
  111.0 2.3 %fusion.26 = (f32[256]{0:T(256)}, f32[256,128]{1,0:T(8,128)}) fusion(f32[16,16,128]{2,1,0:T(8,128)S(1)} %broadcast_multiply_fusion, f32[256,128]{1,0:T(8,128)S(1)} %slice_dynamic-update-slice_fusion, f32[256]{0:T(256)} %mul.269, f32[256]{0:T(256)} %mul.238, f32[16,128]{1,0:T(8,128)} %bitcast.205, f32[264,128]{1,0:T(8,128)} %copy-done.9, f32[264,128]{1,0:T(8,128)} %copy-done.3), kind=kLoop, calls=%fused_computation.40 | loop fusion | flops 425728 | bytes 666624 | tf_op jit(solution)/shard_map/reduce_sum | solution.py:165
  113.4 1.3 reduce_sum.95
  114.7 1.2 reduce_sum.96
  115.9 1.6 %reshape.146 = f32[16,2048]{1,0:T(8,128)} reshape(f32[256,128]{1,0:T(8,128)} %get-tuple-element.20) | data formatting | bytes 262144 | tf_op jit(solution)/shard_map/reshape | solution.py:149
  117.5 1.6 %fusion.30 = f32[48,16,128]{2,0,1:T(8,128)S(1)} fusion(s32[48]{0:T(128)} %param.13, f32[16,2048]{1,0:T(8,128)} %reshape.146, f32[2,8,16,128]{3,2,1,0:T(8,128)} %bitcast.198, f32[2,8,16,128]{3,2,1,0:T(8,128)} %bitcast.196, f32[16,2048]{1,0:T(8,128)} %reshape.138, f32[16,2048]{1,0:T(8,128)} %reshape.139, f32[2048]{0:T(1024)} %broadcast_bitcast_fusion, ...), kind=kOutput, calls=%fused_computation.47 | convolution fusion | flops 19301120 | bytes 1073344 | tf_op jit(solution)/shard_map/dot_general | solution.py:157
  119.2 5.0 %fusion.16 = f32[48,16,128]{2,1,0:T(8,128)S(1)} fusion(f32[48,128,128]{2,1,0:T(8,128)S(1)} %copy-done.1, f32[48,16,128]{2,0,1:T(8,128)S(1)} %fusion.30), kind=kOutput, calls=%fused_computation.21 | convolution fusion | flops 150994944 | bytes 3932160 | tf_op jit(solution)/shard_map/tij,tsj->tsi/dot_general | solution.py:160
  124.9 1.4 collective-permute-start.10
  126.3 2.2 %collective-permute-done.10 = f32[32]{0:T(128)S(1)} collective-permute-done((f32[32]{0:T(128)S(1)}, f32[32]{0:T(128)S(1)}, u32[]{:S(2)}, u32[]{:S(2)}) %collective-permute-start.10) | collective-permute-done | bytes 160 | tf_op jit(solution)/shard_map/ppermute | solution.py:14
  128.5 0.7 fusion.94
  129.2 1.4 collective-permute-start.11
  130.5 0.8 subtract_multiply_fusion
  131.3 1.4 collective-permute-done.11
  132.8 0.7 constant_dynamic-slice_fusion
  134.5 1.4 fusion.47
  135.9 1.6 %collective-permute-done.13 = f32[16]{0:T(128)S(1)} collective-permute-done((f32[16]{0:T(128)S(1)}, f32[16]{0:T(128)S(1)}, u32[]{:S(2)}, u32[]{:S(2)}) %collective-permute-start.13) | collective-permute-done | bytes 96 | tf_op jit(solution)/shard_map/ppermute | solution.py:14
  137.5 1.9 %collective-permute-start.14 = (f32[16]{0:T(128)S(1)}, f32[16]{0:T(128)S(1)}, u32[]{:S(2)}, u32[]{:S(2)}) collective-permute-start(f32[16]{0:T(128)S(1)} %add.145), channel_id=1, source_target_pairs={{0,4},{1,5},{2,6},{3,7},{4,0},{5,1},{6,2},{7,3},{8,12},{9,13},{10,... | collective-permute-start | bytes 200 | tf_op jit(solution)/shard_map/ppermute | solution.py:14
  140.0 1.9 %collective-permute-done.14 = f32[16]{0:T(128)S(1)} collective-permute-done((f32[16]{0:T(128)S(1)}, f32[16]{0:T(128)S(1)}, u32[]{:S(2)}, u32[]{:S(2)}) %collective-permute-start.14) | collective-permute-done | bytes 96 | tf_op jit(solution)/shard_map/ppermute | solution.py:14
  142.0 1.2 multiply_sqrt_fusion
  (139 shorter events, 20.4 us)
Async XLA Ops:
  0.6 5.4 %copy-start = (f32[32,128]{1,0:T(8,128)S(1)}, f32[32,128]{1,0:T(8,128)}, u32[]{:S(2)}) copy-start(f32[32,128]{1,0:T(8,128)} %param.20) | copy-start | bytes 49156
  0.6 10.4 %copy-start.1 = (f32[48,128,128]{2,1,0:T(8,128)S(1)}, f32[48,128,128]{2,1,0:T(8,128)}, u32[]{:S(2)}) copy-start(f32[48,128,128]{2,1,0:T(8,128)} %param.11) | copy-start | bytes 9437188
  0.7 5.3 %copy-start.39 = (s32[16]{0:T(128)S(1)}, s32[16]{0:T(128)}, u32[]{:S(2)}) copy-start(s32[16]{0:T(128)} %param.21) | copy-start | bytes 196
  0.7 5.5 %copy-start.31 = (f32[2,128]{1,0:T(2,128)S(1)}, f32[2,128]{1,0:T(2,128)}, u32[]{:S(2)}) copy-start(f32[2,128]{1,0:T(2,128)} %param.16) | copy-start | bytes 3076
  0.7 10.0 %copy-start.19 = (s32[48]{0:T(128)S(1)}, s32[48]{0:T(128)}, u32[]{:S(2)}) copy-start(s32[48]{0:T(128)} %param.12) | copy-start | bytes 580
  0.7 10.0 %copy-start.16 = (f32[2,16,128]{2,1,0:T(8,128)S(1)}, f32[2,16,128]{2,1,0:T(8,128)}, u32[]{:S(2)}) copy-start(f32[2,16,128]{2,1,0:T(8,128)} %param.19) | copy-start | bytes 49156
  2.9 11.8 %copy-start.18 = (f32[2,16,128]{2,1,0:T(8,128)S(1)}, f32[2,16,128]{2,1,0:T(8,128)}, u32[]{:S(2)}) copy-start(f32[2,16,128]{2,1,0:T(8,128)} %param.18) | copy-start | bytes 49156
  2.9 12.5 %copy-start.23 = (s32[48]{0:T(128)S(1)}, s32[48]{0:T(128)}, u32[]{:S(2)}) copy-start(s32[48]{0:T(128)} %param.13) | copy-start | bytes 580
  5.3 11.5 %copy-start.37 = (f32[2,128]{1,0:T(2,128)S(1)}, f32[2,128]{1,0:T(2,128)}, u32[]{:S(2)}) copy-start(f32[2,128]{1,0:T(2,128)} %param.17) | copy-start | bytes 3076
  6.2 8.6 %copy-start.11 = (f32[16,128]{1,0:T(8,128)}, f32[16,128]{1,0:T(8,128)S(1)}, u32[]{:S(2)}) copy-start(f32[16,128]{1,0:T(8,128)S(1)} %fusion.57) | copy-start | bytes 24580
  7.7 9.9 %collective-permute-start = (f32[18]{0:T(128)S(1)}, f32[18]{0:T(128)S(1)}, u32[]{:S(2)}, u32[]{:S(2)}) collective-permute-start(f32[18]{0:T(128)S(1)} %pad_maximum_fusion.4), channel_id=1, source_target_pairs={{0,8},{8,0},{16,24},{24,16},{1,9},{9,1},{17,25},{25,17},{2,10},{10... | collective-permute-start | bytes 224 | tf_op jit(solution)/shard_map/ppermute | solution.py:14
  10.7 8.9 %copy-start.25 = (f32[48]{0:T(128)}, f32[48]{0:T(128)S(1)}, u32[]{:S(2)}) copy-start(f32[48]{0:T(128)S(1)} %compare_convert_fusion) | copy-start | bytes 580
  16.9 2.6 %copy-start.12 = (f32[64,128]{1,0:T(8,128)}, f32[64,128]{1,0:T(8,128)S(1)}, u32[]{:S(2)}) copy-start(f32[64,128]{1,0:T(8,128)S(1)} %constant_dynamic-update-slice_fusion.2) | copy-start | bytes 98308
  19.5 3.7 %collective-permute-start.1 = (f32[18]{0:T(128)}, f32[18]{0:T(128)}, u32[]{:S(2)}, u32[]{:S(2)}) collective-permute-start(f32[18]{0:T(128)} %fusion.96), channel_id=1, source_target_pairs={{0,16},{8,24},{16,0},{24,8},{1,17},{9,25},{17,1},{25,9},{2,18},{10... | collective-permute-start | bytes 224 | tf_op jit(solution)/shard_map/ppermute | solution.py:14
  21.1 8.6 %copy-start.4 = (f32[256,128]{1,0:T(8,128)}, f32[256,128]{1,0:T(8,128)S(1)}, u32[]{:S(2)}) copy-start(f32[256,128]{1,0:T(8,128)S(1)} %reshape_reshape.6) | copy-start | bytes 393220
  25.3 1.7 %collective-permute-start.2 = (f32[304,128]{1,0:T(8,128)}, f32[304,128]{1,0:T(8,128)}, u32[]{:S(2)}, u32[]{:S(2)}) collective-permute-start(f32[304,128]{1,0:T(8,128)} %pad_maximum_fusion.2), channel_id=1, source_target_pairs={{0,1},{1,0},{2,3},{3,2},{4,5},{5,4},{6,7},{7,6},{8,9},{9,8},{10,11... | collective-permute-start | bytes 466952 | tf_op jit(solution)/shard_map/ppermute | solution.py:14
  31.4 6.8 %collective-permute-start.3 = (f32[344,128]{1,0:T(8,128)}, f32[344,128]{1,0:T(8,128)}, u32[]{:S(2)}, u32[]{:S(2)}) collective-permute-start(f32[344,128]{1,0:T(8,128)} %pad_maximum_fusion.1), channel_id=1, source_target_pairs={{0,2},{1,3},{2,0},{3,1},{4,6},{5,7},{6,4},{7,5},{8,10},{9,11},{10,... | collective-permute-start | bytes 528392 | tf_op jit(solution)/shard_map/ppermute | solution.py:14
  41.9 0.6 copy-start.2
  43.3 12.3 %collective-permute-start.4 = (f32[424,128]{1,0:T(8,128)}, f32[424,128]{1,0:T(8,128)S(1)}, u32[]{:S(2)}, u32[]{:S(2)}) collective-permute-start(f32[424,128]{1,0:T(8,128)} %pad_maximum_fusion), channel_id=1, source_target_pairs={{0,4},{1,5},{2,6},{3,7},{4,0},{5,1},{6,2},{7,3},{8,12},{9,13},{10,... | collective-permute-start | bytes 651272 | tf_op jit(solution)/shard_map/ppermute | solution.py:14
  55.6 7.6 %copy-start.10 = (f32[424,128]{1,0:T(8,128)}, f32[424,128]{1,0:T(8,128)S(1)}, u32[]{:S(2)}) copy-start(f32[424,128]{1,0:T(8,128)S(1)} %collective-permute-done.4) | copy-start | bytes 651268
  57.7 7.8 %copy-start.15 = (f32[8,2,128]{2,1,0:T(2,128)}, f32[8,2,128]{2,1,0:T(2,128)S(1)}, u32[]{:S(2)}) copy-start(f32[8,2,128]{2,1,0:T(2,128)S(1)} %get-tuple-element.24) | copy-start | bytes 24580
  58.6 0.7 copy-start.3
  61.9 0.7 copy-start.22
  67.2 16.8 %copy-start.5 = (f32[256,128]{1,0:T(8,128)}, f32[256,128]{1,0:T(8,128)S(1)}, u32[]{:S(2)}) copy-start(f32[256,128]{1,0:T(8,128)S(1)} %get-tuple-element.22) | copy-start | bytes 393220
  70.5 8.6 %copy-start.17 = (f32[2,16,128]{2,1,0:T(8,128)S(1)}, f32[2,16,128]{2,1,0:T(8,128)}, u32[]{:S(2)}) copy-start(f32[2,16,128]{2,1,0:T(8,128)} %param.19) | copy-start | bytes 49156
  70.5 8.6 %copy-start.20 = (s32[48]{0:T(128)S(1)}, s32[48]{0:T(128)}, u32[]{:S(2)}) copy-start(s32[48]{0:T(128)} %param.12) | copy-start | bytes 580
  70.5 8.6 %copy-start.26 = (f32[48]{0:T(128)S(1)}, f32[48]{0:T(128)}, u32[]{:S(2)}) copy-start(f32[48]{0:T(128)} %copy-done.25) | copy-start | bytes 580
  70.5 8.6 %copy-start.29 = (f32[2,128]{1,0:T(2,128)S(1)}, f32[2,128]{1,0:T(2,128)}, u32[]{:S(2)}) copy-start(f32[2,128]{1,0:T(2,128)} %param.15) | copy-start | bytes 3076
  70.5 8.6 %copy-start.32 = (f32[16]{0:T(128)S(1)}, f32[16]{0:T(128)}, u32[]{:S(2)}) copy-start(f32[16]{0:T(128)} %get-tuple-element.17) | copy-start | bytes 196
  70.5 9.2 %copy-start.36 = (f32[16]{0:T(128)S(1)}, f32[16]{0:T(128)}, u32[]{:S(2)}) copy-start(f32[16]{0:T(128)} %reduce_sum.92) | copy-start | bytes 196
  71.2 0.8 copy-start.7
  72.0 0.7 copy-start.8
  79.1 6.9 %copy-start.24 = (s32[48]{0:T(128)S(1)}, s32[48]{0:T(128)}, u32[]{:S(2)}) copy-start(s32[48]{0:T(128)} %param.13) | copy-start | bytes 580
  79.7 0.8 copy-start.13
  79.8 4.1 %collective-permute-start.5 = (f32[32]{0:T(128)S(1)}, f32[32]{0:T(128)S(1)}, u32[]{:S(2)}, u32[]{:S(2)}) collective-permute-start(f32[32]{0:T(128)S(1)} %pad_maximum_fusion.5), channel_id=1, source_target_pairs={{0,8},{8,0},{16,24},{24,16},{1,9},{9,1},{17,25},{25,17},{2,10},{10... | collective-permute-start | bytes 392 | tf_op jit(solution)/shard_map/ppermute | solution.py:14
  84.5 3.7 %collective-permute-start.6 = (f32[32]{0:T(128)}, f32[32]{0:T(128)}, u32[]{:S(2)}, u32[]{:S(2)}) collective-permute-start(f32[32]{0:T(128)} %fusion.95), channel_id=1, source_target_pairs={{0,16},{8,24},{16,0},{24,8},{1,17},{9,25},{17,1},{25,9},{2,18},{10... | collective-permute-start | bytes 392 | tf_op jit(solution)/shard_map/ppermute | solution.py:14
  88.9 0.6 copy-start.38
  89.5 1.4 collective-permute-start.7
  90.9 5.7 %collective-permute-start.8 = (f32[264,128]{1,0:T(8,128)S(1)}, f32[264,128]{1,0:T(8,128)S(1)}, u32[]{:S(2)}, u32[]{:S(2)}) collective-permute-start(f32[264,128]{1,0:T(8,128)S(1)} %fusion.86), channel_id=1, source_target_pairs={{0,2},{1,3},{2,0},{3,1},{4,6},{5,7},{6,4},{7,5},{8,10},{9,11},{10,... | collective-permute-start | bytes 405512 | tf_op jit(solution)/shard_map/ppermute | solution.py:14
  97.3 8.9 %collective-permute-start.9 = (f32[264,128]{1,0:T(8,128)}, f32[264,128]{1,0:T(8,128)}, u32[]{:S(2)}, u32[]{:S(2)}) collective-permute-start(f32[264,128]{1,0:T(8,128)} %add.136), channel_id=1, source_target_pairs={{0,4},{1,5},{2,6},{3,7},{4,0},{5,1},{6,2},{7,3},{8,12},{9,13},{10,... | collective-permute-start | bytes 405512 | tf_op jit(solution)/shard_map/ppermute | solution.py:14
  107.2 0.7 copy-start.9
  109.1 0.6 copy-start.34
  109.7 0.7 copy-start.28
  111.0 19.5 %copy-start.6 = (f32[256,128]{1,0:T(8,128)S(1)}, f32[256,128]{1,0:T(8,128)}, u32[]{:S(2)}) copy-start(f32[256,128]{1,0:T(8,128)} %copy-done.5) | copy-start | bytes 393220
  117.5 6.7 %copy-start.14 = (f32[2,16,128]{2,0,1:T(2,128)S(1)}, f32[2,16,128]{2,0,1:T(2,128)}, u32[]{:S(2)}) copy-start(f32[2,16,128]{2,0,1:T(2,128)} %copy-done.13) | copy-start | bytes 49156
  117.5 6.7 %copy-start.21 = (s32[48]{0:T(128)S(1)}, s32[48]{0:T(128)}, u32[]{:S(2)}) copy-start(s32[48]{0:T(128)} %param.12) | copy-start | bytes 580
  117.5 6.7 %copy-start.27 = (f32[48]{0:T(128)S(1)}, f32[48]{0:T(128)}, u32[]{:S(2)}) copy-start(f32[48]{0:T(128)} %copy-done.25) | copy-start | bytes 580
  117.5 6.7 %copy-start.30 = (f32[2,128]{1,0:T(2,128)S(1)}, f32[2,128]{1,0:T(2,128)}, u32[]{:S(2)}) copy-start(f32[2,128]{1,0:T(2,128)} %param.15) | copy-start | bytes 3076
  117.5 6.7 %copy-start.33 = (f32[16]{0:T(128)S(1)}, f32[16]{0:T(128)}, u32[]{:S(2)}) copy-start(f32[16]{0:T(128)} %get-tuple-element.15) | copy-start | bytes 196
  117.5 7.3 %copy-start.35 = (f32[16]{0:T(128)S(1)}, f32[16]{0:T(128)}, u32[]{:S(2)}) copy-start(f32[16]{0:T(128)} %reduce_sum.96) | copy-start | bytes 196
  124.9 3.5 %collective-permute-start.10 = (f32[32]{0:T(128)S(1)}, f32[32]{0:T(128)S(1)}, u32[]{:S(2)}, u32[]{:S(2)}) collective-permute-start(f32[32]{0:T(128)S(1)} %pad_maximum_fusion.6), channel_id=1, source_target_pairs={{0,8},{8,0},{16,24},{24,16},{1,9},{9,1},{17,25},{25,17},{2,10},{10... | collective-permute-start | bytes 392 | tf_op jit(solution)/shard_map/ppermute | solution.py:14
  129.2 3.5 %collective-permute-start.11 = (f32[32]{0:T(128)S(1)}, f32[32]{0:T(128)S(1)}, u32[]{:S(2)}, u32[]{:S(2)}) collective-permute-start(f32[32]{0:T(128)S(1)} %fusion.94), channel_id=1, source_target_pairs={{0,16},{8,24},{16,0},{24,8},{1,17},{9,25},{17,1},{25,9},{2,18},{10... | collective-permute-start | bytes 392 | tf_op jit(solution)/shard_map/ppermute | solution.py:14
  132.8 1.1 collective-permute-start.12
  134.0 3.5 %collective-permute-start.13 = (f32[16]{0:T(128)S(1)}, f32[16]{0:T(128)S(1)}, u32[]{:S(2)}, u32[]{:S(2)}) collective-permute-start(f32[16]{0:T(128)S(1)} %slice_add_fusion.3), channel_id=1, source_target_pairs={{0,2},{1,3},{2,0},{3,1},{4,6},{5,7},{6,4},{7,5},{8,10},{9,11},{10,... | collective-permute-start | bytes 200 | tf_op jit(solution)/shard_map/ppermute | solution.py:14
  137.5 4.4 %collective-permute-start.14 = (f32[16]{0:T(128)S(1)}, f32[16]{0:T(128)S(1)}, u32[]{:S(2)}, u32[]{:S(2)}) collective-permute-start(f32[16]{0:T(128)S(1)} %add.145), channel_id=1, source_target_pairs={{0,4},{1,5},{2,6},{3,7},{4,0},{5,1},{6,2},{7,3},{8,12},{9,13},{10,... | collective-permute-start | bytes 200 | tf_op jit(solution)/shard_map/ppermute | solution.py:14

commit v4 on v1

--- a/solution.py
+++ b/solution.py
@@ -14,23 +14,27 @@
     return lax.ppermute(x, axis, [(i, i ^ (1 << bit)) for i in range(n)])
 
 
-def _rounds(axis, sums, chunk=None):
+def _rounds(axis, sums, own=None):
     n = lax.axis_size(axis)
     if not _pow2(n):
         sums = [lax.psum(s, axis) for s in sums]
-        if chunk is not None:
-            chunk = lax.all_gather(chunk, axis, axis=0, tiled=False)
-        return sums, chunk
+        if own is not None:
+            own = lax.all_gather(own, axis, axis=0, tiled=False)
+        return sums, own
     shapes = [s.shape for s in sums]
     sizes = [s.size for s in sums]
     me = lax.axis_index(axis)
-    if chunk is not None:
-        chunk = chunk[None]
-    bits = n.bit_length() - 1
-    for bit in range(bits):
+    buf = None
+    if own is not None:
+        buf = jnp.zeros((n,) + own.shape, own.dtype)
+        buf = lax.dynamic_update_index_in_dim(buf, own, me, 0)
+    for bit in range(n.bit_length() - 1):
         parts = [s.reshape(-1) for s in sums]
-        if chunk is not None:
-            parts.append(chunk.reshape(-1))
+        if buf is not None:
+            used = sum(sizes)
+            parts.append(jnp.zeros((-used % 1024,), jnp.float32))
+            start = (me >> bit) << bit
+            parts.append(lax.dynamic_slice_in_dim(buf, start, 1 << bit, axis=0).reshape(-1))
         flat = jnp.concatenate(parts) if len(parts) > 1 else parts[0]
         got = _exchange(flat, axis, n, bit)
         off = 0
@@ -39,15 +43,12 @@
             new_sums.append(s + got[off : off + size].reshape(shape))
             off += size
         sums = new_sums
-        if chunk is not None:
-            theirs = got[off:].reshape(chunk.shape)
-            low = ((me >> bit) & 1) == 0
-            chunk = jnp.where(
-                low,
-                jnp.concatenate([chunk, theirs], axis=0),
-                jnp.concatenate([theirs, chunk], axis=0),
-            )
-    return sums, chunk
+        if buf is not None:
+            off += -off % 1024
+            theirs = ((me ^ (1 << bit)) >> bit) << bit
+            chunk = got[off:].reshape((1 << bit,) + own.shape)
+            buf = lax.dynamic_update_slice_in_dim(buf, chunk, theirs, axis=0)
+    return sums, buf
 
 
 def local(
@@ -104,15 +105,25 @@
     (local_a, local_c, local_b), _ = _rounds(
         "region", [local_a.reshape(1), local_c, local_b.reshape(1)]
     )
-    own = jnp.concatenate([primal, base_cost[:, None, :], upper[:, None, :]], axis=1)
+    own_rows = own_blocks * (scenarios + 2)
+    own = jnp.concatenate(
+        [
+            primal.reshape(own_blocks * scenarios, lanes),
+            base_cost,
+            upper,
+            jnp.zeros((-own_rows % 8, lanes), jnp.float32),
+        ],
+        axis=0,
+    )
     partial_value = transposed_product(dual)
     (grad, sq_a, sq_c, sq_b), gathered = _rounds(
         "col", [partial_value, local_a, local_c, local_b], own
     )
-    gathered = gathered.reshape(region_blocks, scenarios + 2, lanes)
-    primal_reg = gathered[:, :scenarios, :]
-    cost_reg = gathered[:, scenarios, :][:, None, :] * factor[None, :, :]
-    upper_reg = gathered[:, scenarios + 1, :][:, None, :]
+    primal_reg = gathered[:, : own_blocks * scenarios].reshape(region_blocks, scenarios, lanes)
+    base_reg = gathered[:, own_blocks * scenarios : own_blocks * (scenarios + 1)]
+    upper_reg = gathered[:, own_blocks * (scenarios + 1) : own_rows]
+    cost_reg = base_reg.reshape(region_blocks, lanes)[:, None, :] * factor[None, :, :]
+    upper_reg = upper_reg.reshape(region_blocks, lanes)[:, None, :]
     eta = 0.5 / jnp.sqrt(sq_a[0] / (lanes * row_blocks * devices))
     weight = jnp.sqrt(sq_c) / jnp.sqrt(sq_b[0])
     for step in range(ITERS):

time: 130 us -> 128 us (0.985)
  other arithmetic: 17 us -> 14.4 us
  waiting for transfers between devices: 43.2 us -> 41.7 us
  matrix products: 20.1 us -> 21.5 us
    unnamed x45 -> x43, local copies, waits for them, and re-layouts: 0.82 us -> 4.69 us
    slice x4 -> x2, other arithmetic: 3.24 us -> 0.04 us  [_rounds(): new_sums.append(s + got[off:off + size].reshape(shape))]
    select_n x3 -> x0, other arithmetic: 2 us -> none  [_rounds(): jnp.where(low, jnp.concatenate([chunk, theirs], axis=0), jnp.concatenate(...]
    slice x4, local copies, waits for them, and re-layouts: 2.63 us -> 0.81 us  [the longest x2 0.79 us: _rounds(): chunk = got[off:].reshape((1 << bit,) + own.shape)]
    add x12 -> x14, other arithmetic: 2.47 us -> 4.23 us  [_rounds(): new_sums.append(s + got[off:off + size].reshape(shape))]
    ppermute x15, waiting for transfers between devices: 43.2 us -> 41.7 us  [_exchange(): return lax.ppermute(x, axis, [(i, i ^ 1 << bit) for i in range(n)])]
    slice x7 -> x9, local copies, waits for them, and re-layouts: 6.09 us -> 7.05 us  [_rounds(): new_sums.append(s + got[off:off + size].reshape(shape))]
  transfers between devices with their start and end apart: 15 -> 15, of which waited for: 13 -> 12; matrix products, arithmetic and copies ran while one was open for 7% -> 10% of each run, Pallas kernels for 0% -> 0%
where the time goes in v4:
time: 128 us
  waiting for transfers between devices  41.7 us (33%)
  matrix products  21.5 us (17%)
  local copies, waits for them, and re-layouts  20.9 us (16%)
  starting transfers between devices  19.5 us (15%)
  other arithmetic  14.4 us (11%)
  between operations  9.51 us (7%)
    ppermute x15, waiting for transfers between devices, _exchange(): return lax.ppermute(x, axis, [(i, i ^ 1 << bit) for i in range(n)])  41.7 us
    ppermute x15, starting transfers between devices, _exchange(): return lax.ppermute(x, axis, [(i, i ^ 1 << bit) for i in range(n)])  19.5 us
    dot_general x2, matrix products, local(): image = jnp.einsum('tij,tsj->tsi', tiles, selected, precision=hp)  10 us
    slice x9, local copies, waits for them, and re-layouts, _rounds(): new_sums.append(s + got[off:off + size].reshape(shape))  7.05 us
    concatenate x3, local copies, waits for them, and re-layouts, _rounds(): flat = jnp.concatenate(parts) if len(parts) > 1 else parts[0]  6.36 us
    dot_general x2, matrix products, transposed_product(): contrib = jnp.einsum('tij,tsi->tsj', tiles, dual_rows, precision=hp)  5.74 us
    unnamed x43, local copies, waits for them, and re-layouts  4.69 us
    add x14, other arithmetic, _rounds(): new_sums.append(s + got[off:off + size].reshape(shape))  4.23 us
  transfers between devices with their start and end apart: 15, of which 12 were waited for; matrix products, arithmetic and copies ran while one was open for 10% of the time, Pallas kernels for 0%

profile of v4, /device:TPU:0, one launch (start us, length us, event | category | flops | bytes accessed | tf_op | source)
XLA Modules:
  0.0 127.5 jit_solution(9556297170324304765)
XLA Ops:
  1.5 2.5 %multiply_reduce_fusion = f32[48]{0:T(128)S(1)} fusion(f32[48,128,128]{2,1,0:T(8,128)} %param.11), kind=kLoop, calls=%fused_computation | loop fusion | flops 1572816 | bytes 3145920 | tf_op jit(solution)/shard_map/reduce_sum | solution.py:91
  4.0 0.6 multiply_reduce_fusion.6
  4.6 0.6 fusion.67
  5.4 0.6 copy-done.5
  6.2 0.6 copy-done.17
  6.7 1.8 %pad_maximum_fusion.3 = f32[18]{0:T(128)} fusion(f32[1]{0:T(128)} %bitcast.7, f32[16]{0:T(128)S(1)} %multiply_reduce_fusion.5, f32[1]{0:T(128)} %bitcast.6), kind=kLoop, calls=%fused_computation.111 | loop fusion | flops 36 | bytes 144 | tf_op jit(solution)/shard_map/concatenate | solution.py:38
  8.6 2.9 %collective-permute-start = (f32[18]{0:T(128)}, f32[18]{0:T(128)}, u32[]{:S(2)}, u32[]{:S(2)}) collective-permute-start(f32[18]{0:T(128)} %pad_maximum_fusion.3), channel_id=1, source_target_pairs={{0,8},{8,0},{16,24},{24,16},{1,9},{9,1},{17,25},{25,17},{2,10},{10... | collective-permute-start | bytes 224 | tf_op jit(solution)/shard_map/ppermute | solution.py:14
  11.9 2.9 %fusion.22 = f32[48,16,128]{2,1,0:T(8,128)S(1)} fusion(f32[48,128,128]{2,1,0:T(8,128)S(1)} %copy-done.1, f32[48,16,128]{2,0,1:T(8,128)S(1)} %fusion.42), kind=kOutput, calls=%fused_computation.27 | convolution fusion | flops 150994944 | bytes 3932160 | tf_op jit(solution)/shard_map/tij,tsi->tsj/dot_general | solution.py:100
  15.3 0.6 pad.23.clone
  15.9 1.1 fusion.9
  17.0 0.9 fusion.41
  17.9 1.3 %fusion.92 = (f32[1]{0:T(128)}, f32[1]{0:T(128)}) fusion(f32[18]{0:T(128)} %collective-permute-done), kind=kLoop, calls=%fused_computation.154 | loop fusion | bytes 16 | tf_op jit(solution)/shard_map/slice | solution.py:43
  21.7 0.8 slice_add_fusion.13
  22.5 1.5 %collective-permute-start.1 = (f32[18]{0:T(128)S(1)}, f32[18]{0:T(128)S(1)}, u32[]{:S(2)}, u32[]{:S(2)}) collective-permute-start(f32[18]{0:T(128)S(1)} %pad_maximum_fusion.4), channel_id=1, source_target_pairs={{0,16},{8,24},{16,0},{24,8},{1,17},{9,25},{17,1},{25,9},{2,18},{10... | collective-permute-start | bytes 224 | tf_op jit(solution)/shard_map/ppermute | solution.py:14
  24.1 2.0 %collective-permute-done.1 = f32[18]{0:T(128)S(1)} collective-permute-done((f32[18]{0:T(128)S(1)}, f32[18]{0:T(128)S(1)}, u32[]{:S(2)}, u32[]{:S(2)}) %collective-permute-start.1) | collective-permute-done | bytes 104 | tf_op jit(solution)/shard_map/ppermute | solution.py:14
  26.0 0.6 fusion.91
  27.9 0.7 concatenate.42
  28.7 1.6 %copy.49 = f32[2,8,16,128]{3,2,1,0:T(8,128)} copy(f32[2,8,16,128]{3,1,2,0:T(8,128)} %bitcast.162) | data formatting | bytes 262144
  30.3 0.6 fusion.88
  32.2 0.9 bitcast_add_fusion.1
  33.2 0.7 fusion.40
  33.9 0.7 slice_add_fusion.5
  34.7 0.7 concatenate.43
  35.4 1.6 %collective-permute-start.3 = (f32[44032]{0:T(1024)}, f32[44032]{0:T(1024)}, u32[]{:S(2)}, u32[]{:S(2)}) collective-permute-start(f32[44032]{0:T(1024)} %concatenate.43), channel_id=1, source_target_pairs={{0,2},{1,3},{2,0},{3,1},{4,6},{5,7},{6,4},{7,5},{8,10},{9,11},{10,... | collective-permute-start | bytes 528392 | tf_op jit(solution)/shard_map/ppermute | solution.py:14
  37.0 5.6 %collective-permute-done.3 = f32[44032]{0:T(1024)} collective-permute-done((f32[44032]{0:T(1024)}, f32[44032]{0:T(1024)}, u32[]{:S(2)}, u32[]{:S(2)}) %collective-permute-start.3) | collective-permute-done | bytes 176160 | tf_op jit(solution)/shard_map/ppermute | solution.py:14
  42.6 0.9 slice.169
  43.5 0.7 add.170
  44.2 1.3 %fusion.86 = (f32[1]{0:T(128)}, f32[1]{0:T(128)}) fusion(f32[44032]{0:T(1024)} %collective-permute-done.3), kind=kLoop, calls=%fused_computation.148 | loop fusion | bytes 16 | tf_op jit(solution)/shard_map/slice | solution.py:43
  46.8 0.8 slice.168
  47.7 0.7 slice_add_fusion.4
  48.9 4.9 %concatenate.44 = f32[54272]{0:T(1024)} concatenate(f32[32768]{0:T(1024)} %bitcast.160, f32[1]{0:T(128)S(6)} %add.171, f32[16]{0:T(128)S(1)} %slice_add_fusion.4, f32[1]{0:T(128)S(6)} %add.173, f32[1006]{0:T(1024)S(1)} %broadcast.40, f32[20480]{0:T(1024)S(1)} %bitcast.177), dimensions={0} | concatenate | bytes 434176 | tf_op jit(solution)/shard_map/concatenate | solution.py:38
  53.8 2.6 %collective-permute-start.4 = (f32[54272]{0:T(1024)}, f32[54272]{0:T(1024)S(1)}, u32[]{:S(2)}, u32[]{:S(2)}) collective-permute-start(f32[54272]{0:T(1024)} %concatenate.44), channel_id=1, source_target_pairs={{0,4},{1,5},{2,6},{3,7},{4,0},{5,1},{6,2},{7,3},{8,12},{9,13},{10,... | collective-permute-start | bytes 651272 | tf_op jit(solution)/shard_map/ppermute | solution.py:14
  56.3 10.1 %collective-permute-done.4 = f32[54272]{0:T(1024)S(1)} collective-permute-done((f32[54272]{0:T(1024)}, f32[54272]{0:T(1024)S(1)}, u32[]{:S(2)}, u32[]{:S(2)}) %collective-permute-start.4) | collective-permute-done | bytes 217120 | tf_op jit(solution)/shard_map/ppermute | solution.py:14
  66.5 0.7 copy-done.3
  67.2 1.3 %fusion.85 = (f32[1]{0:T(128)}, f32[1]{0:T(128)}) fusion(f32[54272]{0:T(1024)} %copy-done.3), kind=kLoop, calls=%fused_computation.147 | loop fusion | bytes 16 | tf_op jit(solution)/shard_map/slice | solution.py:43
  69.9 0.9 slice.180
  70.8 0.8 broadcast_multiply_fusion.1
  71.6 1.1 multiply_reduce_fusion.2
  72.8 1.0 fusion.37
  73.8 5.0 %fusion.20 = f32[48,16,128]{2,1,0:T(8,128)S(1)} fusion(f32[48,128,128]{2,1,0:T(8,128)S(1)} %copy-done.1, f32[48,16,128]{2,0,1:T(8,128)S(1)} %fusion.37), kind=kOutput, calls=%fused_computation.25 | convolution fusion | flops 150994944 | bytes 3932160 | tf_op jit(solution)/shard_map/tij,tsj->tsi/dot_general | solution.py:142
  78.8 1.3 %multiply_reduce_fusion.4 = (f32[16]{0:T(128)S(1)}, f32[2,16,128]{2,0,1:T(2,128)S(1)}) fusion(f32[2,16,128]{2,1,0:T(8,128)S(1)} %copy-done.8, f32[48]{0:T(128)} %compare_convert_fusion, s32[48]{0:T(128)S(1)} %copy-done.10, f32[2,128]{1,0:T(2,128)} %param.15, f32[16]{0:T(128)S(1)} %get-tuple-element.21, f32[6,8,16,128]{3,2,1,0:T(8,128)S(1)} %bitcast.155), kind=kOutput, calls=%fused_computation.69 | convolution fusion | flops 2388144 | bytes 427520 | tf_op jit(solution)/shard_map/dot_general | solution.py:143
  80.2 0.6 collective-permute-start.5
  81.2 2.9 %fusion.18 = f32[48,16,128]{2,1,0:T(8,128)S(1)} fusion(f32[48,128,128]{2,1,0:T(8,128)S(1)} %copy-done.1, f32[48,16,128]{2,0,1:T(8,128)S(1)} %fusion.44), kind=kOutput, calls=%fused_computation.23 | convolution fusion | flops 150994944 | bytes 3932160 | tf_op jit(solution)/shard_map/tij,tsi->tsj/dot_general | solution.py:100
  84.7 1.5 %collective-permute-start.6 = (f32[32]{0:T(128)S(1)}, f32[32]{0:T(128)S(1)}, u32[]{:S(2)}, u32[]{:S(2)}) collective-permute-start(f32[32]{0:T(128)S(1)} %pad_maximum_fusion.6), channel_id=1, source_target_pairs={{0,16},{8,24},{16,0},{24,8},{1,17},{9,25},{17,1},{25,9},{2,18},{10... | collective-permute-start | bytes 392 | tf_op jit(solution)/shard_map/ppermute | solution.py:14
  86.2 2.0 %collective-permute-done.6 = f32[32]{0:T(128)S(1)} collective-permute-done((f32[32]{0:T(128)S(1)}, f32[32]{0:T(128)S(1)}, u32[]{:S(2)}, u32[]{:S(2)}) %collective-permute-start.6) | collective-permute-done | bytes 160 | tf_op jit(solution)/shard_map/ppermute | solution.py:14
  88.4 1.3 %collective-permute-done.7 = f32[32784]{0:T(1024)S(1)} collective-permute-done((f32[32784]{0:T(1024)S(1)}, f32[32784]{0:T(1024)S(1)}, u32[]{:S(2)}, u32[]{:S(2)}) %collective-permute-start.7) | collective-permute-done | bytes 131168 | tf_op jit(solution)/shard_map/ppermute | solution.py:14
  89.8 0.8 collective-permute-start.8
  90.6 4.9 %collective-permute-done.8 = f32[32784]{0:T(1024)S(1)} collective-permute-done((f32[32784]{0:T(1024)S(1)}, f32[32784]{0:T(1024)S(1)}, u32[]{:S(2)}, u32[]{:S(2)}) %collective-permute-start.8) | collective-permute-done | bytes 131168 | tf_op jit(solution)/shard_map/ppermute | solution.py:14
  95.5 2.3 %collective-permute-start.9 = (f32[32784]{0:T(1024)S(1)}, f32[32784]{0:T(1024)S(1)}, u32[]{:S(2)}, u32[]{:S(2)}) collective-permute-start(f32[32784]{0:T(1024)S(1)} %pad_maximum_fusion.2), channel_id=1, source_target_pairs={{0,4},{1,5},{2,6},{3,7},{4,0},{5,1},{6,2},{7,3},{8,12},{9,13},{10,... | collective-permute-start | bytes 393416 | tf_op jit(solution)/shard_map/ppermute | solution.py:14
  97.9 6.3 %collective-permute-done.9 = f32[32784]{0:T(1024)S(1)} collective-permute-done((f32[32784]{0:T(1024)S(1)}, f32[32784]{0:T(1024)S(1)}, u32[]{:S(2)}, u32[]{:S(2)}) %collective-permute-start.9) | collective-permute-done | bytes 131168 | tf_op jit(solution)/shard_map/ppermute | solution.py:14
  104.9 5.0 %fusion.16 = f32[48,16,128]{2,1,0:T(8,128)S(1)} fusion(f32[48,128,128]{2,1,0:T(8,128)S(1)} %copy-done.1, f32[48,16,128]{2,0,1:T(8,128)S(1)} %fusion.34), kind=kOutput, calls=%fused_computation.21 | convolution fusion | flops 150994944 | bytes 3932160 | tf_op jit(solution)/shard_map/tij,tsj->tsi/dot_general | solution.py:142
  109.9 0.6 multiply_reduce_fusion.3
  110.6 1.5 %collective-permute-start.10 = (f32[32]{0:T(128)S(1)}, f32[32]{0:T(128)S(1)}, u32[]{:S(2)}, u32[]{:S(2)}) collective-permute-start(f32[32]{0:T(128)S(1)} %pad_maximum_fusion.7), channel_id=1, source_target_pairs={{0,8},{8,0},{16,24},{24,16},{1,9},{9,1},{17,25},{25,17},{2,10},{10... | collective-permute-start | bytes 392 | tf_op jit(solution)/shard_map/ppermute | solution.py:14
  112.0 2.1 %collective-permute-done.10 = f32[32]{0:T(128)S(1)} collective-permute-done((f32[32]{0:T(128)S(1)}, f32[32]{0:T(128)S(1)}, u32[]{:S(2)}, u32[]{:S(2)}) %collective-permute-start.10) | collective-permute-done | bytes 160 | tf_op jit(solution)/shard_map/ppermute | solution.py:14
  114.3 1.5 %collective-permute-start.11 = (f32[32]{0:T(128)S(1)}, f32[32]{0:T(128)S(1)}, u32[]{:S(2)}, u32[]{:S(2)}) collective-permute-start(f32[32]{0:T(128)S(1)} %pad_maximum_fusion.8), channel_id=1, source_target_pairs={{0,16},{8,24},{16,0},{24,8},{1,17},{9,25},{17,1},{25,9},{2,18},{10... | collective-permute-start | bytes 392 | tf_op jit(solution)/shard_map/ppermute | solution.py:14
  115.8 2.1 %collective-permute-done.11 = f32[32]{0:T(128)S(1)} collective-permute-done((f32[32]{0:T(128)S(1)}, f32[32]{0:T(128)S(1)}, u32[]{:S(2)}, u32[]{:S(2)}) %collective-permute-start.11) | collective-permute-done | bytes 160 | tf_op jit(solution)/shard_map/ppermute | solution.py:14
  117.9 1.1 collective-permute-done.12
  119.0 0.6 collective-permute-start.13
  119.6 0.6 constant_dynamic-slice_fusion
  120.2 2.3 %collective-permute-done.13 = f32[16]{0:T(128)S(1)} collective-permute-done((f32[16]{0:T(128)S(1)}, f32[16]{0:T(128)S(1)}, u32[]{:S(2)}, u32[]{:S(2)}) %collective-permute-start.13) | collective-permute-done | bytes 96 | tf_op jit(solution)/shard_map/ppermute | solution.py:14
  122.5 2.0 %collective-permute-start.14 = (f32[16]{0:T(128)S(1)}, f32[16]{0:T(128)S(1)}, u32[]{:S(2)}, u32[]{:S(2)}) collective-permute-start(f32[16]{0:T(128)S(1)} %add.203), channel_id=1, source_target_pairs={{0,4},{1,5},{2,6},{3,7},{4,0},{5,1},{6,2},{7,3},{8,12},{9,13},{10,... | collective-permute-start | bytes 200 | tf_op jit(solution)/shard_map/ppermute | solution.py:14
  124.5 0.6 copy.41
  125.1 1.8 %collective-permute-done.14 = f32[16]{0:T(128)S(1)} collective-permute-done((f32[16]{0:T(128)S(1)}, f32[16]{0:T(128)S(1)}, u32[]{:S(2)}, u32[]{:S(2)}) %collective-permute-start.14) | collective-permute-done | bytes 96 | tf_op jit(solution)/shard_map/ppermute | solution.py:14
  127.0 0.5 multiply_sqrt_fusion
  (88 shorter events, 4.3 us)
Async XLA Ops:
  0.6 4.6 %copy-start = (f32[32,128]{1,0:T(8,128)S(1)}, f32[32,128]{1,0:T(8,128)}, u32[]{:S(2)}) copy-start(f32[32,128]{1,0:T(8,128)} %param.20) | copy-start | bytes 49156
  0.6 11.2 %copy-start.1 = (f32[48,128,128]{2,1,0:T(8,128)S(1)}, f32[48,128,128]{2,1,0:T(8,128)}, u32[]{:S(2)}) copy-start(f32[48,128,128]{2,1,0:T(8,128)} %param.11) | copy-start | bytes 9437188
  0.7 3.4 %copy-start.13 = (f32[2,128]{1,0:T(2,128)S(1)}, f32[2,128]{1,0:T(2,128)}, u32[]{:S(2)}) copy-start(f32[2,128]{1,0:T(2,128)} %param.15) | copy-start | bytes 3076
  0.7 4.6 %copy-start.18 = (s32[16]{0:T(128)S(1)}, s32[16]{0:T(128)}, u32[]{:S(2)}) copy-start(s32[16]{0:T(128)} %param.21) | copy-start | bytes 196
  0.7 5.4 %copy-start.15 = (f32[2,128]{1,0:T(2,128)S(1)}, f32[2,128]{1,0:T(2,128)}, u32[]{:S(2)}) copy-start(f32[2,128]{1,0:T(2,128)} %param.16) | copy-start | bytes 3076
  0.7 10.8 %copy-start.7 = (f32[2,16,128]{2,1,0:T(8,128)S(1)}, f32[2,16,128]{2,1,0:T(8,128)}, u32[]{:S(2)}) copy-start(f32[2,16,128]{2,1,0:T(8,128)} %param.19) | copy-start | bytes 49156
  0.7 10.8 %copy-start.9 = (s32[48]{0:T(128)S(1)}, s32[48]{0:T(128)}, u32[]{:S(2)}) copy-start(s32[48]{0:T(128)} %param.12) | copy-start | bytes 580
  5.4 0.6 copy-start.5
  6.2 0.6 copy-start.17
  8.6 9.3 %collective-permute-start = (f32[18]{0:T(128)}, f32[18]{0:T(128)}, u32[]{:S(2)}, u32[]{:S(2)}) collective-permute-start(f32[18]{0:T(128)} %pad_maximum_fusion.3), channel_id=1, source_target_pairs={{0,8},{8,0},{16,24},{24,16},{1,9},{9,1},{17,25},{25,17},{2,10},{10... | collective-permute-start | bytes 224 | tf_op jit(solution)/shard_map/ppermute | solution.py:14
  17.0 7.1 %copy-start.2 = (f32[16,2048]{1,0:T(8,128)}, f32[16,2048]{1,0:T(8,128)S(1)}, u32[]{:S(2)}) copy-start(f32[16,2048]{1,0:T(8,128)S(1)} %fusion.9) | copy-start | bytes 393220
  17.0 54.7 %copy-start.6 = (f32[16,128]{1,0:T(8,128)S(1)}, f32[16,128]{1,0:T(8,128)}, u32[]{:S(2)}) copy-start(f32[16,128]{1,0:T(8,128)} %copy-done.5) | copy-start | bytes 24580
  22.5 3.5 %collective-permute-start.1 = (f32[18]{0:T(128)S(1)}, f32[18]{0:T(128)S(1)}, u32[]{:S(2)}, u32[]{:S(2)}) collective-permute-start(f32[18]{0:T(128)S(1)} %pad_maximum_fusion.4), channel_id=1, source_target_pairs={{0,16},{8,24},{16,0},{24,8},{1,17},{9,25},{17,1},{25,9},{2,18},{10... | collective-permute-start | bytes 224 | tf_op jit(solution)/shard_map/ppermute | solution.py:14
  28.7 1.6 %collective-permute-start.2 = (f32[38912]{0:T(1024)}, f32[38912]{0:T(1024)S(1)}, u32[]{:S(2)}, u32[]{:S(2)}) collective-permute-start(f32[38912]{0:T(1024)} %concatenate.42), channel_id=1, source_target_pairs={{0,1},{1,0},{2,3},{3,2},{4,5},{5,4},{6,7},{7,6},{8,9},{9,8},{10,11... | collective-permute-start | bytes 466952 | tf_op jit(solution)/shard_map/ppermute | solution.py:14
  30.3 2.0 %copy-start.4 = (f32[38912]{0:T(1024)}, f32[38912]{0:T(1024)S(1)}, u32[]{:S(2)}) copy-start(f32[38912]{0:T(1024)S(1)} %collective-permute-done.2) | copy-start | bytes 466948
  35.4 7.2 %collective-permute-start.3 = (f32[44032]{0:T(1024)}, f32[44032]{0:T(1024)}, u32[]{:S(2)}, u32[]{:S(2)}) collective-permute-start(f32[44032]{0:T(1024)} %concatenate.43), channel_id=1, source_target_pairs={{0,2},{1,3},{2,0},{3,1},{4,6},{5,7},{6,4},{7,5},{8,10},{9,11},{10,... | collective-permute-start | bytes 528392 | tf_op jit(solution)/shard_map/ppermute | solution.py:14
  48.4 0.5 copy-start.16
  53.8 12.7 %collective-permute-start.4 = (f32[54272]{0:T(1024)}, f32[54272]{0:T(1024)S(1)}, u32[]{:S(2)}, u32[]{:S(2)}) collective-permute-start(f32[54272]{0:T(1024)} %concatenate.44), channel_id=1, source_target_pairs={{0,4},{1,5},{2,6},{3,7},{4,0},{5,1},{6,2},{7,3},{8,12},{9,13},{10,... | collective-permute-start | bytes 651272 | tf_op jit(solution)/shard_map/ppermute | solution.py:14
  56.3 22.5 %copy-start.10 = (s32[48]{0:T(128)S(1)}, s32[48]{0:T(128)}, u32[]{:S(2)}) copy-start(s32[48]{0:T(128)} %param.12) | copy-start | bytes 580
  66.5 0.7 copy-start.3
  67.2 11.6 %copy-start.8 = (f32[2,16,128]{2,1,0:T(8,128)S(1)}, f32[2,16,128]{2,1,0:T(8,128)}, u32[]{:S(2)}) copy-start(f32[2,16,128]{2,1,0:T(8,128)} %param.19) | copy-start | bytes 49156
  78.8 5.3 %copy-start.11 = (s32[48]{0:T(128)S(1)}, s32[48]{0:T(128)}, u32[]{:S(2)}) copy-start(s32[48]{0:T(128)} %param.13) | copy-start | bytes 580
  78.8 5.3 %copy-start.12 = (f32[48]{0:T(128)S(1)}, f32[48]{0:T(128)}, u32[]{:S(2)}) copy-start(f32[48]{0:T(128)} %compare_convert_fusion) | copy-start | bytes 580
  80.2 4.3 %collective-permute-start.5 = (f32[32]{0:T(128)S(1)}, f32[32]{0:T(128)S(1)}, u32[]{:S(2)}, u32[]{:S(2)}) collective-permute-start(f32[32]{0:T(128)S(1)} %pad_maximum_fusion.5), channel_id=1, source_target_pairs={{0,8},{8,0},{16,24},{24,16},{1,9},{9,1},{17,25},{25,17},{2,10},{10... | collective-permute-start | bytes 392 | tf_op jit(solution)/shard_map/ppermute | solution.py:14
  84.7 3.5 %collective-permute-start.6 = (f32[32]{0:T(128)S(1)}, f32[32]{0:T(128)S(1)}, u32[]{:S(2)}, u32[]{:S(2)}) collective-permute-start(f32[32]{0:T(128)S(1)} %pad_maximum_fusion.6), channel_id=1, source_target_pairs={{0,16},{8,24},{16,0},{24,8},{1,17},{9,25},{17,1},{25,9},{2,18},{10... | collective-permute-start | bytes 392 | tf_op jit(solution)/shard_map/ppermute | solution.py:14
  88.3 1.4 %collective-permute-start.7 = (f32[32784]{0:T(1024)S(1)}, f32[32784]{0:T(1024)S(1)}, u32[]{:S(2)}, u32[]{:S(2)}) collective-permute-start(f32[32784]{0:T(1024)S(1)} %pad_maximum_fusion), channel_id=1, source_target_pairs={{0,1},{1,0},{2,3},{3,2},{4,5},{5,4},{6,7},{7,6},{8,9},{9,8},{10,11... | collective-permute-start | bytes 393416 | tf_op jit(solution)/shard_map/ppermute | solution.py:14
  89.8 5.7 %collective-permute-start.8 = (f32[32784]{0:T(1024)S(1)}, f32[32784]{0:T(1024)S(1)}, u32[]{:S(2)}, u32[]{:S(2)}) collective-permute-start(f32[32784]{0:T(1024)S(1)} %pad_maximum_fusion.1), channel_id=1, source_target_pairs={{0,2},{1,3},{2,0},{3,1},{4,6},{5,7},{6,4},{7,5},{8,10},{9,11},{10,... | collective-permute-start | bytes 393416 | tf_op jit(solution)/shard_map/ppermute | solution.py:14
  95.5 14.4 %copy-start.14 = (f32[2,128]{1,0:T(2,128)S(1)}, f32[2,128]{1,0:T(2,128)}, u32[]{:S(2)}) copy-start(f32[2,128]{1,0:T(2,128)} %param.15) | copy-start | bytes 3076
  95.5 8.7 %collective-permute-start.9 = (f32[32784]{0:T(1024)S(1)}, f32[32784]{0:T(1024)S(1)}, u32[]{:S(2)}, u32[]{:S(2)}) collective-permute-start(f32[32784]{0:T(1024)S(1)} %pad_maximum_fusion.2), channel_id=1, source_target_pairs={{0,4},{1,5},{2,6},{3,7},{4,0},{5,1},{6,2},{7,3},{8,12},{9,13},{10,... | collective-permute-start | bytes 393416 | tf_op jit(solution)/shard_map/ppermute | solution.py:14
  110.6 3.5 %collective-permute-start.10 = (f32[32]{0:T(128)S(1)}, f32[32]{0:T(128)S(1)}, u32[]{:S(2)}, u32[]{:S(2)}) collective-permute-start(f32[32]{0:T(128)S(1)} %pad_maximum_fusion.7), channel_id=1, source_target_pairs={{0,8},{8,0},{16,24},{24,16},{1,9},{9,1},{17,25},{25,17},{2,10},{10... | collective-permute-start | bytes 392 | tf_op jit(solution)/shard_map/ppermute | solution.py:14
  114.3 3.5 %collective-permute-start.11 = (f32[32]{0:T(128)S(1)}, f32[32]{0:T(128)S(1)}, u32[]{:S(2)}, u32[]{:S(2)}) collective-permute-start(f32[32]{0:T(128)S(1)} %pad_maximum_fusion.8), channel_id=1, source_target_pairs={{0,16},{8,24},{16,0},{24,8},{1,17},{9,25},{17,1},{25,9},{2,18},{10... | collective-permute-start | bytes 392 | tf_op jit(solution)/shard_map/ppermute | solution.py:14
  117.9 1.1 collective-permute-start.12
  119.0 3.5 %collective-permute-start.13 = (f32[16]{0:T(128)S(1)}, f32[16]{0:T(128)S(1)}, u32[]{:S(2)}, u32[]{:S(2)}) collective-permute-start(f32[16]{0:T(128)S(1)} %add.202), channel_id=1, source_target_pairs={{0,2},{1,3},{2,0},{3,1},{4,6},{5,7},{6,4},{7,5},{8,10},{9,11},{10,... | collective-permute-start | bytes 200 | tf_op jit(solution)/shard_map/ppermute | solution.py:14
  122.5 4.4 %collective-permute-start.14 = (f32[16]{0:T(128)S(1)}, f32[16]{0:T(128)S(1)}, u32[]{:S(2)}, u32[]{:S(2)}) collective-permute-start(f32[16]{0:T(128)S(1)} %add.203), channel_id=1, source_target_pairs={{0,4},{1,5},{2,6},{3,7},{4,0},{5,1},{6,2},{7,3},{8,12},{9,13},{10,... | collective-permute-start | bytes 200 | tf_op jit(solution)/shard_map/ppermute | solution.py:14

commit v5 on v4

--- a/solution.py
+++ b/solution.py
@@ -32,7 +32,8 @@
         parts = [s.reshape(-1) for s in sums]
         if buf is not None:
             used = sum(sizes)
-            parts.append(jnp.zeros((-used % 1024,), jnp.float32))
+            if used % 1024:
+                parts.append(jnp.zeros((-used % 1024,), jnp.float32))
             start = (me >> bit) << bit
             parts.append(lax.dynamic_slice_in_dim(buf, start, 1 << bit, axis=0).reshape(-1))
         flat = jnp.concatenate(parts) if len(parts) > 1 else parts[0]
@@ -102,9 +103,6 @@
             region_blocks, scenarios, lanes
         )
 
-    (local_a, local_c, local_b), _ = _rounds(
-        "region", [local_a.reshape(1), local_c, local_b.reshape(1)]
-    )
     own_rows = own_blocks * (scenarios + 2)
     own = jnp.concatenate(
         [
@@ -115,10 +113,15 @@
         ],
         axis=0,
     )
+    _, gathered = _rounds("col", [], own)
+    gathered, local_a, local_c, local_b = lax.optimization_barrier(
+        (gathered, local_a, local_c, local_b)
+    )
+    (local_a, local_c, local_b), _ = _rounds(
+        "region", [local_a.reshape(1), local_c, local_b.reshape(1)]
+    )
     partial_value = transposed_product(dual)
-    (grad, sq_a, sq_c, sq_b), gathered = _rounds(
-        "col", [partial_value, local_a, local_c, local_b], own
-    )
+    (grad, sq_a, sq_c, sq_b), _ = _rounds("col", [partial_value, local_a, local_c, local_b])
     primal_reg = gathered[:, : own_blocks * scenarios].reshape(region_blocks, scenarios, lanes)
     base_reg = gathered[:, own_blocks * scenarios : own_blocks * (scenarios + 1)]
     upper_reg = gathered[:, own_blocks * (scenarios + 1) : own_rows]

time: 128 us -> 155 us (1.21)
  other arithmetic: 14.4 us -> 27.1 us
  local copies, waits for them, and re-layouts: 20.9 us -> 31.8 us
  matrix products: 21.5 us -> 25 us
  waiting for transfers between devices: 41.7 us -> 38.9 us
  starting transfers between devices: 19.5 us -> 21.2 us
    reshape x0 -> x9, local copies, waits for them, and re-layouts: none -> 9.05 us  [the longest x6 6.77 us: _rounds(): new_sums.append(s + got[off:off + size].reshape(shape))]
    mul x0 -> x7, local copies, waits for them, and re-layouts: none -> 4.17 us  [the longest x6 3.46 us: local(): new_primal = jnp.clip(primal_reg - tau * (cost_reg - grad), 0.0, upper_reg)]
    reduce_sum x2 -> x4, other arithmetic: 1.35 us -> 4.45 us  [local(): local_x = jnp.sum((new_primal - primal_reg) ** 2, axis=(0, 2))]
    slice x2 -> x4, other arithmetic: 0.04 us -> 3.01 us  [_rounds(): new_sums.append(s + got[off:off + size].reshape(shape))]
    ppermute x15 -> x18, waiting for transfers between devices: 41.7 us -> 38.9 us  [_exchange(): return lax.ppermute(x, axis, [(i, i ^ 1 << bit) for i in range(n)])]
    concatenate x3, local copies, waits for them, and re-layouts: 6.36 us -> 4 us  [_rounds(): flat = jnp.concatenate(parts) if len(parts) > 1 else parts[0]]
    unnamed x0 -> x1, other arithmetic: none -> 1.9 us
    mul x2, other arithmetic: 0.78 us -> 2.59 us  [local(): sigma = (eta * weight)[None, :, None]]
  transfers between devices with their start and end apart: 15 -> 18, of which waited for: 12 -> 16; matrix products, arithmetic and copies ran while one was open for 10% -> 16% of each run, Pallas kernels for 0% -> 0%
where the time goes in v5:
time: 155 us; the launch traced here: 153 us
  waiting for transfers between devices  38.9 us (25%)
  local copies, waits for them, and re-layouts  31.8 us (21%)
  other arithmetic  27.1 us (17%)
  matrix products  25 us (16%)
  starting transfers between devices  21.2 us (14%)
  between operations  9.46 us (6%)
    ppermute x18, waiting for transfers between devices, _exchange(): return lax.ppermute(x, axis, [(i, i ^ 1 << bit) for i in range(n)])  38.9 us
    ppermute x18, starting transfers between devices, _exchange(): return lax.ppermute(x, axis, [(i, i ^ 1 << bit) for i in range(n)])  21.2 us
    dot_general x2, matrix products, local(): image = jnp.einsum('tij,tsj->tsi', tiles, selected, precision=hp)  10.8 us
    slice x7, local copies, waits for them, and re-layouts, _rounds(): new_sums.append(s + got[off:off + size].reshape(shape))  7.62 us
    reshape x6, local copies, waits for them, and re-layouts, _rounds(): new_sums.append(s + got[off:off + size].reshape(shape))  6.77 us
    dot_general x2, matrix products, transposed_product(): contrib = jnp.einsum('tij,tsi->tsj', tiles, dual_rows, precision=hp)  6.68 us
    reduce_sum x4, other arithmetic, local(): local_x = jnp.sum((new_primal - primal_reg) ** 2, axis=(0, 2))  4.45 us
    concatenate x3, local copies, waits for them, and re-layouts, _rounds(): flat = jnp.concatenate(parts) if len(parts) > 1 else parts[0]  4 us
  transfers between devices with their start and end apart: 18, of which 16 were waited for; matrix products, arithmetic and copies ran while one was open for 16% of the time, Pallas kernels for 0%

profile of v5, /device:TPU:0, one launch (start us, length us, event | category | flops | bytes accessed | tf_op | source)
XLA Modules:
  0.0 153.5 jit_solution(16545641566290192350)
XLA Ops:
  0.8 1.0 fusion.47
  2.3 2.3 %multiply_reduce_fusion = f32[48]{0:T(128)S(1)} fusion(f32[48,128,128]{2,1,0:T(8,128)} %param.11), kind=kLoop, calls=%fused_computation | loop fusion | flops 1572816 | bytes 3145920 | tf_op jit(solution)/shard_map/reduce_sum | solution.py:92
  5.1 3.6 %fusion.22 = f32[48,16,128]{2,1,0:T(8,128)} fusion(f32[48,128,128]{2,1,0:T(8,128)S(1)} %copy-done.1, f32[48,16,128]{2,0,1:T(8,128)S(1)} %fusion.48), kind=kOutput, calls=%fused_computation.27 | convolution fusion | flops 150994944 | bytes 3932160 | tf_op jit(solution)/shard_map/tij,tsi->tsj/dot_general | solution.py:101
  10.9 2.6 %collective-permute-start.1 = (f32[10240]{0:T(1024)S(1)}, f32[10240]{0:T(1024)S(1)}, u32[]{:S(2)}, u32[]{:S(2)}) collective-permute-start(f32[10240]{0:T(1024)S(1)} %bitcast.247), channel_id=1, source_target_pairs={{0,2},{1,3},{2,0},{3,1},{4,6},{5,7},{6,4},{7,5},{8,10},{9,11},{10,... | collective-permute-start | bytes 122888 | tf_op jit(solution)/shard_map/ppermute | solution.py:14
  14.1 1.6 %collective-permute-done.1 = f32[10240]{0:T(1024)S(1)} collective-permute-done((f32[10240]{0:T(1024)S(1)}, f32[10240]{0:T(1024)S(1)}, u32[]{:S(2)}, u32[]{:S(2)}) %collective-permute-start.1) | collective-permute-done | bytes 40992 | tf_op jit(solution)/shard_map/ppermute | solution.py:14
  15.8 2.9 %collective-permute-start.2 = (f32[20480]{0:T(1024)S(1)}, f32[20480]{0:T(1024)S(1)}, u32[]{:S(2)}, u32[]{:S(2)}) collective-permute-start(f32[20480]{0:T(1024)S(1)} %bitcast.242), channel_id=1, source_target_pairs={{0,4},{1,5},{2,6},{3,7},{4,0},{5,1},{6,2},{7,3},{8,12},{9,13},{10,... | collective-permute-start | bytes 245768 | tf_op jit(solution)/shard_map/ppermute | solution.py:14
  18.7 4.1 %collective-permute-done.2 = f32[20480]{0:T(1024)S(1)} collective-permute-done((f32[20480]{0:T(1024)S(1)}, f32[20480]{0:T(1024)S(1)}, u32[]{:S(2)}, u32[]{:S(2)}) %collective-permute-start.2) | collective-permute-done | bytes 81952 | tf_op jit(solution)/shard_map/ppermute | solution.py:14
  22.8 1.3 pad_maximum_fusion.3
  24.1 1.3 collective-permute-start.3
  25.4 1.4 fusion.9
  26.8 0.9 collective-permute-done.3
  30.9 1.3 collective-permute-start.4
  32.2 2.2 %collective-permute-done.4 = f32[18]{0:T(128)S(1)} collective-permute-done((f32[18]{0:T(128)S(1)}, f32[18]{0:T(128)S(1)}, u32[]{:S(2)}, u32[]{:S(2)}) %collective-permute-start.4) | collective-permute-done | bytes 104 | tf_op jit(solution)/shard_map/ppermute | solution.py:14
  36.4 0.7 concatenate.42
  37.1 1.6 %collective-permute-done.5 = f32[32786]{0:T(1024)S(1)} collective-permute-done((f32[32786]{0:T(1024)}, f32[32786]{0:T(1024)S(1)}, u32[]{:S(2)}, u32[]{:S(2)}) %collective-permute-start.5) | collective-permute-done | bytes 131176 | tf_op jit(solution)/shard_map/ppermute | solution.py:14
  41.9 1.6 %concatenate.43 = f32[32786]{0:T(1024)} concatenate(f32[32768]{0:T(1024)} %get-tuple-element.39, f32[1]{0:T(128)S(6)} %add.217, f32[16]{0:T(128)S(1)} %slice_add_fusion.5, f32[1]{0:T(128)S(6)} %add.220), dimensions={0} | concatenate | bytes 262288 | tf_op jit(solution)/shard_map/concatenate | solution.py:39
  45.2 4.3 %collective-permute-done.6 = f32[32786]{0:T(1024)} collective-permute-done((f32[32786]{0:T(1024)}, f32[32786]{0:T(1024)}, u32[]{:S(2)}, u32[]{:S(2)}) %collective-permute-start.6) | collective-permute-done | bytes 131176 | tf_op jit(solution)/shard_map/ppermute | solution.py:14
  49.5 1.3 fusion.101
  52.1 1.7 %fusion.100 = (f32[32768]{0:T(1024)S(1)}, f32[32768]{0:T(1024)}) fusion(f32[32786]{0:T(1024)} %collective-permute-done.6, f32[32768]{0:T(1024)} %get-tuple-element.39), kind=kLoop, calls=%fused_computation.173 | loop fusion | flops 32768 | bytes 524288 | tf_op jit(solution)/shard_map/slice | solution.py:44
  53.8 1.3 slice_add_fusion.4
  55.0 1.6 %concatenate.44 = f32[32786]{0:T(1024)} concatenate(f32[32768]{0:T(1024)} %get-tuple-element.41, f32[1]{0:T(128)S(6)} %add.221, f32[16]{0:T(128)} %slice_add_fusion.4, f32[1]{0:T(128)S(6)} %add.224), dimensions={0} | concatenate | bytes 262288 | tf_op jit(solution)/shard_map/concatenate | solution.py:39
  56.7 1.9 %collective-permute-start.7 = (f32[32786]{0:T(1024)}, f32[32786]{0:T(1024)}, u32[]{:S(2)}, u32[]{:S(2)}) collective-permute-start(f32[32786]{0:T(1024)} %concatenate.44), channel_id=1, source_target_pairs={{0,4},{1,5},{2,6},{3,7},{4,0},{5,1},{6,2},{7,3},{8,12},{9,13},{10,... | collective-permute-start | bytes 393440 | tf_op jit(solution)/shard_map/ppermute | solution.py:14
  58.6 1.4 fusion.95
  61.4 4.2 %collective-permute-done.7 = f32[32786]{0:T(1024)} collective-permute-done((f32[32786]{0:T(1024)}, f32[32786]{0:T(1024)}, u32[]{:S(2)}, u32[]{:S(2)}) %collective-permute-start.7) | collective-permute-done | bytes 131176 | tf_op jit(solution)/shard_map/ppermute | solution.py:14
  65.6 1.4 fusion.98
  68.4 1.4 broadcast_multiply_fusion.2
  71.0 1.3 mul.182
  72.3 1.6 %slice.151 = f32[32768]{0:T(1024)} slice(f32[32786]{0:T(1024)} %collective-permute-done.7), slice={[0:32768]} | slice | bytes 262144 | tf_op jit(solution)/shard_map/slice | solution.py:44
  73.9 1.6 %reshape.225 = f32[16,2048]{1,0:T(8,128)} reshape(f32[32768]{0:T(1024)} %slice.151) | data formatting | bytes 262144 | tf_op jit(solution)/shard_map/reshape | solution.py:44
  75.5 1.7 %fusion.31 = (f32[16,16,128]{2,1,0:T(8,128)}, f32[16,16,128]{2,1,0:T(8,128)S(1)}) fusion(f32[16,16,128]{2,1,0:T(8,128)} %bitcast.222, f32[16,16,128]{2,1,0:T(8,128)S(1)} %bitcast.220, f32[16,16,128]{2,1,0:T(8,128)S(1)} %bitcast.218, f32[2,8,16,128]{3,2,1,0:T(8,128)} %copy.45, f32[16]{0:T(128)} %copy-done.16, f32[16,128]{1,0:T(8,128)} %copy-done.7, ...), kind=kLoop, calls=%fused_computation.43 | loop fusion | flops 196608 | bytes 802880 | tf_op jit(solution)/shard_map/mul | solution.py:140
  77.9 2.5 %multiply_reduce_fusion.1 = (f32[8,32]{1,0:T(8,128)}, f32[8,32,128]{2,1,0:T(8,128)}, f32[8,32,128]{2,1,0:T(8,128)}) fusion(f32[8,40,128]{2,1,0:T(8,128)} %copy-done.4, f32[8,32,128]{2,1,0:T(8,128)} %bitcast.223, f32[8,32,128]{2,1,0:T(8,128)} %bitcast.221, f32[8,32,128]{2,1,0:T(8,128)} %reshape.218, f32[8,32,128]{2,1,0:T(8,128)S(1)} %bitcast.219, ...), kind=kLoop, calls=%fused_computation.65 | loop fusion | flops 360192 | bytes 1180800 | tf_op jit(solution)/shard_map/reduce_sum | solution.py:150
  80.4 0.7 reduce_sum.91
  81.8 0.9 reshape.222
  82.8 0.7 mul.177
  83.5 1.9 %subtract_bitcast_fusion = (f32[2,16,8,128]{3,2,1,0:T(8,128)S(1)}, f32[16,2048]{1,0:T(8,128)}) fusion(f32[16,2048]{1,0:T(8,128)S(1)} %reshape.222, f32[16,2048]{1,0:T(8,128)} %reshape.225, f32[16,2048]{1,0:T(8,128)} %reshape.224, f32[16,2048]{1,0:T(8,128)S(1)} %fusion.9, f32[16,2048]{1,0:T(8,128)} %reshape.223, f32[2048]{0:T(1024)} %bitcast.239, ...), kind=kLoop, calls=%fused_computation.64 | loop fusion | flops 360448 | bytes 1196032
  85.4 1.0 fusion.38
  86.4 5.0 %fusion.20 = f32[48,16,128]{2,1,0:T(8,128)S(1)} fusion(f32[48,128,128]{2,1,0:T(8,128)S(1)} %copy-done.1, f32[48,16,128]{2,0,1:T(8,128)S(1)} %fusion.38), kind=kOutput, calls=%fused_computation.25 | convolution fusion | flops 150994944 | bytes 3932160 | tf_op jit(solution)/shard_map/tij,tsj->tsi/dot_general | solution.py:145
  92.2 1.3 collective-permute-start.8
  93.8 3.0 %fusion.18 = f32[48,16,128]{2,1,0:T(8,128)S(1)} fusion(f32[48,128,128]{2,1,0:T(8,128)S(1)} %copy-done.1, f32[48,16,128]{2,0,1:T(8,128)S(1)} %fusion.56), kind=kOutput, calls=%fused_computation.23 | convolution fusion | flops 150994944 | bytes 3932160 | tf_op jit(solution)/shard_map/tij,tsi->tsj/dot_general | solution.py:101
  97.5 1.5 collective-permute-start.9
  99.0 2.0 %collective-permute-done.9 = f32[32]{0:T(128)S(1)} collective-permute-done((f32[32]{0:T(128)S(1)}, f32[32]{0:T(128)S(1)}, u32[]{:S(2)}, u32[]{:S(2)}) %collective-permute-start.9) | collective-permute-done | bytes 160 | tf_op jit(solution)/shard_map/ppermute | solution.py:14
  101.7 1.3 collective-permute-done.10
  103.7 5.1 %collective-permute-done.11 = f32[32784]{0:T(1024)S(1)} collective-permute-done((f32[32784]{0:T(1024)S(1)}, f32[32784]{0:T(1024)S(1)}, u32[]{:S(2)}, u32[]{:S(2)}) %collective-permute-start.11) | collective-permute-done | bytes 131168 | tf_op jit(solution)/shard_map/ppermute | solution.py:14
  110.1 2.2 %collective-permute-start.12 = (f32[32784]{0:T(1024)}, f32[32784]{0:T(1024)}, u32[]{:S(2)}, u32[]{:S(2)}) collective-permute-start(f32[32784]{0:T(1024)} %pad_maximum_fusion.2), channel_id=1, source_target_pairs={{0,4},{1,5},{2,6},{3,7},{4,0},{5,1},{6,2},{7,3},{8,12},{9,13},{10,... | collective-permute-start | bytes 393416 | tf_op jit(solution)/shard_map/ppermute | solution.py:14
  113.6 1.6 %reshape.234 = f32[16,2048]{1,0:T(8,128)} reshape(f32[32768]{0:T(1024)} %get-tuple-element.34) | data formatting | bytes 262144 | tf_op jit(solution)/shard_map/reshape | solution.py:44
  115.2 3.8 %collective-permute-done.12 = f32[32784]{0:T(1024)} collective-permute-done((f32[32784]{0:T(1024)}, f32[32784]{0:T(1024)}, u32[]{:S(2)}, u32[]{:S(2)}) %collective-permute-start.12) | collective-permute-done | bytes 131168 | tf_op jit(solution)/shard_map/ppermute | solution.py:14
  119.0 1.2 broadcast_multiply_fusion.1
  121.4 1.6 %slice.157 = f32[32768]{0:T(1024)} slice(f32[32784]{0:T(1024)} %collective-permute-done.12), slice={[0:32768]} | slice | bytes 262144 | tf_op jit(solution)/shard_map/slice | solution.py:44
  122.9 1.6 %reshape.235 = f32[16,2048]{1,0:T(8,128)} reshape(f32[32768]{0:T(1024)} %slice.157) | data formatting | bytes 262144 | tf_op jit(solution)/shard_map/reshape | solution.py:44
  124.5 0.8 broadcast_bitcast_fusion
  125.3 1.6 %fusion.35 = f32[48,16,128]{2,0,1:T(8,128)S(1)} fusion(s32[48]{0:T(128)} %param.13, f32[16,2048]{1,0:T(8,128)} %get-tuple-element.27, f32[16,2048]{1,0:T(8,128)} %reshape.235, f32[16,2048]{1,0:T(8,128)} %reshape.234, f32[16,2048]{1,0:T(8,128)S(1)} %fusion.6, f32[16,2048]{1,0:T(8,128)} %reshape.233, f32[2,8,16,128]{3,2,1,0:T(8,128)S(1)} %bitcast.208, ...), kind=kOutput, calls=%fused_computation.50 | convolution fusion | flops 19235584 | bytes 1327296 | tf_op jit(solution)/shard_map/dot_general | solution.py:142
  126.9 5.8 %fusion.16 = f32[48,16,128]{2,1,0:T(8,128)} fusion(f32[48,128,128]{2,1,0:T(8,128)S(1)} %copy-done.1, f32[48,16,128]{2,0,1:T(8,128)S(1)} %fusion.35), kind=kOutput, calls=%fused_computation.21 | convolution fusion | flops 150994944 | bytes 3932160 | tf_op jit(solution)/shard_map/tij,tsj->tsi/dot_general | solution.py:145
  132.7 1.3 fusion.26
  134.2 1.6 %multiply_reduce_fusion.2 = (f32[16]{0:T(128)S(1)}, f32[2,16,128]{2,0,1:T(2,128)S(1)}) fusion(f32[2,16,128]{2,0,1:T(2,128)} %copy-done.6, f32[48]{0:T(128)} %copy-done.14, s32[48]{0:T(128)} %param.12, f32[2,128]{1,0:T(2,128)} %param.15, f32[16]{0:T(128)} %get-tuple-element.20, f32[6,8,16,128]{3,2,1,0:T(8,128)} %bitcast.225), kind=kOutput, calls=%fused_computation.85 | convolution fusion | flops 2388144 | bytes 427520 | tf_op jit(solution)/shard_map/dot_general | solution.py:146
  135.9 0.8 collective-permute-start.13
  137.4 2.1 %collective-permute-done.13 = f32[32]{0:T(128)S(1)} collective-permute-done((f32[32]{0:T(128)S(1)}, f32[32]{0:T(128)S(1)}, u32[]{:S(2)}, u32[]{:S(2)}) %collective-permute-start.13) | collective-permute-done | bytes 160 | tf_op jit(solution)/shard_map/ppermute | solution.py:14
  139.6 1.5 collective-permute-start.14
  141.2 2.0 %collective-permute-done.14 = f32[32]{0:T(128)S(1)} collective-permute-done((f32[32]{0:T(128)S(1)}, f32[32]{0:T(128)S(1)}, u32[]{:S(2)}, u32[]{:S(2)}) %collective-permute-start.14) | collective-permute-done | bytes 160 | tf_op jit(solution)/shard_map/ppermute | solution.py:14
  143.2 0.9 fusion.27
  144.9 1.4 fusion.53
  146.3 1.6 %collective-permute-done.16 = f32[16]{0:T(128)S(1)} collective-permute-done((f32[16]{0:T(128)S(1)}, f32[16]{0:T(128)S(1)}, u32[]{:S(2)}, u32[]{:S(2)}) %collective-permute-start.16) | collective-permute-done | bytes 96 | tf_op jit(solution)/shard_map/ppermute | solution.py:14
  147.9 1.9 %collective-permute-start.17 = (f32[16]{0:T(128)S(1)}, f32[16]{0:T(128)S(1)}, u32[]{:S(2)}, u32[]{:S(2)}) collective-permute-start(f32[16]{0:T(128)S(1)} %add.266), channel_id=1, source_target_pairs={{0,4},{1,5},{2,6},{3,7},{4,0},{5,1},{6,2},{7,3},{8,12},{9,13},{10,... | collective-permute-start | bytes 200 | tf_op jit(solution)/shard_map/ppermute | solution.py:14
  150.4 1.9 %collective-permute-done.17 = f32[16]{0:T(128)S(1)} collective-permute-done((f32[16]{0:T(128)S(1)}, f32[16]{0:T(128)S(1)}, u32[]{:S(2)}, u32[]{:S(2)}) %collective-permute-start.17) | collective-permute-done | bytes 96 | tf_op jit(solution)/shard_map/ppermute | solution.py:14
  152.3 1.2 multiply_sqrt_fusion
  (133 shorter events, 21.4 us)
Async XLA Ops:
  0.6 8.7 %copy-start = (f32[32,128]{1,0:T(8,128)S(1)}, f32[32,128]{1,0:T(8,128)}, u32[]{:S(2)}) copy-start(f32[32,128]{1,0:T(8,128)} %param.20) | copy-start | bytes 49156
  0.6 4.4 %copy-start.1 = (f32[48,128,128]{2,1,0:T(8,128)S(1)}, f32[48,128,128]{2,1,0:T(8,128)}, u32[]{:S(2)}) copy-start(f32[48,128,128]{2,1,0:T(8,128)} %param.11) | copy-start | bytes 9437188
  0.7 4.0 %copy-start.8 = (f32[2,16,128]{2,1,0:T(8,128)S(1)}, f32[2,16,128]{2,1,0:T(8,128)}, u32[]{:S(2)}) copy-start(f32[2,16,128]{2,1,0:T(8,128)} %param.19) | copy-start | bytes 49156
  0.7 4.0 %copy-start.12 = (s32[48]{0:T(128)S(1)}, s32[48]{0:T(128)}, u32[]{:S(2)}) copy-start(s32[48]{0:T(128)} %param.12) | copy-start | bytes 580
  1.8 7.6 %copy-start.29 = (s32[16]{0:T(128)S(1)}, s32[16]{0:T(128)}, u32[]{:S(2)}) copy-start(s32[16]{0:T(128)} %param.21) | copy-start | bytes 196
  1.8 8.4 %copy-start.19 = (f32[2,128]{1,0:T(2,128)S(1)}, f32[2,128]{1,0:T(2,128)}, u32[]{:S(2)}) copy-start(f32[2,128]{1,0:T(2,128)} %param.16) | copy-start | bytes 3076
  1.8 11.8 %copy-start.17 = (f32[2,128]{1,0:T(2,128)S(1)}, f32[2,128]{1,0:T(2,128)}, u32[]{:S(2)}) copy-start(f32[2,128]{1,0:T(2,128)} %param.15) | copy-start | bytes 3076
  1.8 9.1 %collective-permute-start = (f32[5120]{0:T(1024)S(1)}, f32[5120]{0:T(1024)S(1)}, u32[]{:S(2)}, u32[]{:S(2)}) collective-permute-start(f32[5120]{0:T(1024)S(1)} %dynamic-slice_bitcast_fusion), channel_id=1, source_target_pairs={{0,1},{1,0},{2,3},{3,2},{4,5},{5,4},{6,7},{7,6},{8,9},{9,8},{10,11... | collective-permute-start | bytes 61448 | tf_op jit(solution)/shard_map/ppermute | solution.py:14
  4.7 20.7 %copy-start.10 = (s32[48]{0:T(128)S(1)}, s32[48]{0:T(128)}, u32[]{:S(2)}) copy-start(s32[48]{0:T(128)} %param.13) | copy-start | bytes 580
  9.6 0.6 copy-start.7
  10.9 4.9 %collective-permute-start.1 = (f32[10240]{0:T(1024)S(1)}, f32[10240]{0:T(1024)S(1)}, u32[]{:S(2)}, u32[]{:S(2)}) collective-permute-start(f32[10240]{0:T(1024)S(1)} %bitcast.247), channel_id=1, source_target_pairs={{0,2},{1,3},{2,0},{3,1},{4,6},{5,7},{6,4},{7,5},{8,10},{9,11},{10,... | collective-permute-start | bytes 122888 | tf_op jit(solution)/shard_map/ppermute | solution.py:14
  15.8 7.0 %collective-permute-start.2 = (f32[20480]{0:T(1024)S(1)}, f32[20480]{0:T(1024)S(1)}, u32[]{:S(2)}, u32[]{:S(2)}) collective-permute-start(f32[20480]{0:T(1024)S(1)} %bitcast.242), channel_id=1, source_target_pairs={{0,4},{1,5},{2,6},{3,7},{4,0},{5,1},{6,2},{7,3},{8,12},{9,13},{10,... | collective-permute-start | bytes 245768 | tf_op jit(solution)/shard_map/ppermute | solution.py:14
  18.7 13.5 %copy-start.14 = (f32[48]{0:T(128)}, f32[48]{0:T(128)S(1)}, u32[]{:S(2)}) copy-start(f32[48]{0:T(128)S(1)} %compare_convert_fusion) | copy-start | bytes 580
  22.8 2.6 %copy-start.4 = (f32[8,40,128]{2,1,0:T(8,128)}, f32[8,40,128]{2,1,0:T(8,128)S(1)}, u32[]{:S(2)}) copy-start(f32[8,40,128]{2,1,0:T(8,128)S(1)} %constant_dynamic-update-slice_fusion) | copy-start | bytes 491524
  24.1 3.5 %collective-permute-start.3 = (f32[18]{0:T(128)S(1)}, f32[18]{0:T(128)S(1)}, u32[]{:S(2)}, u32[]{:S(2)}) collective-permute-start(f32[18]{0:T(128)S(1)} %pad_maximum_fusion.3), channel_id=1, source_target_pairs={{0,8},{8,0},{16,24},{24,16},{1,9},{9,1},{17,25},{25,17},{2,10},{10... | collective-permute-start | bytes 224 | tf_op jit(solution)/shard_map/ppermute | solution.py:14
  30.9 3.5 %collective-permute-start.4 = (f32[18]{0:T(128)S(1)}, f32[18]{0:T(128)S(1)}, u32[]{:S(2)}, u32[]{:S(2)}) collective-permute-start(f32[18]{0:T(128)S(1)} %pad_maximum_fusion.4), channel_id=1, source_target_pairs={{0,16},{8,24},{16,0},{24,8},{1,17},{9,25},{17,1},{25,9},{2,18},{10... | collective-permute-start | bytes 224 | tf_op jit(solution)/shard_map/ppermute | solution.py:14
  36.4 3.5 %copy-start.27 = (f32[16]{0:T(128)}, f32[16]{0:T(128)S(1)}, u32[]{:S(2)}) copy-start(f32[16]{0:T(128)S(1)} %slice_add_fusion.12) | copy-start | bytes 196
  37.1 1.6 %collective-permute-start.5 = (f32[32786]{0:T(1024)}, f32[32786]{0:T(1024)S(1)}, u32[]{:S(2)}, u32[]{:S(2)}) collective-permute-start(f32[32786]{0:T(1024)} %concatenate.42), channel_id=1, source_target_pairs={{0,1},{1,0},{2,3},{3,2},{4,5},{5,4},{6,7},{7,6},{8,9},{9,8},{10,11... | collective-permute-start | bytes 393440 | tf_op jit(solution)/shard_map/ppermute | solution.py:14
  41.9 9.6 %copy-start.26 = (f32[16]{0:T(128)}, f32[16]{0:T(128)S(1)}, u32[]{:S(2)}) copy-start(f32[16]{0:T(128)S(1)} %slice_add_fusion.5) | copy-start | bytes 196
  43.5 6.0 %collective-permute-start.6 = (f32[32786]{0:T(1024)}, f32[32786]{0:T(1024)}, u32[]{:S(2)}, u32[]{:S(2)}) collective-permute-start(f32[32786]{0:T(1024)} %concatenate.43), channel_id=1, source_target_pairs={{0,2},{1,3},{2,0},{3,1},{4,6},{5,7},{6,4},{7,5},{8,10},{9,11},{10,... | collective-permute-start | bytes 393440 | tf_op jit(solution)/shard_map/ppermute | solution.py:14
  53.8 23.4 %copy-start.2 = (f32[32768]{0:T(1024)}, f32[32768]{0:T(1024)S(1)}, u32[]{:S(2)}) copy-start(f32[32768]{0:T(1024)S(1)} %get-tuple-element.40) | copy-start | bytes 393220
  56.7 8.9 %collective-permute-start.7 = (f32[32786]{0:T(1024)}, f32[32786]{0:T(1024)}, u32[]{:S(2)}, u32[]{:S(2)}) collective-permute-start(f32[32786]{0:T(1024)} %concatenate.44), channel_id=1, source_target_pairs={{0,4},{1,5},{2,6},{3,7},{4,0},{5,1},{6,2},{7,3},{8,12},{9,13},{10,... | collective-permute-start | bytes 393440 | tf_op jit(solution)/shard_map/ppermute | solution.py:14
  69.7 0.7 copy-start.16
  77.2 3.2 %copy-start.3 = (f32[16,16,128]{2,1,0:T(8,128)}, f32[16,16,128]{2,1,0:T(8,128)S(1)}, u32[]{:S(2)}) copy-start(f32[16,16,128]{2,1,0:T(8,128)S(1)} %get-tuple-element.47) | copy-start | bytes 393220
  82.7 8.7 %copy-start.9 = (f32[2,16,128]{2,1,0:T(8,128)S(1)}, f32[2,16,128]{2,1,0:T(8,128)}, u32[]{:S(2)}) copy-start(f32[2,16,128]{2,1,0:T(8,128)} %param.19) | copy-start | bytes 49156
  82.7 8.7 %copy-start.13 = (s32[48]{0:T(128)S(1)}, s32[48]{0:T(128)}, u32[]{:S(2)}) copy-start(s32[48]{0:T(128)} %param.12) | copy-start | bytes 580
  82.7 8.7 %copy-start.15 = (f32[48]{0:T(128)S(1)}, f32[48]{0:T(128)}, u32[]{:S(2)}) copy-start(f32[48]{0:T(128)} %copy-done.14) | copy-start | bytes 580
  82.7 8.7 %copy-start.18 = (f32[2,128]{1,0:T(2,128)S(1)}, f32[2,128]{1,0:T(2,128)}, u32[]{:S(2)}) copy-start(f32[2,128]{1,0:T(2,128)} %param.15) | copy-start | bytes 3076
  82.7 8.7 %copy-start.21 = (f32[16]{0:T(128)S(1)}, f32[16]{0:T(128)}, u32[]{:S(2)}) copy-start(f32[16]{0:T(128)} %get-tuple-element.24) | copy-start | bytes 196
  82.8 9.3 %copy-start.23 = (f32[16]{0:T(128)S(1)}, f32[16]{0:T(128)}, u32[]{:S(2)}) copy-start(f32[16]{0:T(128)} %reduce_sum.92) | copy-start | bytes 196
  83.5 1.9 %copy-start.5 = (f32[16,16,128]{2,1,0:T(8,128)}, f32[16,16,128]{2,1,0:T(8,128)S(1)}, u32[]{:S(2)}) copy-start(f32[16,16,128]{2,1,0:T(8,128)S(1)} %mul.177) | copy-start | bytes 393220
  91.4 5.4 %copy-start.11 = (s32[48]{0:T(128)S(1)}, s32[48]{0:T(128)}, u32[]{:S(2)}) copy-start(s32[48]{0:T(128)} %param.13) | copy-start | bytes 580
  92.1 1.3 copy-start.6
  92.2 5.1 %collective-permute-start.8 = (f32[32]{0:T(128)S(1)}, f32[32]{0:T(128)S(1)}, u32[]{:S(2)}, u32[]{:S(2)}) collective-permute-start(f32[32]{0:T(128)S(1)} %pad_maximum_fusion.5), channel_id=1, source_target_pairs={{0,8},{8,0},{16,24},{24,16},{1,9},{9,1},{17,25},{25,17},{2,10},{10... | collective-permute-start | bytes 392 | tf_op jit(solution)/shard_map/ppermute | solution.py:14
  97.4 12.7 %copy-start.25 = (f32[16]{0:T(128)}, f32[16]{0:T(128)S(1)}, u32[]{:S(2)}) copy-start(f32[16]{0:T(128)S(1)} %get-tuple-element.50) | copy-start | bytes 196
  97.5 3.5 %collective-permute-start.9 = (f32[32]{0:T(128)S(1)}, f32[32]{0:T(128)S(1)}, u32[]{:S(2)}, u32[]{:S(2)}) collective-permute-start(f32[32]{0:T(128)S(1)} %pad_maximum_fusion.6), channel_id=1, source_target_pairs={{0,16},{8,24},{16,0},{24,8},{1,17},{9,25},{17,1},{25,9},{2,18},{10... | collective-permute-start | bytes 392 | tf_op jit(solution)/shard_map/ppermute | solution.py:14
  101.0 0.6 copy-start.28
  101.6 1.4 collective-permute-start.10
  103.0 5.7 %collective-permute-start.11 = (f32[32784]{0:T(1024)S(1)}, f32[32784]{0:T(1024)S(1)}, u32[]{:S(2)}, u32[]{:S(2)}) collective-permute-start(f32[32784]{0:T(1024)S(1)} %pad_maximum_fusion.1), channel_id=1, source_target_pairs={{0,2},{1,3},{2,0},{3,1},{4,6},{5,7},{6,4},{7,5},{8,10},{9,11},{10,... | collective-permute-start | bytes 393416 | tf_op jit(solution)/shard_map/ppermute | solution.py:14
  108.8 1.3 copy-start.22
  110.1 8.9 %collective-permute-start.12 = (f32[32784]{0:T(1024)}, f32[32784]{0:T(1024)}, u32[]{:S(2)}, u32[]{:S(2)}) collective-permute-start(f32[32784]{0:T(1024)} %pad_maximum_fusion.2), channel_id=1, source_target_pairs={{0,4},{1,5},{2,6},{3,7},{4,0},{5,1},{6,2},{7,3},{8,12},{9,13},{10,... | collective-permute-start | bytes 393416 | tf_op jit(solution)/shard_map/ppermute | solution.py:14
  120.2 0.5 copy-start.24
  124.5 8.1 %copy-start.20 = (f32[16]{0:T(128)S(1)}, f32[16]{0:T(128)}, u32[]{:S(2)}) copy-start(f32[16]{0:T(128)} %broadcast_divide_fusion.1) | copy-start | bytes 196
  135.9 3.5 %collective-permute-start.13 = (f32[32]{0:T(128)S(1)}, f32[32]{0:T(128)S(1)}, u32[]{:S(2)}, u32[]{:S(2)}) collective-permute-start(f32[32]{0:T(128)S(1)} %pad_maximum_fusion.7), channel_id=1, source_target_pairs={{0,8},{8,0},{16,24},{24,16},{1,9},{9,1},{17,25},{25,17},{2,10},{10... | collective-permute-start | bytes 392 | tf_op jit(solution)/shard_map/ppermute | solution.py:14
  139.6 3.5 %collective-permute-start.14 = (f32[32]{0:T(128)S(1)}, f32[32]{0:T(128)S(1)}, u32[]{:S(2)}, u32[]{:S(2)}) collective-permute-start(f32[32]{0:T(128)S(1)} %pad_maximum_fusion.8), channel_id=1, source_target_pairs={{0,16},{8,24},{16,0},{24,8},{1,17},{9,25},{17,1},{25,9},{2,18},{10... | collective-permute-start | bytes 392 | tf_op jit(solution)/shard_map/ppermute | solution.py:14
  143.2 1.1 collective-permute-start.15
  144.3 3.5 %collective-permute-start.16 = (f32[16]{0:T(128)S(1)}, f32[16]{0:T(128)S(1)}, u32[]{:S(2)}, u32[]{:S(2)}) collective-permute-start(f32[16]{0:T(128)S(1)} %add.265), channel_id=1, source_target_pairs={{0,2},{1,3},{2,0},{3,1},{4,6},{5,7},{6,4},{7,5},{8,10},{9,11},{10,... | collective-permute-start | bytes 200 | tf_op jit(solution)/shard_map/ppermute | solution.py:14
  147.9 4.4 %collective-permute-start.17 = (f32[16]{0:T(128)S(1)}, f32[16]{0:T(128)S(1)}, u32[]{:S(2)}, u32[]{:S(2)}) collective-permute-start(f32[16]{0:T(128)S(1)} %add.266), channel_id=1, source_target_pairs={{0,4},{1,5},{2,6},{3,7},{4,0},{5,1},{6,2},{7,3},{8,12},{9,13},{10,... | collective-permute-start | bytes 200 | tf_op jit(solution)/shard_map/ppermute | solution.py:14

commit v6 on v4

--- a/solution.py
+++ b/solution.py
@@ -105,25 +105,25 @@
     (local_a, local_c, local_b), _ = _rounds(
         "region", [local_a.reshape(1), local_c, local_b.reshape(1)]
     )
-    own_rows = own_blocks * (scenarios + 2)
-    own = jnp.concatenate(
+    def placed(x):
+        slot = jnp.zeros((region_blocks,) + x.shape[1:], x.dtype)
+        return lax.dynamic_update_slice_in_dim(slot, x, me * own_blocks, axis=0)
+
+    partial_value = transposed_product(dual)
+    (grad, primal_reg, base_reg, upper_reg, sq_a, sq_c, sq_b), _ = _rounds(
+        "col",
         [
-            primal.reshape(own_blocks * scenarios, lanes),
-            base_cost,
-            upper,
-            jnp.zeros((-own_rows % 8, lanes), jnp.float32),
+            partial_value,
+            placed(primal),
+            placed(base_cost),
+            placed(upper),
+            local_a,
+            local_c,
+            local_b,
         ],
-        axis=0,
     )
-    partial_value = transposed_product(dual)
-    (grad, sq_a, sq_c, sq_b), gathered = _rounds(
-        "col", [partial_value, local_a, local_c, local_b], own
-    )
-    primal_reg = gathered[:, : own_blocks * scenarios].reshape(region_blocks, scenarios, lanes)
-    base_reg = gathered[:, own_blocks * scenarios : own_blocks * (scenarios + 1)]
-    upper_reg = gathered[:, own_blocks * (scenarios + 1) : own_rows]
-    cost_reg = base_reg.reshape(region_blocks, lanes)[:, None, :] * factor[None, :, :]
-    upper_reg = upper_reg.reshape(region_blocks, lanes)[:, None, :]
+    cost_reg = base_reg[:, None, :] * factor[None, :, :]
+    upper_reg = upper_reg[:, None, :]
     eta = 0.5 / jnp.sqrt(sq_a[0] / (lanes * row_blocks * devices))
     weight = jnp.sqrt(sq_c) / jnp.sqrt(sq_b[0])
     for step in range(ITERS):

time: 128 us -> 143 us (1.12)
  waiting for transfers between devices: 41.7 us -> 48.4 us
  local copies, waits for them, and re-layouts: 20.9 us -> 26.7 us
  other arithmetic: 14.4 us -> 17.9 us
    concatenate x3, local copies, waits for them, and re-layouts: 6.36 us -> 16.6 us  [_rounds(): flat = jnp.concatenate(parts) if len(parts) > 1 else parts[0]]
    ppermute x15, waiting for transfers between devices: 41.7 us -> 48.4 us  [_exchange(): return lax.ppermute(x, axis, [(i, i ^ 1 << bit) for i in range(n)])]
    slice x2 -> x4, other arithmetic: 0.04 us -> 2.46 us  [_rounds(): new_sums.append(s + got[off:off + size].reshape(shape))]
    slice x9 -> x7, local copies, waits for them, and re-layouts: 7.05 us -> 4.7 us  [_rounds(): new_sums.append(s + got[off:off + size].reshape(shape))]
    unnamed x43 -> x55, local copies, waits for them, and re-layouts: 4.69 us -> 2.67 us
    add x14 -> x16, other arithmetic: 4.23 us -> 4.71 us  [_rounds(): new_sums.append(s + got[off:off + size].reshape(shape))]
  transfers between devices with their start and end apart: 15 -> 15, of which waited for: 12 -> 13; matrix products, arithmetic and copies ran while one was open for 10% -> 8% of each run, Pallas kernels for 0% -> 0%
where the time goes in v6:
time: 143 us; the launch traced here: 142 us
  waiting for transfers between devices  48.4 us (34%)
  local copies, waits for them, and re-layouts  26.7 us (19%)
  matrix products  20.8 us (15%)
  starting transfers between devices  18.8 us (13%)
  other arithmetic  17.9 us (13%)
  between operations  9.48 us (7%)
    ppermute x15, waiting for transfers between devices, _exchange(): return lax.ppermute(x, axis, [(i, i ^ 1 << bit) for i in range(n)])  48.4 us
    ppermute x15, starting transfers between devices, _exchange(): return lax.ppermute(x, axis, [(i, i ^ 1 << bit) for i in range(n)])  18.8 us
    concatenate x3, local copies, waits for them, and re-layouts, _rounds(): flat = jnp.concatenate(parts) if len(parts) > 1 else parts[0]  16.6 us
    dot_general x2, matrix products, local(): image = jnp.einsum('tij,tsj->tsi', tiles, selected, precision=hp)  10 us
    dot_general x2, matrix products, transposed_product(): contrib = jnp.einsum('tij,tsi->tsj', tiles, dual_rows, precision=hp)  5.74 us
    add x16, other arithmetic, _rounds(): new_sums.append(s + got[off:off + size].reshape(shape))  4.71 us
    slice x7, local copies, waits for them, and re-layouts, _rounds(): new_sums.append(s + got[off:off + size].reshape(shape))  4.7 us
    reduce_sum x2, other arithmetic, local(): local_a = jnp.sum(jnp.sum(tiles * tiles, axis=(1, 2)) * live)  2.94 us
  transfers between devices with their start and end apart: 15, of which 13 were waited for; matrix products, arithmetic and copies ran while one was open for 8% of the time, Pallas kernels for 0%

profile of v6, /device:TPU:0, one launch (start us, length us, event | category | flops | bytes accessed | tf_op | source)
XLA Modules:
  0.0 142.2 jit_solution(12498321292183420618)
XLA Ops:
  1.5 1.4 %multiply_reduce_fusion.6 = f32[]{:T(128)} fusion(f32[2,128]{1,0:T(2,128)} %param.15), kind=kLoop, calls=%fused_computation.114 | loop fusion | flops 511 | bytes 1028 | tf_op jit(solution)/shard_map/reduce_sum | solution.py:93
  2.9 2.3 %multiply_reduce_fusion = f32[48]{0:T(128)S(1)} fusion(f32[48,128,128]{2,1,0:T(8,128)} %param.11), kind=kLoop, calls=%fused_computation | loop fusion | flops 1572816 | bytes 3145920 | tf_op jit(solution)/shard_map/reduce_sum | solution.py:91
  5.3 0.6 fusion.75
  6.1 0.6 copy-done.9
  7.3 1.8 %pad_maximum_fusion.3 = f32[18]{0:T(128)} fusion(f32[1]{0:T(128)} %bitcast.8, f32[16]{0:T(128)S(1)} %multiply_reduce_fusion.5, f32[1]{0:T(128)} %bitcast.7), kind=kLoop, calls=%fused_computation.126 | loop fusion | flops 36 | bytes 144 | tf_op jit(solution)/shard_map/concatenate | solution.py:38
  9.1 2.9 %collective-permute-start = (f32[18]{0:T(128)}, f32[18]{0:T(128)}, u32[]{:S(2)}, u32[]{:S(2)}) collective-permute-start(f32[18]{0:T(128)} %pad_maximum_fusion.3), channel_id=1, source_target_pairs={{0,8},{8,0},{16,24},{24,16},{1,9},{9,1},{17,25},{25,17},{2,10},{10... | collective-permute-start | bytes 224 | tf_op jit(solution)/shard_map/ppermute | solution.py:14
  12.0 0.5 compare_convert_fusion
  13.0 2.9 %fusion.22 = f32[48,16,128]{2,1,0:T(8,128)S(1)} fusion(f32[48,128,128]{2,1,0:T(8,128)S(1)} %copy-done.1, f32[48,16,128]{2,0,1:T(8,128)S(1)} %fusion.42), kind=kOutput, calls=%fused_computation.27 | convolution fusion | flops 150994944 | bytes 3932160 | tf_op jit(solution)/shard_map/tij,tsi->tsj/dot_general | solution.py:100
  15.8 0.7 constant_dynamic-update-slice_fusion.3
  16.5 0.7 constant_dynamic-update-slice_fusion.4
  17.3 1.1 fusion.9
  18.4 0.7 constant_dynamic-update-slice_fusion.2
  19.1 1.3 fusion.102
  22.9 0.7 slice_add_fusion.13
  23.7 1.5 %collective-permute-start.1 = (f32[18]{0:T(128)S(1)}, f32[18]{0:T(128)S(1)}, u32[]{:S(2)}, u32[]{:S(2)}) collective-permute-start(f32[18]{0:T(128)S(1)} %pad_maximum_fusion.4), channel_id=1, source_target_pairs={{0,16},{8,24},{16,0},{24,8},{1,17},{9,25},{17,1},{25,9},{2,18},{10... | collective-permute-start | bytes 224 | tf_op jit(solution)/shard_map/ppermute | solution.py:14
  25.3 2.0 %collective-permute-done.1 = f32[18]{0:T(128)S(1)} collective-permute-done((f32[18]{0:T(128)S(1)}, f32[18]{0:T(128)S(1)}, u32[]{:S(2)}, u32[]{:S(2)}) %collective-permute-start.1) | collective-permute-done | bytes 104 | tf_op jit(solution)/shard_map/ppermute | solution.py:14
  27.3 0.6 fusion.101
  29.2 6.0 %concatenate.38 = f32[69650]{0:T(1024)} concatenate(f32[32768]{0:T(1024)S(1)} %bitcast.189, f32[32768]{0:T(1024)} %bitcast.201, f32[2048]{0:T(1024)} %bitcast.213, f32[2048]{0:T(1024)S(1)} %bitcast.212, f32[1]{0:T(128)S(6)} %add.177, f32[16]{0:T(128)S(1)} %slice_add_fusion.12, f32[1]{0:T(128)S(6)} %add.179), dimensions={0} | concatenate | bytes 557200 | tf_op jit(solution)/shard_map/concatenate | solution.py:38
  35.2 1.8 %collective-permute-done.2 = f32[69650]{0:T(1024)S(1)} collective-permute-done((f32[69650]{0:T(1024)}, f32[69650]{0:T(1024)S(1)}, u32[]{:S(2)}, u32[]{:S(2)}) %collective-permute-start.2) | collective-permute-done | bytes 278632 | tf_op jit(solution)/shard_map/ppermute | solution.py:14
  37.0 0.6 fusion.98
  38.9 0.8 fusion.94
  39.7 0.7 add_dynamic-update-slice_fusion
  40.4 0.7 constant_dynamic-update-slice_fusion
  41.1 0.7 slice_add_fusion.5
  41.8 5.3 %concatenate.39 = f32[69650]{0:T(1024)} concatenate(f32[32768]{0:T(1024)} %get-tuple-element.29, f32[32768]{0:T(1024)S(1)} %bitcast.188, f32[2048]{0:T(1024)S(1)} %bitcast.210, f32[2048]{0:T(1024)S(1)} %bitcast.209, f32[1]{0:T(128)S(6)} %add.184, f32[16]{0:T(128)S(1)} %slice_add_fusion.5, f32[1]{0:T(128)S(6)} %add.186), dimensions={0} | concatenate | bytes 557200 | tf_op jit(solution)/shard_map/concatenate | solution.py:38
  47.1 1.6 %collective-permute-start.3 = (f32[69650]{0:T(1024)}, f32[69650]{0:T(1024)S(1)}, u32[]{:S(2)}, u32[]{:S(2)}) collective-permute-start(f32[69650]{0:T(1024)} %concatenate.39), channel_id=1, source_target_pairs={{0,2},{1,3},{2,0},{3,1},{4,6},{5,7},{6,4},{7,5},{8,10},{9,11},{10,... | collective-permute-start | bytes 835808 | tf_op jit(solution)/shard_map/ppermute | solution.py:14
  48.7 7.4 %collective-permute-done.3 = f32[69650]{0:T(1024)S(1)} collective-permute-done((f32[69650]{0:T(1024)}, f32[69650]{0:T(1024)S(1)}, u32[]{:S(2)}, u32[]{:S(2)}) %collective-permute-start.3) | collective-permute-done | bytes 278632 | tf_op jit(solution)/shard_map/ppermute | solution.py:14
  56.1 0.6 fusion.97
  58.0 1.7 %fusion.95 = (f32[32768]{0:T(1024)}, f32[32768]{0:T(1024)}, f32[32768]{0:T(1024)S(1)}) fusion(f32[69650]{0:T(1024)S(1)} %collective-permute-done.3, f32[32768]{0:T(1024)} %get-tuple-element.29), kind=kLoop, calls=%fused_computation.166 | loop fusion | flops 32768 | bytes 786432 | tf_op jit(solution)/shard_map/slice | solution.py:43
  59.7 0.7 slice_add_fusion.4
  60.4 0.7 fusion.65
  61.1 5.3 %concatenate.40 = f32[69650]{0:T(1024)} concatenate(f32[32768]{0:T(1024)} %get-tuple-element.32, f32[32768]{0:T(1024)S(1)} %bitcast.182, f32[2048]{0:T(1024)S(1)} %get-tuple-element.39, f32[2048]{0:T(1024)S(1)} %get-tuple-element.38, f32[1]{0:T(128)S(6)} %add.191, f32[16]{0:T(128)S(1)} %slice_add_fusion.4, f32[1]{0:T(128)S(6)} %add.193), dimensions={0} | concatenate | bytes 557200 | tf_op jit(solution)/shard_map/concatenate | solution.py:38
  66.4 2.6 %collective-permute-start.4 = (f32[69650]{0:T(1024)}, f32[69650]{0:T(1024)S(1)}, u32[]{:S(2)}, u32[]{:S(2)}) collective-permute-start(f32[69650]{0:T(1024)} %concatenate.40), channel_id=1, source_target_pairs={{0,4},{1,5},{2,6},{3,7},{4,0},{5,1},{6,2},{7,3},{8,12},{9,13},{10,... | collective-permute-start | bytes 835808 | tf_op jit(solution)/shard_map/ppermute | solution.py:14
  69.0 12.5 %collective-permute-done.4 = f32[69650]{0:T(1024)S(1)} collective-permute-done((f32[69650]{0:T(1024)}, f32[69650]{0:T(1024)S(1)}, u32[]{:S(2)}, u32[]{:S(2)}) %collective-permute-start.4) | collective-permute-done | bytes 278632 | tf_op jit(solution)/shard_map/ppermute | solution.py:14
  81.5 0.7 copy-done.6
  82.2 0.6 fusion.93
  84.2 0.8 fusion.49
  85.0 1.0 fusion.96
  86.0 0.8 broadcast_multiply_fusion.1
  86.8 1.2 multiply_reduce_fusion.2
  88.0 1.0 fusion.39
  89.0 5.0 %fusion.20 = f32[48,16,128]{2,1,0:T(8,128)S(1)} fusion(f32[48,128,128]{2,1,0:T(8,128)S(1)} %copy-done.1, f32[48,16,128]{2,0,1:T(8,128)S(1)} %fusion.39), kind=kOutput, calls=%fused_computation.25 | convolution fusion | flops 150994944 | bytes 3932160 | tf_op jit(solution)/shard_map/tij,tsj->tsi/dot_general | solution.py:142
  94.1 0.6 multiply_reduce_fusion.4
  94.8 0.7 collective-permute-start.5
  95.8 2.9 %fusion.18 = f32[48,16,128]{2,1,0:T(8,128)S(1)} fusion(f32[48,128,128]{2,1,0:T(8,128)S(1)} %copy-done.1, f32[48,16,128]{2,0,1:T(8,128)S(1)} %fusion.44), kind=kOutput, calls=%fused_computation.23 | convolution fusion | flops 150994944 | bytes 3932160 | tf_op jit(solution)/shard_map/tij,tsi->tsj/dot_general | solution.py:100
  99.3 1.4 collective-permute-start.6
  100.7 2.1 %collective-permute-done.6 = f32[32]{0:T(128)S(1)} collective-permute-done((f32[32]{0:T(128)S(1)}, f32[32]{0:T(128)S(1)}, u32[]{:S(2)}, u32[]{:S(2)}) %collective-permute-start.6) | collective-permute-done | bytes 160 | tf_op jit(solution)/shard_map/ppermute | solution.py:14
  103.0 1.3 collective-permute-done.7
  104.4 0.7 collective-permute-start.8
  105.1 5.0 %collective-permute-done.8 = f32[32784]{0:T(1024)S(1)} collective-permute-done((f32[32784]{0:T(1024)S(1)}, f32[32784]{0:T(1024)S(1)}, u32[]{:S(2)}, u32[]{:S(2)}) %collective-permute-start.8) | collective-permute-done | bytes 131168 | tf_op jit(solution)/shard_map/ppermute | solution.py:14
  110.1 2.2 %collective-permute-start.9 = (f32[32784]{0:T(1024)S(1)}, f32[32784]{0:T(1024)S(1)}, u32[]{:S(2)}, u32[]{:S(2)}) collective-permute-start(f32[32784]{0:T(1024)S(1)} %pad_maximum_fusion.2), channel_id=1, source_target_pairs={{0,4},{1,5},{2,6},{3,7},{4,0},{5,1},{6,2},{7,3},{8,12},{9,13},{10,... | collective-permute-start | bytes 393416 | tf_op jit(solution)/shard_map/ppermute | solution.py:14
  112.4 6.4 %collective-permute-done.9 = f32[32784]{0:T(1024)S(1)} collective-permute-done((f32[32784]{0:T(1024)S(1)}, f32[32784]{0:T(1024)S(1)}, u32[]{:S(2)}, u32[]{:S(2)}) %collective-permute-start.9) | collective-permute-done | bytes 131168 | tf_op jit(solution)/shard_map/ppermute | solution.py:14
  119.5 5.0 %fusion.16 = f32[48,16,128]{2,1,0:T(8,128)S(1)} fusion(f32[48,128,128]{2,1,0:T(8,128)S(1)} %copy-done.1, f32[48,16,128]{2,0,1:T(8,128)S(1)} %fusion.36), kind=kOutput, calls=%fused_computation.21 | convolution fusion | flops 150994944 | bytes 3932160 | tf_op jit(solution)/shard_map/tij,tsj->tsi/dot_general | solution.py:142
  124.5 0.6 multiply_reduce_fusion.3
  125.2 1.3 collective-permute-start.10
  126.5 2.2 %collective-permute-done.10 = f32[32]{0:T(128)S(1)} collective-permute-done((f32[32]{0:T(128)S(1)}, f32[32]{0:T(128)S(1)}, u32[]{:S(2)}, u32[]{:S(2)}) %collective-permute-start.10) | collective-permute-done | bytes 160 | tf_op jit(solution)/shard_map/ppermute | solution.py:14
  128.9 1.4 collective-permute-start.11
  130.3 2.2 %collective-permute-done.11 = f32[32]{0:T(128)S(1)} collective-permute-done((f32[32]{0:T(128)S(1)}, f32[32]{0:T(128)S(1)}, u32[]{:S(2)}, u32[]{:S(2)}) %collective-permute-start.11) | collective-permute-done | bytes 160 | tf_op jit(solution)/shard_map/ppermute | solution.py:14
  132.5 1.1 collective-permute-done.12
  134.2 0.6 constant_dynamic-slice_fusion.1
  134.8 2.4 %collective-permute-done.13 = f32[16]{0:T(128)S(1)} collective-permute-done((f32[16]{0:T(128)S(1)}, f32[16]{0:T(128)S(1)}, u32[]{:S(2)}, u32[]{:S(2)}) %collective-permute-start.13) | collective-permute-done | bytes 96 | tf_op jit(solution)/shard_map/ppermute | solution.py:14
  137.2 1.9 %collective-permute-start.14 = (f32[16]{0:T(128)S(1)}, f32[16]{0:T(128)S(1)}, u32[]{:S(2)}, u32[]{:S(2)}) collective-permute-start(f32[16]{0:T(128)S(1)} %add.225), channel_id=1, source_target_pairs={{0,4},{1,5},{2,6},{3,7},{4,0},{5,1},{6,2},{7,3},{8,12},{9,13},{10,... | collective-permute-start | bytes 200 | tf_op jit(solution)/shard_map/ppermute | solution.py:14
  139.1 0.6 copy.41
  139.7 2.0 %collective-permute-done.14 = f32[16]{0:T(128)S(1)} collective-permute-done((f32[16]{0:T(128)S(1)}, f32[16]{0:T(128)S(1)}, u32[]{:S(2)}, u32[]{:S(2)}) %collective-permute-start.14) | collective-permute-done | bytes 96 | tf_op jit(solution)/shard_map/ppermute | solution.py:14
  (95 shorter events, 4.9 us)
Async XLA Ops:
  0.6 5.3 %copy-start = (f32[32,128]{1,0:T(8,128)S(1)}, f32[32,128]{1,0:T(8,128)}, u32[]{:S(2)}) copy-start(f32[32,128]{1,0:T(8,128)} %param.20) | copy-start | bytes 49156
  0.6 12.3 %copy-start.1 = (f32[48,128,128]{2,1,0:T(8,128)S(1)}, f32[48,128,128]{2,1,0:T(8,128)}, u32[]{:S(2)}) copy-start(f32[48,128,128]{2,1,0:T(8,128)} %param.11) | copy-start | bytes 9437188
  0.7 5.2 %copy-start.24 = (s32[16]{0:T(128)S(1)}, s32[16]{0:T(128)}, u32[]{:S(2)}) copy-start(s32[16]{0:T(128)} %param.21) | copy-start | bytes 196
  0.7 6.0 %copy-start.14 = (f32[2,128]{1,0:T(2,128)S(1)}, f32[2,128]{1,0:T(2,128)}, u32[]{:S(2)}) copy-start(f32[2,128]{1,0:T(2,128)} %param.16) | copy-start | bytes 3076
  0.7 11.9 %copy-start.15 = (s32[48]{0:T(128)S(1)}, s32[48]{0:T(128)}, u32[]{:S(2)}) copy-start(s32[48]{0:T(128)} %param.12) | copy-start | bytes 580
  0.7 11.9 %copy-start.11 = (f32[2,16,128]{2,1,0:T(8,128)S(1)}, f32[2,16,128]{2,1,0:T(8,128)}, u32[]{:S(2)}) copy-start(f32[2,16,128]{2,1,0:T(8,128)} %param.19) | copy-start | bytes 49156
  6.1 0.6 copy-start.9
  6.8 0.5 copy-start.21
  9.1 10.0 %collective-permute-start = (f32[18]{0:T(128)}, f32[18]{0:T(128)}, u32[]{:S(2)}, u32[]{:S(2)}) collective-permute-start(f32[18]{0:T(128)} %pad_maximum_fusion.3), channel_id=1, source_target_pairs={{0,8},{8,0},{16,24},{24,16},{1,9},{9,1},{17,25},{25,17},{2,10},{10... | collective-permute-start | bytes 224 | tf_op jit(solution)/shard_map/ppermute | solution.py:14
  16.5 10.7 %copy-start.13 = (f32[16,128]{1,0:T(8,128)}, f32[16,128]{1,0:T(8,128)S(1)}, u32[]{:S(2)}) copy-start(f32[16,128]{1,0:T(8,128)S(1)} %constant_dynamic-update-slice_fusion.3) | copy-start | bytes 24580
  17.3 8.0 %copy-start.4 = (f32[16,16,128]{2,1,0:T(8,128)}, f32[16,16,128]{2,1,0:T(8,128)S(1)}, u32[]{:S(2)}) copy-start(f32[16,16,128]{2,1,0:T(8,128)S(1)} %constant_dynamic-update-slice_fusion.4) | copy-start | bytes 393220
  18.4 6.9 %copy-start.2 = (f32[16,2048]{1,0:T(8,128)}, f32[16,2048]{1,0:T(8,128)S(1)}, u32[]{:S(2)}) copy-start(f32[16,2048]{1,0:T(8,128)S(1)} %fusion.9) | copy-start | bytes 393220
  23.7 3.5 %collective-permute-start.1 = (f32[18]{0:T(128)S(1)}, f32[18]{0:T(128)S(1)}, u32[]{:S(2)}, u32[]{:S(2)}) collective-permute-start(f32[18]{0:T(128)S(1)} %pad_maximum_fusion.4), channel_id=1, source_target_pairs={{0,16},{8,24},{16,0},{24,8},{1,17},{9,25},{17,1},{25,9},{2,18},{10... | collective-permute-start | bytes 224 | tf_op jit(solution)/shard_map/ppermute | solution.py:14
  25.3 43.7 %copy-start.3 = (f32[16,2048]{1,0:T(8,128)S(1)}, f32[16,2048]{1,0:T(8,128)}, u32[]{:S(2)}) copy-start(f32[16,2048]{1,0:T(8,128)} %copy-done.2) | copy-start | bytes 393220
  29.2 9.0 %copy-start.22 = (f32[16]{0:T(128)}, f32[16]{0:T(128)S(1)}, u32[]{:S(2)}) copy-start(f32[16]{0:T(128)S(1)} %slice_add_fusion.12) | copy-start | bytes 196
  35.2 1.8 %collective-permute-start.2 = (f32[69650]{0:T(1024)}, f32[69650]{0:T(1024)S(1)}, u32[]{:S(2)}, u32[]{:S(2)}) collective-permute-start(f32[69650]{0:T(1024)} %concatenate.38), channel_id=1, source_target_pairs={{0,1},{1,0},{2,3},{3,2},{4,5},{5,4},{6,7},{7,6},{8,9},{9,8},{10,11... | collective-permute-start | bytes 835808 | tf_op jit(solution)/shard_map/ppermute | solution.py:14
  41.1 18.5 %copy-start.7 = (f32[16,128]{1,0:T(8,128)}, f32[16,128]{1,0:T(8,128)S(1)}, u32[]{:S(2)}) copy-start(f32[16,128]{1,0:T(8,128)S(1)} %get-tuple-element.61) | copy-start | bytes 24580
  41.1 18.5 %copy-start.8 = (f32[16,128]{1,0:T(8,128)}, f32[16,128]{1,0:T(8,128)S(1)}, u32[]{:S(2)}) copy-start(f32[16,128]{1,0:T(8,128)S(1)} %get-tuple-element.60) | copy-start | bytes 24580
  41.8 17.9 %copy-start.23 = (f32[16]{0:T(128)}, f32[16]{0:T(128)S(1)}, u32[]{:S(2)}) copy-start(f32[16]{0:T(128)S(1)} %slice_add_fusion.5) | copy-start | bytes 196
  47.1 9.0 %collective-permute-start.3 = (f32[69650]{0:T(1024)}, f32[69650]{0:T(1024)S(1)}, u32[]{:S(2)}, u32[]{:S(2)}) collective-permute-start(f32[69650]{0:T(1024)} %concatenate.39), channel_id=1, source_target_pairs={{0,2},{1,3},{2,0},{3,1},{4,6},{5,7},{6,4},{7,5},{8,10},{9,11},{10,... | collective-permute-start | bytes 835808 | tf_op jit(solution)/shard_map/ppermute | solution.py:14
  56.1 4.3 %copy-start.5 = (f32[69650]{0:T(1024)}, f32[69650]{0:T(1024)S(1)}, u32[]{:S(2)}) copy-start(f32[69650]{0:T(1024)S(1)} %collective-permute-done.3) | copy-start | bytes 835804
  60.4 8.6 %copy-start.20 = (f32[16]{0:T(128)}, f32[16]{0:T(128)S(1)}, u32[]{:S(2)}) copy-start(f32[16]{0:T(128)S(1)} %slice_add_fusion.4) | copy-start | bytes 196
  66.4 15.1 %collective-permute-start.4 = (f32[69650]{0:T(1024)}, f32[69650]{0:T(1024)S(1)}, u32[]{:S(2)}, u32[]{:S(2)}) collective-permute-start(f32[69650]{0:T(1024)} %concatenate.40), channel_id=1, source_target_pairs={{0,4},{1,5},{2,6},{3,7},{4,0},{5,1},{6,2},{7,3},{8,12},{9,13},{10,... | collective-permute-start | bytes 835808 | tf_op jit(solution)/shard_map/ppermute | solution.py:14
  81.5 0.7 copy-start.6
  85.0 9.1 %copy-start.12 = (f32[2,16,128]{2,1,0:T(8,128)S(1)}, f32[2,16,128]{2,1,0:T(8,128)}, u32[]{:S(2)}) copy-start(f32[2,16,128]{2,1,0:T(8,128)} %param.19) | copy-start | bytes 49156
  85.0 9.1 %copy-start.16 = (s32[48]{0:T(128)S(1)}, s32[48]{0:T(128)}, u32[]{:S(2)}) copy-start(s32[48]{0:T(128)} %param.12) | copy-start | bytes 580
  85.0 9.1 %copy-start.18 = (f32[48]{0:T(128)S(1)}, f32[48]{0:T(128)}, u32[]{:S(2)}) copy-start(f32[48]{0:T(128)} %compare_convert_fusion) | copy-start | bytes 580
  85.0 9.1 %copy-start.19 = (f32[2,128]{1,0:T(2,128)S(1)}, f32[2,128]{1,0:T(2,128)}, u32[]{:S(2)}) copy-start(f32[2,128]{1,0:T(2,128)} %param.15) | copy-start | bytes 3076
  94.0 4.7 %copy-start.17 = (s32[48]{0:T(128)S(1)}, s32[48]{0:T(128)}, u32[]{:S(2)}) copy-start(s32[48]{0:T(128)} %param.13) | copy-start | bytes 580
  94.8 4.4 %collective-permute-start.5 = (f32[32]{0:T(128)S(1)}, f32[32]{0:T(128)S(1)}, u32[]{:S(2)}, u32[]{:S(2)}) collective-permute-start(f32[32]{0:T(128)S(1)} %pad_maximum_fusion.5), channel_id=1, source_target_pairs={{0,8},{8,0},{16,24},{24,16},{1,9},{9,1},{17,25},{25,17},{2,10},{10... | collective-permute-start | bytes 392 | tf_op jit(solution)/shard_map/ppermute | solution.py:14
  95.8 23.1 %copy-start.10 = (f32[16,128]{1,0:T(8,128)S(1)}, f32[16,128]{1,0:T(8,128)}, u32[]{:S(2)}) copy-start(f32[16,128]{1,0:T(8,128)} %copy-done.9) | copy-start | bytes 24580
  99.3 3.5 %collective-permute-start.6 = (f32[32]{0:T(128)S(1)}, f32[32]{0:T(128)S(1)}, u32[]{:S(2)}, u32[]{:S(2)}) collective-permute-start(f32[32]{0:T(128)S(1)} %pad_maximum_fusion.6), channel_id=1, source_target_pairs={{0,16},{8,24},{16,0},{24,8},{1,17},{9,25},{17,1},{25,9},{2,18},{10... | collective-permute-start | bytes 392 | tf_op jit(solution)/shard_map/ppermute | solution.py:14
  102.9 1.4 collective-permute-start.7
  104.4 5.7 %collective-permute-start.8 = (f32[32784]{0:T(1024)S(1)}, f32[32784]{0:T(1024)S(1)}, u32[]{:S(2)}, u32[]{:S(2)}) collective-permute-start(f32[32784]{0:T(1024)S(1)} %pad_maximum_fusion.1), channel_id=1, source_target_pairs={{0,2},{1,3},{2,0},{3,1},{4,6},{5,7},{6,4},{7,5},{8,10},{9,11},{10,... | collective-permute-start | bytes 393416 | tf_op jit(solution)/shard_map/ppermute | solution.py:14
  110.1 8.7 %collective-permute-start.9 = (f32[32784]{0:T(1024)S(1)}, f32[32784]{0:T(1024)S(1)}, u32[]{:S(2)}, u32[]{:S(2)}) collective-permute-start(f32[32784]{0:T(1024)S(1)} %pad_maximum_fusion.2), channel_id=1, source_target_pairs={{0,4},{1,5},{2,6},{3,7},{4,0},{5,1},{6,2},{7,3},{8,12},{9,13},{10,... | collective-permute-start | bytes 393416 | tf_op jit(solution)/shard_map/ppermute | solution.py:14
  125.2 3.5 %collective-permute-start.10 = (f32[32]{0:T(128)S(1)}, f32[32]{0:T(128)S(1)}, u32[]{:S(2)}, u32[]{:S(2)}) collective-permute-start(f32[32]{0:T(128)S(1)} %pad_maximum_fusion.7), channel_id=1, source_target_pairs={{0,8},{8,0},{16,24},{24,16},{1,9},{9,1},{17,25},{25,17},{2,10},{10... | collective-permute-start | bytes 392 | tf_op jit(solution)/shard_map/ppermute | solution.py:14
  128.9 3.5 %collective-permute-start.11 = (f32[32]{0:T(128)S(1)}, f32[32]{0:T(128)S(1)}, u32[]{:S(2)}, u32[]{:S(2)}) collective-permute-start(f32[32]{0:T(128)S(1)} %pad_maximum_fusion.8), channel_id=1, source_target_pairs={{0,16},{8,24},{16,0},{24,8},{1,17},{9,25},{17,1},{25,9},{2,18},{10... | collective-permute-start | bytes 392 | tf_op jit(solution)/shard_map/ppermute | solution.py:14
  132.5 1.1 collective-permute-start.12
  133.6 3.5 %collective-permute-start.13 = (f32[16]{0:T(128)S(1)}, f32[16]{0:T(128)S(1)}, u32[]{:S(2)}, u32[]{:S(2)}) collective-permute-start(f32[16]{0:T(128)S(1)} %add.224), channel_id=1, source_target_pairs={{0,2},{1,3},{2,0},{3,1},{4,6},{5,7},{6,4},{7,5},{8,10},{9,11},{10,... | collective-permute-start | bytes 200 | tf_op jit(solution)/shard_map/ppermute | solution.py:14
  137.2 4.4 %collective-permute-start.14 = (f32[16]{0:T(128)S(1)}, f32[16]{0:T(128)S(1)}, u32[]{:S(2)}, u32[]{:S(2)}) collective-permute-start(f32[16]{0:T(128)S(1)} %add.225), channel_id=1, source_target_pairs={{0,4},{1,5},{2,6},{3,7},{4,0},{5,1},{6,2},{7,3},{8,12},{9,13},{10,... | collective-permute-start | bytes 200 | tf_op jit(solution)/shard_map/ppermute | solution.py:14

commit v7 on v5

--- a/solution.py
+++ b/solution.py
@@ -120,13 +120,18 @@
     (local_a, local_c, local_b), _ = _rounds(
         "region", [local_a.reshape(1), local_c, local_b.reshape(1)]
     )
-    partial_value = transposed_product(dual)
-    (grad, sq_a, sq_c, sq_b), _ = _rounds("col", [partial_value, local_a, local_c, local_b])
     primal_reg = gathered[:, : own_blocks * scenarios].reshape(region_blocks, scenarios, lanes)
     base_reg = gathered[:, own_blocks * scenarios : own_blocks * (scenarios + 1)]
     upper_reg = gathered[:, own_blocks * (scenarios + 1) : own_rows]
     cost_reg = base_reg.reshape(region_blocks, lanes)[:, None, :] * factor[None, :, :]
-    upper_reg = upper_reg.reshape(region_blocks, lanes)[:, None, :]
+    upper_reg = jnp.broadcast_to(
+        upper_reg.reshape(region_blocks, lanes)[:, None, :], (region_blocks, scenarios, lanes)
+    )
+    partial_value = transposed_product(dual)
+    partial_value, primal_reg, cost_reg, upper_reg = lax.optimization_barrier(
+        (partial_value, primal_reg, cost_reg, upper_reg)
+    )
+    (grad, sq_a, sq_c, sq_b), _ = _rounds("col", [partial_value, local_a, local_c, local_b])
     eta = 0.5 / jnp.sqrt(sq_a[0] / (lanes * row_blocks * devices))
     weight = jnp.sqrt(sq_c) / jnp.sqrt(sq_b[0])
     for step in range(ITERS):

time: 155 us -> 131 us (0.85)
  local copies, waits for them, and re-layouts: 31.8 us -> 14.9 us
  other arithmetic: 27.1 us -> 18.9 us
  waiting for transfers between devices: 38.9 us -> 45.4 us
  matrix products: 25 us -> 20.6 us
    reshape x9 -> x0, local copies, waits for them, and re-layouts: 9.05 us -> none  [the longest x6 6.77 us: _rounds(): new_sums.append(s + got[off:off + size].reshape(shape))]
    ppermute x18, waiting for transfers between devices: 38.9 us -> 45.4 us  [_exchange(): return lax.ppermute(x, axis, [(i, i ^ 1 << bit) for i in range(n)])]
    mul x7 -> x0, local copies, waits for them, and re-layouts: 4.17 us -> none  [the longest x6 3.46 us: local(): new_primal = jnp.clip(primal_reg - tau * (cost_reg - grad), 0.0, upper_reg)]
    slice x7 -> x9, local copies, waits for them, and re-layouts: 7.62 us -> 3.86 us  [_rounds(): new_sums.append(s + got[off:off + size].reshape(shape))]
    slice x4 -> x2, other arithmetic: 3.01 us -> 0.04 us  [_rounds(): new_sums.append(s + got[off:off + size].reshape(shape))]
    reduce_sum x4 -> x2, other arithmetic: 4.45 us -> 1.6 us  [local(): local_x = jnp.sum((new_primal - primal_reg) ** 2, axis=(0, 2))]
    add x13 -> x14, other arithmetic: 3.3 us -> 5.77 us  [_rounds(): new_sums.append(s + got[off:off + size].reshape(shape))]
    unnamed x1 -> x0, other arithmetic: 1.9 us -> none
  transfers between devices with their start and end apart: 18 -> 18, of which waited for: 16 -> 16; matrix products, arithmetic and copies ran while one was open for 16% -> 13% of each run, Pallas kernels for 0% -> 0%
where the time goes in v7:
time: 131 us
  waiting for transfers between devices  45.4 us (35%)
  starting transfers between devices  21.3 us (16%)
  matrix products  20.6 us (16%)
  other arithmetic  18.9 us (14%)
  local copies, waits for them, and re-layouts  14.9 us (11%)
  between operations  9.52 us (7%)
    ppermute x18, waiting for transfers between devices, _exchange(): return lax.ppermute(x, axis, [(i, i ^ 1 << bit) for i in range(n)])  45.4 us
    ppermute x18, starting transfers between devices, _exchange(): return lax.ppermute(x, axis, [(i, i ^ 1 << bit) for i in range(n)])  21.3 us
    dot_general x2, matrix products, local(): image = jnp.einsum('tij,tsj->tsi', tiles, selected, precision=hp)  9.99 us
    dot_general x2, matrix products, transposed_product(): contrib = jnp.einsum('tij,tsi->tsj', tiles, dual_rows, precision=hp)  5.92 us
    add x14, other arithmetic, _rounds(): new_sums.append(s + got[off:off + size].reshape(shape))  5.77 us
    concatenate x3, local copies, waits for them, and re-layouts, _rounds(): flat = jnp.concatenate(parts) if len(parts) > 1 else parts[0]  4.62 us
    reduce_sum x2, other arithmetic, local(): local_a = jnp.sum(jnp.sum(tiles * tiles, axis=(1, 2)) * live)  4.12 us
    slice x9, local copies, waits for them, and re-layouts, _rounds(): new_sums.append(s + got[off:off + size].reshape(shape))  3.86 us
  transfers between devices with their start and end apart: 18, of which 16 were waited for; matrix products, arithmetic and copies ran while one was open for 13% of the time, Pallas kernels for 0%

profile of v7, /device:TPU:0, one launch (start us, length us, event | category | flops | bytes accessed | tf_op | source)
XLA Modules:
  0.0 130.5 jit_solution(13293115816516843323)
XLA Ops:
  0.8 1.0 fusion.41
  3.0 2.9 %multiply_reduce_fusion = f32[48]{0:T(128)} fusion(f32[48,128,128]{2,1,0:T(8,128)} %param.11), kind=kLoop, calls=%fused_computation | loop fusion | flops 1572816 | bytes 3145920 | tf_op jit(solution)/shard_map/reduce_sum | solution.py:92
  6.2 2.9 %fusion.21 = f32[48,16,128]{2,1,0:T(8,128)S(1)} fusion(f32[48,128,128]{2,1,0:T(8,128)S(1)} %copy-done.1, f32[48,16,128]{2,0,1:T(8,128)S(1)} %fusion.42), kind=kOutput, calls=%fused_computation.28 | convolution fusion | flops 150994944 | bytes 3932160 | tf_op jit(solution)/shard_map/tij,tsi->tsj/dot_general | solution.py:101
  9.8 0.7 multiply_reduce_fusion.5
  10.5 2.6 %collective-permute-start.1 = (f32[10240]{0:T(1024)S(1)}, f32[10240]{0:T(1024)S(1)}, u32[]{:S(2)}, u32[]{:S(2)}) collective-permute-start(f32[10240]{0:T(1024)S(1)} %bitcast.197), channel_id=1, source_target_pairs={{0,2},{1,3},{2,0},{3,1},{4,6},{5,7},{6,4},{7,5},{8,10},{9,11},{10,... | collective-permute-start | bytes 122888 | tf_op jit(solution)/shard_map/ppermute | solution.py:14
  13.1 1.3 fusion.66
  14.4 1.0 collective-permute-done.1
  15.4 2.8 %collective-permute-start.2 = (f32[20480]{0:T(1024)S(1)}, f32[20480]{0:T(1024)S(1)}, u32[]{:S(2)}, u32[]{:S(2)}) collective-permute-start(f32[20480]{0:T(1024)S(1)} %bitcast.194), channel_id=1, source_target_pairs={{0,4},{1,5},{2,6},{3,7},{4,0},{5,1},{6,2},{7,3},{8,12},{9,13},{10,... | collective-permute-start | bytes 245768 | tf_op jit(solution)/shard_map/ppermute | solution.py:14
  18.2 1.3 multiply_reduce_fusion.6
  19.5 2.9 %collective-permute-done.2 = f32[20480]{0:T(1024)S(1)} collective-permute-done((f32[20480]{0:T(1024)S(1)}, f32[20480]{0:T(1024)S(1)}, u32[]{:S(2)}, u32[]{:S(2)}) %collective-permute-start.2) | collective-permute-done | bytes 81952 | tf_op jit(solution)/shard_map/ppermute | solution.py:14
  22.4 0.7 slice.105
  23.0 2.0 %pad_maximum_fusion.3 = f32[18]{0:T(128)S(1)} fusion(f32[1]{0:T(128)} %bitcast.18, f32[16]{0:T(128)} %multiply_reduce_fusion.5, f32[1]{0:T(128)} %bitcast.17), kind=kLoop, calls=%fused_computation.114 | loop fusion | flops 36 | bytes 144 | tf_op jit(solution)/shard_map/concatenate | solution.py:39
  25.1 1.3 collective-permute-start.3
  26.3 2.3 %collective-permute-done.3 = f32[18]{0:T(128)S(1)} collective-permute-done((f32[18]{0:T(128)S(1)}, f32[18]{0:T(128)S(1)}, u32[]{:S(2)}, u32[]{:S(2)}) %collective-permute-start.3) | collective-permute-done | bytes 104 | tf_op jit(solution)/shard_map/ppermute | solution.py:14
  28.6 0.6 fusion.91
  31.7 0.7 slice_add_fusion.13
  32.6 1.3 collective-permute-start.4
  33.8 0.7 copy.42
  34.5 1.6 %collective-permute-done.4 = f32[18]{0:T(128)S(1)} collective-permute-done((f32[18]{0:T(128)S(1)}, f32[18]{0:T(128)S(1)}, u32[]{:S(2)}, u32[]{:S(2)}) %collective-permute-start.4) | collective-permute-done | bytes 104 | tf_op jit(solution)/shard_map/ppermute | solution.py:14
  36.1 0.6 fusion.90
  38.0 0.6 slice_add_fusion.12
  38.6 1.6 %concatenate.42 = f32[32786]{0:T(1024)} concatenate(f32[32768]{0:T(1024)} %bitcast.189, f32[1]{0:T(128)S(6)} %add.165, f32[16]{0:T(128)} %slice_add_fusion.12, f32[1]{0:T(128)S(6)} %add.167), dimensions={0} | concatenate | bytes 262288 | tf_op jit(solution)/shard_map/concatenate | solution.py:39
  40.2 1.6 %collective-permute-done.5 = f32[32786]{0:T(1024)S(1)} collective-permute-done((f32[32786]{0:T(1024)}, f32[32786]{0:T(1024)S(1)}, u32[]{:S(2)}, u32[]{:S(2)}) %collective-permute-start.5) | collective-permute-done | bytes 131176 | tf_op jit(solution)/shard_map/ppermute | solution.py:14
  43.7 1.0 copy_add_fusion.2
  44.6 0.7 copy.44
  45.3 1.2 slice_add_fusion.5
  46.6 1.6 %concatenate.43 = f32[32786]{0:T(1024)} concatenate(f32[32768]{0:T(1024)} %bitcast.190, f32[1]{0:T(128)S(6)} %add.168, f32[16]{0:T(128)} %slice_add_fusion.5, f32[1]{0:T(128)S(6)} %add.171), dimensions={0} | concatenate | bytes 262288 | tf_op jit(solution)/shard_map/concatenate | solution.py:39
  48.5 5.6 %collective-permute-done.6 = f32[32786]{0:T(1024)S(1)} collective-permute-done((f32[32786]{0:T(1024)}, f32[32786]{0:T(1024)S(1)}, u32[]{:S(2)}, u32[]{:S(2)}) %collective-permute-start.6) | collective-permute-done | bytes 131176 | tf_op jit(solution)/shard_map/ppermute | solution.py:14
  56.0 0.6 copy-done.3
  56.7 1.2 slice_add_fusion.4
  57.9 1.4 %concatenate.44 = f32[32786]{0:T(1024)} concatenate(f32[32768]{0:T(1024)S(1)} %bitcast.191, f32[1]{0:T(128)S(6)} %add.172, f32[16]{0:T(128)} %slice_add_fusion.4, f32[1]{0:T(128)S(6)} %add.175), dimensions={0} | concatenate | bytes 262288 | tf_op jit(solution)/shard_map/concatenate | solution.py:39
  59.3 1.9 %collective-permute-start.7 = (f32[32786]{0:T(1024)}, f32[32786]{0:T(1024)S(1)}, u32[]{:S(2)}, u32[]{:S(2)}) collective-permute-start(f32[32786]{0:T(1024)} %concatenate.44), channel_id=1, source_target_pairs={{0,4},{1,5},{2,6},{3,7},{4,0},{5,1},{6,2},{7,3},{8,12},{9,13},{10,... | collective-permute-start | bytes 393440 | tf_op jit(solution)/shard_map/ppermute | solution.py:14
  61.2 6.9 %collective-permute-done.7 = f32[32786]{0:T(1024)S(1)} collective-permute-done((f32[32786]{0:T(1024)}, f32[32786]{0:T(1024)S(1)}, u32[]{:S(2)}, u32[]{:S(2)}) %collective-permute-start.7) | collective-permute-done | bytes 131176 | tf_op jit(solution)/shard_map/ppermute | solution.py:14
  68.1 0.6 copy-done.5
  70.8 0.9 slice.151
  71.7 0.8 broadcast_multiply_fusion.2
  72.5 1.3 multiply_reduce_fusion.2
  73.8 1.3 fusion.33
  75.1 5.0 %fusion.19 = f32[48,16,128]{2,1,0:T(8,128)S(1)} fusion(f32[48,128,128]{2,1,0:T(8,128)S(1)} %copy-done.1, f32[48,16,128]{2,0,1:T(8,128)S(1)} %fusion.33), kind=kOutput, calls=%fused_computation.26 | convolution fusion | flops 150994944 | bytes 3932160 | tf_op jit(solution)/shard_map/tij,tsj->tsi/dot_general | solution.py:150
  80.1 0.6 multiply_reduce_fusion.4
  80.8 1.3 collective-permute-start.8
  82.4 3.0 %fusion.17 = f32[48,16,128]{2,1,0:T(8,128)S(1)} fusion(f32[48,128,128]{2,1,0:T(8,128)S(1)} %copy-done.1, f32[48,16,128]{2,0,1:T(8,128)S(1)} %fusion.44), kind=kOutput, calls=%fused_computation.24 | convolution fusion | flops 150994944 | bytes 3932160 | tf_op jit(solution)/shard_map/tij,tsi->tsj/dot_general | solution.py:101
  85.6 1.5 %collective-permute-start.9 = (f32[32]{0:T(128)S(1)}, f32[32]{0:T(128)S(1)}, u32[]{:S(2)}, u32[]{:S(2)}) collective-permute-start(f32[32]{0:T(128)S(1)} %pad_maximum_fusion.6), channel_id=1, source_target_pairs={{0,16},{8,24},{16,0},{24,8},{1,17},{9,25},{17,1},{25,9},{2,18},{10... | collective-permute-start | bytes 392 | tf_op jit(solution)/shard_map/ppermute | solution.py:14
  87.6 1.6 %collective-permute-done.9 = f32[32]{0:T(128)S(1)} collective-permute-done((f32[32]{0:T(128)S(1)}, f32[32]{0:T(128)S(1)}, u32[]{:S(2)}, u32[]{:S(2)}) %collective-permute-start.9) | collective-permute-done | bytes 160 | tf_op jit(solution)/shard_map/ppermute | solution.py:14
  89.4 1.3 %collective-permute-done.10 = f32[32784]{0:T(1024)S(1)} collective-permute-done((f32[32784]{0:T(1024)S(1)}, f32[32784]{0:T(1024)S(1)}, u32[]{:S(2)}, u32[]{:S(2)}) %collective-permute-start.10) | collective-permute-done | bytes 131168 | tf_op jit(solution)/shard_map/ppermute | solution.py:14
  90.7 0.7 collective-permute-start.11
  91.4 5.0 %collective-permute-done.11 = f32[32784]{0:T(1024)S(1)} collective-permute-done((f32[32784]{0:T(1024)S(1)}, f32[32784]{0:T(1024)S(1)}, u32[]{:S(2)}, u32[]{:S(2)}) %collective-permute-start.11) | collective-permute-done | bytes 131168 | tf_op jit(solution)/shard_map/ppermute | solution.py:14
  96.5 2.2 %collective-permute-start.12 = (f32[32784]{0:T(1024)S(1)}, f32[32784]{0:T(1024)S(1)}, u32[]{:S(2)}, u32[]{:S(2)}) collective-permute-start(f32[32784]{0:T(1024)S(1)} %pad_maximum_fusion.2), channel_id=1, source_target_pairs={{0,4},{1,5},{2,6},{3,7},{4,0},{5,1},{6,2},{7,3},{8,12},{9,13},{10,... | collective-permute-start | bytes 393416 | tf_op jit(solution)/shard_map/ppermute | solution.py:14
  98.7 6.4 %collective-permute-done.12 = f32[32784]{0:T(1024)S(1)} collective-permute-done((f32[32784]{0:T(1024)S(1)}, f32[32784]{0:T(1024)S(1)}, u32[]{:S(2)}, u32[]{:S(2)}) %collective-permute-start.12) | collective-permute-done | bytes 131168 | tf_op jit(solution)/shard_map/ppermute | solution.py:14
  105.5 0.7 copy-done.4
  106.6 5.0 %fusion.15 = f32[48,16,128]{2,1,0:T(8,128)S(1)} fusion(f32[48,128,128]{2,1,0:T(8,128)S(1)} %copy-done.1, f32[48,16,128]{2,0,1:T(8,128)S(1)} %fusion.23), kind=kOutput, calls=%fused_computation.22 | convolution fusion | flops 150994944 | bytes 3932160 | tf_op jit(solution)/shard_map/tij,tsj->tsi/dot_general | solution.py:150
  111.6 0.6 multiply_reduce_fusion.3
  112.3 0.8 collective-permute-start.13
  113.0 2.8 %collective-permute-done.13 = f32[32]{0:T(128)S(1)} collective-permute-done((f32[32]{0:T(128)S(1)}, f32[32]{0:T(128)S(1)}, u32[]{:S(2)}, u32[]{:S(2)}) %collective-permute-start.13) | collective-permute-done | bytes 160 | tf_op jit(solution)/shard_map/ppermute | solution.py:14
  115.8 0.7 slice_add_fusion.8
  116.6 1.5 %collective-permute-start.14 = (f32[32]{0:T(128)S(1)}, f32[32]{0:T(128)S(1)}, u32[]{:S(2)}, u32[]{:S(2)}) collective-permute-start(f32[32]{0:T(128)S(1)} %pad_maximum_fusion.8), channel_id=1, source_target_pairs={{0,16},{8,24},{16,0},{24,8},{1,17},{9,25},{17,1},{25,9},{2,18},{10... | collective-permute-start | bytes 392 | tf_op jit(solution)/shard_map/ppermute | solution.py:14
  118.1 2.0 %collective-permute-done.14 = f32[32]{0:T(128)S(1)} collective-permute-done((f32[32]{0:T(128)S(1)}, f32[32]{0:T(128)S(1)}, u32[]{:S(2)}, u32[]{:S(2)}) %collective-permute-start.14) | collective-permute-done | bytes 160 | tf_op jit(solution)/shard_map/ppermute | solution.py:14
  120.2 0.8 constant_dynamic-slice_fusion
  121.9 0.6 copy.66
  122.5 2.4 %collective-permute-done.16 = f32[16]{0:T(128)S(1)} collective-permute-done((f32[16]{0:T(128)S(1)}, f32[16]{0:T(128)S(1)}, u32[]{:S(2)}, u32[]{:S(2)}) %collective-permute-start.16) | collective-permute-done | bytes 96 | tf_op jit(solution)/shard_map/ppermute | solution.py:14
  124.9 1.9 %collective-permute-start.17 = (f32[16]{0:T(128)S(1)}, f32[16]{0:T(128)S(1)}, u32[]{:S(2)}, u32[]{:S(2)}) collective-permute-start(f32[16]{0:T(128)S(1)} %add.203), channel_id=1, source_target_pairs={{0,4},{1,5},{2,6},{3,7},{4,0},{5,1},{6,2},{7,3},{8,12},{9,13},{10,... | collective-permute-start | bytes 200 | tf_op jit(solution)/shard_map/ppermute | solution.py:14
  126.8 0.6 copy.67
  127.4 1.9 %collective-permute-done.17 = f32[16]{0:T(128)S(1)} collective-permute-done((f32[16]{0:T(128)S(1)}, f32[16]{0:T(128)S(1)}, u32[]{:S(2)}, u32[]{:S(2)}) %collective-permute-start.17) | collective-permute-done | bytes 96 | tf_op jit(solution)/shard_map/ppermute | solution.py:14
  129.3 1.2 multiply_sqrt_fusion
  (92 shorter events, 7.0 us)
Async XLA Ops:
  0.6 8.5 %copy-start = (f32[32,128]{1,0:T(8,128)S(1)}, f32[32,128]{1,0:T(8,128)}, u32[]{:S(2)}) copy-start(f32[32,128]{1,0:T(8,128)} %param.20) | copy-start | bytes 49156
  0.6 5.6 %copy-start.1 = (f32[48,128,128]{2,1,0:T(8,128)S(1)}, f32[48,128,128]{2,1,0:T(8,128)}, u32[]{:S(2)}) copy-start(f32[48,128,128]{2,1,0:T(8,128)} %param.11) | copy-start | bytes 9437188
  0.7 5.2 %copy-start.8 = (s32[48]{0:T(128)S(1)}, s32[48]{0:T(128)}, u32[]{:S(2)}) copy-start(s32[48]{0:T(128)} %param.12) | copy-start | bytes 580
  0.7 5.2 %copy-start.6 = (f32[2,16,128]{2,1,0:T(8,128)S(1)}, f32[2,16,128]{2,1,0:T(8,128)}, u32[]{:S(2)}) copy-start(f32[2,16,128]{2,1,0:T(8,128)} %param.19) | copy-start | bytes 49156
  1.8 8.7 %collective-permute-start = (f32[5120]{0:T(1024)S(1)}, f32[5120]{0:T(1024)S(1)}, u32[]{:S(2)}, u32[]{:S(2)}) collective-permute-start(f32[5120]{0:T(1024)S(1)} %dynamic-slice_bitcast_fusion), channel_id=1, source_target_pairs={{0,1},{1,0},{2,3},{3,2},{4,5},{5,4},{6,7},{7,6},{8,9},{9,8},{10,11... | collective-permute-start | bytes 61448 | tf_op jit(solution)/shard_map/ppermute | solution.py:14
  2.9 6.4 %copy-start.10 = (f32[48]{0:T(128)}, f32[48]{0:T(128)S(1)}, u32[]{:S(2)}) copy-start(f32[48]{0:T(128)S(1)} %compare_convert_fusion) | copy-start | bytes 580
  2.9 6.2 %copy-start.18 = (s32[16]{0:T(128)S(1)}, s32[16]{0:T(128)}, u32[]{:S(2)}) copy-start(s32[16]{0:T(128)} %param.21) | copy-start | bytes 196
  3.0 6.3 %copy-start.12 = (s32[48]{0:T(128)S(1)}, s32[48]{0:T(128)}, u32[]{:S(2)}) copy-start(s32[48]{0:T(128)} %param.13) | copy-start | bytes 580
  5.8 3.9 %copy-start.15 = (f32[2,128]{1,0:T(2,128)S(1)}, f32[2,128]{1,0:T(2,128)}, u32[]{:S(2)}) copy-start(f32[2,128]{1,0:T(2,128)} %param.16) | copy-start | bytes 3076
  9.7 33.9 %copy-start.2 = (f32[16,16,128]{2,0,1:T(8,128)}, f32[16,16,128]{2,0,1:T(8,128)S(1)}, u32[]{:S(2)}) copy-start(f32[16,16,128]{2,0,1:T(8,128)S(1)} %fusion.12) | copy-start | bytes 393220
  10.5 4.9 %collective-permute-start.1 = (f32[10240]{0:T(1024)S(1)}, f32[10240]{0:T(1024)S(1)}, u32[]{:S(2)}, u32[]{:S(2)}) collective-permute-start(f32[10240]{0:T(1024)S(1)} %bitcast.197), channel_id=1, source_target_pairs={{0,2},{1,3},{2,0},{3,1},{4,6},{5,7},{6,4},{7,5},{8,10},{9,11},{10,... | collective-permute-start | bytes 122888 | tf_op jit(solution)/shard_map/ppermute | solution.py:14
  15.4 7.0 %collective-permute-start.2 = (f32[20480]{0:T(1024)S(1)}, f32[20480]{0:T(1024)S(1)}, u32[]{:S(2)}, u32[]{:S(2)}) collective-permute-start(f32[20480]{0:T(1024)S(1)} %bitcast.194), channel_id=1, source_target_pairs={{0,4},{1,5},{2,6},{3,7},{4,0},{5,1},{6,2},{7,3},{8,12},{9,13},{10,... | collective-permute-start | bytes 245768 | tf_op jit(solution)/shard_map/ppermute | solution.py:14
  25.1 3.5 %collective-permute-start.3 = (f32[18]{0:T(128)S(1)}, f32[18]{0:T(128)S(1)}, u32[]{:S(2)}, u32[]{:S(2)}) collective-permute-start(f32[18]{0:T(128)S(1)} %pad_maximum_fusion.3), channel_id=1, source_target_pairs={{0,8},{8,0},{16,24},{24,16},{1,9},{9,1},{17,25},{25,17},{2,10},{10... | collective-permute-start | bytes 224 | tf_op jit(solution)/shard_map/ppermute | solution.py:14
  32.6 3.5 %collective-permute-start.4 = (f32[18]{0:T(128)S(1)}, f32[18]{0:T(128)S(1)}, u32[]{:S(2)}, u32[]{:S(2)}) collective-permute-start(f32[18]{0:T(128)S(1)} %pad_maximum_fusion.4), channel_id=1, source_target_pairs={{0,16},{8,24},{16,0},{24,8},{1,17},{9,25},{17,1},{25,9},{2,18},{10... | collective-permute-start | bytes 224 | tf_op jit(solution)/shard_map/ppermute | solution.py:14
  40.2 1.6 %collective-permute-start.5 = (f32[32786]{0:T(1024)}, f32[32786]{0:T(1024)S(1)}, u32[]{:S(2)}, u32[]{:S(2)}) collective-permute-start(f32[32786]{0:T(1024)} %concatenate.42), channel_id=1, source_target_pairs={{0,1},{1,0},{2,3},{3,2},{4,5},{5,4},{6,7},{7,6},{8,9},{9,8},{10,11... | collective-permute-start | bytes 393440 | tf_op jit(solution)/shard_map/ppermute | solution.py:14
  48.2 5.8 %collective-permute-start.6 = (f32[32786]{0:T(1024)}, f32[32786]{0:T(1024)S(1)}, u32[]{:S(2)}, u32[]{:S(2)}) collective-permute-start(f32[32786]{0:T(1024)} %concatenate.43), channel_id=1, source_target_pairs={{0,2},{1,3},{2,0},{3,1},{4,6},{5,7},{6,4},{7,5},{8,10},{9,11},{10,... | collective-permute-start | bytes 393440 | tf_op jit(solution)/shard_map/ppermute | solution.py:14
  56.0 0.7 copy-start.3
  59.3 8.8 %collective-permute-start.7 = (f32[32786]{0:T(1024)}, f32[32786]{0:T(1024)S(1)}, u32[]{:S(2)}, u32[]{:S(2)}) collective-permute-start(f32[32786]{0:T(1024)} %concatenate.44), channel_id=1, source_target_pairs={{0,4},{1,5},{2,6},{3,7},{4,0},{5,1},{6,2},{7,3},{8,12},{9,13},{10,... | collective-permute-start | bytes 393440 | tf_op jit(solution)/shard_map/ppermute | solution.py:14
  68.1 0.7 copy-start.5
  70.7 9.3 %copy-start.7 = (f32[2,16,128]{2,1,0:T(8,128)S(1)}, f32[2,16,128]{2,1,0:T(8,128)}, u32[]{:S(2)}) copy-start(f32[2,16,128]{2,1,0:T(8,128)} %param.19) | copy-start | bytes 49156
  70.8 9.3 %copy-start.9 = (s32[48]{0:T(128)S(1)}, s32[48]{0:T(128)}, u32[]{:S(2)}) copy-start(s32[48]{0:T(128)} %param.12) | copy-start | bytes 580
  70.8 9.3 %copy-start.11 = (f32[48]{0:T(128)S(1)}, f32[48]{0:T(128)}, u32[]{:S(2)}) copy-start(f32[48]{0:T(128)} %copy-done.10) | copy-start | bytes 580
  70.8 9.3 %copy-start.14 = (f32[2,128]{1,0:T(2,128)S(1)}, f32[2,128]{1,0:T(2,128)}, u32[]{:S(2)}) copy-start(f32[2,128]{1,0:T(2,128)} %param.15) | copy-start | bytes 3076
  80.1 7.1 %copy-start.13 = (s32[48]{0:T(128)S(1)}, s32[48]{0:T(128)}, u32[]{:S(2)}) copy-start(s32[48]{0:T(128)} %param.13) | copy-start | bytes 580
  80.8 4.7 %collective-permute-start.8 = (f32[32]{0:T(128)S(1)}, f32[32]{0:T(128)S(1)}, u32[]{:S(2)}, u32[]{:S(2)}) collective-permute-start(f32[32]{0:T(128)S(1)} %pad_maximum_fusion.5), channel_id=1, source_target_pairs={{0,8},{8,0},{16,24},{24,16},{1,9},{9,1},{17,25},{25,17},{2,10},{10... | collective-permute-start | bytes 392 | tf_op jit(solution)/shard_map/ppermute | solution.py:14
  85.6 3.5 %collective-permute-start.9 = (f32[32]{0:T(128)S(1)}, f32[32]{0:T(128)S(1)}, u32[]{:S(2)}, u32[]{:S(2)}) collective-permute-start(f32[32]{0:T(128)S(1)} %pad_maximum_fusion.6), channel_id=1, source_target_pairs={{0,16},{8,24},{16,0},{24,8},{1,17},{9,25},{17,1},{25,9},{2,18},{10... | collective-permute-start | bytes 392 | tf_op jit(solution)/shard_map/ppermute | solution.py:14
  89.3 1.4 %collective-permute-start.10 = (f32[32784]{0:T(1024)S(1)}, f32[32784]{0:T(1024)S(1)}, u32[]{:S(2)}, u32[]{:S(2)}) collective-permute-start(f32[32784]{0:T(1024)S(1)} %pad_maximum_fusion), channel_id=1, source_target_pairs={{0,1},{1,0},{2,3},{3,2},{4,5},{5,4},{6,7},{7,6},{8,9},{9,8},{10,11... | collective-permute-start | bytes 393416 | tf_op jit(solution)/shard_map/ppermute | solution.py:14
  90.7 5.7 %collective-permute-start.11 = (f32[32784]{0:T(1024)S(1)}, f32[32784]{0:T(1024)S(1)}, u32[]{:S(2)}, u32[]{:S(2)}) collective-permute-start(f32[32784]{0:T(1024)S(1)} %pad_maximum_fusion.1), channel_id=1, source_target_pairs={{0,2},{1,3},{2,0},{3,1},{4,6},{5,7},{6,4},{7,5},{8,10},{9,11},{10,... | collective-permute-start | bytes 393416 | tf_op jit(solution)/shard_map/ppermute | solution.py:14
  96.5 8.7 %collective-permute-start.12 = (f32[32784]{0:T(1024)S(1)}, f32[32784]{0:T(1024)S(1)}, u32[]{:S(2)}, u32[]{:S(2)}) collective-permute-start(f32[32784]{0:T(1024)S(1)} %pad_maximum_fusion.2), channel_id=1, source_target_pairs={{0,4},{1,5},{2,6},{3,7},{4,0},{5,1},{6,2},{7,3},{8,12},{9,13},{10,... | collective-permute-start | bytes 393416 | tf_op jit(solution)/shard_map/ppermute | solution.py:14
  105.2 7.0 %copy-start.17 = (f32[16]{0:T(128)}, f32[16]{0:T(128)S(1)}, u32[]{:S(2)}) copy-start(f32[16]{0:T(128)S(1)} %get-tuple-element.31) | copy-start | bytes 196
  105.5 0.7 copy-start.4
  105.5 6.6 %copy-start.16 = (f32[16]{0:T(128)}, f32[16]{0:T(128)S(1)}, u32[]{:S(2)}) copy-start(f32[16]{0:T(128)S(1)} %get-tuple-element.28) | copy-start | bytes 196
  112.3 3.5 %collective-permute-start.13 = (f32[32]{0:T(128)S(1)}, f32[32]{0:T(128)S(1)}, u32[]{:S(2)}, u32[]{:S(2)}) collective-permute-start(f32[32]{0:T(128)S(1)} %pad_maximum_fusion.7), channel_id=1, source_target_pairs={{0,8},{8,0},{16,24},{24,16},{1,9},{9,1},{17,25},{25,17},{2,10},{10... | collective-permute-start | bytes 392 | tf_op jit(solution)/shard_map/ppermute | solution.py:14
  116.6 3.5 %collective-permute-start.14 = (f32[32]{0:T(128)S(1)}, f32[32]{0:T(128)S(1)}, u32[]{:S(2)}, u32[]{:S(2)}) collective-permute-start(f32[32]{0:T(128)S(1)} %pad_maximum_fusion.8), channel_id=1, source_target_pairs={{0,16},{8,24},{16,0},{24,8},{1,17},{9,25},{17,1},{25,9},{2,18},{10... | collective-permute-start | bytes 392 | tf_op jit(solution)/shard_map/ppermute | solution.py:14
  120.2 1.1 collective-permute-start.15
  121.4 3.5 %collective-permute-start.16 = (f32[16]{0:T(128)S(1)}, f32[16]{0:T(128)S(1)}, u32[]{:S(2)}, u32[]{:S(2)}) collective-permute-start(f32[16]{0:T(128)S(1)} %add.202), channel_id=1, source_target_pairs={{0,2},{1,3},{2,0},{3,1},{4,6},{5,7},{6,4},{7,5},{8,10},{9,11},{10,... | collective-permute-start | bytes 200 | tf_op jit(solution)/shard_map/ppermute | solution.py:14
  124.9 4.4 %collective-permute-start.17 = (f32[16]{0:T(128)S(1)}, f32[16]{0:T(128)S(1)}, u32[]{:S(2)}, u32[]{:S(2)}) collective-permute-start(f32[16]{0:T(128)S(1)} %add.203), channel_id=1, source_target_pairs={{0,4},{1,5},{2,6},{3,7},{4,0},{5,1},{6,2},{7,3},{8,12},{9,13},{10,... | collective-permute-start | bytes 200 | tf_op jit(solution)/shard_map/ppermute | solution.py:14

commit v8 on v4

--- a/solution.py
+++ b/solution.py
@@ -75,14 +75,6 @@
     devices = lax.axis_size(("region", "col"))
     me = lax.axis_index("col")
     live = (jnp.arange(ntiles, dtype=jnp.int32) < tile_count[0]).astype(jnp.float32)
-    row_select = (tile_rows[:, None] == jnp.arange(row_blocks, dtype=jnp.int32)[None, :]).astype(
-        jnp.float32
-    )
-    row_live = row_select * live[:, None]
-    col_select = (tile_cols[:, None] == jnp.arange(region_blocks, dtype=jnp.int32)[None, :]).astype(
-        jnp.float32
-    )
-    col_live = col_select * live[:, None]
     choose = (
         scenario_ids[:, None] == jnp.arange(price_levels.shape[0], dtype=jnp.int32)[None, :]
     ).astype(jnp.float32)
@@ -93,14 +85,19 @@
     local_b = jnp.sum(rhs * rhs)
     width = scenarios * lanes
 
+    place = tile_cols * row_blocks + tile_rows
+    place_live = (
+        place[None, :] == jnp.arange(region_blocks * row_blocks, dtype=jnp.int32)[:, None]
+    ).astype(jnp.float32) * live[None, :]
+    dense = jnp.dot(place_live, tiles.reshape(ntiles, -1), precision=hp)
+    dense = dense.reshape(region_blocks, row_blocks, tiles.shape[1], tiles.shape[2])
+    dense = dense.transpose(1, 2, 0, 3)
+
     def transposed_product(dual):
-        dual_rows = jnp.dot(row_select, dual.reshape(row_blocks, width), precision=hp).reshape(
-            ntiles, scenarios, lanes
-        )
-        contrib = jnp.einsum("tij,tsi->tsj", tiles, dual_rows, precision=hp)
-        return jnp.dot(col_live.T, contrib.reshape(ntiles, width), precision=hp).reshape(
-            region_blocks, scenarios, lanes
-        )
+        return jnp.einsum("rsi,ricj->csj", dual, dense, precision=hp)
+
+    def product_of(point):
+        return jnp.einsum("ricj,csj->rsi", dense, point, precision=hp)
 
     (local_a, local_c, local_b), _ = _rounds(
         "region", [local_a.reshape(1), local_c, local_b.reshape(1)]
@@ -136,13 +133,7 @@
         sigma = (eta * weight)[None, :, None]
         new_primal = jnp.clip(primal_reg - tau * (cost_reg - grad), 0.0, upper_reg)
         point = 2.0 * new_primal - primal_reg
-        selected = jnp.dot(col_select, point.reshape(region_blocks, width), precision=hp).reshape(
-            ntiles, scenarios, lanes
-        )
-        image = jnp.einsum("tij,tsj->tsi", tiles, selected, precision=hp)
-        product = jnp.dot(row_live.T, image.reshape(ntiles, width), precision=hp).reshape(
-            row_blocks, scenarios, lanes
-        )
+        product = product_of(point)
         new_dual = jnp.maximum(dual + sigma * (rhs[:, None, :] - product), 0.0)
         local_x = jnp.sum((new_primal - primal_reg) ** 2, axis=(0, 2))
         local_y = jnp.sum((new_dual - dual) ** 2, axis=(0, 2))

time: 128 us -> 100 us (0.78)
  local copies, waits for them, and re-layouts: 20.9 us -> 4.78 us
  matrix products: 21.5 us -> 14 us
  other arithmetic: 14.4 us -> 8.01 us
  waiting for transfers between devices: 41.7 us -> 44.2 us
    dot_general x12 -> x5, matrix products: 21.3 us -> 13.8 us  [the longest x1 5.56 us: local(): dense = jnp.dot(place_live, tiles.reshape(ntiles, -1), precision=hp)]
    concatenate x3, local copies, waits for them, and re-layouts: 6.36 us -> 0.95 us  [_rounds(): flat = jnp.concatenate(parts) if len(parts) > 1 else parts[0]]
    unnamed x43 -> x18, local copies, waits for them, and re-layouts: 4.69 us -> 0.05 us
    slice x9 -> x11, local copies, waits for them, and re-layouts: 7.05 us -> 2.98 us  [_rounds(): new_sums.append(s + got[off:off + size].reshape(shape))]
    add x14 -> x16, other arithmetic: 4.23 us -> 0.68 us  [_rounds(): new_sums.append(s + got[off:off + size].reshape(shape))]
    ppermute x15, waiting for transfers between devices: 41.7 us -> 44.2 us  [_exchange(): return lax.ppermute(x, axis, [(i, i ^ 1 << bit) for i in range(n)])]
  transfers between devices with their start and end apart: 15 -> 15, of which waited for: 12 -> 14; matrix products, arithmetic and copies ran while one was open for 10% -> 10% of each run, Pallas kernels for 0% -> 0%
where the time goes in v8:
time: 100 us; the launch traced here: 99.6 us
  waiting for transfers between devices  44.2 us (44%)
  starting transfers between devices  19 us (19%)
  matrix products  14 us (14%)
  between operations  9.54 us (10%)
  other arithmetic  8.01 us (8%)
  local copies, waits for them, and re-layouts  4.78 us (5%)
    ppermute x15, waiting for transfers between devices, _exchange(): return lax.ppermute(x, axis, [(i, i ^ 1 << bit) for i in range(n)])  44.2 us
    ppermute x15, starting transfers between devices, _exchange(): return lax.ppermute(x, axis, [(i, i ^ 1 << bit) for i in range(n)])  19 us
    dot_general x1, matrix products, local(): dense = jnp.dot(place_live, tiles.reshape(ntiles, -1), precision=hp)  5.56 us
    dot_general x2, matrix products, product_of(): return jnp.einsum('ricj,csj->rsi', dense, point, precision=hp)  4.81 us
    dot_general x2, matrix products, transposed_product(): return jnp.einsum('rsi,ricj->csj', dual, dense, precision=hp)  3.45 us
    slice x11, local copies, waits for them, and re-layouts, _rounds(): new_sums.append(s + got[off:off + size].reshape(shape))  2.98 us
    reduce_sum x2, other arithmetic, local(): local_a = jnp.sum(jnp.sum(tiles * tiles, axis=(1, 2)) * live)  2.94 us
  transfers between devices with their start and end apart: 15, of which 14 were waited for; matrix products, arithmetic and copies ran while one was open for 10% of the time, Pallas kernels for 0%

profile of v8, /device:TPU:0, one launch (start us, length us, event | category | flops | bytes accessed | tf_op | source)
XLA Modules:
  0.0 99.6 jit_solution(12997831942126975917)
XLA Ops:
  1.4 1.3 %multiply_reduce_fusion.6 = f32[]{:T(128)} fusion(f32[2,128]{1,0:T(2,128)} %param.15), kind=kLoop, calls=%fused_computation.78 | loop fusion | flops 511 | bytes 1028 | tf_op jit(solution)/shard_map/reduce_sum | solution.py:85
  2.7 2.3 %multiply_reduce_fusion = f32[48]{0:T(128)S(1)} fusion(f32[48,128,128]{2,1,0:T(8,128)} %param.11), kind=kLoop, calls=%fused_computation.4 | loop fusion | flops 1572816 | bytes 3145920 | tf_op jit(solution)/shard_map/reduce_sum | solution.py:83
  5.0 0.6 fusion.76
  5.6 0.2 fusion.74
  5.8 0.1 multiply_reduce_fusion.5
  5.9 1.4 %pad_maximum_fusion.3 = f32[18]{0:T(128)S(1)} fusion(f32[1]{0:T(128)} %bitcast.14, f32[16]{0:T(128)S(1)} %multiply_reduce_fusion.5, f32[1]{0:T(128)} %bitcast.13), kind=kLoop, calls=%fused_computation.90 | loop fusion | flops 36 | bytes 144 | tf_op jit(solution)/shard_map/concatenate | solution.py:38
  7.3 2.9 %collective-permute-start = (f32[18]{0:T(128)S(1)}, f32[18]{0:T(128)S(1)}, u32[]{:S(2)}, u32[]{:S(2)}) collective-permute-start(f32[18]{0:T(128)S(1)} %pad_maximum_fusion.3), channel_id=1, source_target_pairs={{0,8},{8,0},{16,24},{24,16},{1,9},{9,1},{17,25},{25,17},{2,10},{10... | collective-permute-start | bytes 224 | tf_op jit(solution)/shard_map/ppermute | solution.py:14
  10.3 0.1 pad.23.clone
  10.4 5.6 %fusion.10 = f32[2,128,16,128]{3,2,1,0:T(8,128)S(1)} fusion(f32[48]{0:T(128)S(1)} %compare_convert_fusion, s32[16,2]{0,1:T(2,128)S(1)} %multiply_add_fusion, s32[48]{0:T(128)S(1)} %multiply_add_fusion.1, f32[6,8,128,128]{3,2,1,0:T(8,128)} %bitcast.131), kind=kOutput, calls=%fused_computation.13 | convolution fusion | flops 301992960 | bytes 5243392 | tf_op jit(solution)/shard_map/dot_general | solution.py:92
  16.0 1.7 %fusion.8 = f32[16,128,16,1]{1,2,3,0:T(8,128)S(1)} fusion(f32[2,128,16,128]{3,2,1,0:T(8,128)S(1)} %fusion.10, f32[2,16,128]{2,1,0:T(8,128)S(1)} %copy-done.1), kind=kOutput, calls=%fused_computation.11 | convolution fusion | flops 100663296 | bytes 2244608 | tf_op jit(solution)/shard_map/rsi,ricj->csj/dot_general | solution.py:97
  17.7 0.1 fusion.64
  17.8 0.6 fusion.90
  21.0 0.1 slice_add_fusion.13
  21.1 0.1 pad_maximum_fusion.4
  21.1 1.5 %collective-permute-start.1 = (f32[18]{0:T(128)S(1)}, f32[18]{0:T(128)S(1)}, u32[]{:S(2)}, u32[]{:S(2)}) collective-permute-start(f32[18]{0:T(128)S(1)} %pad_maximum_fusion.4), channel_id=1, source_target_pairs={{0,16},{8,24},{16,0},{24,8},{1,17},{9,25},{17,1},{25,9},{2,18},{10... | collective-permute-start | bytes 224 | tf_op jit(solution)/shard_map/ppermute | solution.py:14
  22.7 2.0 %collective-permute-done.1 = f32[18]{0:T(128)S(1)} collective-permute-done((f32[18]{0:T(128)S(1)}, f32[18]{0:T(128)S(1)}, u32[]{:S(2)}, u32[]{:S(2)}) %collective-permute-start.1) | collective-permute-done | bytes 104 | tf_op jit(solution)/shard_map/ppermute | solution.py:14
  24.7 0.6 fusion.89
  26.6 0.1 slice_add_fusion.12
  26.6 0.1 concatenate.42
  26.8 1.4 %collective-permute-done.2 = f32[38912]{0:T(1024)S(1)} collective-permute-done((f32[38912]{0:T(1024)S(1)}, f32[38912]{0:T(1024)S(1)}, u32[]{:S(2)}, u32[]{:S(2)}) %collective-permute-start.2) | collective-permute-done | bytes 155680 | tf_op jit(solution)/shard_map/ppermute | solution.py:14
  28.1 0.6 fusion.88
  30.1 0.1 slice_add_fusion.5
  30.2 0.1 concatenate.43
  30.2 1.6 %collective-permute-start.3 = (f32[44032]{0:T(1024)S(1)}, f32[44032]{0:T(1024)S(1)}, u32[]{:S(2)}, u32[]{:S(2)}) collective-permute-start(f32[44032]{0:T(1024)S(1)} %concatenate.43), channel_id=1, source_target_pairs={{0,2},{1,3},{2,0},{3,1},{4,6},{5,7},{6,4},{7,5},{8,10},{9,11},{10,... | collective-permute-start | bytes 528392 | tf_op jit(solution)/shard_map/ppermute | solution.py:14
  31.8 4.9 %collective-permute-done.3 = f32[44032]{0:T(1024)S(1)} collective-permute-done((f32[44032]{0:T(1024)S(1)}, f32[44032]{0:T(1024)S(1)}, u32[]{:S(2)}, u32[]{:S(2)}) %collective-permute-start.3) | collective-permute-done | bytes 176160 | tf_op jit(solution)/shard_map/ppermute | solution.py:14
  36.8 0.6 fusion.86
  38.8 0.1 slice_add_fusion.4
  38.8 0.8 concatenate.44
  39.6 2.7 %collective-permute-start.4 = (f32[54272]{0:T(1024)S(1)}, f32[54272]{0:T(1024)S(1)}, u32[]{:S(2)}, u32[]{:S(2)}) collective-permute-start(f32[54272]{0:T(1024)S(1)} %concatenate.44), channel_id=1, source_target_pairs={{0,4},{1,5},{2,6},{3,7},{4,0},{5,1},{6,2},{7,3},{8,12},{9,13},{10,... | collective-permute-start | bytes 651272 | tf_op jit(solution)/shard_map/ppermute | solution.py:14
  42.3 9.5 %collective-permute-done.4 = f32[54272]{0:T(1024)S(1)} collective-permute-done((f32[54272]{0:T(1024)S(1)}, f32[54272]{0:T(1024)S(1)}, u32[]{:S(2)}, u32[]{:S(2)}) %collective-permute-start.4) | collective-permute-done | bytes 217120 | tf_op jit(solution)/shard_map/ppermute | solution.py:14
  51.9 0.6 fusion.85
  53.8 0.1 broadcast_multiply_fusion.1
  53.9 0.2 multiply_reduce_fusion.2
  54.2 2.1 %multiply_reduce_fusion.4 = (f32[16]{0:T(128)S(1)}, f32[2,16,128]{2,1,0:T(8,128)S(1)}) fusion(f32[2,16,128]{2,1,0:T(8,128)S(1)} %copy-done.1, f32[2,128,16,128]{3,2,1,0:T(8,128)S(1)} %fusion.10, f32[16,16,128]{2,1,0:T(8,128)S(1)} %bitcast.139, f32[16,16,128]{2,1,0:T(8,128)S(1)} %get-tuple-element.8, f32[2,128]{1,0:T(2,128)S(1)} %copy-done.3, ...), kind=kOutput, calls=%fused_computation.60 | convolution fusion | flops 100757488 | bytes 2393216 | tf_op jit(solution)/shard_map/ricj,csj->rsi/dot_general | solution.py:100
  56.3 0.1 pad_maximum_fusion.5
  56.3 0.7 collective-permute-start.5
  57.0 2.9 %collective-permute-done.5 = f32[32]{0:T(128)S(1)} collective-permute-done((f32[32]{0:T(128)S(1)}, f32[32]{0:T(128)S(1)}, u32[]{:S(2)}, u32[]{:S(2)}) %collective-permute-start.5) | collective-permute-done | bytes 160 | tf_op jit(solution)/shard_map/ppermute | solution.py:14
  59.9 0.1 slice_add_fusion.11
  60.0 0.1 pad_maximum_fusion.6
  60.0 1.5 %collective-permute-start.6 = (f32[32]{0:T(128)S(1)}, f32[32]{0:T(128)S(1)}, u32[]{:S(2)}, u32[]{:S(2)}) collective-permute-start(f32[32]{0:T(128)S(1)} %pad_maximum_fusion.6), channel_id=1, source_target_pairs={{0,16},{8,24},{16,0},{24,8},{1,17},{9,25},{17,1},{25,9},{2,18},{10... | collective-permute-start | bytes 392 | tf_op jit(solution)/shard_map/ppermute | solution.py:14
  61.6 1.7 %fusion.6 = f32[16,128,16,1]{1,2,3,0:T(8,128)S(1)} fusion(f32[2,128,16,128]{3,2,1,0:T(8,128)S(1)} %fusion.10, f32[2,16,128]{2,1,0:T(8,128)S(1)} %get-tuple-element.29), kind=kOutput, calls=%fused_computation.9 | convolution fusion | flops 100663296 | bytes 2244608 | tf_op jit(solution)/shard_map/rsi,ricj->csj/dot_general | solution.py:97
  63.3 0.3 collective-permute-done.6
  63.6 0.1 slice_add_fusion.9
  63.7 1.3 %collective-permute-done.7 = f32[32784]{0:T(1024)S(1)} collective-permute-done((f32[32784]{0:T(1024)S(1)}, f32[32784]{0:T(1024)S(1)}, u32[]{:S(2)}, u32[]{:S(2)}) %collective-permute-start.7) | collective-permute-done | bytes 131168 | tf_op jit(solution)/shard_map/ppermute | solution.py:14
  65.2 0.7 collective-permute-start.8
  65.9 5.0 %collective-permute-done.8 = f32[32784]{0:T(1024)S(1)} collective-permute-done((f32[32784]{0:T(1024)S(1)}, f32[32784]{0:T(1024)S(1)}, u32[]{:S(2)}, u32[]{:S(2)}) %collective-permute-start.8) | collective-permute-done | bytes 131168 | tf_op jit(solution)/shard_map/ppermute | solution.py:14
  70.9 2.4 %collective-permute-start.9 = (f32[32784]{0:T(1024)S(1)}, f32[32784]{0:T(1024)S(1)}, u32[]{:S(2)}, u32[]{:S(2)}) collective-permute-start(f32[32784]{0:T(1024)S(1)} %pad_maximum_fusion.2), channel_id=1, source_target_pairs={{0,4},{1,5},{2,6},{3,7},{4,0},{5,1},{6,2},{7,3},{8,12},{9,13},{10,... | collective-permute-start | bytes 393416 | tf_op jit(solution)/shard_map/ppermute | solution.py:14
  73.3 6.3 %collective-permute-done.9 = f32[32784]{0:T(1024)S(1)} collective-permute-done((f32[32784]{0:T(1024)S(1)}, f32[32784]{0:T(1024)S(1)}, u32[]{:S(2)}, u32[]{:S(2)}) %collective-permute-start.9) | collective-permute-done | bytes 131168 | tf_op jit(solution)/shard_map/ppermute | solution.py:14
  79.7 0.2 multiply_reduce_fusion.1
  79.9 2.7 %multiply_reduce_fusion.3 = (f32[16]{0:T(128)S(1)}, f32[2,16,128]{2,1,0:T(8,128)}) fusion(f32[2,16,128]{2,1,0:T(8,128)S(1)} %get-tuple-element.29, f32[2,128,16,128]{3,2,1,0:T(8,128)S(1)} %fusion.10, f32[16,16,128]{2,1,0:T(8,128)S(1)} %get-tuple-element.8, f32[16,16,128]{2,1,0:T(8,128)S(1)} %get-tuple-element.4, f32[2,128]{1,0:T(2,128)S(1)} %copy-done.3, ...), kind=kOutput, calls=%fused_computation.59 | convolution fusion | flops 100757488 | bytes 2393216 | tf_op jit(solution)/shard_map/ricj,csj->rsi/dot_general | solution.py:100
  82.6 0.1 pad_maximum_fusion.7
  82.7 0.7 collective-permute-start.10
  83.4 2.9 %collective-permute-done.10 = f32[32]{0:T(128)S(1)} collective-permute-done((f32[32]{0:T(128)S(1)}, f32[32]{0:T(128)S(1)}, u32[]{:S(2)}, u32[]{:S(2)}) %collective-permute-start.10) | collective-permute-done | bytes 160 | tf_op jit(solution)/shard_map/ppermute | solution.py:14
  86.2 0.1 slice_add_fusion.8
  86.3 0.1 pad_maximum_fusion.8
  86.4 1.5 %collective-permute-start.11 = (f32[32]{0:T(128)S(1)}, f32[32]{0:T(128)S(1)}, u32[]{:S(2)}, u32[]{:S(2)}) collective-permute-start(f32[32]{0:T(128)S(1)} %pad_maximum_fusion.8), channel_id=1, source_target_pairs={{0,16},{8,24},{16,0},{24,8},{1,17},{9,25},{17,1},{25,9},{2,18},{10... | collective-permute-start | bytes 392 | tf_op jit(solution)/shard_map/ppermute | solution.py:14
  87.9 2.0 %collective-permute-done.11 = f32[32]{0:T(128)S(1)} collective-permute-done((f32[32]{0:T(128)S(1)}, f32[32]{0:T(128)S(1)}, u32[]{:S(2)}, u32[]{:S(2)}) %collective-permute-start.11) | collective-permute-done | bytes 160 | tf_op jit(solution)/shard_map/ppermute | solution.py:14
  90.0 1.1 %collective-permute-done.12 = f32[16]{0:T(128)S(1)} collective-permute-done((f32[16]{0:T(128)S(1)}, f32[16]{0:T(128)S(1)}, u32[]{:S(2)}, u32[]{:S(2)}) %collective-permute-start.12) | collective-permute-done | bytes 96 | tf_op jit(solution)/shard_map/ppermute | solution.py:14
  91.1 0.7 collective-permute-start.13
  91.8 2.9 %collective-permute-done.13 = f32[16]{0:T(128)S(1)} collective-permute-done((f32[16]{0:T(128)S(1)}, f32[16]{0:T(128)S(1)}, u32[]{:S(2)}, u32[]{:S(2)}) %collective-permute-start.13) | collective-permute-done | bytes 96 | tf_op jit(solution)/shard_map/ppermute | solution.py:14
  94.6 2.0 %collective-permute-start.14 = (f32[16]{0:T(128)S(1)}, f32[16]{0:T(128)S(1)}, u32[]{:S(2)}, u32[]{:S(2)}) collective-permute-start(f32[16]{0:T(128)S(1)} %add.202), channel_id=1, source_target_pairs={{0,4},{1,5},{2,6},{3,7},{4,0},{5,1},{6,2},{7,3},{8,12},{9,13},{10,... | collective-permute-start | bytes 200 | tf_op jit(solution)/shard_map/ppermute | solution.py:14
  96.7 0.6 constant_dynamic-slice_fusion
  97.3 1.8 %collective-permute-done.14 = f32[16]{0:T(128)S(1)} collective-permute-done((f32[16]{0:T(128)S(1)}, f32[16]{0:T(128)S(1)}, u32[]{:S(2)}, u32[]{:S(2)}) %collective-permute-start.14) | collective-permute-done | bytes 96 | tf_op jit(solution)/shard_map/ppermute | solution.py:14
  99.1 0.5 multiply_sqrt_fusion
  (58 shorter events, 0.6 us)
Async XLA Ops:
  0.6 5.0 %copy-start = (f32[32,128]{1,0:T(8,128)S(1)}, f32[32,128]{1,0:T(8,128)}, u32[]{:S(2)}) copy-start(f32[32,128]{1,0:T(8,128)} %param.20) | copy-start | bytes 49156
  0.6 5.0 %copy-start.6 = (s32[16]{0:T(128)S(1)}, s32[16]{0:T(128)}, u32[]{:S(2)}) copy-start(s32[16]{0:T(128)} %param.21) | copy-start | bytes 196
  0.7 5.1 %copy-start.4 = (f32[2,128]{1,0:T(2,128)S(1)}, f32[2,128]{1,0:T(2,128)}, u32[]{:S(2)}) copy-start(f32[2,128]{1,0:T(2,128)} %param.16) | copy-start | bytes 3076
  0.7 9.6 %copy-start.8 = (s32[48]{0:T(128)S(1)}, s32[48]{0:T(128)}, u32[]{:S(2)}) copy-start(s32[48]{0:T(128)} %param.13) | copy-start | bytes 580
  0.7 9.6 %copy-start.7 = (s32[48]{0:T(128)S(1)}, s32[48]{0:T(128)}, u32[]{:S(2)}) copy-start(s32[48]{0:T(128)} %param.12) | copy-start | bytes 580
  7.3 10.5 %collective-permute-start = (f32[18]{0:T(128)S(1)}, f32[18]{0:T(128)S(1)}, u32[]{:S(2)}, u32[]{:S(2)}) collective-permute-start(f32[18]{0:T(128)S(1)} %pad_maximum_fusion.3), channel_id=1, source_target_pairs={{0,8},{8,0},{16,24},{24,16},{1,9},{9,1},{17,25},{25,17},{2,10},{10... | collective-permute-start | bytes 224 | tf_op jit(solution)/shard_map/ppermute | solution.py:14
  10.4 5.6 %copy-start.1 = (f32[2,16,128]{2,1,0:T(8,128)S(1)}, f32[2,16,128]{2,1,0:T(8,128)}, u32[]{:S(2)}) copy-start(f32[2,16,128]{2,1,0:T(8,128)} %param.19) | copy-start | bytes 49156
  15.9 1.8 %copy-start.2 = (f32[2,16,128]{2,1,0:T(8,128)S(1)}, f32[2,16,128]{2,1,0:T(8,128)}, u32[]{:S(2)}) copy-start(f32[2,16,128]{2,1,0:T(8,128)} %param.18) | copy-start | bytes 49156
  16.0 1.8 %copy-start.5 = (f32[2,128]{1,0:T(2,128)S(1)}, f32[2,128]{1,0:T(2,128)}, u32[]{:S(2)}) copy-start(f32[2,128]{1,0:T(2,128)} %param.17) | copy-start | bytes 3076
  21.1 3.5 %collective-permute-start.1 = (f32[18]{0:T(128)S(1)}, f32[18]{0:T(128)S(1)}, u32[]{:S(2)}, u32[]{:S(2)}) collective-permute-start(f32[18]{0:T(128)S(1)} %pad_maximum_fusion.4), channel_id=1, source_target_pairs={{0,16},{8,24},{16,0},{24,8},{1,17},{9,25},{17,1},{25,9},{2,18},{10... | collective-permute-start | bytes 224 | tf_op jit(solution)/shard_map/ppermute | solution.py:14
  26.7 27.4 %copy-start.3 = (f32[2,128]{1,0:T(2,128)S(1)}, f32[2,128]{1,0:T(2,128)}, u32[]{:S(2)}) copy-start(f32[2,128]{1,0:T(2,128)} %param.15) | copy-start | bytes 3076
  26.7 1.4 %collective-permute-start.2 = (f32[38912]{0:T(1024)S(1)}, f32[38912]{0:T(1024)S(1)}, u32[]{:S(2)}, u32[]{:S(2)}) collective-permute-start(f32[38912]{0:T(1024)S(1)} %concatenate.42), channel_id=1, source_target_pairs={{0,1},{1,0},{2,3},{3,2},{4,5},{5,4},{6,7},{7,6},{8,9},{9,8},{10,11... | collective-permute-start | bytes 466952 | tf_op jit(solution)/shard_map/ppermute | solution.py:14
  30.2 6.5 %collective-permute-start.3 = (f32[44032]{0:T(1024)S(1)}, f32[44032]{0:T(1024)S(1)}, u32[]{:S(2)}, u32[]{:S(2)}) collective-permute-start(f32[44032]{0:T(1024)S(1)} %concatenate.43), channel_id=1, source_target_pairs={{0,2},{1,3},{2,0},{3,1},{4,6},{5,7},{6,4},{7,5},{8,10},{9,11},{10,... | collective-permute-start | bytes 528392 | tf_op jit(solution)/shard_map/ppermute | solution.py:14
  39.6 12.2 %collective-permute-start.4 = (f32[54272]{0:T(1024)S(1)}, f32[54272]{0:T(1024)S(1)}, u32[]{:S(2)}, u32[]{:S(2)}) collective-permute-start(f32[54272]{0:T(1024)S(1)} %concatenate.44), channel_id=1, source_target_pairs={{0,4},{1,5},{2,6},{3,7},{4,0},{5,1},{6,2},{7,3},{8,12},{9,13},{10,... | collective-permute-start | bytes 651272 | tf_op jit(solution)/shard_map/ppermute | solution.py:14
  56.3 3.5 %collective-permute-start.5 = (f32[32]{0:T(128)S(1)}, f32[32]{0:T(128)S(1)}, u32[]{:S(2)}, u32[]{:S(2)}) collective-permute-start(f32[32]{0:T(128)S(1)} %pad_maximum_fusion.5), channel_id=1, source_target_pairs={{0,8},{8,0},{16,24},{24,16},{1,9},{9,1},{17,25},{25,17},{2,10},{10... | collective-permute-start | bytes 392 | tf_op jit(solution)/shard_map/ppermute | solution.py:14
  60.0 3.5 %collective-permute-start.6 = (f32[32]{0:T(128)S(1)}, f32[32]{0:T(128)S(1)}, u32[]{:S(2)}, u32[]{:S(2)}) collective-permute-start(f32[32]{0:T(128)S(1)} %pad_maximum_fusion.6), channel_id=1, source_target_pairs={{0,16},{8,24},{16,0},{24,8},{1,17},{9,25},{17,1},{25,9},{2,18},{10... | collective-permute-start | bytes 392 | tf_op jit(solution)/shard_map/ppermute | solution.py:14
  63.7 1.4 %collective-permute-start.7 = (f32[32784]{0:T(1024)S(1)}, f32[32784]{0:T(1024)S(1)}, u32[]{:S(2)}, u32[]{:S(2)}) collective-permute-start(f32[32784]{0:T(1024)S(1)} %pad_maximum_fusion), channel_id=1, source_target_pairs={{0,1},{1,0},{2,3},{3,2},{4,5},{5,4},{6,7},{7,6},{8,9},{9,8},{10,11... | collective-permute-start | bytes 393416 | tf_op jit(solution)/shard_map/ppermute | solution.py:14
  65.2 5.7 %collective-permute-start.8 = (f32[32784]{0:T(1024)S(1)}, f32[32784]{0:T(1024)S(1)}, u32[]{:S(2)}, u32[]{:S(2)}) collective-permute-start(f32[32784]{0:T(1024)S(1)} %pad_maximum_fusion.1), channel_id=1, source_target_pairs={{0,2},{1,3},{2,0},{3,1},{4,6},{5,7},{6,4},{7,5},{8,10},{9,11},{10,... | collective-permute-start | bytes 393416 | tf_op jit(solution)/shard_map/ppermute | solution.py:14
  70.9 8.7 %collective-permute-start.9 = (f32[32784]{0:T(1024)S(1)}, f32[32784]{0:T(1024)S(1)}, u32[]{:S(2)}, u32[]{:S(2)}) collective-permute-start(f32[32784]{0:T(1024)S(1)} %pad_maximum_fusion.2), channel_id=1, source_target_pairs={{0,4},{1,5},{2,6},{3,7},{4,0},{5,1},{6,2},{7,3},{8,12},{9,13},{10,... | collective-permute-start | bytes 393416 | tf_op jit(solution)/shard_map/ppermute | solution.py:14
  82.7 3.5 %collective-permute-start.10 = (f32[32]{0:T(128)S(1)}, f32[32]{0:T(128)S(1)}, u32[]{:S(2)}, u32[]{:S(2)}) collective-permute-start(f32[32]{0:T(128)S(1)} %pad_maximum_fusion.7), channel_id=1, source_target_pairs={{0,8},{8,0},{16,24},{24,16},{1,9},{9,1},{17,25},{25,17},{2,10},{10... | collective-permute-start | bytes 392 | tf_op jit(solution)/shard_map/ppermute | solution.py:14
  86.4 3.5 %collective-permute-start.11 = (f32[32]{0:T(128)S(1)}, f32[32]{0:T(128)S(1)}, u32[]{:S(2)}, u32[]{:S(2)}) collective-permute-start(f32[32]{0:T(128)S(1)} %pad_maximum_fusion.8), channel_id=1, source_target_pairs={{0,16},{8,24},{16,0},{24,8},{1,17},{9,25},{17,1},{25,9},{2,18},{10... | collective-permute-start | bytes 392 | tf_op jit(solution)/shard_map/ppermute | solution.py:14
  90.0 1.1 %collective-permute-start.12 = (f32[16]{0:T(128)S(1)}, f32[16]{0:T(128)S(1)}, u32[]{:S(2)}, u32[]{:S(2)}) collective-permute-start(f32[16]{0:T(128)S(1)} %slice_add_fusion.6), channel_id=1, source_target_pairs={{0,1},{1,0},{2,3},{3,2},{4,5},{5,4},{6,7},{7,6},{8,9},{9,8},{10,11... | collective-permute-start | bytes 200 | tf_op jit(solution)/shard_map/ppermute | solution.py:14
  91.1 3.5 %collective-permute-start.13 = (f32[16]{0:T(128)S(1)}, f32[16]{0:T(128)S(1)}, u32[]{:S(2)}, u32[]{:S(2)}) collective-permute-start(f32[16]{0:T(128)S(1)} %add.201), channel_id=1, source_target_pairs={{0,2},{1,3},{2,0},{3,1},{4,6},{5,7},{6,4},{7,5},{8,10},{9,11},{10,... | collective-permute-start | bytes 200 | tf_op jit(solution)/shard_map/ppermute | solution.py:14
  94.6 4.4 %collective-permute-start.14 = (f32[16]{0:T(128)S(1)}, f32[16]{0:T(128)S(1)}, u32[]{:S(2)}, u32[]{:S(2)}) collective-permute-start(f32[16]{0:T(128)S(1)} %add.202), channel_id=1, source_target_pairs={{0,4},{1,5},{2,6},{3,7},{4,0},{5,1},{6,2},{7,3},{8,12},{9,13},{10,... | collective-permute-start | bytes 200 | tf_op jit(solution)/shard_map/ppermute | solution.py:14

commit v9 on v8

--- a/solution.py
+++ b/solution.py
@@ -14,13 +14,19 @@
     return lax.ppermute(x, axis, [(i, i ^ (1 << bit)) for i in range(n)])
 
 
-def _rounds(axis, sums, own=None):
+def _rounds(axis, sums, own=None, split=None):
     n = lax.axis_size(axis)
+    if split is not None and (not _pow2(n) or n < 2 or split.shape[0] % 2):
+        sums = [split] + list(sums)
+        split = None
+        joined = True
+    else:
+        joined = False
     if not _pow2(n):
         sums = [lax.psum(s, axis) for s in sums]
         if own is not None:
             own = lax.all_gather(own, axis, axis=0, tiled=False)
-        return sums, own
+        return (sums[0] if joined else None), sums[1:] if joined else sums, own
     shapes = [s.shape for s in sums]
     sizes = [s.size for s in sums]
     me = lax.axis_index(axis)
@@ -28,16 +34,28 @@
     if own is not None:
         buf = jnp.zeros((n,) + own.shape, own.dtype)
         buf = lax.dynamic_update_index_in_dim(buf, own, me, 0)
+    if split is not None:
+        half = lax.rem(me, 2)
+        halves = split.reshape((2, split.shape[0] // 2) + split.shape[1:])
+        keep = lax.dynamic_index_in_dim(halves, half, 0, keepdims=False)
+        give = lax.dynamic_index_in_dim(halves, 1 - half, 0, keepdims=False)
     for bit in range(n.bit_length() - 1):
-        parts = [s.reshape(-1) for s in sums]
+        parts = []
+        if split is not None:
+            parts.append((give if bit == 0 else keep).reshape(-1))
+        parts += [s.reshape(-1) for s in sums]
         if buf is not None:
-            used = sum(sizes)
-            parts.append(jnp.zeros((-used % 1024,), jnp.float32))
+            used = sum(p.shape[0] for p in parts)
+            if used % 1024:
+                parts.append(jnp.zeros((-used % 1024,), jnp.float32))
             start = (me >> bit) << bit
             parts.append(lax.dynamic_slice_in_dim(buf, start, 1 << bit, axis=0).reshape(-1))
         flat = jnp.concatenate(parts) if len(parts) > 1 else parts[0]
         got = _exchange(flat, axis, n, bit)
         off = 0
+        if split is not None:
+            keep = keep + got[: keep.size].reshape(keep.shape)
+            off = keep.size
         new_sums = []
         for shape, size, s in zip(shapes, sizes, sums):
             new_sums.append(s + got[off : off + size].reshape(shape))
@@ -48,7 +66,14 @@
             theirs = ((me ^ (1 << bit)) >> bit) << bit
             chunk = got[off:].reshape((1 << bit,) + own.shape)
             buf = lax.dynamic_update_slice_in_dim(buf, chunk, theirs, axis=0)
-    return sums, buf
+    full = None
+    if split is not None:
+        other = _exchange(keep, axis, n, 0)
+        both = jnp.concatenate([keep, other, keep], axis=0)
+        full = lax.dynamic_slice_in_dim(both, half * keep.shape[0], 2 * keep.shape[0], axis=0)
+    elif joined:
+        full, sums = sums[0], sums[1:]
+    return full, sums, buf
 
 
 def local(
@@ -99,7 +124,7 @@
     def product_of(point):
         return jnp.einsum("ricj,csj->rsi", dense, point, precision=hp)
 
-    (local_a, local_c, local_b), _ = _rounds(
+    _, (local_a, local_c, local_b), _ = _rounds(
         "region", [local_a.reshape(1), local_c, local_b.reshape(1)]
     )
     own_rows = own_blocks * (scenarios + 2)
@@ -113,8 +138,8 @@
         axis=0,
     )
     partial_value = transposed_product(dual)
-    (grad, sq_a, sq_c, sq_b), gathered = _rounds(
-        "col", [partial_value, local_a, local_c, local_b], own
+    grad, (sq_a, sq_c, sq_b), gathered = _rounds(
+        "col", [local_a, local_c, local_b], own, split=partial_value
     )
     primal_reg = gathered[:, : own_blocks * scenarios].reshape(region_blocks, scenarios, lanes)
     base_reg = gathered[:, own_blocks * scenarios : own_blocks * (scenarios + 1)]
@@ -125,9 +150,9 @@
     weight = jnp.sqrt(sq_c) / jnp.sqrt(sq_b[0])
     for step in range(ITERS):
         if step > 0:
-            (step_x, part_y), _ = _rounds("region", [local_x, local_y])
+            _, (step_x, part_y), _ = _rounds("region", [local_x, local_y])
             partial_value = transposed_product(dual)
-            (grad, step_y), _ = _rounds("col", [partial_value, part_y])
+            grad, (step_y,), _ = _rounds("col", [part_y], split=partial_value)
             weight = jnp.sqrt(weight * jnp.sqrt((step_x + 1e-06) / (step_y + 1e-06)))
         tau = (eta / weight)[None, :, None]
         sigma = (eta * weight)[None, :, None]
@@ -138,8 +163,8 @@
         local_x = jnp.sum((new_primal - primal_reg) ** 2, axis=(0, 2))
         local_y = jnp.sum((new_dual - dual) ** 2, axis=(0, 2))
         primal_reg, dual = (new_primal, new_dual)
-    (step_x, part_y), _ = _rounds("region", [local_x, local_y])
-    (step_y,), _ = _rounds("col", [part_y])
+    _, (step_x, part_y), _ = _rounds("region", [local_x, local_y])
+    _, (step_y,), _ = _rounds("col", [part_y])
     weight = jnp.sqrt(weight * jnp.sqrt((step_x + 1e-06) / (step_y + 1e-06)))
     primal_out = lax.dynamic_slice_in_dim(primal_reg, me * own_blocks, own_blocks, axis=0)
     return (primal_out, dual, weight)

time: 100 us -> 93.3 us (0.933)
  waiting for transfers between devices: 44.2 us -> 38.8 us
    ppermute x15 -> x17, waiting for transfers between devices: 44.2 us -> 38.8 us  [_exchange(): return lax.ppermute(x, axis, [(i, i ^ 1 << bit) for i in range(n)])]
    ppermute x15 -> x17, starting transfers between devices: 19 us -> 18.4 us  [_exchange(): return lax.ppermute(x, axis, [(i, i ^ 1 << bit) for i in range(n)])]
    slice x11 -> x5, local copies, waits for them, and re-layouts: 2.98 us -> 2.92 us  [_rounds(): new_sums.append(s + got[off:off + size].reshape(shape))]
  transfers between devices with their start and end apart: 15 -> 17, of which waited for: 14 -> 16; matrix products, arithmetic and copies ran while one was open for 10% -> 11% of each run, Pallas kernels for 0% -> 0%
where the time goes in v9:
time: 93.3 us; the launch traced here: 93 us
  waiting for transfers between devices  38.8 us (42%)
  starting transfers between devices  18.4 us (20%)
  matrix products  14 us (15%)
  between operations  9.63 us (10%)
  other arithmetic  7.98 us (9%)
  local copies, waits for them, and re-layouts  4.07 us (4%)
    ppermute x17, waiting for transfers between devices, _exchange(): return lax.ppermute(x, axis, [(i, i ^ 1 << bit) for i in range(n)])  38.8 us
    ppermute x17, starting transfers between devices, _exchange(): return lax.ppermute(x, axis, [(i, i ^ 1 << bit) for i in range(n)])  18.4 us
    dot_general x1, matrix products, local(): dense = jnp.dot(place_live, tiles.reshape(ntiles, -1), precision=hp)  5.57 us
    dot_general x2, matrix products, product_of(): return jnp.einsum('ricj,csj->rsi', dense, point, precision=hp)  4.81 us
    dot_general x2, matrix products, transposed_product(): return jnp.einsum('rsi,ricj->csj', dual, dense, precision=hp)  3.45 us
    reduce_sum x2, other arithmetic, local(): local_a = jnp.sum(jnp.sum(tiles * tiles, axis=(1, 2)) * live)  2.94 us
    slice x5, local copies, waits for them, and re-layouts, _rounds(): new_sums.append(s + got[off:off + size].reshape(shape))  2.92 us
  transfers between devices with their start and end apart: 17, of which 16 were waited for; matrix products, arithmetic and copies ran while one was open for 11% of the time, Pallas kernels for 0%

profile of v9, /device:TPU:0, one launch (start us, length us, event | category | flops | bytes accessed | tf_op | source)
XLA Modules:
  0.0 93.0 jit_solution(16264963647637645841)
XLA Ops:
  1.4 1.3 %multiply_reduce_fusion.6 = f32[]{:T(128)} fusion(f32[2,128]{1,0:T(2,128)} %param.15), kind=kLoop, calls=%fused_computation.93 | loop fusion | flops 511 | bytes 1028 | tf_op jit(solution)/shard_map/reduce_sum | solution.py:110
  2.7 2.3 %multiply_reduce_fusion = f32[48]{0:T(128)S(1)} fusion(f32[48,128,128]{2,1,0:T(8,128)} %param.11), kind=kLoop, calls=%fused_computation.4 | loop fusion | flops 1572816 | bytes 3145920 | tf_op jit(solution)/shard_map/reduce_sum | solution.py:108
  5.0 0.6 fusion.82
  5.6 0.2 fusion.80
  5.8 0.1 multiply_reduce_fusion.5
  5.9 1.4 %pad_maximum_fusion.3 = f32[18]{0:T(128)S(1)} fusion(f32[1]{0:T(128)} %bitcast.15, f32[16]{0:T(128)S(1)} %multiply_reduce_fusion.5, f32[1]{0:T(128)} %bitcast.14), kind=kLoop, calls=%fused_computation.105 | loop fusion | flops 36 | bytes 144 | tf_op jit(solution)/shard_map/concatenate | solution.py:53
  7.3 2.9 %collective-permute-start = (f32[18]{0:T(128)S(1)}, f32[18]{0:T(128)S(1)}, u32[]{:S(2)}, u32[]{:S(2)}) collective-permute-start(f32[18]{0:T(128)S(1)} %pad_maximum_fusion.3), channel_id=1, source_target_pairs={{0,8},{8,0},{16,24},{24,16},{1,9},{9,1},{17,25},{25,17},{2,10},{10... | collective-permute-start | bytes 224 | tf_op jit(solution)/shard_map/ppermute | solution.py:14
  10.3 0.1 pad.29.clone
  10.4 5.6 %fusion.10 = f32[2,128,16,128]{3,2,1,0:T(8,128)S(1)} fusion(f32[48]{0:T(128)S(1)} %compare_convert_fusion, s32[16,2]{0,1:T(2,128)S(1)} %multiply_add_fusion, s32[48]{0:T(128)S(1)} %multiply_add_fusion.1, f32[6,8,128,128]{3,2,1,0:T(8,128)} %bitcast.138), kind=kOutput, calls=%fused_computation.13 | convolution fusion | flops 301992960 | bytes 5243392 | tf_op jit(solution)/shard_map/dot_general | solution.py:117
  16.0 1.7 %fusion.8 = f32[16,128,16,1]{1,2,3,0:T(8,128)S(1)} fusion(f32[2,128,16,128]{3,2,1,0:T(8,128)S(1)} %fusion.10, f32[2,16,128]{2,1,0:T(8,128)S(1)} %copy-done.1), kind=kOutput, calls=%fused_computation.11 | convolution fusion | flops 100663296 | bytes 2244608 | tf_op jit(solution)/shard_map/rsi,ricj->csj/dot_general | solution.py:122
  17.8 0.1 fusion.70
  17.9 0.6 fusion.98
  21.1 0.1 slice_add_fusion.13
  21.2 0.1 pad_maximum_fusion.4
  21.2 1.5 %collective-permute-start.1 = (f32[18]{0:T(128)S(1)}, f32[18]{0:T(128)S(1)}, u32[]{:S(2)}, u32[]{:S(2)}) collective-permute-start(f32[18]{0:T(128)S(1)} %pad_maximum_fusion.4), channel_id=1, source_target_pairs={{0,16},{8,24},{16,0},{24,8},{1,17},{9,25},{17,1},{25,9},{2,18},{10... | collective-permute-start | bytes 224 | tf_op jit(solution)/shard_map/ppermute | solution.py:14
  22.8 2.0 %collective-permute-done.1 = f32[18]{0:T(128)S(1)} collective-permute-done((f32[18]{0:T(128)S(1)}, f32[18]{0:T(128)S(1)}, u32[]{:S(2)}, u32[]{:S(2)}) %collective-permute-start.1) | collective-permute-done | bytes 104 | tf_op jit(solution)/shard_map/ppermute | solution.py:14
  24.8 0.6 fusion.97
  26.7 0.1 slice_add_fusion.12
  26.7 0.1 concatenate.48
  26.9 1.3 %collective-permute-done.2 = f32[22528]{0:T(1024)S(1)} collective-permute-done((f32[22528]{0:T(1024)S(1)}, f32[22528]{0:T(1024)S(1)}, u32[]{:S(2)}, u32[]{:S(2)}) %collective-permute-start.2) | collective-permute-done | bytes 90144 | tf_op jit(solution)/shard_map/ppermute | solution.py:14
  28.1 0.6 fusion.94
  30.1 0.1 slice_add_fusion.5
  30.1 0.1 concatenate.49
  30.2 1.6 %collective-permute-start.3 = (f32[27648]{0:T(1024)S(1)}, f32[27648]{0:T(1024)S(1)}, u32[]{:S(2)}, u32[]{:S(2)}) collective-permute-start(f32[27648]{0:T(1024)S(1)} %concatenate.49), channel_id=1, source_target_pairs={{0,2},{1,3},{2,0},{3,1},{4,6},{5,7},{6,4},{7,5},{8,10},{9,11},{10,... | collective-permute-start | bytes 331784 | tf_op jit(solution)/shard_map/ppermute | solution.py:14
  31.8 3.5 %collective-permute-done.3 = f32[27648]{0:T(1024)S(1)} collective-permute-done((f32[27648]{0:T(1024)S(1)}, f32[27648]{0:T(1024)S(1)}, u32[]{:S(2)}, u32[]{:S(2)}) %collective-permute-start.3) | collective-permute-done | bytes 110624 | tf_op jit(solution)/shard_map/ppermute | solution.py:14
  35.4 0.6 fusion.93
  37.3 0.1 slice_add_fusion.4
  37.4 0.1 concatenate.50
  37.5 2.6 %collective-permute-start.4 = (f32[37888]{0:T(1024)S(1)}, f32[37888]{0:T(1024)S(1)}, u32[]{:S(2)}, u32[]{:S(2)}) collective-permute-start(f32[37888]{0:T(1024)S(1)} %concatenate.50), channel_id=1, source_target_pairs={{0,4},{1,5},{2,6},{3,7},{4,0},{5,1},{6,2},{7,3},{8,12},{9,13},{10,... | collective-permute-start | bytes 454664 | tf_op jit(solution)/shard_map/ppermute | solution.py:14
  40.1 6.7 %collective-permute-done.4 = f32[37888]{0:T(1024)S(1)} collective-permute-done((f32[37888]{0:T(1024)S(1)}, f32[37888]{0:T(1024)S(1)}, u32[]{:S(2)}, u32[]{:S(2)}) %collective-permute-start.4) | collective-permute-done | bytes 151584 | tf_op jit(solution)/shard_map/ppermute | solution.py:14
  46.8 0.6 fusion.92
  48.9 0.1 broadcast_multiply_fusion.1
  49.0 1.1 %collective-permute-done.5 = f32[8,16,128]{2,1,0:T(8,128)S(1)} collective-permute-done((f32[8,16,128]{2,1,0:T(8,128)S(1)}, f32[8,16,128]{2,1,0:T(8,128)S(1)}, u32[]{:S(2)}, u32[]{:S(2)}) %collective-permute-start.5) | collective-permute-done | bytes 65568 | tf_op jit(solution)/shard_map/ppermute | solution.py:14
  50.2 0.2 multiply_reduce_fusion.2
  50.4 2.1 %multiply_reduce_fusion.4 = (f32[16]{0:T(128)S(1)}, f32[2,16,128]{2,1,0:T(8,128)S(1)}) fusion(f32[2,16,128]{2,1,0:T(8,128)S(1)} %copy-done.1, f32[2,128,16,128]{3,2,1,0:T(8,128)S(1)} %fusion.10, f32[16,16,128]{2,1,0:T(8,128)S(1)} %bitcast.140, f32[16,16,128]{2,1,0:T(8,128)S(1)} %get-tuple-element.8, f32[2,128]{1,0:T(2,128)S(1)} %copy-done.3, ...), kind=kOutput, calls=%fused_computation.72 | convolution fusion | flops 100757488 | bytes 2393216 | tf_op jit(solution)/shard_map/ricj,csj->rsi/dot_general | solution.py:125
  52.5 0.1 pad_maximum_fusion.5
  52.6 0.7 collective-permute-start.6
  53.3 1.7 %fusion.6 = f32[16,128,16,1]{1,2,3,0:T(8,128)S(1)} fusion(f32[2,128,16,128]{3,2,1,0:T(8,128)S(1)} %fusion.10, f32[2,16,128]{2,1,0:T(8,128)S(1)} %get-tuple-element.35), kind=kOutput, calls=%fused_computation.9 | convolution fusion | flops 100663296 | bytes 2244608 | tf_op jit(solution)/shard_map/rsi,ricj->csj/dot_general | solution.py:122
  55.0 1.1 %collective-permute-done.6 = f32[32]{0:T(128)S(1)} collective-permute-done((f32[32]{0:T(128)S(1)}, f32[32]{0:T(128)S(1)}, u32[]{:S(2)}, u32[]{:S(2)}) %collective-permute-start.6) | collective-permute-done | bytes 160 | tf_op jit(solution)/shard_map/ppermute | solution.py:14
  56.2 0.1 pad_maximum_fusion.6
  56.3 1.5 %collective-permute-start.7 = (f32[32]{0:T(128)S(1)}, f32[32]{0:T(128)S(1)}, u32[]{:S(2)}, u32[]{:S(2)}) collective-permute-start(f32[32]{0:T(128)S(1)} %pad_maximum_fusion.6), channel_id=1, source_target_pairs={{0,16},{8,24},{16,0},{24,8},{1,17},{9,25},{17,1},{25,9},{2,18},{10... | collective-permute-start | bytes 392 | tf_op jit(solution)/shard_map/ppermute | solution.py:14
  57.8 2.0 %collective-permute-done.7 = f32[32]{0:T(128)S(1)} collective-permute-done((f32[32]{0:T(128)S(1)}, f32[32]{0:T(128)S(1)}, u32[]{:S(2)}, u32[]{:S(2)}) %collective-permute-start.7) | collective-permute-done | bytes 160 | tf_op jit(solution)/shard_map/ppermute | solution.py:14
  59.8 0.1 slice_add_fusion.9
  59.9 1.2 %collective-permute-done.8 = f32[16400]{0:T(1024)S(1)} collective-permute-done((f32[16400]{0:T(1024)S(1)}, f32[16400]{0:T(1024)S(1)}, u32[]{:S(2)}, u32[]{:S(2)}) %collective-permute-start.8) | collective-permute-done | bytes 65632 | tf_op jit(solution)/shard_map/ppermute | solution.py:14
  61.2 0.7 collective-permute-start.9
  62.0 3.6 %collective-permute-done.9 = f32[16400]{0:T(1024)S(1)} collective-permute-done((f32[16400]{0:T(1024)S(1)}, f32[16400]{0:T(1024)S(1)}, u32[]{:S(2)}, u32[]{:S(2)}) %collective-permute-start.9) | collective-permute-done | bytes 65632 | tf_op jit(solution)/shard_map/ppermute | solution.py:14
  65.6 2.3 %collective-permute-start.10 = (f32[16400]{0:T(1024)S(1)}, f32[16400]{0:T(1024)S(1)}, u32[]{:S(2)}, u32[]{:S(2)}) collective-permute-start(f32[16400]{0:T(1024)S(1)} %pad_maximum_fusion.2), channel_id=1, source_target_pairs={{0,4},{1,5},{2,6},{3,7},{4,0},{5,1},{6,2},{7,3},{8,12},{9,13},{10,... | collective-permute-start | bytes 196808 | tf_op jit(solution)/shard_map/ppermute | solution.py:14
  67.9 3.7 %collective-permute-done.10 = f32[16400]{0:T(1024)S(1)} collective-permute-done((f32[16400]{0:T(1024)S(1)}, f32[16400]{0:T(1024)S(1)}, u32[]{:S(2)}, u32[]{:S(2)}) %collective-permute-start.10) | collective-permute-done | bytes 65632 | tf_op jit(solution)/shard_map/ppermute | solution.py:14
  71.8 1.2 %collective-permute-done.11 = f32[8,16,128]{2,1,0:T(8,128)S(1)} collective-permute-done((f32[8,16,128]{2,1,0:T(8,128)S(1)}, f32[8,16,128]{2,1,0:T(8,128)S(1)}, u32[]{:S(2)}, u32[]{:S(2)}) %collective-permute-start.11) | collective-permute-done | bytes 65568 | tf_op jit(solution)/shard_map/ppermute | solution.py:14
  73.0 0.2 multiply_reduce_fusion.1
  73.2 2.7 %multiply_reduce_fusion.3 = (f32[16]{0:T(128)S(1)}, f32[2,16,128]{2,1,0:T(8,128)}) fusion(f32[2,16,128]{2,1,0:T(8,128)S(1)} %get-tuple-element.35, f32[2,128,16,128]{3,2,1,0:T(8,128)S(1)} %fusion.10, f32[16,16,128]{2,1,0:T(8,128)S(1)} %get-tuple-element.8, f32[16,16,128]{2,1,0:T(8,128)S(1)} %get-tuple-element.4, f32[2,128]{1,0:T(2,128)S(1)} %copy-done.3, ...), kind=kOutput, calls=%fused_computation.71 | convolution fusion | flops 100757488 | bytes 2393216 | tf_op jit(solution)/shard_map/ricj,csj->rsi/dot_general | solution.py:125
  75.9 0.1 pad_maximum_fusion.7
  76.0 0.7 collective-permute-start.12
  76.7 2.9 %collective-permute-done.12 = f32[32]{0:T(128)S(1)} collective-permute-done((f32[32]{0:T(128)S(1)}, f32[32]{0:T(128)S(1)}, u32[]{:S(2)}, u32[]{:S(2)}) %collective-permute-start.12) | collective-permute-done | bytes 160 | tf_op jit(solution)/shard_map/ppermute | solution.py:14
  79.6 0.1 pad_maximum_fusion.8
  79.7 1.5 %collective-permute-start.13 = (f32[32]{0:T(128)S(1)}, f32[32]{0:T(128)S(1)}, u32[]{:S(2)}, u32[]{:S(2)}) collective-permute-start(f32[32]{0:T(128)S(1)} %pad_maximum_fusion.8), channel_id=1, source_target_pairs={{0,16},{8,24},{16,0},{24,8},{1,17},{9,25},{17,1},{25,9},{2,18},{10... | collective-permute-start | bytes 392 | tf_op jit(solution)/shard_map/ppermute | solution.py:14
  81.2 2.0 %collective-permute-done.13 = f32[32]{0:T(128)S(1)} collective-permute-done((f32[32]{0:T(128)S(1)}, f32[32]{0:T(128)S(1)}, u32[]{:S(2)}, u32[]{:S(2)}) %collective-permute-start.13) | collective-permute-done | bytes 160 | tf_op jit(solution)/shard_map/ppermute | solution.py:14
  83.3 1.1 %collective-permute-done.14 = f32[16]{0:T(128)S(1)} collective-permute-done((f32[16]{0:T(128)S(1)}, f32[16]{0:T(128)S(1)}, u32[]{:S(2)}, u32[]{:S(2)}) %collective-permute-start.14) | collective-permute-done | bytes 96 | tf_op jit(solution)/shard_map/ppermute | solution.py:14
  84.4 0.5 collective-permute-start.15
  84.9 3.1 %collective-permute-done.15 = f32[16]{0:T(128)S(1)} collective-permute-done((f32[16]{0:T(128)S(1)}, f32[16]{0:T(128)S(1)}, u32[]{:S(2)}, u32[]{:S(2)}) %collective-permute-start.15) | collective-permute-done | bytes 96 | tf_op jit(solution)/shard_map/ppermute | solution.py:14
  88.0 1.7 %collective-permute-start.16 = (f32[16]{0:T(128)S(1)}, f32[16]{0:T(128)S(1)}, u32[]{:S(2)}, u32[]{:S(2)}) collective-permute-start(f32[16]{0:T(128)S(1)} %add.228), channel_id=1, source_target_pairs={{0,4},{1,5},{2,6},{3,7},{4,0},{5,1},{6,2},{7,3},{8,12},{9,13},{10,... | collective-permute-start | bytes 200 | tf_op jit(solution)/shard_map/ppermute | solution.py:14
  89.7 0.6 constant_dynamic-slice_fusion
  90.3 2.2 %collective-permute-done.16 = f32[16]{0:T(128)S(1)} collective-permute-done((f32[16]{0:T(128)S(1)}, f32[16]{0:T(128)S(1)}, u32[]{:S(2)}, u32[]{:S(2)}) %collective-permute-start.16) | collective-permute-done | bytes 96 | tf_op jit(solution)/shard_map/ppermute | solution.py:14
  92.4 0.5 multiply_sqrt_fusion
  (64 shorter events, 0.8 us)
Async XLA Ops:
  0.6 5.0 %copy-start = (f32[32,128]{1,0:T(8,128)S(1)}, f32[32,128]{1,0:T(8,128)}, u32[]{:S(2)}) copy-start(f32[32,128]{1,0:T(8,128)} %param.20) | copy-start | bytes 49156
  0.6 5.0 %copy-start.6 = (s32[16]{0:T(128)S(1)}, s32[16]{0:T(128)}, u32[]{:S(2)}) copy-start(s32[16]{0:T(128)} %param.21) | copy-start | bytes 196
  0.7 5.1 %copy-start.4 = (f32[2,128]{1,0:T(2,128)S(1)}, f32[2,128]{1,0:T(2,128)}, u32[]{:S(2)}) copy-start(f32[2,128]{1,0:T(2,128)} %param.16) | copy-start | bytes 3076
  0.7 9.6 %copy-start.8 = (s32[48]{0:T(128)S(1)}, s32[48]{0:T(128)}, u32[]{:S(2)}) copy-start(s32[48]{0:T(128)} %param.13) | copy-start | bytes 580
  0.7 9.6 %copy-start.7 = (s32[48]{0:T(128)S(1)}, s32[48]{0:T(128)}, u32[]{:S(2)}) copy-start(s32[48]{0:T(128)} %param.12) | copy-start | bytes 580
  7.3 10.6 %collective-permute-start = (f32[18]{0:T(128)S(1)}, f32[18]{0:T(128)S(1)}, u32[]{:S(2)}, u32[]{:S(2)}) collective-permute-start(f32[18]{0:T(128)S(1)} %pad_maximum_fusion.3), channel_id=1, source_target_pairs={{0,8},{8,0},{16,24},{24,16},{1,9},{9,1},{17,25},{25,17},{2,10},{10... | collective-permute-start | bytes 224 | tf_op jit(solution)/shard_map/ppermute | solution.py:14
  10.4 5.6 %copy-start.1 = (f32[2,16,128]{2,1,0:T(8,128)S(1)}, f32[2,16,128]{2,1,0:T(8,128)}, u32[]{:S(2)}) copy-start(f32[2,16,128]{2,1,0:T(8,128)} %param.19) | copy-start | bytes 49156
  15.9 1.8 %copy-start.2 = (f32[2,16,128]{2,1,0:T(8,128)S(1)}, f32[2,16,128]{2,1,0:T(8,128)}, u32[]{:S(2)}) copy-start(f32[2,16,128]{2,1,0:T(8,128)} %param.18) | copy-start | bytes 49156
  16.0 1.8 %copy-start.5 = (f32[2,128]{1,0:T(2,128)S(1)}, f32[2,128]{1,0:T(2,128)}, u32[]{:S(2)}) copy-start(f32[2,128]{1,0:T(2,128)} %param.17) | copy-start | bytes 3076
  17.7 32.7 %copy-start.3 = (f32[2,128]{1,0:T(2,128)S(1)}, f32[2,128]{1,0:T(2,128)}, u32[]{:S(2)}) copy-start(f32[2,128]{1,0:T(2,128)} %param.15) | copy-start | bytes 3076
  21.2 3.5 %collective-permute-start.1 = (f32[18]{0:T(128)S(1)}, f32[18]{0:T(128)S(1)}, u32[]{:S(2)}, u32[]{:S(2)}) collective-permute-start(f32[18]{0:T(128)S(1)} %pad_maximum_fusion.4), channel_id=1, source_target_pairs={{0,16},{8,24},{16,0},{24,8},{1,17},{9,25},{17,1},{25,9},{2,18},{10... | collective-permute-start | bytes 224 | tf_op jit(solution)/shard_map/ppermute | solution.py:14
  26.8 1.3 %collective-permute-start.2 = (f32[22528]{0:T(1024)S(1)}, f32[22528]{0:T(1024)S(1)}, u32[]{:S(2)}, u32[]{:S(2)}) collective-permute-start(f32[22528]{0:T(1024)S(1)} %concatenate.48), channel_id=1, source_target_pairs={{0,1},{1,0},{2,3},{3,2},{4,5},{5,4},{6,7},{7,6},{8,9},{9,8},{10,11... | collective-permute-start | bytes 270344 | tf_op jit(solution)/shard_map/ppermute | solution.py:14
  30.2 5.1 %collective-permute-start.3 = (f32[27648]{0:T(1024)S(1)}, f32[27648]{0:T(1024)S(1)}, u32[]{:S(2)}, u32[]{:S(2)}) collective-permute-start(f32[27648]{0:T(1024)S(1)} %concatenate.49), channel_id=1, source_target_pairs={{0,2},{1,3},{2,0},{3,1},{4,6},{5,7},{6,4},{7,5},{8,10},{9,11},{10,... | collective-permute-start | bytes 331784 | tf_op jit(solution)/shard_map/ppermute | solution.py:14
  37.5 9.3 %collective-permute-start.4 = (f32[37888]{0:T(1024)S(1)}, f32[37888]{0:T(1024)S(1)}, u32[]{:S(2)}, u32[]{:S(2)}) collective-permute-start(f32[37888]{0:T(1024)S(1)} %concatenate.50), channel_id=1, source_target_pairs={{0,4},{1,5},{2,6},{3,7},{4,0},{5,1},{6,2},{7,3},{8,12},{9,13},{10,... | collective-permute-start | bytes 454664 | tf_op jit(solution)/shard_map/ppermute | solution.py:14
  48.9 1.3 %collective-permute-start.5 = (f32[8,16,128]{2,1,0:T(8,128)S(1)}, f32[8,16,128]{2,1,0:T(8,128)S(1)}, u32[]{:S(2)}, u32[]{:S(2)}) collective-permute-start(f32[8,16,128]{2,1,0:T(8,128)S(1)} %add.203), channel_id=1, source_target_pairs={{0,1},{1,0},{2,3},{3,2},{4,5},{5,4},{6,7},{7,6},{8,9},{9,8},{10,11... | collective-permute-start | bytes 196616 | tf_op jit(solution)/shard_map/ppermute | solution.py:14
  52.6 3.5 %collective-permute-start.6 = (f32[32]{0:T(128)S(1)}, f32[32]{0:T(128)S(1)}, u32[]{:S(2)}, u32[]{:S(2)}) collective-permute-start(f32[32]{0:T(128)S(1)} %pad_maximum_fusion.5), channel_id=1, source_target_pairs={{0,8},{8,0},{16,24},{24,16},{1,9},{9,1},{17,25},{25,17},{2,10},{10... | collective-permute-start | bytes 392 | tf_op jit(solution)/shard_map/ppermute | solution.py:14
  56.3 3.5 %collective-permute-start.7 = (f32[32]{0:T(128)S(1)}, f32[32]{0:T(128)S(1)}, u32[]{:S(2)}, u32[]{:S(2)}) collective-permute-start(f32[32]{0:T(128)S(1)} %pad_maximum_fusion.6), channel_id=1, source_target_pairs={{0,16},{8,24},{16,0},{24,8},{1,17},{9,25},{17,1},{25,9},{2,18},{10... | collective-permute-start | bytes 392 | tf_op jit(solution)/shard_map/ppermute | solution.py:14
  59.9 1.3 %collective-permute-start.8 = (f32[16400]{0:T(1024)S(1)}, f32[16400]{0:T(1024)S(1)}, u32[]{:S(2)}, u32[]{:S(2)}) collective-permute-start(f32[16400]{0:T(1024)S(1)} %pad_maximum_fusion), channel_id=1, source_target_pairs={{0,1},{1,0},{2,3},{3,2},{4,5},{5,4},{6,7},{7,6},{8,9},{9,8},{10,11... | collective-permute-start | bytes 196808 | tf_op jit(solution)/shard_map/ppermute | solution.py:14
  61.2 4.4 %collective-permute-start.9 = (f32[16400]{0:T(1024)S(1)}, f32[16400]{0:T(1024)S(1)}, u32[]{:S(2)}, u32[]{:S(2)}) collective-permute-start(f32[16400]{0:T(1024)S(1)} %pad_maximum_fusion.1), channel_id=1, source_target_pairs={{0,2},{1,3},{2,0},{3,1},{4,6},{5,7},{6,4},{7,5},{8,10},{9,11},{10,... | collective-permute-start | bytes 196808 | tf_op jit(solution)/shard_map/ppermute | solution.py:14
  65.6 6.0 %collective-permute-start.10 = (f32[16400]{0:T(1024)S(1)}, f32[16400]{0:T(1024)S(1)}, u32[]{:S(2)}, u32[]{:S(2)}) collective-permute-start(f32[16400]{0:T(1024)S(1)} %pad_maximum_fusion.2), channel_id=1, source_target_pairs={{0,4},{1,5},{2,6},{3,7},{4,0},{5,1},{6,2},{7,3},{8,12},{9,13},{10,... | collective-permute-start | bytes 196808 | tf_op jit(solution)/shard_map/ppermute | solution.py:14
  71.7 1.3 %collective-permute-start.11 = (f32[8,16,128]{2,1,0:T(8,128)S(1)}, f32[8,16,128]{2,1,0:T(8,128)S(1)}, u32[]{:S(2)}, u32[]{:S(2)}) collective-permute-start(f32[8,16,128]{2,1,0:T(8,128)S(1)} %fusion.66), channel_id=1, source_target_pairs={{0,1},{1,0},{2,3},{3,2},{4,5},{5,4},{6,7},{7,6},{8,9},{9,8},{10,11... | collective-permute-start | bytes 196616 | tf_op jit(solution)/shard_map/ppermute | solution.py:14
  76.0 3.5 %collective-permute-start.12 = (f32[32]{0:T(128)S(1)}, f32[32]{0:T(128)S(1)}, u32[]{:S(2)}, u32[]{:S(2)}) collective-permute-start(f32[32]{0:T(128)S(1)} %pad_maximum_fusion.7), channel_id=1, source_target_pairs={{0,8},{8,0},{16,24},{24,16},{1,9},{9,1},{17,25},{25,17},{2,10},{10... | collective-permute-start | bytes 392 | tf_op jit(solution)/shard_map/ppermute | solution.py:14
  79.7 3.5 %collective-permute-start.13 = (f32[32]{0:T(128)S(1)}, f32[32]{0:T(128)S(1)}, u32[]{:S(2)}, u32[]{:S(2)}) collective-permute-start(f32[32]{0:T(128)S(1)} %pad_maximum_fusion.8), channel_id=1, source_target_pairs={{0,16},{8,24},{16,0},{24,8},{1,17},{9,25},{17,1},{25,9},{2,18},{10... | collective-permute-start | bytes 392 | tf_op jit(solution)/shard_map/ppermute | solution.py:14
  83.3 1.1 %collective-permute-start.14 = (f32[16]{0:T(128)S(1)}, f32[16]{0:T(128)S(1)}, u32[]{:S(2)}, u32[]{:S(2)}) collective-permute-start(f32[16]{0:T(128)S(1)} %slice_add_fusion.6), channel_id=1, source_target_pairs={{0,1},{1,0},{2,3},{3,2},{4,5},{5,4},{6,7},{7,6},{8,9},{9,8},{10,11... | collective-permute-start | bytes 200 | tf_op jit(solution)/shard_map/ppermute | solution.py:14
  84.4 3.5 %collective-permute-start.15 = (f32[16]{0:T(128)S(1)}, f32[16]{0:T(128)S(1)}, u32[]{:S(2)}, u32[]{:S(2)}) collective-permute-start(f32[16]{0:T(128)S(1)} %add.227), channel_id=1, source_target_pairs={{0,2},{1,3},{2,0},{3,1},{4,6},{5,7},{6,4},{7,5},{8,10},{9,11},{10,... | collective-permute-start | bytes 200 | tf_op jit(solution)/shard_map/ppermute | solution.py:14
  88.0 4.4 %collective-permute-start.16 = (f32[16]{0:T(128)S(1)}, f32[16]{0:T(128)S(1)}, u32[]{:S(2)}, u32[]{:S(2)}) collective-permute-start(f32[16]{0:T(128)S(1)} %add.228), channel_id=1, source_target_pairs={{0,4},{1,5},{2,6},{3,7},{4,0},{5,1},{6,2},{7,3},{8,12},{9,13},{10,... | collective-permute-start | bytes 200 | tf_op jit(solution)/shard_map/ppermute | solution.py:14

commit v10 on v9

--- a/solution.py
+++ b/solution.py
@@ -124,9 +124,6 @@
     def product_of(point):
         return jnp.einsum("ricj,csj->rsi", dense, point, precision=hp)
 
-    _, (local_a, local_c, local_b), _ = _rounds(
-        "region", [local_a.reshape(1), local_c, local_b.reshape(1)]
-    )
     own_rows = own_blocks * (scenarios + 2)
     own = jnp.concatenate(
         [
@@ -137,15 +134,27 @@
         ],
         axis=0,
     )
-    partial_value = transposed_product(dual)
-    grad, (sq_a, sq_c, sq_b), gathered = _rounds(
-        "col", [local_a, local_c, local_b], own, split=partial_value
+    _, _, gathered = _rounds("col", [], own)
+    gathered, local_a, local_c, local_b = lax.optimization_barrier(
+        (gathered, local_a, local_c, local_b)
+    )
+    _, (local_a, local_c, local_b), _ = _rounds(
+        "region", [local_a.reshape(1), local_c, local_b.reshape(1)]
     )
     primal_reg = gathered[:, : own_blocks * scenarios].reshape(region_blocks, scenarios, lanes)
     base_reg = gathered[:, own_blocks * scenarios : own_blocks * (scenarios + 1)]
     upper_reg = gathered[:, own_blocks * (scenarios + 1) : own_rows]
     cost_reg = base_reg.reshape(region_blocks, lanes)[:, None, :] * factor[None, :, :]
-    upper_reg = upper_reg.reshape(region_blocks, lanes)[:, None, :]
+    upper_reg = jnp.broadcast_to(
+        upper_reg.reshape(region_blocks, lanes)[:, None, :], (region_blocks, scenarios, lanes)
+    )
+    partial_value = transposed_product(dual)
+    partial_value, primal_reg, cost_reg, upper_reg = lax.optimization_barrier(
+        (partial_value, primal_reg, cost_reg, upper_reg)
+    )
+    grad, (sq_a, sq_c, sq_b), _ = _rounds(
+        "col", [local_a, local_c, local_b], split=partial_value
+    )
     eta = 0.5 / jnp.sqrt(sq_a[0] / (lanes * row_blocks * devices))
     weight = jnp.sqrt(sq_c) / jnp.sqrt(sq_b[0])
     for step in range(ITERS):

time: 93.3 us -> 98.9 us (1.060)
  waiting for transfers between devices: 38.8 us -> 45.5 us
  matrix products: 14 us -> 12.2 us
    ppermute x17 -> x20, waiting for transfers between devices: 38.8 us -> 45.5 us  [_exchange(): return lax.ppermute(x, axis, [(i, i ^ 1 << bit) for i in range(n)])]
    dot_general x1, matrix products: 5.57 us -> 3.73 us  [local(): dense = jnp.dot(place_live, tiles.reshape(ntiles, -1), precision=hp)]
    ppermute x17 -> x20, starting transfers between devices: 18.4 us -> 19.2 us  [_exchange(): return lax.ppermute(x, axis, [(i, i ^ 1 << bit) for i in range(n)])]
  transfers between devices with their start and end apart: 17 -> 20, of which waited for: 16 -> 19; matrix products, arithmetic and copies ran while one was open for 11% -> 12% of each run, Pallas kernels for 0% -> 0%
where the time goes in v10:
time: 98.9 us; the launch traced here: 98.5 us
  waiting for transfers between devices  45.5 us (46%)
  starting transfers between devices  19.2 us (19%)
  matrix products  12.2 us (12%)
  between operations  9.47 us (10%)
  other arithmetic  8.2 us (8%)
  local copies, waits for them, and re-layouts  4.02 us (4%)
    ppermute x20, waiting for transfers between devices, _exchange(): return lax.ppermute(x, axis, [(i, i ^ 1 << bit) for i in range(n)])  45.5 us
    ppermute x20, starting transfers between devices, _exchange(): return lax.ppermute(x, axis, [(i, i ^ 1 << bit) for i in range(n)])  19.2 us
    dot_general x2, matrix products, product_of(): return jnp.einsum('ricj,csj->rsi', dense, point, precision=hp)  4.81 us
    dot_general x1, matrix products, local(): dense = jnp.dot(place_live, tiles.reshape(ntiles, -1), precision=hp)  3.73 us
    dot_general x2, matrix products, transposed_product(): return jnp.einsum('rsi,ricj->csj', dual, dense, precision=hp)  3.45 us
    reduce_sum x2, other arithmetic, local(): local_a = jnp.sum(jnp.sum(tiles * tiles, axis=(1, 2)) * live)  2.94 us
    slice x5, local copies, waits for them, and re-layouts, _rounds(): new_sums.append(s + got[off:off + size].reshape(shape))  2.91 us
  transfers between devices with their start and end apart: 20, of which 19 were waited for; matrix products, arithmetic and copies ran while one was open for 12% of the time, Pallas kernels for 0%

profile of v10, /device:TPU:0, one launch (start us, length us, event | category | flops | bytes accessed | tf_op | source)
XLA Modules:
  0.0 98.5 jit_solution(6984011788467492016)
XLA Ops:
  0.7 0.1 pad.29.clone
  0.8 1.0 fusion.76
  1.8 0.5 collective-permute-start
  2.9 2.3 %multiply_reduce_fusion = f32[48]{0:T(128)S(1)} fusion(f32[48,128,128]{2,1,0:T(8,128)} %param.11), kind=kLoop, calls=%fused_computation.4 | loop fusion | flops 1572816 | bytes 3145920 | tf_op jit(solution)/shard_map/reduce_sum | solution.py:108
  5.3 0.2 fusion.86
  5.5 3.7 %fusion.10 = f32[2,128,16,128]{3,2,1,0:T(8,128)S(1)} fusion(f32[48]{0:T(128)S(1)} %compare_convert_fusion, s32[16,2]{0,1:T(2,128)S(1)} %multiply_add_fusion, s32[48]{0:T(128)S(1)} %multiply_add_fusion.1, f32[6,8,128,128]{3,2,1,0:T(8,128)S(1)} %bitcast.139), kind=kOutput, calls=%fused_computation.13 | convolution fusion | flops 301992960 | bytes 5243392 | tf_op jit(solution)/shard_map/dot_general | solution.py:117
  9.3 1.7 %fusion.11 = f32[16,16,128]{2,1,0:T(8,128)S(1)} fusion(f32[2,128,16,128]{3,2,1,0:T(8,128)S(1)} %fusion.10, f32[2,16,128]{2,1,0:T(8,128)S(1)} %copy-done.2), kind=kOutput, calls=%fused_computation.14 | convolution fusion | flops 100663296 | bytes 2244608 | tf_op jit(solution)/shard_map/rsi,ricj->csj/dot_general | solution.py:122
  11.0 0.1 multiply_reduce_fusion.5
  11.2 2.7 %collective-permute-start.1 = (f32[10240]{0:T(1024)S(1)}, f32[10240]{0:T(1024)S(1)}, u32[]{:S(2)}, u32[]{:S(2)}) collective-permute-start(f32[10240]{0:T(1024)S(1)} %bitcast.157), channel_id=1, source_target_pairs={{0,2},{1,3},{2,0},{3,1},{4,6},{5,7},{6,4},{7,5},{8,10},{9,11},{10,... | collective-permute-start | bytes 122888 | tf_op jit(solution)/shard_map/ppermute | solution.py:14
  13.9 0.6 fusion.88
  14.5 1.6 %collective-permute-done.1 = f32[10240]{0:T(1024)S(1)} collective-permute-done((f32[10240]{0:T(1024)S(1)}, f32[10240]{0:T(1024)S(1)}, u32[]{:S(2)}, u32[]{:S(2)}) %collective-permute-start.1) | collective-permute-done | bytes 40992 | tf_op jit(solution)/shard_map/ppermute | solution.py:14
  16.1 2.9 %collective-permute-start.2 = (f32[20480]{0:T(1024)S(1)}, f32[20480]{0:T(1024)S(1)}, u32[]{:S(2)}, u32[]{:S(2)}) collective-permute-start(f32[20480]{0:T(1024)S(1)} %bitcast.155), channel_id=1, source_target_pairs={{0,4},{1,5},{2,6},{3,7},{4,0},{5,1},{6,2},{7,3},{8,12},{9,13},{10,... | collective-permute-start | bytes 245768 | tf_op jit(solution)/shard_map/ppermute | solution.py:14
  19.0 0.6 multiply_reduce_fusion.6
  19.6 3.5 %collective-permute-done.2 = f32[20480]{0:T(1024)S(1)} collective-permute-done((f32[20480]{0:T(1024)S(1)}, f32[20480]{0:T(1024)S(1)}, u32[]{:S(2)}, u32[]{:S(2)}) %collective-permute-start.2) | collective-permute-done | bytes 81952 | tf_op jit(solution)/shard_map/ppermute | solution.py:14
  23.1 1.4 %pad_maximum_fusion.3 = f32[18]{0:T(128)S(1)} fusion(f32[1]{0:T(128)} %bitcast.22, f32[16]{0:T(128)S(1)} %multiply_reduce_fusion.5, f32[1]{0:T(128)} %bitcast.21), kind=kLoop, calls=%fused_computation.109 | loop fusion | flops 36 | bytes 144 | tf_op jit(solution)/shard_map/concatenate | solution.py:53
  24.5 1.3 %collective-permute-start.3 = (f32[18]{0:T(128)S(1)}, f32[18]{0:T(128)S(1)}, u32[]{:S(2)}, u32[]{:S(2)}) collective-permute-start(f32[18]{0:T(128)S(1)} %pad_maximum_fusion.3), channel_id=1, source_target_pairs={{0,8},{8,0},{16,24},{24,16},{1,9},{9,1},{17,25},{25,17},{2,10},{10... | collective-permute-start | bytes 224 | tf_op jit(solution)/shard_map/ppermute | solution.py:14
  25.8 2.3 %collective-permute-done.3 = f32[18]{0:T(128)S(1)} collective-permute-done((f32[18]{0:T(128)S(1)}, f32[18]{0:T(128)S(1)}, u32[]{:S(2)}, u32[]{:S(2)}) %collective-permute-start.3) | collective-permute-done | bytes 104 | tf_op jit(solution)/shard_map/ppermute | solution.py:14
  28.1 0.6 fusion.106
  31.3 0.1 pad_maximum_fusion.4
  31.4 1.3 %collective-permute-start.4 = (f32[18]{0:T(128)S(1)}, f32[18]{0:T(128)S(1)}, u32[]{:S(2)}, u32[]{:S(2)}) collective-permute-start(f32[18]{0:T(128)S(1)} %pad_maximum_fusion.4), channel_id=1, source_target_pairs={{0,16},{8,24},{16,0},{24,8},{1,17},{9,25},{17,1},{25,9},{2,18},{10... | collective-permute-start | bytes 224 | tf_op jit(solution)/shard_map/ppermute | solution.py:14
  32.7 2.2 %collective-permute-done.4 = f32[18]{0:T(128)S(1)} collective-permute-done((f32[18]{0:T(128)S(1)}, f32[18]{0:T(128)S(1)}, u32[]{:S(2)}, u32[]{:S(2)}) %collective-permute-start.4) | collective-permute-done | bytes 104 | tf_op jit(solution)/shard_map/ppermute | solution.py:14
  34.9 0.6 fusion.105
  36.9 0.1 concatenate.48
  37.0 1.3 %collective-permute-done.5 = f32[16402]{0:T(1024)S(1)} collective-permute-done((f32[16402]{0:T(1024)S(1)}, f32[16402]{0:T(1024)S(1)}, u32[]{:S(2)}, u32[]{:S(2)}) %collective-permute-start.5) | collective-permute-done | bytes 65640 | tf_op jit(solution)/shard_map/ppermute | solution.py:14
  38.2 0.6 fusion.104
  40.2 0.1 concatenate.49
  40.3 0.3 collective-permute-start.6
  40.6 4.0 %collective-permute-done.6 = f32[16402]{0:T(1024)S(1)} collective-permute-done((f32[16402]{0:T(1024)S(1)}, f32[16402]{0:T(1024)S(1)}, u32[]{:S(2)}, u32[]{:S(2)}) %collective-permute-start.6) | collective-permute-done | bytes 65640 | tf_op jit(solution)/shard_map/ppermute | solution.py:14
  44.6 0.6 fusion.103
  46.5 0.1 concatenate.50
  46.6 1.9 %collective-permute-start.7 = (f32[16402]{0:T(1024)S(1)}, f32[16402]{0:T(1024)S(1)}, u32[]{:S(2)}, u32[]{:S(2)}) collective-permute-start(f32[16402]{0:T(1024)S(1)} %concatenate.50), channel_id=1, source_target_pairs={{0,4},{1,5},{2,6},{3,7},{4,0},{5,1},{6,2},{7,3},{8,12},{9,13},{10,... | collective-permute-start | bytes 196832 | tf_op jit(solution)/shard_map/ppermute | solution.py:14
  48.5 4.1 %collective-permute-done.7 = f32[16402]{0:T(1024)S(1)} collective-permute-done((f32[16402]{0:T(1024)S(1)}, f32[16402]{0:T(1024)S(1)}, u32[]{:S(2)}, u32[]{:S(2)}) %collective-permute-start.7) | collective-permute-done | bytes 65640 | tf_op jit(solution)/shard_map/ppermute | solution.py:14
  52.6 0.6 fusion.100
  54.7 0.1 broadcast_multiply_fusion.2
  54.8 1.1 %collective-permute-done.8 = f32[8,16,128]{2,1,0:T(8,128)S(1)} collective-permute-done((f32[8,16,128]{2,1,0:T(8,128)S(1)}, f32[8,16,128]{2,1,0:T(8,128)S(1)}, u32[]{:S(2)}, u32[]{:S(2)}) %collective-permute-start.8) | collective-permute-done | bytes 65568 | tf_op jit(solution)/shard_map/ppermute | solution.py:14
  55.9 0.2 multiply_reduce_fusion.2
  56.1 2.1 %multiply_reduce_fusion.4 = (f32[16]{0:T(128)S(1)}, f32[2,16,128]{2,1,0:T(8,128)S(1)}) fusion(f32[2,16,128]{2,1,0:T(8,128)S(1)} %copy-done.2, f32[2,128,16,128]{3,2,1,0:T(8,128)S(1)} %fusion.10, f32[16,16,128]{2,1,0:T(8,128)S(1)} %bitcast.141, f32[16,16,128]{2,1,0:T(8,128)S(1)} %get-tuple-element.24, f32[2,128]{1,0:T(2,128)S(1)} %copy-done.3, ...), kind=kOutput, calls=%fused_computation.75 | convolution fusion | flops 100757488 | bytes 2393216 | tf_op jit(solution)/shard_map/ricj,csj->rsi/dot_general | solution.py:125
  58.2 0.1 pad_maximum_fusion.5
  58.3 1.3 %collective-permute-start.9 = (f32[32]{0:T(128)S(1)}, f32[32]{0:T(128)S(1)}, u32[]{:S(2)}, u32[]{:S(2)}) collective-permute-start(f32[32]{0:T(128)S(1)} %pad_maximum_fusion.5), channel_id=1, source_target_pairs={{0,8},{8,0},{16,24},{24,16},{1,9},{9,1},{17,25},{25,17},{2,10},{10... | collective-permute-start | bytes 392 | tf_op jit(solution)/shard_map/ppermute | solution.py:14
  59.6 1.7 %fusion.6 = f32[16,128,16,1]{1,2,3,0:T(8,128)S(1)} fusion(f32[2,128,16,128]{3,2,1,0:T(8,128)S(1)} %fusion.10, f32[2,16,128]{2,1,0:T(8,128)S(1)} %get-tuple-element.57), kind=kOutput, calls=%fused_computation.9 | convolution fusion | flops 100663296 | bytes 2244608 | tf_op jit(solution)/shard_map/rsi,ricj->csj/dot_general | solution.py:122
  61.3 0.6 collective-permute-done.9
  61.9 0.1 pad_maximum_fusion.6
  62.0 1.3 %collective-permute-start.10 = (f32[32]{0:T(128)S(1)}, f32[32]{0:T(128)S(1)}, u32[]{:S(2)}, u32[]{:S(2)}) collective-permute-start(f32[32]{0:T(128)S(1)} %pad_maximum_fusion.6), channel_id=1, source_target_pairs={{0,16},{8,24},{16,0},{24,8},{1,17},{9,25},{17,1},{25,9},{2,18},{10... | collective-permute-start | bytes 392 | tf_op jit(solution)/shard_map/ppermute | solution.py:14
  63.3 2.2 %collective-permute-done.10 = f32[32]{0:T(128)S(1)} collective-permute-done((f32[32]{0:T(128)S(1)}, f32[32]{0:T(128)S(1)}, u32[]{:S(2)}, u32[]{:S(2)}) %collective-permute-start.10) | collective-permute-done | bytes 160 | tf_op jit(solution)/shard_map/ppermute | solution.py:14
  65.7 1.2 %collective-permute-done.11 = f32[16400]{0:T(1024)S(1)} collective-permute-done((f32[16400]{0:T(1024)S(1)}, f32[16400]{0:T(1024)S(1)}, u32[]{:S(2)}, u32[]{:S(2)}) %collective-permute-start.11) | collective-permute-done | bytes 65632 | tf_op jit(solution)/shard_map/ppermute | solution.py:14
  67.0 0.2 collective-permute-start.12
  67.1 4.2 %collective-permute-done.12 = f32[16400]{0:T(1024)S(1)} collective-permute-done((f32[16400]{0:T(1024)S(1)}, f32[16400]{0:T(1024)S(1)}, u32[]{:S(2)}, u32[]{:S(2)}) %collective-permute-start.12) | collective-permute-done | bytes 65632 | tf_op jit(solution)/shard_map/ppermute | solution.py:14
  71.4 1.6 %collective-permute-start.13 = (f32[16400]{0:T(1024)S(1)}, f32[16400]{0:T(1024)S(1)}, u32[]{:S(2)}, u32[]{:S(2)}) collective-permute-start(f32[16400]{0:T(1024)S(1)} %pad_maximum_fusion.2), channel_id=1, source_target_pairs={{0,4},{1,5},{2,6},{3,7},{4,0},{5,1},{6,2},{7,3},{8,12},{9,13},{10,... | collective-permute-start | bytes 196808 | tf_op jit(solution)/shard_map/ppermute | solution.py:14
  73.0 4.3 %collective-permute-done.13 = f32[16400]{0:T(1024)S(1)} collective-permute-done((f32[16400]{0:T(1024)S(1)}, f32[16400]{0:T(1024)S(1)}, u32[]{:S(2)}, u32[]{:S(2)}) %collective-permute-start.13) | collective-permute-done | bytes 65632 | tf_op jit(solution)/shard_map/ppermute | solution.py:14
  77.4 1.2 %collective-permute-done.14 = f32[8,16,128]{2,1,0:T(8,128)S(1)} collective-permute-done((f32[8,16,128]{2,1,0:T(8,128)S(1)}, f32[8,16,128]{2,1,0:T(8,128)S(1)}, u32[]{:S(2)}, u32[]{:S(2)}) %collective-permute-start.14) | collective-permute-done | bytes 65568 | tf_op jit(solution)/shard_map/ppermute | solution.py:14
  78.6 0.2 multiply_reduce_fusion.1
  78.8 2.7 %multiply_reduce_fusion.3 = (f32[16]{0:T(128)S(1)}, f32[2,16,128]{2,1,0:T(8,128)}) fusion(f32[2,16,128]{2,1,0:T(8,128)S(1)} %get-tuple-element.57, f32[2,128,16,128]{3,2,1,0:T(8,128)S(1)} %fusion.10, f32[16,16,128]{2,1,0:T(8,128)S(1)} %get-tuple-element.24, f32[16,16,128]{2,1,0:T(8,128)S(1)} %get-tuple-element.20, f32[2,128]{1,0:T(2,128)S(1)} %copy-done.3, ...), kind=kOutput, calls=%fused_computation.74 | convolution fusion | flops 100757488 | bytes 2393216 | tf_op jit(solution)/shard_map/ricj,csj->rsi/dot_general | solution.py:125
  81.5 0.1 pad_maximum_fusion.7
  81.6 1.4 %collective-permute-start.15 = (f32[32]{0:T(128)S(1)}, f32[32]{0:T(128)S(1)}, u32[]{:S(2)}, u32[]{:S(2)}) collective-permute-start(f32[32]{0:T(128)S(1)} %pad_maximum_fusion.7), channel_id=1, source_target_pairs={{0,8},{8,0},{16,24},{24,16},{1,9},{9,1},{17,25},{25,17},{2,10},{10... | collective-permute-start | bytes 392 | tf_op jit(solution)/shard_map/ppermute | solution.py:14
  83.0 2.1 %collective-permute-done.15 = f32[32]{0:T(128)S(1)} collective-permute-done((f32[32]{0:T(128)S(1)}, f32[32]{0:T(128)S(1)}, u32[]{:S(2)}, u32[]{:S(2)}) %collective-permute-start.15) | collective-permute-done | bytes 160 | tf_op jit(solution)/shard_map/ppermute | solution.py:14
  85.2 0.1 pad_maximum_fusion.8
  85.3 1.4 %collective-permute-start.16 = (f32[32]{0:T(128)S(1)}, f32[32]{0:T(128)S(1)}, u32[]{:S(2)}, u32[]{:S(2)}) collective-permute-start(f32[32]{0:T(128)S(1)} %pad_maximum_fusion.8), channel_id=1, source_target_pairs={{0,16},{8,24},{16,0},{24,8},{1,17},{9,25},{17,1},{25,9},{2,18},{10... | collective-permute-start | bytes 392 | tf_op jit(solution)/shard_map/ppermute | solution.py:14
  86.7 2.1 %collective-permute-done.16 = f32[32]{0:T(128)S(1)} collective-permute-done((f32[32]{0:T(128)S(1)}, f32[32]{0:T(128)S(1)}, u32[]{:S(2)}, u32[]{:S(2)}) %collective-permute-start.16) | collective-permute-done | bytes 160 | tf_op jit(solution)/shard_map/ppermute | solution.py:14
  88.9 1.1 %collective-permute-done.17 = f32[16]{0:T(128)S(1)} collective-permute-done((f32[16]{0:T(128)S(1)}, f32[16]{0:T(128)S(1)}, u32[]{:S(2)}, u32[]{:S(2)}) %collective-permute-start.17) | collective-permute-done | bytes 96 | tf_op jit(solution)/shard_map/ppermute | solution.py:14
  90.0 3.5 %collective-permute-done.18 = f32[16]{0:T(128)S(1)} collective-permute-done((f32[16]{0:T(128)S(1)}, f32[16]{0:T(128)S(1)}, u32[]{:S(2)}, u32[]{:S(2)}) %collective-permute-start.18) | collective-permute-done | bytes 96 | tf_op jit(solution)/shard_map/ppermute | solution.py:14
  93.6 1.1 %collective-permute-start.19 = (f32[16]{0:T(128)S(1)}, f32[16]{0:T(128)S(1)}, u32[]{:S(2)}, u32[]{:S(2)}) collective-permute-start(f32[16]{0:T(128)S(1)} %add.237), channel_id=1, source_target_pairs={{0,4},{1,5},{2,6},{3,7},{4,0},{5,1},{6,2},{7,3},{8,12},{9,13},{10,... | collective-permute-start | bytes 200 | tf_op jit(solution)/shard_map/ppermute | solution.py:14
  94.7 0.6 constant_dynamic-slice_fusion
  95.3 2.7 %collective-permute-done.19 = f32[16]{0:T(128)S(1)} collective-permute-done((f32[16]{0:T(128)S(1)}, f32[16]{0:T(128)S(1)}, u32[]{:S(2)}, u32[]{:S(2)}) %collective-permute-start.19) | collective-permute-done | bytes 96 | tf_op jit(solution)/shard_map/ppermute | solution.py:14
  98.0 0.5 multiply_sqrt_fusion
  (65 shorter events, 1.1 us)
Async XLA Ops:
  0.6 4.7 %copy-start = (f32[32,128]{1,0:T(8,128)S(1)}, f32[32,128]{1,0:T(8,128)}, u32[]{:S(2)}) copy-start(f32[32,128]{1,0:T(8,128)} %param.20) | copy-start | bytes 49156
  0.6 4.6 %copy-start.6 = (s32[48]{0:T(128)S(1)}, s32[48]{0:T(128)}, u32[]{:S(2)}) copy-start(s32[48]{0:T(128)} %param.13) | copy-start | bytes 580
  0.7 4.6 %copy-start.5 = (s32[48]{0:T(128)S(1)}, s32[48]{0:T(128)}, u32[]{:S(2)}) copy-start(s32[48]{0:T(128)} %param.12) | copy-start | bytes 580
  0.7 4.7 %copy-start.7 = (s32[16]{0:T(128)S(1)}, s32[16]{0:T(128)}, u32[]{:S(2)}) copy-start(s32[16]{0:T(128)} %param.21) | copy-start | bytes 196
  0.7 4.8 %copy-start.1 = (f32[48,128,128]{2,1,0:T(8,128)S(1)}, f32[48,128,128]{2,1,0:T(8,128)}, u32[]{:S(2)}) copy-start(f32[48,128,128]{2,1,0:T(8,128)} %param.11) | copy-start | bytes 9437188
  1.8 9.4 %collective-permute-start = (f32[5120]{0:T(1024)S(1)}, f32[5120]{0:T(1024)S(1)}, u32[]{:S(2)}, u32[]{:S(2)}) collective-permute-start(f32[5120]{0:T(1024)S(1)} %dynamic-slice_bitcast_fusion), channel_id=1, source_target_pairs={{0,1},{1,0},{2,3},{3,2},{4,5},{5,4},{6,7},{7,6},{8,9},{9,8},{10,11... | collective-permute-start | bytes 61448 | tf_op jit(solution)/shard_map/ppermute | solution.py:14
  5.5 3.7 %copy-start.2 = (f32[2,16,128]{2,1,0:T(8,128)S(1)}, f32[2,16,128]{2,1,0:T(8,128)}, u32[]{:S(2)}) copy-start(f32[2,16,128]{2,1,0:T(8,128)} %param.19) | copy-start | bytes 49156
  9.3 1.8 %copy-start.4 = (f32[2,128]{1,0:T(2,128)S(1)}, f32[2,128]{1,0:T(2,128)}, u32[]{:S(2)}) copy-start(f32[2,128]{1,0:T(2,128)} %param.16) | copy-start | bytes 3076
  9.3 9.7 %copy-start.3 = (f32[2,128]{1,0:T(2,128)S(1)}, f32[2,128]{1,0:T(2,128)}, u32[]{:S(2)}) copy-start(f32[2,128]{1,0:T(2,128)} %param.15) | copy-start | bytes 3076
  11.2 4.9 %collective-permute-start.1 = (f32[10240]{0:T(1024)S(1)}, f32[10240]{0:T(1024)S(1)}, u32[]{:S(2)}, u32[]{:S(2)}) collective-permute-start(f32[10240]{0:T(1024)S(1)} %bitcast.157), channel_id=1, source_target_pairs={{0,2},{1,3},{2,0},{3,1},{4,6},{5,7},{6,4},{7,5},{8,10},{9,11},{10,... | collective-permute-start | bytes 122888 | tf_op jit(solution)/shard_map/ppermute | solution.py:14
  16.1 7.0 %collective-permute-start.2 = (f32[20480]{0:T(1024)S(1)}, f32[20480]{0:T(1024)S(1)}, u32[]{:S(2)}, u32[]{:S(2)}) collective-permute-start(f32[20480]{0:T(1024)S(1)} %bitcast.155), channel_id=1, source_target_pairs={{0,4},{1,5},{2,6},{3,7},{4,0},{5,1},{6,2},{7,3},{8,12},{9,13},{10,... | collective-permute-start | bytes 245768 | tf_op jit(solution)/shard_map/ppermute | solution.py:14
  24.5 3.5 %collective-permute-start.3 = (f32[18]{0:T(128)S(1)}, f32[18]{0:T(128)S(1)}, u32[]{:S(2)}, u32[]{:S(2)}) collective-permute-start(f32[18]{0:T(128)S(1)} %pad_maximum_fusion.3), channel_id=1, source_target_pairs={{0,8},{8,0},{16,24},{24,16},{1,9},{9,1},{17,25},{25,17},{2,10},{10... | collective-permute-start | bytes 224 | tf_op jit(solution)/shard_map/ppermute | solution.py:14
  31.4 3.5 %collective-permute-start.4 = (f32[18]{0:T(128)S(1)}, f32[18]{0:T(128)S(1)}, u32[]{:S(2)}, u32[]{:S(2)}) collective-permute-start(f32[18]{0:T(128)S(1)} %pad_maximum_fusion.4), channel_id=1, source_target_pairs={{0,16},{8,24},{16,0},{24,8},{1,17},{9,25},{17,1},{25,9},{2,18},{10... | collective-permute-start | bytes 224 | tf_op jit(solution)/shard_map/ppermute | solution.py:14
  36.9 1.3 %collective-permute-start.5 = (f32[16402]{0:T(1024)S(1)}, f32[16402]{0:T(1024)S(1)}, u32[]{:S(2)}, u32[]{:S(2)}) collective-permute-start(f32[16402]{0:T(1024)S(1)} %concatenate.48), channel_id=1, source_target_pairs={{0,1},{1,0},{2,3},{3,2},{4,5},{5,4},{6,7},{7,6},{8,9},{9,8},{10,11... | collective-permute-start | bytes 196832 | tf_op jit(solution)/shard_map/ppermute | solution.py:14
  40.3 4.3 %collective-permute-start.6 = (f32[16402]{0:T(1024)S(1)}, f32[16402]{0:T(1024)S(1)}, u32[]{:S(2)}, u32[]{:S(2)}) collective-permute-start(f32[16402]{0:T(1024)S(1)} %concatenate.49), channel_id=1, source_target_pairs={{0,2},{1,3},{2,0},{3,1},{4,6},{5,7},{6,4},{7,5},{8,10},{9,11},{10,... | collective-permute-start | bytes 196832 | tf_op jit(solution)/shard_map/ppermute | solution.py:14
  46.6 6.0 %collective-permute-start.7 = (f32[16402]{0:T(1024)S(1)}, f32[16402]{0:T(1024)S(1)}, u32[]{:S(2)}, u32[]{:S(2)}) collective-permute-start(f32[16402]{0:T(1024)S(1)} %concatenate.50), channel_id=1, source_target_pairs={{0,4},{1,5},{2,6},{3,7},{4,0},{5,1},{6,2},{7,3},{8,12},{9,13},{10,... | collective-permute-start | bytes 196832 | tf_op jit(solution)/shard_map/ppermute | solution.py:14
  54.6 1.3 %collective-permute-start.8 = (f32[8,16,128]{2,1,0:T(8,128)S(1)}, f32[8,16,128]{2,1,0:T(8,128)S(1)}, u32[]{:S(2)}, u32[]{:S(2)}) collective-permute-start(f32[8,16,128]{2,1,0:T(8,128)S(1)} %fusion.73), channel_id=1, source_target_pairs={{0,1},{1,0},{2,3},{3,2},{4,5},{5,4},{6,7},{7,6},{8,9},{9,8},{10,11... | collective-permute-start | bytes 196616 | tf_op jit(solution)/shard_map/ppermute | solution.py:14
  58.3 3.5 %collective-permute-start.9 = (f32[32]{0:T(128)S(1)}, f32[32]{0:T(128)S(1)}, u32[]{:S(2)}, u32[]{:S(2)}) collective-permute-start(f32[32]{0:T(128)S(1)} %pad_maximum_fusion.5), channel_id=1, source_target_pairs={{0,8},{8,0},{16,24},{24,16},{1,9},{9,1},{17,25},{25,17},{2,10},{10... | collective-permute-start | bytes 392 | tf_op jit(solution)/shard_map/ppermute | solution.py:14
  62.0 3.5 %collective-permute-start.10 = (f32[32]{0:T(128)S(1)}, f32[32]{0:T(128)S(1)}, u32[]{:S(2)}, u32[]{:S(2)}) collective-permute-start(f32[32]{0:T(128)S(1)} %pad_maximum_fusion.6), channel_id=1, source_target_pairs={{0,16},{8,24},{16,0},{24,8},{1,17},{9,25},{17,1},{25,9},{2,18},{10... | collective-permute-start | bytes 392 | tf_op jit(solution)/shard_map/ppermute | solution.py:14
  65.6 1.3 %collective-permute-start.11 = (f32[16400]{0:T(1024)S(1)}, f32[16400]{0:T(1024)S(1)}, u32[]{:S(2)}, u32[]{:S(2)}) collective-permute-start(f32[16400]{0:T(1024)S(1)} %pad_maximum_fusion), channel_id=1, source_target_pairs={{0,1},{1,0},{2,3},{3,2},{4,5},{5,4},{6,7},{7,6},{8,9},{9,8},{10,11... | collective-permute-start | bytes 196808 | tf_op jit(solution)/shard_map/ppermute | solution.py:14
  67.0 4.4 %collective-permute-start.12 = (f32[16400]{0:T(1024)S(1)}, f32[16400]{0:T(1024)S(1)}, u32[]{:S(2)}, u32[]{:S(2)}) collective-permute-start(f32[16400]{0:T(1024)S(1)} %pad_maximum_fusion.1), channel_id=1, source_target_pairs={{0,2},{1,3},{2,0},{3,1},{4,6},{5,7},{6,4},{7,5},{8,10},{9,11},{10,... | collective-permute-start | bytes 196808 | tf_op jit(solution)/shard_map/ppermute | solution.py:14
  71.4 5.9 %collective-permute-start.13 = (f32[16400]{0:T(1024)S(1)}, f32[16400]{0:T(1024)S(1)}, u32[]{:S(2)}, u32[]{:S(2)}) collective-permute-start(f32[16400]{0:T(1024)S(1)} %pad_maximum_fusion.2), channel_id=1, source_target_pairs={{0,4},{1,5},{2,6},{3,7},{4,0},{5,1},{6,2},{7,3},{8,12},{9,13},{10,... | collective-permute-start | bytes 196808 | tf_op jit(solution)/shard_map/ppermute | solution.py:14
  77.3 1.3 %collective-permute-start.14 = (f32[8,16,128]{2,1,0:T(8,128)S(1)}, f32[8,16,128]{2,1,0:T(8,128)S(1)}, u32[]{:S(2)}, u32[]{:S(2)}) collective-permute-start(f32[8,16,128]{2,1,0:T(8,128)S(1)} %fusion.71), channel_id=1, source_target_pairs={{0,1},{1,0},{2,3},{3,2},{4,5},{5,4},{6,7},{7,6},{8,9},{9,8},{10,11... | collective-permute-start | bytes 196616 | tf_op jit(solution)/shard_map/ppermute | solution.py:14
  81.6 3.5 %collective-permute-start.15 = (f32[32]{0:T(128)S(1)}, f32[32]{0:T(128)S(1)}, u32[]{:S(2)}, u32[]{:S(2)}) collective-permute-start(f32[32]{0:T(128)S(1)} %pad_maximum_fusion.7), channel_id=1, source_target_pairs={{0,8},{8,0},{16,24},{24,16},{1,9},{9,1},{17,25},{25,17},{2,10},{10... | collective-permute-start | bytes 392 | tf_op jit(solution)/shard_map/ppermute | solution.py:14
  85.3 3.5 %collective-permute-start.16 = (f32[32]{0:T(128)S(1)}, f32[32]{0:T(128)S(1)}, u32[]{:S(2)}, u32[]{:S(2)}) collective-permute-start(f32[32]{0:T(128)S(1)} %pad_maximum_fusion.8), channel_id=1, source_target_pairs={{0,16},{8,24},{16,0},{24,8},{1,17},{9,25},{17,1},{25,9},{2,18},{10... | collective-permute-start | bytes 392 | tf_op jit(solution)/shard_map/ppermute | solution.py:14
  88.9 1.1 %collective-permute-start.17 = (f32[16]{0:T(128)S(1)}, f32[16]{0:T(128)S(1)}, u32[]{:S(2)}, u32[]{:S(2)}) collective-permute-start(f32[16]{0:T(128)S(1)} %slice_add_fusion.6), channel_id=1, source_target_pairs={{0,1},{1,0},{2,3},{3,2},{4,5},{5,4},{6,7},{7,6},{8,9},{9,8},{10,11... | collective-permute-start | bytes 200 | tf_op jit(solution)/shard_map/ppermute | solution.py:14
  90.0 3.5 %collective-permute-start.18 = (f32[16]{0:T(128)S(1)}, f32[16]{0:T(128)S(1)}, u32[]{:S(2)}, u32[]{:S(2)}) collective-permute-start(f32[16]{0:T(128)S(1)} %add.236), channel_id=1, source_target_pairs={{0,2},{1,3},{2,0},{3,1},{4,6},{5,7},{6,4},{7,5},{8,10},{9,11},{10,... | collective-permute-start | bytes 200 | tf_op jit(solution)/shard_map/ppermute | solution.py:14
  93.6 4.4 %collective-permute-start.19 = (f32[16]{0:T(128)S(1)}, f32[16]{0:T(128)S(1)}, u32[]{:S(2)}, u32[]{:S(2)}) collective-permute-start(f32[16]{0:T(128)S(1)} %add.237), channel_id=1, source_target_pairs={{0,4},{1,5},{2,6},{3,7},{4,0},{5,1},{6,2},{7,3},{8,12},{9,13},{10,... | collective-permute-start | bytes 200 | tf_op jit(solution)/shard_map/ppermute | solution.py:14

commit v11 on v9

--- a/solution.py
+++ b/solution.py
@@ -119,10 +119,10 @@
     dense = dense.transpose(1, 2, 0, 3)
 
     def transposed_product(dual):
-        return jnp.einsum("rsi,ricj->csj", dual, dense, precision=hp)
+        return jnp.einsum("rsi,ricj->csj", dual, dense, precision=lax.Precision.HIGH)
 
     def product_of(point):
-        return jnp.einsum("ricj,csj->rsi", dense, point, precision=hp)
+        return jnp.einsum("ricj,csj->rsi", dense, point, precision=lax.Precision.HIGH)
 
     _, (local_a, local_c, local_b), _ = _rounds(
         "region", [local_a.reshape(1), local_c, local_b.reshape(1)]

time: 93.3 us -> 91.5 us (0.981)
  matrix products: 14 us -> 11.5 us
    dot_general x4, matrix products: 8.26 us -> 5.77 us  [the longest x2 3.64 us: product_of(): jnp.einsum('ricj,csj->rsi', dense, point, precision=lax.Precision.HIGH)]
  transfers between devices with their start and end apart: 17 -> 17, of which waited for: 16 -> 16; matrix products, arithmetic and copies ran while one was open for 11% -> 9% of each run, Pallas kernels for 0% -> 0%
where the time goes in v11:
time: 91.5 us; the launch traced here: 91.1 us
  waiting for transfers between devices  39.5 us (43%)
  starting transfers between devices  18.4 us (20%)
  matrix products  11.5 us (13%)
  between operations  9.63 us (11%)
  other arithmetic  7.98 us (9%)
  local copies, waits for them, and re-layouts  4.07 us (4%)
    ppermute x17, waiting for transfers between devices, _exchange(): return lax.ppermute(x, axis, [(i, i ^ 1 << bit) for i in range(n)])  39.5 us
    ppermute x17, starting transfers between devices, _exchange(): return lax.ppermute(x, axis, [(i, i ^ 1 << bit) for i in range(n)])  18.4 us
    dot_general x1, matrix products, local(): dense = jnp.dot(place_live, tiles.reshape(ntiles, -1), precision=hp)  5.57 us
    dot_general x2, matrix products, product_of(): jnp.einsum('ricj,csj->rsi', dense, point, precision=lax.Precision.HIGH)  3.64 us
    reduce_sum x2, other arithmetic, local(): local_a = jnp.sum(jnp.sum(tiles * tiles, axis=(1, 2)) * live)  2.94 us
    slice x5, local copies, waits for them, and re-layouts, _rounds(): new_sums.append(s + got[off:off + size].reshape(shape))  2.92 us
    dot_general x2, matrix products, transposed_product(): jnp.einsum('rsi,ricj->csj', dual, dense, precision=lax.Precision.HIGH)  2.13 us
  transfers between devices with their start and end apart: 17, of which 16 were waited for; matrix products, arithmetic and copies ran while one was open for 9% of the time, Pallas kernels for 0%

profile of v11, /device:TPU:0, one launch (start us, length us, event | category | flops | bytes accessed | tf_op | source)
XLA Modules:
  0.0 91.1 jit_solution(2864312375743144171)
XLA Ops:
  1.4 1.3 %multiply_reduce_fusion.6 = f32[]{:T(128)} fusion(f32[2,128]{1,0:T(2,128)} %param.15), kind=kLoop, calls=%fused_computation.93 | loop fusion | flops 511 | bytes 1028 | tf_op jit(solution)/shard_map/reduce_sum | solution.py:110
  2.7 2.3 %multiply_reduce_fusion = f32[48]{0:T(128)S(1)} fusion(f32[48,128,128]{2,1,0:T(8,128)} %param.11), kind=kLoop, calls=%fused_computation.4 | loop fusion | flops 1572816 | bytes 3145920 | tf_op jit(solution)/shard_map/reduce_sum | solution.py:108
  5.0 0.6 fusion.82
  5.6 0.2 fusion.80
  5.8 0.1 multiply_reduce_fusion.5
  5.9 1.4 %pad_maximum_fusion.3 = f32[18]{0:T(128)S(1)} fusion(f32[1]{0:T(128)} %bitcast.15, f32[16]{0:T(128)S(1)} %multiply_reduce_fusion.5, f32[1]{0:T(128)} %bitcast.14), kind=kLoop, calls=%fused_computation.105 | loop fusion | flops 36 | bytes 144 | tf_op jit(solution)/shard_map/concatenate | solution.py:53
  7.3 2.9 %collective-permute-start = (f32[18]{0:T(128)S(1)}, f32[18]{0:T(128)S(1)}, u32[]{:S(2)}, u32[]{:S(2)}) collective-permute-start(f32[18]{0:T(128)S(1)} %pad_maximum_fusion.3), channel_id=1, source_target_pairs={{0,8},{8,0},{16,24},{24,16},{1,9},{9,1},{17,25},{25,17},{2,10},{10... | collective-permute-start | bytes 224 | tf_op jit(solution)/shard_map/ppermute | solution.py:14
  10.3 0.1 pad.29.clone
  10.4 5.6 %fusion.10 = f32[2,128,16,128]{3,2,1,0:T(8,128)S(1)} fusion(f32[48]{0:T(128)S(1)} %compare_convert_fusion, s32[16,2]{0,1:T(2,128)S(1)} %multiply_add_fusion, s32[48]{0:T(128)S(1)} %multiply_add_fusion.1, f32[6,8,128,128]{3,2,1,0:T(8,128)} %bitcast.138), kind=kOutput, calls=%fused_computation.13 | convolution fusion | flops 301992960 | bytes 5243392 | tf_op jit(solution)/shard_map/dot_general | solution.py:117
  16.0 1.1 %fusion.8 = f32[16,128,16,1]{1,2,3,0:T(8,128)S(1)} fusion(f32[2,128,16,128]{3,2,1,0:T(8,128)S(1)} %fusion.10, f32[2,16,128]{2,1,0:T(8,128)S(1)} %copy-done.1), kind=kOutput, calls=%fused_computation.11 | convolution fusion | flops 50331648 | bytes 2244608 | tf_op jit(solution)/shard_map/rsi,ricj->csj/dot_general | solution.py:122
  17.1 0.1 fusion.70
  17.2 0.6 fusion.98
  20.4 0.1 slice_add_fusion.13
  20.5 0.1 pad_maximum_fusion.4
  20.6 1.5 %collective-permute-start.1 = (f32[18]{0:T(128)S(1)}, f32[18]{0:T(128)S(1)}, u32[]{:S(2)}, u32[]{:S(2)}) collective-permute-start(f32[18]{0:T(128)S(1)} %pad_maximum_fusion.4), channel_id=1, source_target_pairs={{0,16},{8,24},{16,0},{24,8},{1,17},{9,25},{17,1},{25,9},{2,18},{10... | collective-permute-start | bytes 224 | tf_op jit(solution)/shard_map/ppermute | solution.py:14
  22.1 2.0 %collective-permute-done.1 = f32[18]{0:T(128)S(1)} collective-permute-done((f32[18]{0:T(128)S(1)}, f32[18]{0:T(128)S(1)}, u32[]{:S(2)}, u32[]{:S(2)}) %collective-permute-start.1) | collective-permute-done | bytes 104 | tf_op jit(solution)/shard_map/ppermute | solution.py:14
  24.1 0.6 fusion.97
  26.0 0.1 slice_add_fusion.12
  26.1 0.1 concatenate.48
  26.2 1.3 %collective-permute-done.2 = f32[22528]{0:T(1024)S(1)} collective-permute-done((f32[22528]{0:T(1024)S(1)}, f32[22528]{0:T(1024)S(1)}, u32[]{:S(2)}, u32[]{:S(2)}) %collective-permute-start.2) | collective-permute-done | bytes 90144 | tf_op jit(solution)/shard_map/ppermute | solution.py:14
  27.4 0.6 fusion.94
  29.4 0.1 slice_add_fusion.5
  29.5 0.1 concatenate.49
  29.6 1.6 %collective-permute-start.3 = (f32[27648]{0:T(1024)S(1)}, f32[27648]{0:T(1024)S(1)}, u32[]{:S(2)}, u32[]{:S(2)}) collective-permute-start(f32[27648]{0:T(1024)S(1)} %concatenate.49), channel_id=1, source_target_pairs={{0,2},{1,3},{2,0},{3,1},{4,6},{5,7},{6,4},{7,5},{8,10},{9,11},{10,... | collective-permute-start | bytes 331784 | tf_op jit(solution)/shard_map/ppermute | solution.py:14
  31.1 3.5 %collective-permute-done.3 = f32[27648]{0:T(1024)S(1)} collective-permute-done((f32[27648]{0:T(1024)S(1)}, f32[27648]{0:T(1024)S(1)}, u32[]{:S(2)}, u32[]{:S(2)}) %collective-permute-start.3) | collective-permute-done | bytes 110624 | tf_op jit(solution)/shard_map/ppermute | solution.py:14
  34.7 0.6 fusion.93
  36.7 0.1 slice_add_fusion.4
  36.7 0.1 concatenate.50
  36.8 2.6 %collective-permute-start.4 = (f32[37888]{0:T(1024)S(1)}, f32[37888]{0:T(1024)S(1)}, u32[]{:S(2)}, u32[]{:S(2)}) collective-permute-start(f32[37888]{0:T(1024)S(1)} %concatenate.50), channel_id=1, source_target_pairs={{0,4},{1,5},{2,6},{3,7},{4,0},{5,1},{6,2},{7,3},{8,12},{9,13},{10,... | collective-permute-start | bytes 454664 | tf_op jit(solution)/shard_map/ppermute | solution.py:14
  39.4 6.7 %collective-permute-done.4 = f32[37888]{0:T(1024)S(1)} collective-permute-done((f32[37888]{0:T(1024)S(1)}, f32[37888]{0:T(1024)S(1)}, u32[]{:S(2)}, u32[]{:S(2)}) %collective-permute-start.4) | collective-permute-done | bytes 151584 | tf_op jit(solution)/shard_map/ppermute | solution.py:14
  46.1 0.6 fusion.92
  48.3 0.1 broadcast_multiply_fusion.1
  48.4 1.1 %collective-permute-done.5 = f32[8,16,128]{2,1,0:T(8,128)S(1)} collective-permute-done((f32[8,16,128]{2,1,0:T(8,128)S(1)}, f32[8,16,128]{2,1,0:T(8,128)S(1)}, u32[]{:S(2)}, u32[]{:S(2)}) %collective-permute-start.5) | collective-permute-done | bytes 65568 | tf_op jit(solution)/shard_map/ppermute | solution.py:14
  49.5 0.2 multiply_reduce_fusion.2
  49.7 1.5 %multiply_reduce_fusion.4 = (f32[16]{0:T(128)S(1)}, f32[2,16,128]{2,1,0:T(8,128)S(1)}) fusion(f32[2,16,128]{2,1,0:T(8,128)S(1)} %copy-done.1, f32[2,128,16,128]{3,2,1,0:T(8,128)S(1)} %fusion.10, f32[16,16,128]{2,1,0:T(8,128)S(1)} %bitcast.140, f32[16,16,128]{2,1,0:T(8,128)S(1)} %get-tuple-element.8, f32[2,128]{1,0:T(2,128)S(1)} %copy-done.3, ...), kind=kOutput, calls=%fused_computation.72 | convolution fusion | flops 50425840 | bytes 2393216 | tf_op jit(solution)/shard_map/ricj,csj->rsi/dot_general | solution.py:125
  51.2 0.1 pad_maximum_fusion.5
  51.3 0.7 collective-permute-start.6
  52.0 1.1 %fusion.6 = f32[16,128,16,1]{1,2,3,0:T(8,128)S(1)} fusion(f32[2,128,16,128]{3,2,1,0:T(8,128)S(1)} %fusion.10, f32[2,16,128]{2,1,0:T(8,128)S(1)} %get-tuple-element.35), kind=kOutput, calls=%fused_computation.9 | convolution fusion | flops 50331648 | bytes 2244608 | tf_op jit(solution)/shard_map/rsi,ricj->csj/dot_general | solution.py:122
  53.1 1.8 %collective-permute-done.6 = f32[32]{0:T(128)S(1)} collective-permute-done((f32[32]{0:T(128)S(1)}, f32[32]{0:T(128)S(1)}, u32[]{:S(2)}, u32[]{:S(2)}) %collective-permute-start.6) | collective-permute-done | bytes 160 | tf_op jit(solution)/shard_map/ppermute | solution.py:14
  54.9 0.1 slice_add_fusion.11
  54.9 0.1 pad_maximum_fusion.6
  55.0 1.5 %collective-permute-start.7 = (f32[32]{0:T(128)S(1)}, f32[32]{0:T(128)S(1)}, u32[]{:S(2)}, u32[]{:S(2)}) collective-permute-start(f32[32]{0:T(128)S(1)} %pad_maximum_fusion.6), channel_id=1, source_target_pairs={{0,16},{8,24},{16,0},{24,8},{1,17},{9,25},{17,1},{25,9},{2,18},{10... | collective-permute-start | bytes 392 | tf_op jit(solution)/shard_map/ppermute | solution.py:14
  56.6 2.0 %collective-permute-done.7 = f32[32]{0:T(128)S(1)} collective-permute-done((f32[32]{0:T(128)S(1)}, f32[32]{0:T(128)S(1)}, u32[]{:S(2)}, u32[]{:S(2)}) %collective-permute-start.7) | collective-permute-done | bytes 160 | tf_op jit(solution)/shard_map/ppermute | solution.py:14
  58.7 1.2 %collective-permute-done.8 = f32[16400]{0:T(1024)S(1)} collective-permute-done((f32[16400]{0:T(1024)S(1)}, f32[16400]{0:T(1024)S(1)}, u32[]{:S(2)}, u32[]{:S(2)}) %collective-permute-start.8) | collective-permute-done | bytes 65632 | tf_op jit(solution)/shard_map/ppermute | solution.py:14
  60.0 0.7 collective-permute-start.9
  60.7 3.6 %collective-permute-done.9 = f32[16400]{0:T(1024)S(1)} collective-permute-done((f32[16400]{0:T(1024)S(1)}, f32[16400]{0:T(1024)S(1)}, u32[]{:S(2)}, u32[]{:S(2)}) %collective-permute-start.9) | collective-permute-done | bytes 65632 | tf_op jit(solution)/shard_map/ppermute | solution.py:14
  64.4 2.3 %collective-permute-start.10 = (f32[16400]{0:T(1024)S(1)}, f32[16400]{0:T(1024)S(1)}, u32[]{:S(2)}, u32[]{:S(2)}) collective-permute-start(f32[16400]{0:T(1024)S(1)} %pad_maximum_fusion.2), channel_id=1, source_target_pairs={{0,4},{1,5},{2,6},{3,7},{4,0},{5,1},{6,2},{7,3},{8,12},{9,13},{10,... | collective-permute-start | bytes 196808 | tf_op jit(solution)/shard_map/ppermute | solution.py:14
  66.7 3.7 %collective-permute-done.10 = f32[16400]{0:T(1024)S(1)} collective-permute-done((f32[16400]{0:T(1024)S(1)}, f32[16400]{0:T(1024)S(1)}, u32[]{:S(2)}, u32[]{:S(2)}) %collective-permute-start.10) | collective-permute-done | bytes 65632 | tf_op jit(solution)/shard_map/ppermute | solution.py:14
  70.5 1.2 %collective-permute-done.11 = f32[8,16,128]{2,1,0:T(8,128)S(1)} collective-permute-done((f32[8,16,128]{2,1,0:T(8,128)S(1)}, f32[8,16,128]{2,1,0:T(8,128)S(1)}, u32[]{:S(2)}, u32[]{:S(2)}) %collective-permute-start.11) | collective-permute-done | bytes 65568 | tf_op jit(solution)/shard_map/ppermute | solution.py:14
  71.7 0.2 multiply_reduce_fusion.1
  72.0 2.1 %multiply_reduce_fusion.3 = (f32[16]{0:T(128)S(1)}, f32[2,16,128]{2,1,0:T(8,128)}) fusion(f32[2,16,128]{2,1,0:T(8,128)S(1)} %get-tuple-element.35, f32[2,128,16,128]{3,2,1,0:T(8,128)S(1)} %fusion.10, f32[16,16,128]{2,1,0:T(8,128)S(1)} %get-tuple-element.8, f32[16,16,128]{2,1,0:T(8,128)S(1)} %get-tuple-element.4, f32[2,128]{1,0:T(2,128)S(1)} %copy-done.3, ...), kind=kOutput, calls=%fused_computation.71 | convolution fusion | flops 50425840 | bytes 2393216 | tf_op jit(solution)/shard_map/ricj,csj->rsi/dot_general | solution.py:125
  74.1 0.1 pad_maximum_fusion.7
  74.2 0.7 collective-permute-start.12
  74.8 2.9 %collective-permute-done.12 = f32[32]{0:T(128)S(1)} collective-permute-done((f32[32]{0:T(128)S(1)}, f32[32]{0:T(128)S(1)}, u32[]{:S(2)}, u32[]{:S(2)}) %collective-permute-start.12) | collective-permute-done | bytes 160 | tf_op jit(solution)/shard_map/ppermute | solution.py:14
  77.8 0.1 pad_maximum_fusion.8
  77.9 1.5 %collective-permute-start.13 = (f32[32]{0:T(128)S(1)}, f32[32]{0:T(128)S(1)}, u32[]{:S(2)}, u32[]{:S(2)}) collective-permute-start(f32[32]{0:T(128)S(1)} %pad_maximum_fusion.8), channel_id=1, source_target_pairs={{0,16},{8,24},{16,0},{24,8},{1,17},{9,25},{17,1},{25,9},{2,18},{10... | collective-permute-start | bytes 392 | tf_op jit(solution)/shard_map/ppermute | solution.py:14
  79.4 2.0 %collective-permute-done.13 = f32[32]{0:T(128)S(1)} collective-permute-done((f32[32]{0:T(128)S(1)}, f32[32]{0:T(128)S(1)}, u32[]{:S(2)}, u32[]{:S(2)}) %collective-permute-start.13) | collective-permute-done | bytes 160 | tf_op jit(solution)/shard_map/ppermute | solution.py:14
  81.5 1.1 %collective-permute-done.14 = f32[16]{0:T(128)S(1)} collective-permute-done((f32[16]{0:T(128)S(1)}, f32[16]{0:T(128)S(1)}, u32[]{:S(2)}, u32[]{:S(2)}) %collective-permute-start.14) | collective-permute-done | bytes 96 | tf_op jit(solution)/shard_map/ppermute | solution.py:14
  82.6 0.5 collective-permute-start.15
  83.1 3.1 %collective-permute-done.15 = f32[16]{0:T(128)S(1)} collective-permute-done((f32[16]{0:T(128)S(1)}, f32[16]{0:T(128)S(1)}, u32[]{:S(2)}, u32[]{:S(2)}) %collective-permute-start.15) | collective-permute-done | bytes 96 | tf_op jit(solution)/shard_map/ppermute | solution.py:14
  86.1 1.7 %collective-permute-start.16 = (f32[16]{0:T(128)S(1)}, f32[16]{0:T(128)S(1)}, u32[]{:S(2)}, u32[]{:S(2)}) collective-permute-start(f32[16]{0:T(128)S(1)} %add.228), channel_id=1, source_target_pairs={{0,4},{1,5},{2,6},{3,7},{4,0},{5,1},{6,2},{7,3},{8,12},{9,13},{10,... | collective-permute-start | bytes 200 | tf_op jit(solution)/shard_map/ppermute | solution.py:14
  87.8 0.6 constant_dynamic-slice_fusion
  88.4 2.2 %collective-permute-done.16 = f32[16]{0:T(128)S(1)} collective-permute-done((f32[16]{0:T(128)S(1)}, f32[16]{0:T(128)S(1)}, u32[]{:S(2)}, u32[]{:S(2)}) %collective-permute-start.16) | collective-permute-done | bytes 96 | tf_op jit(solution)/shard_map/ppermute | solution.py:14
  90.6 0.5 multiply_sqrt_fusion
  (64 shorter events, 0.8 us)
Async XLA Ops:
  0.6 5.0 %copy-start = (f32[32,128]{1,0:T(8,128)S(1)}, f32[32,128]{1,0:T(8,128)}, u32[]{:S(2)}) copy-start(f32[32,128]{1,0:T(8,128)} %param.20) | copy-start | bytes 49156
  0.6 5.0 %copy-start.6 = (s32[16]{0:T(128)S(1)}, s32[16]{0:T(128)}, u32[]{:S(2)}) copy-start(s32[16]{0:T(128)} %param.21) | copy-start | bytes 196
  0.7 5.1 %copy-start.4 = (f32[2,128]{1,0:T(2,128)S(1)}, f32[2,128]{1,0:T(2,128)}, u32[]{:S(2)}) copy-start(f32[2,128]{1,0:T(2,128)} %param.16) | copy-start | bytes 3076
  0.7 9.6 %copy-start.8 = (s32[48]{0:T(128)S(1)}, s32[48]{0:T(128)}, u32[]{:S(2)}) copy-start(s32[48]{0:T(128)} %param.13) | copy-start | bytes 580
  0.7 9.6 %copy-start.7 = (s32[48]{0:T(128)S(1)}, s32[48]{0:T(128)}, u32[]{:S(2)}) copy-start(s32[48]{0:T(128)} %param.12) | copy-start | bytes 580
  7.3 9.9 %collective-permute-start = (f32[18]{0:T(128)S(1)}, f32[18]{0:T(128)S(1)}, u32[]{:S(2)}, u32[]{:S(2)}) collective-permute-start(f32[18]{0:T(128)S(1)} %pad_maximum_fusion.3), channel_id=1, source_target_pairs={{0,8},{8,0},{16,24},{24,16},{1,9},{9,1},{17,25},{25,17},{2,10},{10... | collective-permute-start | bytes 224 | tf_op jit(solution)/shard_map/ppermute | solution.py:14
  10.4 5.6 %copy-start.1 = (f32[2,16,128]{2,1,0:T(8,128)S(1)}, f32[2,16,128]{2,1,0:T(8,128)}, u32[]{:S(2)}) copy-start(f32[2,16,128]{2,1,0:T(8,128)} %param.19) | copy-start | bytes 49156
  15.9 1.1 %copy-start.2 = (f32[2,16,128]{2,1,0:T(8,128)S(1)}, f32[2,16,128]{2,1,0:T(8,128)}, u32[]{:S(2)}) copy-start(f32[2,16,128]{2,1,0:T(8,128)} %param.18) | copy-start | bytes 49156
  16.0 1.1 %copy-start.5 = (f32[2,128]{1,0:T(2,128)S(1)}, f32[2,128]{1,0:T(2,128)}, u32[]{:S(2)}) copy-start(f32[2,128]{1,0:T(2,128)} %param.17) | copy-start | bytes 3076
  17.0 32.7 %copy-start.3 = (f32[2,128]{1,0:T(2,128)S(1)}, f32[2,128]{1,0:T(2,128)}, u32[]{:S(2)}) copy-start(f32[2,128]{1,0:T(2,128)} %param.15) | copy-start | bytes 3076
  20.6 3.5 %collective-permute-start.1 = (f32[18]{0:T(128)S(1)}, f32[18]{0:T(128)S(1)}, u32[]{:S(2)}, u32[]{:S(2)}) collective-permute-start(f32[18]{0:T(128)S(1)} %pad_maximum_fusion.4), channel_id=1, source_target_pairs={{0,16},{8,24},{16,0},{24,8},{1,17},{9,25},{17,1},{25,9},{2,18},{10... | collective-permute-start | bytes 224 | tf_op jit(solution)/shard_map/ppermute | solution.py:14
  26.2 1.3 %collective-permute-start.2 = (f32[22528]{0:T(1024)S(1)}, f32[22528]{0:T(1024)S(1)}, u32[]{:S(2)}, u32[]{:S(2)}) collective-permute-start(f32[22528]{0:T(1024)S(1)} %concatenate.48), channel_id=1, source_target_pairs={{0,1},{1,0},{2,3},{3,2},{4,5},{5,4},{6,7},{7,6},{8,9},{9,8},{10,11... | collective-permute-start | bytes 270344 | tf_op jit(solution)/shard_map/ppermute | solution.py:14
  29.6 5.1 %collective-permute-start.3 = (f32[27648]{0:T(1024)S(1)}, f32[27648]{0:T(1024)S(1)}, u32[]{:S(2)}, u32[]{:S(2)}) collective-permute-start(f32[27648]{0:T(1024)S(1)} %concatenate.49), channel_id=1, source_target_pairs={{0,2},{1,3},{2,0},{3,1},{4,6},{5,7},{6,4},{7,5},{8,10},{9,11},{10,... | collective-permute-start | bytes 331784 | tf_op jit(solution)/shard_map/ppermute | solution.py:14
  36.8 9.3 %collective-permute-start.4 = (f32[37888]{0:T(1024)S(1)}, f32[37888]{0:T(1024)S(1)}, u32[]{:S(2)}, u32[]{:S(2)}) collective-permute-start(f32[37888]{0:T(1024)S(1)} %concatenate.50), channel_id=1, source_target_pairs={{0,4},{1,5},{2,6},{3,7},{4,0},{5,1},{6,2},{7,3},{8,12},{9,13},{10,... | collective-permute-start | bytes 454664 | tf_op jit(solution)/shard_map/ppermute | solution.py:14
  48.2 1.3 %collective-permute-start.5 = (f32[8,16,128]{2,1,0:T(8,128)S(1)}, f32[8,16,128]{2,1,0:T(8,128)S(1)}, u32[]{:S(2)}, u32[]{:S(2)}) collective-permute-start(f32[8,16,128]{2,1,0:T(8,128)S(1)} %add.203), channel_id=1, source_target_pairs={{0,1},{1,0},{2,3},{3,2},{4,5},{5,4},{6,7},{7,6},{8,9},{9,8},{10,11... | collective-permute-start | bytes 196616 | tf_op jit(solution)/shard_map/ppermute | solution.py:14
  51.3 3.5 %collective-permute-start.6 = (f32[32]{0:T(128)S(1)}, f32[32]{0:T(128)S(1)}, u32[]{:S(2)}, u32[]{:S(2)}) collective-permute-start(f32[32]{0:T(128)S(1)} %pad_maximum_fusion.5), channel_id=1, source_target_pairs={{0,8},{8,0},{16,24},{24,16},{1,9},{9,1},{17,25},{25,17},{2,10},{10... | collective-permute-start | bytes 392 | tf_op jit(solution)/shard_map/ppermute | solution.py:14
  55.0 3.5 %collective-permute-start.7 = (f32[32]{0:T(128)S(1)}, f32[32]{0:T(128)S(1)}, u32[]{:S(2)}, u32[]{:S(2)}) collective-permute-start(f32[32]{0:T(128)S(1)} %pad_maximum_fusion.6), channel_id=1, source_target_pairs={{0,16},{8,24},{16,0},{24,8},{1,17},{9,25},{17,1},{25,9},{2,18},{10... | collective-permute-start | bytes 392 | tf_op jit(solution)/shard_map/ppermute | solution.py:14
  58.6 1.3 %collective-permute-start.8 = (f32[16400]{0:T(1024)S(1)}, f32[16400]{0:T(1024)S(1)}, u32[]{:S(2)}, u32[]{:S(2)}) collective-permute-start(f32[16400]{0:T(1024)S(1)} %pad_maximum_fusion), channel_id=1, source_target_pairs={{0,1},{1,0},{2,3},{3,2},{4,5},{5,4},{6,7},{7,6},{8,9},{9,8},{10,11... | collective-permute-start | bytes 196808 | tf_op jit(solution)/shard_map/ppermute | solution.py:14
  60.0 4.4 %collective-permute-start.9 = (f32[16400]{0:T(1024)S(1)}, f32[16400]{0:T(1024)S(1)}, u32[]{:S(2)}, u32[]{:S(2)}) collective-permute-start(f32[16400]{0:T(1024)S(1)} %pad_maximum_fusion.1), channel_id=1, source_target_pairs={{0,2},{1,3},{2,0},{3,1},{4,6},{5,7},{6,4},{7,5},{8,10},{9,11},{10,... | collective-permute-start | bytes 196808 | tf_op jit(solution)/shard_map/ppermute | solution.py:14
  64.4 6.0 %collective-permute-start.10 = (f32[16400]{0:T(1024)S(1)}, f32[16400]{0:T(1024)S(1)}, u32[]{:S(2)}, u32[]{:S(2)}) collective-permute-start(f32[16400]{0:T(1024)S(1)} %pad_maximum_fusion.2), channel_id=1, source_target_pairs={{0,4},{1,5},{2,6},{3,7},{4,0},{5,1},{6,2},{7,3},{8,12},{9,13},{10,... | collective-permute-start | bytes 196808 | tf_op jit(solution)/shard_map/ppermute | solution.py:14
  70.4 1.3 %collective-permute-start.11 = (f32[8,16,128]{2,1,0:T(8,128)S(1)}, f32[8,16,128]{2,1,0:T(8,128)S(1)}, u32[]{:S(2)}, u32[]{:S(2)}) collective-permute-start(f32[8,16,128]{2,1,0:T(8,128)S(1)} %fusion.66), channel_id=1, source_target_pairs={{0,1},{1,0},{2,3},{3,2},{4,5},{5,4},{6,7},{7,6},{8,9},{9,8},{10,11... | collective-permute-start | bytes 196616 | tf_op jit(solution)/shard_map/ppermute | solution.py:14
  74.2 3.5 %collective-permute-start.12 = (f32[32]{0:T(128)S(1)}, f32[32]{0:T(128)S(1)}, u32[]{:S(2)}, u32[]{:S(2)}) collective-permute-start(f32[32]{0:T(128)S(1)} %pad_maximum_fusion.7), channel_id=1, source_target_pairs={{0,8},{8,0},{16,24},{24,16},{1,9},{9,1},{17,25},{25,17},{2,10},{10... | collective-permute-start | bytes 392 | tf_op jit(solution)/shard_map/ppermute | solution.py:14
  77.9 3.5 %collective-permute-start.13 = (f32[32]{0:T(128)S(1)}, f32[32]{0:T(128)S(1)}, u32[]{:S(2)}, u32[]{:S(2)}) collective-permute-start(f32[32]{0:T(128)S(1)} %pad_maximum_fusion.8), channel_id=1, source_target_pairs={{0,16},{8,24},{16,0},{24,8},{1,17},{9,25},{17,1},{25,9},{2,18},{10... | collective-permute-start | bytes 392 | tf_op jit(solution)/shard_map/ppermute | solution.py:14
  81.5 1.1 %collective-permute-start.14 = (f32[16]{0:T(128)S(1)}, f32[16]{0:T(128)S(1)}, u32[]{:S(2)}, u32[]{:S(2)}) collective-permute-start(f32[16]{0:T(128)S(1)} %slice_add_fusion.6), channel_id=1, source_target_pairs={{0,1},{1,0},{2,3},{3,2},{4,5},{5,4},{6,7},{7,6},{8,9},{9,8},{10,11... | collective-permute-start | bytes 200 | tf_op jit(solution)/shard_map/ppermute | solution.py:14
  82.6 3.5 %collective-permute-start.15 = (f32[16]{0:T(128)S(1)}, f32[16]{0:T(128)S(1)}, u32[]{:S(2)}, u32[]{:S(2)}) collective-permute-start(f32[16]{0:T(128)S(1)} %add.227), channel_id=1, source_target_pairs={{0,2},{1,3},{2,0},{3,1},{4,6},{5,7},{6,4},{7,5},{8,10},{9,11},{10,... | collective-permute-start | bytes 200 | tf_op jit(solution)/shard_map/ppermute | solution.py:14
  86.1 4.4 %collective-permute-start.16 = (f32[16]{0:T(128)S(1)}, f32[16]{0:T(128)S(1)}, u32[]{:S(2)}, u32[]{:S(2)}) collective-permute-start(f32[16]{0:T(128)S(1)} %add.228), channel_id=1, source_target_pairs={{0,4},{1,5},{2,6},{3,7},{4,0},{5,1},{6,2},{7,3},{8,12},{9,13},{10,... | collective-permute-start | bytes 200 | tf_op jit(solution)/shard_map/ppermute | solution.py:14

commit v12 on v11

--- a/solution.py
+++ b/solution.py
@@ -138,9 +138,8 @@
         axis=0,
     )
     partial_value = transposed_product(dual)
-    grad, (sq_a, sq_c, sq_b), gathered = _rounds(
-        "col", [local_a, local_c, local_b], own, split=partial_value
-    )
+    _, (sq_a, sq_c, sq_b), _ = _rounds("col", [local_a, local_c, local_b])
+    grad, _, gathered = _rounds("col", [], own, split=partial_value)
     primal_reg = gathered[:, : own_blocks * scenarios].reshape(region_blocks, scenarios, lanes)
     base_reg = gathered[:, own_blocks * scenarios : own_blocks * (scenarios + 1)]
     upper_reg = gathered[:, own_blocks * (scenarios + 1) : own_rows]
@@ -151,8 +150,9 @@
     for step in range(ITERS):
         if step > 0:
             _, (step_x, part_y), _ = _rounds("region", [local_x, local_y])
+            _, (step_y,), _ = _rounds("col", [part_y])
             partial_value = transposed_product(dual)
-            grad, (step_y,), _ = _rounds("col", [part_y], split=partial_value)
+            grad, _, _ = _rounds("col", [], split=partial_value)
             weight = jnp.sqrt(weight * jnp.sqrt((step_x + 1e-06) / (step_y + 1e-06)))
         tau = (eta / weight)[None, :, None]
         sigma = (eta * weight)[None, :, None]

time: 91.5 us -> 93 us (1.016)
  starting transfers between devices: 18.4 us -> 23.1 us
  waiting for transfers between devices: 39.5 us -> 36.3 us
    ppermute x17 -> x23, starting transfers between devices: 18.4 us -> 23.1 us  [_exchange(): return lax.ppermute(x, axis, [(i, i ^ 1 << bit) for i in range(n)])]
    ppermute x17 -> x23, waiting for transfers between devices: 39.5 us -> 36.3 us  [_exchange(): return lax.ppermute(x, axis, [(i, i ^ 1 << bit) for i in range(n)])]
    concatenate x9 -> x12, other arithmetic: 1.79 us -> 2.03 us  [_rounds(): flat = jnp.concatenate(parts) if len(parts) > 1 else parts[0]]
  transfers between devices with their start and end apart: 17 -> 23, of which waited for: 16 -> 19; matrix products, arithmetic and copies ran while one was open for 9% -> 13% of each run, Pallas kernels for 0% -> 0%
where the time goes in v12:
time: 93 us; the launch traced here: 92.6 us
  waiting for transfers between devices  36.3 us (39%)
  starting transfers between devices  23.1 us (25%)
  matrix products  11.5 us (12%)
  between operations  9.63 us (10%)
  other arithmetic  8.21 us (9%)
  local copies, waits for them, and re-layouts  3.79 us (4%)
    ppermute x23, waiting for transfers between devices, _exchange(): return lax.ppermute(x, axis, [(i, i ^ 1 << bit) for i in range(n)])  36.3 us
    ppermute x23, starting transfers between devices, _exchange(): return lax.ppermute(x, axis, [(i, i ^ 1 << bit) for i in range(n)])  23.1 us
    dot_general x1, matrix products, local(): dense = jnp.dot(place_live, tiles.reshape(ntiles, -1), precision=hp)  5.57 us
    dot_general x2, matrix products, product_of(): jnp.einsum('ricj,csj->rsi', dense, point, precision=lax.Precision.HIGH)  3.64 us
    reduce_sum x2, other arithmetic, local(): local_a = jnp.sum(jnp.sum(tiles * tiles, axis=(1, 2)) * live)  2.94 us
    slice x5, local copies, waits for them, and re-layouts, _rounds(): new_sums.append(s + got[off:off + size].reshape(shape))  2.93 us
    dot_general x2, matrix products, transposed_product(): jnp.einsum('rsi,ricj->csj', dual, dense, precision=lax.Precision.HIGH)  2.13 us
    concatenate x12, other arithmetic, _rounds(): flat = jnp.concatenate(parts) if len(parts) > 1 else parts[0]  2.03 us
  transfers between devices with their start and end apart: 23, of which 19 were waited for; matrix products, arithmetic and copies ran while one was open for 13% of the time, Pallas kernels for 0%

profile of v12, /device:TPU:0, one launch (start us, length us, event | category | flops | bytes accessed | tf_op | source)
XLA Modules:
  0.0 92.6 jit_solution(12531987671632216293)
XLA Ops:
  1.4 1.3 %multiply_reduce_fusion.6 = f32[]{:T(128)} fusion(f32[2,128]{1,0:T(2,128)} %param.15), kind=kLoop, calls=%fused_computation.95 | loop fusion | flops 511 | bytes 1028 | tf_op jit(solution)/shard_map/reduce_sum | solution.py:110
  2.7 2.3 %multiply_reduce_fusion = f32[48]{0:T(128)S(1)} fusion(f32[48,128,128]{2,1,0:T(8,128)} %param.11), kind=kLoop, calls=%fused_computation.4 | loop fusion | flops 1572816 | bytes 3145920 | tf_op jit(solution)/shard_map/reduce_sum | solution.py:108
  5.0 0.6 fusion.83
  5.6 0.2 fusion.81
  5.8 0.1 multiply_reduce_fusion.5
  5.9 1.4 %pad_maximum_fusion.3 = f32[18]{0:T(128)S(1)} fusion(f32[1]{0:T(128)} %bitcast.30, f32[16]{0:T(128)S(1)} %multiply_reduce_fusion.5, f32[1]{0:T(128)} %bitcast.29), kind=kLoop, calls=%fused_computation.98 | loop fusion | flops 36 | bytes 144 | tf_op jit(solution)/shard_map/concatenate | solution.py:53
  7.3 2.9 %collective-permute-start.3 = (f32[18]{0:T(128)S(1)}, f32[18]{0:T(128)S(1)}, u32[]{:S(2)}, u32[]{:S(2)}) collective-permute-start(f32[18]{0:T(128)S(1)} %pad_maximum_fusion.3), channel_id=1, source_target_pairs={{0,8},{8,0},{16,24},{24,16},{1,9},{9,1},{17,25},{25,17},{2,10},{10... | collective-permute-start | bytes 224 | tf_op jit(solution)/shard_map/ppermute | solution.py:14
  10.4 0.1 fusion.71
  10.5 5.6 %fusion.10 = f32[2,128,16,128]{3,2,1,0:T(8,128)S(1)} fusion(f32[48]{0:T(128)S(1)} %compare_convert_fusion, s32[16,2]{0,1:T(2,128)S(1)} %multiply_add_fusion, s32[48]{0:T(128)S(1)} %multiply_add_fusion.1, f32[6,8,128,128]{3,2,1,0:T(8,128)} %bitcast.140), kind=kOutput, calls=%fused_computation.13 | convolution fusion | flops 301992960 | bytes 5243392 | tf_op jit(solution)/shard_map/dot_general | solution.py:117
  16.1 1.1 %fusion.8 = f32[16,128,16,1]{1,2,3,0:T(8,128)S(1)} fusion(f32[2,128,16,128]{3,2,1,0:T(8,128)S(1)} %fusion.10, f32[2,16,128]{2,1,0:T(8,128)S(1)} %copy-done.1), kind=kOutput, calls=%fused_computation.11 | convolution fusion | flops 50331648 | bytes 2244608 | tf_op jit(solution)/shard_map/rsi,ricj->csj/dot_general | solution.py:122
  17.3 0.6 fusion.95
  20.6 0.1 pad_maximum_fusion.4
  20.7 1.5 %collective-permute-start.4 = (f32[18]{0:T(128)S(1)}, f32[18]{0:T(128)S(1)}, u32[]{:S(2)}, u32[]{:S(2)}) collective-permute-start(f32[18]{0:T(128)S(1)} %pad_maximum_fusion.4), channel_id=1, source_target_pairs={{0,16},{8,24},{16,0},{24,8},{1,17},{9,25},{17,1},{25,9},{2,18},{10... | collective-permute-start | bytes 224 | tf_op jit(solution)/shard_map/ppermute | solution.py:14
  22.2 2.0 %collective-permute-done.4 = f32[18]{0:T(128)S(1)} collective-permute-done((f32[18]{0:T(128)S(1)}, f32[18]{0:T(128)S(1)}, u32[]{:S(2)}, u32[]{:S(2)}) %collective-permute-start.4) | collective-permute-done | bytes 104 | tf_op jit(solution)/shard_map/ppermute | solution.py:14
  24.3 0.6 fusion.94
  26.2 0.1 pad_maximum_fusion.5
  26.3 1.1 %collective-permute-done.5 = f32[18]{0:T(128)S(1)} collective-permute-done((f32[18]{0:T(128)S(1)}, f32[18]{0:T(128)S(1)}, u32[]{:S(2)}, u32[]{:S(2)}) %collective-permute-start.5) | collective-permute-done | bytes 104 | tf_op jit(solution)/shard_map/ppermute | solution.py:14
  27.4 0.6 fusion.93
  29.4 0.1 pad_maximum_fusion.6
  29.5 1.6 %collective-permute-start.6 = (f32[18]{0:T(128)S(1)}, f32[18]{0:T(128)S(1)}, u32[]{:S(2)}, u32[]{:S(2)}) collective-permute-start(f32[18]{0:T(128)S(1)} %pad_maximum_fusion.6), channel_id=1, source_target_pairs={{0,2},{1,3},{2,0},{3,1},{4,6},{5,7},{6,4},{7,5},{8,10},{9,11},{10,... | collective-permute-start | bytes 224 | tf_op jit(solution)/shard_map/ppermute | solution.py:14
  31.0 2.0 %collective-permute-done.6 = f32[18]{0:T(128)S(1)} collective-permute-done((f32[18]{0:T(128)S(1)}, f32[18]{0:T(128)S(1)}, u32[]{:S(2)}, u32[]{:S(2)}) %collective-permute-start.6) | collective-permute-done | bytes 104 | tf_op jit(solution)/shard_map/ppermute | solution.py:14
  33.0 0.6 fusion.92
  35.0 0.1 pad_maximum_fusion.7
  35.0 2.6 %collective-permute-start.7 = (f32[18]{0:T(128)S(1)}, f32[18]{0:T(128)S(1)}, u32[]{:S(2)}, u32[]{:S(2)}) collective-permute-start(f32[18]{0:T(128)S(1)} %pad_maximum_fusion.7), channel_id=1, source_target_pairs={{0,4},{1,5},{2,6},{3,7},{4,0},{5,1},{6,2},{7,3},{8,12},{9,13},{10,... | collective-permute-start | bytes 224 | tf_op jit(solution)/shard_map/ppermute | solution.py:14
  37.7 1.6 %collective-permute-start.1 = (f32[26624]{0:T(1024)S(1)}, f32[26624]{0:T(1024)S(1)}, u32[]{:S(2)}, u32[]{:S(2)}) collective-permute-start(f32[26624]{0:T(1024)S(1)} %pad_maximum_fusion.1), channel_id=1, source_target_pairs={{0,2},{1,3},{2,0},{3,1},{4,6},{5,7},{6,4},{7,5},{8,10},{9,11},{10,... | collective-permute-start | bytes 319496 | tf_op jit(solution)/shard_map/ppermute | solution.py:14
  39.3 0.2 collective-permute-done.7
  39.5 0.6 fusion.91
  41.5 1.0 %collective-permute-done.1 = f32[26624]{0:T(1024)S(1)} collective-permute-done((f32[26624]{0:T(1024)S(1)}, f32[26624]{0:T(1024)S(1)}, u32[]{:S(2)}, u32[]{:S(2)}) %collective-permute-start.1) | collective-permute-done | bytes 106528 | tf_op jit(solution)/shard_map/ppermute | solution.py:14
  42.6 1.7 %collective-permute-start.2 = (f32[36864]{0:T(1024)S(1)}, f32[36864]{0:T(1024)S(1)}, u32[]{:S(2)}, u32[]{:S(2)}) collective-permute-start(f32[36864]{0:T(1024)S(1)} %pad_maximum_fusion), channel_id=1, source_target_pairs={{0,4},{1,5},{2,6},{3,7},{4,0},{5,1},{6,2},{7,3},{8,12},{9,13},{10,... | collective-permute-start | bytes 442376 | tf_op jit(solution)/shard_map/ppermute | solution.py:14
  44.2 0.1 broadcast_multiply_fusion.1
  44.3 5.9 %collective-permute-done.2 = f32[36864]{0:T(1024)S(1)} collective-permute-done((f32[36864]{0:T(1024)S(1)}, f32[36864]{0:T(1024)S(1)}, u32[]{:S(2)}, u32[]{:S(2)}) %collective-permute-start.2) | collective-permute-done | bytes 147488 | tf_op jit(solution)/shard_map/ppermute | solution.py:14
  50.4 1.2 %collective-permute-done.8 = f32[8,16,128]{2,1,0:T(8,128)S(1)} collective-permute-done((f32[8,16,128]{2,1,0:T(8,128)S(1)}, f32[8,16,128]{2,1,0:T(8,128)S(1)}, u32[]{:S(2)}, u32[]{:S(2)}) %collective-permute-start.8) | collective-permute-done | bytes 65568 | tf_op jit(solution)/shard_map/ppermute | solution.py:14
  51.6 0.2 multiply_reduce_fusion.2
  51.8 1.5 %multiply_reduce_fusion.4 = (f32[16]{0:T(128)S(1)}, f32[2,16,128]{2,1,0:T(8,128)S(1)}) fusion(f32[2,16,128]{2,1,0:T(8,128)S(1)} %copy-done.1, f32[2,128,16,128]{3,2,1,0:T(8,128)S(1)} %fusion.10, f32[16,16,128]{2,1,0:T(8,128)S(1)} %bitcast.142, f32[16,16,128]{2,1,0:T(8,128)S(1)} %get-tuple-element.8, f32[2,128]{1,0:T(2,128)S(1)} %copy-done.3, ...), kind=kOutput, calls=%fused_computation.73 | convolution fusion | flops 50425840 | bytes 2393216 | tf_op jit(solution)/shard_map/ricj,csj->rsi/dot_general | solution.py:125
  53.3 0.1 pad_maximum_fusion.8
  53.4 0.5 collective-permute-start.9
  53.9 1.1 %fusion.6 = f32[16,128,16,1]{1,2,3,0:T(8,128)S(1)} fusion(f32[2,128,16,128]{3,2,1,0:T(8,128)S(1)} %fusion.10, f32[2,16,128]{2,1,0:T(8,128)S(1)} %get-tuple-element.35), kind=kOutput, calls=%fused_computation.9 | convolution fusion | flops 50331648 | bytes 2244608 | tf_op jit(solution)/shard_map/rsi,ricj->csj/dot_general | solution.py:122
  55.1 1.8 %collective-permute-done.9 = f32[32]{0:T(128)S(1)} collective-permute-done((f32[32]{0:T(128)S(1)}, f32[32]{0:T(128)S(1)}, u32[]{:S(2)}, u32[]{:S(2)}) %collective-permute-start.9) | collective-permute-done | bytes 160 | tf_op jit(solution)/shard_map/ppermute | solution.py:14
  57.0 0.1 pad_maximum_fusion.9
  57.1 1.5 %collective-permute-start.10 = (f32[32]{0:T(128)S(1)}, f32[32]{0:T(128)S(1)}, u32[]{:S(2)}, u32[]{:S(2)}) collective-permute-start(f32[32]{0:T(128)S(1)} %pad_maximum_fusion.9), channel_id=1, source_target_pairs={{0,16},{8,24},{16,0},{24,8},{1,17},{9,25},{17,1},{25,9},{2,18},{10... | collective-permute-start | bytes 392 | tf_op jit(solution)/shard_map/ppermute | solution.py:14
  58.6 0.2 collective-permute-start.15
  58.8 1.8 %collective-permute-done.10 = f32[32]{0:T(128)S(1)} collective-permute-done((f32[32]{0:T(128)S(1)}, f32[32]{0:T(128)S(1)}, u32[]{:S(2)}, u32[]{:S(2)}) %collective-permute-start.10) | collective-permute-done | bytes 160 | tf_op jit(solution)/shard_map/ppermute | solution.py:14
  60.7 1.1 %collective-permute-done.11 = f32[16]{0:T(128)S(1)} collective-permute-done((f32[16]{0:T(128)S(1)}, f32[16]{0:T(128)S(1)}, u32[]{:S(2)}, u32[]{:S(2)}) %collective-permute-start.11) | collective-permute-done | bytes 96 | tf_op jit(solution)/shard_map/ppermute | solution.py:14
  61.8 0.1 collective-permute-start.12
  61.9 3.4 %collective-permute-done.12 = f32[16]{0:T(128)S(1)} collective-permute-done((f32[16]{0:T(128)S(1)}, f32[16]{0:T(128)S(1)}, u32[]{:S(2)}, u32[]{:S(2)}) %collective-permute-start.12) | collective-permute-done | bytes 96 | tf_op jit(solution)/shard_map/ppermute | solution.py:14
  65.4 1.2 %collective-permute-start.13 = (f32[16]{0:T(128)S(1)}, f32[16]{0:T(128)S(1)}, u32[]{:S(2)}, u32[]{:S(2)}) collective-permute-start(f32[16]{0:T(128)S(1)} %add.216), channel_id=1, source_target_pairs={{0,4},{1,5},{2,6},{3,7},{4,0},{5,1},{6,2},{7,3},{8,12},{9,13},{10,... | collective-permute-start | bytes 200 | tf_op jit(solution)/shard_map/ppermute | solution.py:14
  66.6 1.8 %collective-permute-start.16 = (f32[16384]{0:T(1024)S(1)}, f32[16384]{0:T(1024)S(1)}, u32[]{:S(2)}, u32[]{:S(2)}) collective-permute-start(f32[16384]{0:T(1024)S(1)} %add.222), channel_id=1, source_target_pairs={{0,4},{1,5},{2,6},{3,7},{4,0},{5,1},{6,2},{7,3},{8,12},{9,13},{10,... | collective-permute-start | bytes 196616 | tf_op jit(solution)/shard_map/ppermute | solution.py:14
  68.4 1.4 %collective-permute-done.13 = f32[16]{0:T(128)S(1)} collective-permute-done((f32[16]{0:T(128)S(1)}, f32[16]{0:T(128)S(1)}, u32[]{:S(2)}, u32[]{:S(2)}) %collective-permute-start.13) | collective-permute-done | bytes 96 | tf_op jit(solution)/shard_map/ppermute | solution.py:14
  69.8 2.0 %collective-permute-done.16 = f32[16384]{0:T(1024)S(1)} collective-permute-done((f32[16384]{0:T(1024)S(1)}, f32[16384]{0:T(1024)S(1)}, u32[]{:S(2)}, u32[]{:S(2)}) %collective-permute-start.16) | collective-permute-done | bytes 65568 | tf_op jit(solution)/shard_map/ppermute | solution.py:14
  72.0 1.2 %collective-permute-done.17 = f32[8,16,128]{2,1,0:T(8,128)S(1)} collective-permute-done((f32[8,16,128]{2,1,0:T(8,128)S(1)}, f32[8,16,128]{2,1,0:T(8,128)S(1)}, u32[]{:S(2)}, u32[]{:S(2)}) %collective-permute-start.17) | collective-permute-done | bytes 65568 | tf_op jit(solution)/shard_map/ppermute | solution.py:14
  73.2 0.2 multiply_reduce_fusion.1
  73.4 2.1 %multiply_reduce_fusion.3 = (f32[16]{0:T(128)S(1)}, f32[2,16,128]{2,1,0:T(8,128)}) fusion(f32[2,16,128]{2,1,0:T(8,128)S(1)} %get-tuple-element.35, f32[2,128,16,128]{3,2,1,0:T(8,128)S(1)} %fusion.10, f32[16,16,128]{2,1,0:T(8,128)S(1)} %get-tuple-element.8, f32[16,16,128]{2,1,0:T(8,128)S(1)} %get-tuple-element.4, f32[2,128]{1,0:T(2,128)S(1)} %copy-done.3, ...), kind=kOutput, calls=%fused_computation.72 | convolution fusion | flops 50425840 | bytes 2393216 | tf_op jit(solution)/shard_map/ricj,csj->rsi/dot_general | solution.py:125
  75.5 0.1 pad_maximum_fusion.10
  75.6 0.5 collective-permute-start.18
  76.2 3.0 %collective-permute-done.18 = f32[32]{0:T(128)S(1)} collective-permute-done((f32[32]{0:T(128)S(1)}, f32[32]{0:T(128)S(1)}, u32[]{:S(2)}, u32[]{:S(2)}) %collective-permute-start.18) | collective-permute-done | bytes 160 | tf_op jit(solution)/shard_map/ppermute | solution.py:14
  79.3 1.4 %collective-permute-start.19 = (f32[32]{0:T(128)S(1)}, f32[32]{0:T(128)S(1)}, u32[]{:S(2)}, u32[]{:S(2)}) collective-permute-start(f32[32]{0:T(128)S(1)} %pad_maximum_fusion.11), channel_id=1, source_target_pairs={{0,16},{8,24},{16,0},{24,8},{1,17},{9,25},{17,1},{25,9},{2,18},{10... | collective-permute-start | bytes 392 | tf_op jit(solution)/shard_map/ppermute | solution.py:14
  80.8 2.1 %collective-permute-done.19 = f32[32]{0:T(128)S(1)} collective-permute-done((f32[32]{0:T(128)S(1)}, f32[32]{0:T(128)S(1)}, u32[]{:S(2)}, u32[]{:S(2)}) %collective-permute-start.19) | collective-permute-done | bytes 160 | tf_op jit(solution)/shard_map/ppermute | solution.py:14
  82.9 1.1 %collective-permute-done.20 = f32[16]{0:T(128)S(1)} collective-permute-done((f32[16]{0:T(128)S(1)}, f32[16]{0:T(128)S(1)}, u32[]{:S(2)}, u32[]{:S(2)}) %collective-permute-start.20) | collective-permute-done | bytes 96 | tf_op jit(solution)/shard_map/ppermute | solution.py:14
  84.1 1.9 %collective-permute-start.21 = (f32[16]{0:T(128)S(1)}, f32[16]{0:T(128)S(1)}, u32[]{:S(2)}, u32[]{:S(2)}) collective-permute-start(f32[16]{0:T(128)S(1)} %add.231), channel_id=1, source_target_pairs={{0,2},{1,3},{2,0},{3,1},{4,6},{5,7},{6,4},{7,5},{8,10},{9,11},{10,... | collective-permute-start | bytes 200 | tf_op jit(solution)/shard_map/ppermute | solution.py:14
  86.0 1.6 %collective-permute-done.21 = f32[16]{0:T(128)S(1)} collective-permute-done((f32[16]{0:T(128)S(1)}, f32[16]{0:T(128)S(1)}, u32[]{:S(2)}, u32[]{:S(2)}) %collective-permute-start.21) | collective-permute-done | bytes 96 | tf_op jit(solution)/shard_map/ppermute | solution.py:14
  87.6 1.7 %collective-permute-start.22 = (f32[16]{0:T(128)S(1)}, f32[16]{0:T(128)S(1)}, u32[]{:S(2)}, u32[]{:S(2)}) collective-permute-start(f32[16]{0:T(128)S(1)} %add.232), channel_id=1, source_target_pairs={{0,4},{1,5},{2,6},{3,7},{4,0},{5,1},{6,2},{7,3},{8,12},{9,13},{10,... | collective-permute-start | bytes 200 | tf_op jit(solution)/shard_map/ppermute | solution.py:14
  89.3 0.6 constant_dynamic-slice_fusion
  89.9 2.1 %collective-permute-done.22 = f32[16]{0:T(128)S(1)} collective-permute-done((f32[16]{0:T(128)S(1)}, f32[16]{0:T(128)S(1)}, u32[]{:S(2)}, u32[]{:S(2)}) %collective-permute-start.22) | collective-permute-done | bytes 96 | tf_op jit(solution)/shard_map/ppermute | solution.py:14
  92.0 0.5 multiply_sqrt_fusion
  (73 shorter events, 1.4 us)
Async XLA Ops:
  0.6 5.0 %copy-start = (f32[32,128]{1,0:T(8,128)S(1)}, f32[32,128]{1,0:T(8,128)}, u32[]{:S(2)}) copy-start(f32[32,128]{1,0:T(8,128)} %param.20) | copy-start | bytes 49156
  0.6 5.0 %copy-start.6 = (s32[16]{0:T(128)S(1)}, s32[16]{0:T(128)}, u32[]{:S(2)}) copy-start(s32[16]{0:T(128)} %param.21) | copy-start | bytes 196
  0.7 5.2 %copy-start.4 = (f32[2,128]{1,0:T(2,128)S(1)}, f32[2,128]{1,0:T(2,128)}, u32[]{:S(2)}) copy-start(f32[2,128]{1,0:T(2,128)} %param.16) | copy-start | bytes 3076
  0.7 9.6 %copy-start.8 = (s32[48]{0:T(128)S(1)}, s32[48]{0:T(128)}, u32[]{:S(2)}) copy-start(s32[48]{0:T(128)} %param.13) | copy-start | bytes 580
  0.7 9.6 %copy-start.7 = (s32[48]{0:T(128)S(1)}, s32[48]{0:T(128)}, u32[]{:S(2)}) copy-start(s32[48]{0:T(128)} %param.12) | copy-start | bytes 580
  0.7 9.7 %copy-start.2 = (f32[2,16,128]{2,1,0:T(8,128)S(1)}, f32[2,16,128]{2,1,0:T(8,128)}, u32[]{:S(2)}) copy-start(f32[2,16,128]{2,1,0:T(8,128)} %param.18) | copy-start | bytes 49156
  0.7 9.7 %copy-start.5 = (f32[2,128]{1,0:T(2,128)S(1)}, f32[2,128]{1,0:T(2,128)}, u32[]{:S(2)}) copy-start(f32[2,128]{1,0:T(2,128)} %param.17) | copy-start | bytes 3076
  7.3 10.0 %collective-permute-start.3 = (f32[18]{0:T(128)S(1)}, f32[18]{0:T(128)S(1)}, u32[]{:S(2)}, u32[]{:S(2)}) collective-permute-start(f32[18]{0:T(128)S(1)} %pad_maximum_fusion.3), channel_id=1, source_target_pairs={{0,8},{8,0},{16,24},{24,16},{1,9},{9,1},{17,25},{25,17},{2,10},{10... | collective-permute-start | bytes 224 | tf_op jit(solution)/shard_map/ppermute | solution.py:14
  10.5 5.6 %copy-start.1 = (f32[2,16,128]{2,1,0:T(8,128)S(1)}, f32[2,16,128]{2,1,0:T(8,128)}, u32[]{:S(2)}) copy-start(f32[2,16,128]{2,1,0:T(8,128)} %param.19) | copy-start | bytes 49156
  17.2 34.6 %copy-start.3 = (f32[2,128]{1,0:T(2,128)S(1)}, f32[2,128]{1,0:T(2,128)}, u32[]{:S(2)}) copy-start(f32[2,128]{1,0:T(2,128)} %param.15) | copy-start | bytes 3076
  17.2 20.4 %collective-permute-start = (f32[21504]{0:T(1024)S(1)}, f32[21504]{0:T(1024)S(1)}, u32[]{:S(2)}, u32[]{:S(2)}) collective-permute-start(f32[21504]{0:T(1024)S(1)} %pad_maximum_fusion.2), channel_id=1, source_target_pairs={{0,1},{1,0},{2,3},{3,2},{4,5},{5,4},{6,7},{7,6},{8,9},{9,8},{10,11... | collective-permute-start | bytes 258056 | tf_op jit(solution)/shard_map/ppermute | solution.py:14
  20.7 3.5 %collective-permute-start.4 = (f32[18]{0:T(128)S(1)}, f32[18]{0:T(128)S(1)}, u32[]{:S(2)}, u32[]{:S(2)}) collective-permute-start(f32[18]{0:T(128)S(1)} %pad_maximum_fusion.4), channel_id=1, source_target_pairs={{0,16},{8,24},{16,0},{24,8},{1,17},{9,25},{17,1},{25,9},{2,18},{10... | collective-permute-start | bytes 224 | tf_op jit(solution)/shard_map/ppermute | solution.py:14
  26.3 1.1 %collective-permute-start.5 = (f32[18]{0:T(128)S(1)}, f32[18]{0:T(128)S(1)}, u32[]{:S(2)}, u32[]{:S(2)}) collective-permute-start(f32[18]{0:T(128)S(1)} %pad_maximum_fusion.5), channel_id=1, source_target_pairs={{0,1},{1,0},{2,3},{3,2},{4,5},{5,4},{6,7},{7,6},{8,9},{9,8},{10,11... | collective-permute-start | bytes 224 | tf_op jit(solution)/shard_map/ppermute | solution.py:14
  29.5 3.5 %collective-permute-start.6 = (f32[18]{0:T(128)S(1)}, f32[18]{0:T(128)S(1)}, u32[]{:S(2)}, u32[]{:S(2)}) collective-permute-start(f32[18]{0:T(128)S(1)} %pad_maximum_fusion.6), channel_id=1, source_target_pairs={{0,2},{1,3},{2,0},{3,1},{4,6},{5,7},{6,4},{7,5},{8,10},{9,11},{10,... | collective-permute-start | bytes 224 | tf_op jit(solution)/shard_map/ppermute | solution.py:14
  35.0 4.4 %collective-permute-start.7 = (f32[18]{0:T(128)S(1)}, f32[18]{0:T(128)S(1)}, u32[]{:S(2)}, u32[]{:S(2)}) collective-permute-start(f32[18]{0:T(128)S(1)} %pad_maximum_fusion.7), channel_id=1, source_target_pairs={{0,4},{1,5},{2,6},{3,7},{4,0},{5,1},{6,2},{7,3},{8,12},{9,13},{10,... | collective-permute-start | bytes 224 | tf_op jit(solution)/shard_map/ppermute | solution.py:14
  37.7 4.8 %collective-permute-start.1 = (f32[26624]{0:T(1024)S(1)}, f32[26624]{0:T(1024)S(1)}, u32[]{:S(2)}, u32[]{:S(2)}) collective-permute-start(f32[26624]{0:T(1024)S(1)} %pad_maximum_fusion.1), channel_id=1, source_target_pairs={{0,2},{1,3},{2,0},{3,1},{4,6},{5,7},{6,4},{7,5},{8,10},{9,11},{10,... | collective-permute-start | bytes 319496 | tf_op jit(solution)/shard_map/ppermute | solution.py:14
  42.6 7.7 %collective-permute-start.2 = (f32[36864]{0:T(1024)S(1)}, f32[36864]{0:T(1024)S(1)}, u32[]{:S(2)}, u32[]{:S(2)}) collective-permute-start(f32[36864]{0:T(1024)S(1)} %pad_maximum_fusion), channel_id=1, source_target_pairs={{0,4},{1,5},{2,6},{3,7},{4,0},{5,1},{6,2},{7,3},{8,12},{9,13},{10,... | collective-permute-start | bytes 442376 | tf_op jit(solution)/shard_map/ppermute | solution.py:14
  50.3 1.3 %collective-permute-start.8 = (f32[8,16,128]{2,1,0:T(8,128)S(1)}, f32[8,16,128]{2,1,0:T(8,128)S(1)}, u32[]{:S(2)}, u32[]{:S(2)}) collective-permute-start(f32[8,16,128]{2,1,0:T(8,128)S(1)} %add.207), channel_id=1, source_target_pairs={{0,1},{1,0},{2,3},{3,2},{4,5},{5,4},{6,7},{7,6},{8,9},{9,8},{10,11... | collective-permute-start | bytes 196616 | tf_op jit(solution)/shard_map/ppermute | solution.py:14
  53.4 3.5 %collective-permute-start.9 = (f32[32]{0:T(128)S(1)}, f32[32]{0:T(128)S(1)}, u32[]{:S(2)}, u32[]{:S(2)}) collective-permute-start(f32[32]{0:T(128)S(1)} %pad_maximum_fusion.8), channel_id=1, source_target_pairs={{0,8},{8,0},{16,24},{24,16},{1,9},{9,1},{17,25},{25,17},{2,10},{10... | collective-permute-start | bytes 392 | tf_op jit(solution)/shard_map/ppermute | solution.py:14
  55.0 3.6 %collective-permute-start.14 = (f32[16384]{0:T(1024)S(1)}, f32[16384]{0:T(1024)S(1)}, u32[]{:S(2)}, u32[]{:S(2)}) collective-permute-start(f32[16384]{0:T(1024)S(1)} %bitcast.163), channel_id=1, source_target_pairs={{0,1},{1,0},{2,3},{3,2},{4,5},{5,4},{6,7},{7,6},{8,9},{9,8},{10,11... | collective-permute-start | bytes 196616 | tf_op jit(solution)/shard_map/ppermute | solution.py:14
  57.1 3.5 %collective-permute-start.10 = (f32[32]{0:T(128)S(1)}, f32[32]{0:T(128)S(1)}, u32[]{:S(2)}, u32[]{:S(2)}) collective-permute-start(f32[32]{0:T(128)S(1)} %pad_maximum_fusion.9), channel_id=1, source_target_pairs={{0,16},{8,24},{16,0},{24,8},{1,17},{9,25},{17,1},{25,9},{2,18},{10... | collective-permute-start | bytes 392 | tf_op jit(solution)/shard_map/ppermute | solution.py:14
  58.6 8.0 %collective-permute-start.15 = (f32[16384]{0:T(1024)S(1)}, f32[16384]{0:T(1024)S(1)}, u32[]{:S(2)}, u32[]{:S(2)}) collective-permute-start(f32[16384]{0:T(1024)S(1)} %add.220), channel_id=1, source_target_pairs={{0,2},{1,3},{2,0},{3,1},{4,6},{5,7},{6,4},{7,5},{8,10},{9,11},{10,... | collective-permute-start | bytes 196616 | tf_op jit(solution)/shard_map/ppermute | solution.py:14
  60.7 1.1 %collective-permute-start.11 = (f32[16]{0:T(128)S(1)}, f32[16]{0:T(128)S(1)}, u32[]{:S(2)}, u32[]{:S(2)}) collective-permute-start(f32[16]{0:T(128)S(1)} %slice_add_fusion.3), channel_id=1, source_target_pairs={{0,1},{1,0},{2,3},{3,2},{4,5},{5,4},{6,7},{7,6},{8,9},{9,8},{10,11... | collective-permute-start | bytes 200 | tf_op jit(solution)/shard_map/ppermute | solution.py:14
  61.8 3.5 %collective-permute-start.12 = (f32[16]{0:T(128)S(1)}, f32[16]{0:T(128)S(1)}, u32[]{:S(2)}, u32[]{:S(2)}) collective-permute-start(f32[16]{0:T(128)S(1)} %add.215), channel_id=1, source_target_pairs={{0,2},{1,3},{2,0},{3,1},{4,6},{5,7},{6,4},{7,5},{8,10},{9,11},{10,... | collective-permute-start | bytes 200 | tf_op jit(solution)/shard_map/ppermute | solution.py:14
  65.4 4.4 %collective-permute-start.13 = (f32[16]{0:T(128)S(1)}, f32[16]{0:T(128)S(1)}, u32[]{:S(2)}, u32[]{:S(2)}) collective-permute-start(f32[16]{0:T(128)S(1)} %add.216), channel_id=1, source_target_pairs={{0,4},{1,5},{2,6},{3,7},{4,0},{5,1},{6,2},{7,3},{8,12},{9,13},{10,... | collective-permute-start | bytes 200 | tf_op jit(solution)/shard_map/ppermute | solution.py:14
  66.6 5.2 %collective-permute-start.16 = (f32[16384]{0:T(1024)S(1)}, f32[16384]{0:T(1024)S(1)}, u32[]{:S(2)}, u32[]{:S(2)}) collective-permute-start(f32[16384]{0:T(1024)S(1)} %add.222), channel_id=1, source_target_pairs={{0,4},{1,5},{2,6},{3,7},{4,0},{5,1},{6,2},{7,3},{8,12},{9,13},{10,... | collective-permute-start | bytes 196616 | tf_op jit(solution)/shard_map/ppermute | solution.py:14
  71.9 1.3 %collective-permute-start.17 = (f32[8,16,128]{2,1,0:T(8,128)S(1)}, f32[8,16,128]{2,1,0:T(8,128)S(1)}, u32[]{:S(2)}, u32[]{:S(2)}) collective-permute-start(f32[8,16,128]{2,1,0:T(8,128)S(1)} %fusion.66), channel_id=1, source_target_pairs={{0,1},{1,0},{2,3},{3,2},{4,5},{5,4},{6,7},{7,6},{8,9},{9,8},{10,11... | collective-permute-start | bytes 196616 | tf_op jit(solution)/shard_map/ppermute | solution.py:14
  75.6 3.5 %collective-permute-start.18 = (f32[32]{0:T(128)S(1)}, f32[32]{0:T(128)S(1)}, u32[]{:S(2)}, u32[]{:S(2)}) collective-permute-start(f32[32]{0:T(128)S(1)} %pad_maximum_fusion.10), channel_id=1, source_target_pairs={{0,8},{8,0},{16,24},{24,16},{1,9},{9,1},{17,25},{25,17},{2,10},{10... | collective-permute-start | bytes 392 | tf_op jit(solution)/shard_map/ppermute | solution.py:14
  79.3 3.5 %collective-permute-start.19 = (f32[32]{0:T(128)S(1)}, f32[32]{0:T(128)S(1)}, u32[]{:S(2)}, u32[]{:S(2)}) collective-permute-start(f32[32]{0:T(128)S(1)} %pad_maximum_fusion.11), channel_id=1, source_target_pairs={{0,16},{8,24},{16,0},{24,8},{1,17},{9,25},{17,1},{25,9},{2,18},{10... | collective-permute-start | bytes 392 | tf_op jit(solution)/shard_map/ppermute | solution.py:14
  82.9 1.1 %collective-permute-start.20 = (f32[16]{0:T(128)S(1)}, f32[16]{0:T(128)S(1)}, u32[]{:S(2)}, u32[]{:S(2)}) collective-permute-start(f32[16]{0:T(128)S(1)} %slice_add_fusion), channel_id=1, source_target_pairs={{0,1},{1,0},{2,3},{3,2},{4,5},{5,4},{6,7},{7,6},{8,9},{9,8},{10,11... | collective-permute-start | bytes 200 | tf_op jit(solution)/shard_map/ppermute | solution.py:14
  84.1 3.5 %collective-permute-start.21 = (f32[16]{0:T(128)S(1)}, f32[16]{0:T(128)S(1)}, u32[]{:S(2)}, u32[]{:S(2)}) collective-permute-start(f32[16]{0:T(128)S(1)} %add.231), channel_id=1, source_target_pairs={{0,2},{1,3},{2,0},{3,1},{4,6},{5,7},{6,4},{7,5},{8,10},{9,11},{10,... | collective-permute-start | bytes 200 | tf_op jit(solution)/shard_map/ppermute | solution.py:14
  87.6 4.4 %collective-permute-start.22 = (f32[16]{0:T(128)S(1)}, f32[16]{0:T(128)S(1)}, u32[]{:S(2)}, u32[]{:S(2)}) collective-permute-start(f32[16]{0:T(128)S(1)} %add.232), channel_id=1, source_target_pairs={{0,4},{1,5},{2,6},{3,7},{4,0},{5,1},{6,2},{7,3},{8,12},{9,13},{10,... | collective-permute-start | bytes 200 | tf_op jit(solution)/shard_map/ppermute | solution.py:14

commit v13 on v11

--- a/solution.py
+++ b/solution.py
@@ -105,7 +105,7 @@
     ).astype(jnp.float32)
     factor = jnp.dot(choose, price_levels, precision=hp)
     cost = base_cost[:, None, :] * factor[None, :, :]
-    local_a = jnp.sum(jnp.sum(tiles * tiles, axis=(1, 2)) * live)
+    local_a = jnp.sum(jnp.sum(tiles * tiles * live[:, None, None], axis=(0, 1)))
     local_c = jnp.sum(cost * cost, axis=(0, 2))
     local_b = jnp.sum(rhs * rhs)
     width = scenarios * lanes

time: 91.5 us -> 91.8 us (level)
    reduce_sum x2 -> x1, other arithmetic: 2.94 us -> 3.37 us  [local(): local_a = jnp.sum(jnp.sum(tiles * tiles * live[:, None, None], axis=(0, 1)))]
where the time goes in v13:
time: 91.8 us; the launch traced here: 91.5 us
  waiting for transfers between devices  39.4 us (43%)
  starting transfers between devices  18.5 us (20%)
  matrix products  11.5 us (13%)
  between operations  9.56 us (10%)
  other arithmetic  8.41 us (9%)
  local copies, waits for them, and re-layouts  4.06 us (4%)
    ppermute x17, waiting for transfers between devices, _exchange(): return lax.ppermute(x, axis, [(i, i ^ 1 << bit) for i in range(n)])  39.4 us
    ppermute x17, starting transfers between devices, _exchange(): return lax.ppermute(x, axis, [(i, i ^ 1 << bit) for i in range(n)])  18.5 us
    dot_general x1, matrix products, local(): dense = jnp.dot(place_live, tiles.reshape(ntiles, -1), precision=hp)  5.56 us
    dot_general x2, matrix products, product_of(): jnp.einsum('ricj,csj->rsi', dense, point, precision=lax.Precision.HIGH)  3.64 us
    reduce_sum x1, other arithmetic, local(): local_a = jnp.sum(jnp.sum(tiles * tiles * live[:, None, None], axis=(0, 1)))  3.37 us
    slice x5, local copies, waits for them, and re-layouts, _rounds(): new_sums.append(s + got[off:off + size].reshape(shape))  2.91 us
    dot_general x2, matrix products, transposed_product(): jnp.einsum('rsi,ricj->csj', dual, dense, precision=lax.Precision.HIGH)  2.13 us
  transfers between devices with their start and end apart: 17, of which 16 were waited for; matrix products, arithmetic and copies ran while one was open for 9% of the time, Pallas kernels for 0%

profile of v13, /device:TPU:0, one launch (start us, length us, event | category | flops | bytes accessed | tf_op | source)
XLA Modules:
  0.0 91.5 jit_solution(17470887158205259023)
XLA Ops:
  1.4 1.3 %multiply_reduce_fusion.6 = f32[]{:T(128)} fusion(f32[2,128]{1,0:T(2,128)} %param.15), kind=kLoop, calls=%fused_computation.92 | loop fusion | flops 511 | bytes 1028 | tf_op jit(solution)/shard_map/reduce_sum | solution.py:110
  2.7 3.4 %multiply_reduce_fusion = f32[]{:T(128)} fusion(f32[48,128,128]{2,1,0:T(8,128)} %param.11, f32[48]{0:T(128)S(1)} %compare_convert_fusion), kind=kLoop, calls=%fused_computation.4 | loop fusion | flops 2359295 | bytes 3145924 | tf_op jit(solution)/shard_map/reduce_sum | solution.py:108
  6.0 0.2 fusion.80
  6.2 0.1 multiply_reduce_fusion.5
  6.3 1.4 %pad_maximum_fusion.3 = f32[18]{0:T(128)S(1)} fusion(f32[1]{0:T(128)} %bitcast.15, f32[16]{0:T(128)S(1)} %multiply_reduce_fusion.5, f32[1]{0:T(128)} %bitcast.14), kind=kLoop, calls=%fused_computation.103 | loop fusion | flops 36 | bytes 144 | tf_op jit(solution)/shard_map/concatenate | solution.py:53
  7.7 2.9 %collective-permute-start = (f32[18]{0:T(128)S(1)}, f32[18]{0:T(128)S(1)}, u32[]{:S(2)}, u32[]{:S(2)}) collective-permute-start(f32[18]{0:T(128)S(1)} %pad_maximum_fusion.3), channel_id=1, source_target_pairs={{0,8},{8,0},{16,24},{24,16},{1,9},{9,1},{17,25},{25,17},{2,10},{10... | collective-permute-start | bytes 224 | tf_op jit(solution)/shard_map/ppermute | solution.py:14
  10.7 0.1 pad.29.clone
  10.8 5.6 %fusion.10 = f32[2,128,16,128]{3,2,1,0:T(8,128)S(1)} fusion(f32[48]{0:T(128)S(1)} %compare_convert_fusion, s32[16,2]{0,1:T(2,128)S(1)} %multiply_add_fusion, s32[48]{0:T(128)S(1)} %multiply_add_fusion.1, f32[6,8,128,128]{3,2,1,0:T(8,128)} %bitcast.137), kind=kOutput, calls=%fused_computation.13 | convolution fusion | flops 301992960 | bytes 5243392 | tf_op jit(solution)/shard_map/dot_general | solution.py:117
  16.4 1.1 %fusion.8 = f32[16,128,16,1]{1,2,3,0:T(8,128)S(1)} fusion(f32[2,128,16,128]{3,2,1,0:T(8,128)S(1)} %fusion.10, f32[2,16,128]{2,1,0:T(8,128)S(1)} %copy-done.1), kind=kOutput, calls=%fused_computation.11 | convolution fusion | flops 50331648 | bytes 2244608 | tf_op jit(solution)/shard_map/rsi,ricj->csj/dot_general | solution.py:122
  17.5 0.1 fusion.70
  17.6 0.6 fusion.97
  20.8 0.1 slice_add_fusion.13
  20.8 0.1 pad_maximum_fusion.4
  20.9 1.5 %collective-permute-start.1 = (f32[18]{0:T(128)S(1)}, f32[18]{0:T(128)S(1)}, u32[]{:S(2)}, u32[]{:S(2)}) collective-permute-start(f32[18]{0:T(128)S(1)} %pad_maximum_fusion.4), channel_id=1, source_target_pairs={{0,16},{8,24},{16,0},{24,8},{1,17},{9,25},{17,1},{25,9},{2,18},{10... | collective-permute-start | bytes 224 | tf_op jit(solution)/shard_map/ppermute | solution.py:14
  22.4 2.0 %collective-permute-done.1 = f32[18]{0:T(128)S(1)} collective-permute-done((f32[18]{0:T(128)S(1)}, f32[18]{0:T(128)S(1)}, u32[]{:S(2)}, u32[]{:S(2)}) %collective-permute-start.1) | collective-permute-done | bytes 104 | tf_op jit(solution)/shard_map/ppermute | solution.py:14
  24.5 0.6 fusion.96
  26.3 0.1 slice_add_fusion.12
  26.4 0.1 concatenate.48
  26.5 1.3 %collective-permute-done.2 = f32[22528]{0:T(1024)S(1)} collective-permute-done((f32[22528]{0:T(1024)S(1)}, f32[22528]{0:T(1024)S(1)}, u32[]{:S(2)}, u32[]{:S(2)}) %collective-permute-start.2) | collective-permute-done | bytes 90144 | tf_op jit(solution)/shard_map/ppermute | solution.py:14
  27.8 0.6 fusion.93
  29.8 0.1 slice_add_fusion.5
  29.8 0.1 concatenate.49
  29.9 1.6 %collective-permute-start.3 = (f32[27648]{0:T(1024)S(1)}, f32[27648]{0:T(1024)S(1)}, u32[]{:S(2)}, u32[]{:S(2)}) collective-permute-start(f32[27648]{0:T(1024)S(1)} %concatenate.49), channel_id=1, source_target_pairs={{0,2},{1,3},{2,0},{3,1},{4,6},{5,7},{6,4},{7,5},{8,10},{9,11},{10,... | collective-permute-start | bytes 331784 | tf_op jit(solution)/shard_map/ppermute | solution.py:14
  31.5 3.5 %collective-permute-done.3 = f32[27648]{0:T(1024)S(1)} collective-permute-done((f32[27648]{0:T(1024)S(1)}, f32[27648]{0:T(1024)S(1)}, u32[]{:S(2)}, u32[]{:S(2)}) %collective-permute-start.3) | collective-permute-done | bytes 110624 | tf_op jit(solution)/shard_map/ppermute | solution.py:14
  35.0 0.6 fusion.92
  37.0 0.1 slice_add_fusion.4
  37.1 0.1 concatenate.50
  37.2 2.6 %collective-permute-start.4 = (f32[37888]{0:T(1024)S(1)}, f32[37888]{0:T(1024)S(1)}, u32[]{:S(2)}, u32[]{:S(2)}) collective-permute-start(f32[37888]{0:T(1024)S(1)} %concatenate.50), channel_id=1, source_target_pairs={{0,4},{1,5},{2,6},{3,7},{4,0},{5,1},{6,2},{7,3},{8,12},{9,13},{10,... | collective-permute-start | bytes 454664 | tf_op jit(solution)/shard_map/ppermute | solution.py:14
  39.8 6.7 %collective-permute-done.4 = f32[37888]{0:T(1024)S(1)} collective-permute-done((f32[37888]{0:T(1024)S(1)}, f32[37888]{0:T(1024)S(1)}, u32[]{:S(2)}, u32[]{:S(2)}) %collective-permute-start.4) | collective-permute-done | bytes 151584 | tf_op jit(solution)/shard_map/ppermute | solution.py:14
  46.5 0.6 fusion.91
  48.6 0.1 broadcast_multiply_fusion.1
  48.7 1.1 %collective-permute-done.5 = f32[8,16,128]{2,1,0:T(8,128)S(1)} collective-permute-done((f32[8,16,128]{2,1,0:T(8,128)S(1)}, f32[8,16,128]{2,1,0:T(8,128)S(1)}, u32[]{:S(2)}, u32[]{:S(2)}) %collective-permute-start.5) | collective-permute-done | bytes 65568 | tf_op jit(solution)/shard_map/ppermute | solution.py:14
  49.9 0.2 multiply_reduce_fusion.2
  50.1 1.5 %multiply_reduce_fusion.4 = (f32[16]{0:T(128)S(1)}, f32[2,16,128]{2,1,0:T(8,128)S(1)}) fusion(f32[2,16,128]{2,1,0:T(8,128)S(1)} %copy-done.1, f32[2,128,16,128]{3,2,1,0:T(8,128)S(1)} %fusion.10, f32[16,16,128]{2,1,0:T(8,128)S(1)} %bitcast.139, f32[16,16,128]{2,1,0:T(8,128)S(1)} %get-tuple-element.8, f32[2,128]{1,0:T(2,128)S(1)} %copy-done.3, ...), kind=kOutput, calls=%fused_computation.72 | convolution fusion | flops 50425840 | bytes 2393216 | tf_op jit(solution)/shard_map/ricj,csj->rsi/dot_general | solution.py:125
  51.6 0.1 pad_maximum_fusion.5
  51.7 0.7 collective-permute-start.6
  52.4 1.1 %fusion.6 = f32[16,128,16,1]{1,2,3,0:T(8,128)S(1)} fusion(f32[2,128,16,128]{3,2,1,0:T(8,128)S(1)} %fusion.10, f32[2,16,128]{2,1,0:T(8,128)S(1)} %get-tuple-element.35), kind=kOutput, calls=%fused_computation.9 | convolution fusion | flops 50331648 | bytes 2244608 | tf_op jit(solution)/shard_map/rsi,ricj->csj/dot_general | solution.py:122
  53.4 1.8 %collective-permute-done.6 = f32[32]{0:T(128)S(1)} collective-permute-done((f32[32]{0:T(128)S(1)}, f32[32]{0:T(128)S(1)}, u32[]{:S(2)}, u32[]{:S(2)}) %collective-permute-start.6) | collective-permute-done | bytes 160 | tf_op jit(solution)/shard_map/ppermute | solution.py:14
  55.2 0.1 slice_add_fusion.11
  55.3 0.1 pad_maximum_fusion.6
  55.4 1.5 %collective-permute-start.7 = (f32[32]{0:T(128)S(1)}, f32[32]{0:T(128)S(1)}, u32[]{:S(2)}, u32[]{:S(2)}) collective-permute-start(f32[32]{0:T(128)S(1)} %pad_maximum_fusion.6), channel_id=1, source_target_pairs={{0,16},{8,24},{16,0},{24,8},{1,17},{9,25},{17,1},{25,9},{2,18},{10... | collective-permute-start | bytes 392 | tf_op jit(solution)/shard_map/ppermute | solution.py:14
  56.9 2.0 %collective-permute-done.7 = f32[32]{0:T(128)S(1)} collective-permute-done((f32[32]{0:T(128)S(1)}, f32[32]{0:T(128)S(1)}, u32[]{:S(2)}, u32[]{:S(2)}) %collective-permute-start.7) | collective-permute-done | bytes 160 | tf_op jit(solution)/shard_map/ppermute | solution.py:14
  58.9 0.1 slice_add_fusion.9
  59.0 1.2 %collective-permute-done.8 = f32[16400]{0:T(1024)S(1)} collective-permute-done((f32[16400]{0:T(1024)S(1)}, f32[16400]{0:T(1024)S(1)}, u32[]{:S(2)}, u32[]{:S(2)}) %collective-permute-start.8) | collective-permute-done | bytes 65632 | tf_op jit(solution)/shard_map/ppermute | solution.py:14
  60.3 0.7 collective-permute-start.9
  61.1 3.6 %collective-permute-done.9 = f32[16400]{0:T(1024)S(1)} collective-permute-done((f32[16400]{0:T(1024)S(1)}, f32[16400]{0:T(1024)S(1)}, u32[]{:S(2)}, u32[]{:S(2)}) %collective-permute-start.9) | collective-permute-done | bytes 65632 | tf_op jit(solution)/shard_map/ppermute | solution.py:14
  64.7 2.3 %collective-permute-start.10 = (f32[16400]{0:T(1024)S(1)}, f32[16400]{0:T(1024)S(1)}, u32[]{:S(2)}, u32[]{:S(2)}) collective-permute-start(f32[16400]{0:T(1024)S(1)} %pad_maximum_fusion.2), channel_id=1, source_target_pairs={{0,4},{1,5},{2,6},{3,7},{4,0},{5,1},{6,2},{7,3},{8,12},{9,13},{10,... | collective-permute-start | bytes 196808 | tf_op jit(solution)/shard_map/ppermute | solution.py:14
  67.0 3.7 %collective-permute-done.10 = f32[16400]{0:T(1024)S(1)} collective-permute-done((f32[16400]{0:T(1024)S(1)}, f32[16400]{0:T(1024)S(1)}, u32[]{:S(2)}, u32[]{:S(2)}) %collective-permute-start.10) | collective-permute-done | bytes 65632 | tf_op jit(solution)/shard_map/ppermute | solution.py:14
  70.9 1.2 %collective-permute-done.11 = f32[8,16,128]{2,1,0:T(8,128)S(1)} collective-permute-done((f32[8,16,128]{2,1,0:T(8,128)S(1)}, f32[8,16,128]{2,1,0:T(8,128)S(1)}, u32[]{:S(2)}, u32[]{:S(2)}) %collective-permute-start.11) | collective-permute-done | bytes 65568 | tf_op jit(solution)/shard_map/ppermute | solution.py:14
  72.1 0.2 multiply_reduce_fusion.1
  72.3 2.1 %multiply_reduce_fusion.3 = (f32[16]{0:T(128)S(1)}, f32[2,16,128]{2,1,0:T(8,128)}) fusion(f32[2,16,128]{2,1,0:T(8,128)S(1)} %get-tuple-element.35, f32[2,128,16,128]{3,2,1,0:T(8,128)S(1)} %fusion.10, f32[16,16,128]{2,1,0:T(8,128)S(1)} %get-tuple-element.8, f32[16,16,128]{2,1,0:T(8,128)S(1)} %get-tuple-element.4, f32[2,128]{1,0:T(2,128)S(1)} %copy-done.3, ...), kind=kOutput, calls=%fused_computation.71 | convolution fusion | flops 50425840 | bytes 2393216 | tf_op jit(solution)/shard_map/ricj,csj->rsi/dot_general | solution.py:125
  74.4 0.1 pad_maximum_fusion.7
  74.5 0.7 collective-permute-start.12
  75.2 2.8 %collective-permute-done.12 = f32[32]{0:T(128)S(1)} collective-permute-done((f32[32]{0:T(128)S(1)}, f32[32]{0:T(128)S(1)}, u32[]{:S(2)}, u32[]{:S(2)}) %collective-permute-start.12) | collective-permute-done | bytes 160 | tf_op jit(solution)/shard_map/ppermute | solution.py:14
  78.1 0.1 pad_maximum_fusion.8
  78.2 1.5 %collective-permute-start.13 = (f32[32]{0:T(128)S(1)}, f32[32]{0:T(128)S(1)}, u32[]{:S(2)}, u32[]{:S(2)}) collective-permute-start(f32[32]{0:T(128)S(1)} %pad_maximum_fusion.8), channel_id=1, source_target_pairs={{0,16},{8,24},{16,0},{24,8},{1,17},{9,25},{17,1},{25,9},{2,18},{10... | collective-permute-start | bytes 392 | tf_op jit(solution)/shard_map/ppermute | solution.py:14
  79.7 2.0 %collective-permute-done.13 = f32[32]{0:T(128)S(1)} collective-permute-done((f32[32]{0:T(128)S(1)}, f32[32]{0:T(128)S(1)}, u32[]{:S(2)}, u32[]{:S(2)}) %collective-permute-start.13) | collective-permute-done | bytes 160 | tf_op jit(solution)/shard_map/ppermute | solution.py:14
  81.8 1.1 %collective-permute-done.14 = f32[16]{0:T(128)S(1)} collective-permute-done((f32[16]{0:T(128)S(1)}, f32[16]{0:T(128)S(1)}, u32[]{:S(2)}, u32[]{:S(2)}) %collective-permute-start.14) | collective-permute-done | bytes 96 | tf_op jit(solution)/shard_map/ppermute | solution.py:14
  82.9 0.5 collective-permute-start.15
  83.4 3.0 %collective-permute-done.15 = f32[16]{0:T(128)S(1)} collective-permute-done((f32[16]{0:T(128)S(1)}, f32[16]{0:T(128)S(1)}, u32[]{:S(2)}, u32[]{:S(2)}) %collective-permute-start.15) | collective-permute-done | bytes 96 | tf_op jit(solution)/shard_map/ppermute | solution.py:14
  86.5 1.7 %collective-permute-start.16 = (f32[16]{0:T(128)S(1)}, f32[16]{0:T(128)S(1)}, u32[]{:S(2)}, u32[]{:S(2)}) collective-permute-start(f32[16]{0:T(128)S(1)} %add.228), channel_id=1, source_target_pairs={{0,4},{1,5},{2,6},{3,7},{4,0},{5,1},{6,2},{7,3},{8,12},{9,13},{10,... | collective-permute-start | bytes 200 | tf_op jit(solution)/shard_map/ppermute | solution.py:14
  88.2 0.6 constant_dynamic-slice_fusion
  88.8 2.1 %collective-permute-done.16 = f32[16]{0:T(128)S(1)} collective-permute-done((f32[16]{0:T(128)S(1)}, f32[16]{0:T(128)S(1)}, u32[]{:S(2)}, u32[]{:S(2)}) %collective-permute-start.16) | collective-permute-done | bytes 96 | tf_op jit(solution)/shard_map/ppermute | solution.py:14
  90.9 0.5 multiply_sqrt_fusion
  (63 shorter events, 0.7 us)
Async XLA Ops:
  0.6 5.4 %copy-start = (f32[32,128]{1,0:T(8,128)S(1)}, f32[32,128]{1,0:T(8,128)}, u32[]{:S(2)}) copy-start(f32[32,128]{1,0:T(8,128)} %param.20) | copy-start | bytes 49156
  0.6 5.4 %copy-start.6 = (s32[16]{0:T(128)S(1)}, s32[16]{0:T(128)}, u32[]{:S(2)}) copy-start(s32[16]{0:T(128)} %param.21) | copy-start | bytes 196
  0.7 5.6 %copy-start.4 = (f32[2,128]{1,0:T(2,128)S(1)}, f32[2,128]{1,0:T(2,128)}, u32[]{:S(2)}) copy-start(f32[2,128]{1,0:T(2,128)} %param.16) | copy-start | bytes 3076
  0.7 10.0 %copy-start.8 = (s32[48]{0:T(128)S(1)}, s32[48]{0:T(128)}, u32[]{:S(2)}) copy-start(s32[48]{0:T(128)} %param.13) | copy-start | bytes 580
  0.7 10.0 %copy-start.7 = (s32[48]{0:T(128)S(1)}, s32[48]{0:T(128)}, u32[]{:S(2)}) copy-start(s32[48]{0:T(128)} %param.12) | copy-start | bytes 580
  7.7 9.9 %collective-permute-start = (f32[18]{0:T(128)S(1)}, f32[18]{0:T(128)S(1)}, u32[]{:S(2)}, u32[]{:S(2)}) collective-permute-start(f32[18]{0:T(128)S(1)} %pad_maximum_fusion.3), channel_id=1, source_target_pairs={{0,8},{8,0},{16,24},{24,16},{1,9},{9,1},{17,25},{25,17},{2,10},{10... | collective-permute-start | bytes 224 | tf_op jit(solution)/shard_map/ppermute | solution.py:14
  10.8 5.6 %copy-start.1 = (f32[2,16,128]{2,1,0:T(8,128)S(1)}, f32[2,16,128]{2,1,0:T(8,128)}, u32[]{:S(2)}) copy-start(f32[2,16,128]{2,1,0:T(8,128)} %param.19) | copy-start | bytes 49156
  16.4 1.1 %copy-start.2 = (f32[2,16,128]{2,1,0:T(8,128)S(1)}, f32[2,16,128]{2,1,0:T(8,128)}, u32[]{:S(2)}) copy-start(f32[2,16,128]{2,1,0:T(8,128)} %param.18) | copy-start | bytes 49156
  16.4 1.1 %copy-start.5 = (f32[2,128]{1,0:T(2,128)S(1)}, f32[2,128]{1,0:T(2,128)}, u32[]{:S(2)}) copy-start(f32[2,128]{1,0:T(2,128)} %param.17) | copy-start | bytes 3076
  17.5 32.6 %copy-start.3 = (f32[2,128]{1,0:T(2,128)S(1)}, f32[2,128]{1,0:T(2,128)}, u32[]{:S(2)}) copy-start(f32[2,128]{1,0:T(2,128)} %param.15) | copy-start | bytes 3076
  20.9 3.5 %collective-permute-start.1 = (f32[18]{0:T(128)S(1)}, f32[18]{0:T(128)S(1)}, u32[]{:S(2)}, u32[]{:S(2)}) collective-permute-start(f32[18]{0:T(128)S(1)} %pad_maximum_fusion.4), channel_id=1, source_target_pairs={{0,16},{8,24},{16,0},{24,8},{1,17},{9,25},{17,1},{25,9},{2,18},{10... | collective-permute-start | bytes 224 | tf_op jit(solution)/shard_map/ppermute | solution.py:14
  26.5 1.3 %collective-permute-start.2 = (f32[22528]{0:T(1024)S(1)}, f32[22528]{0:T(1024)S(1)}, u32[]{:S(2)}, u32[]{:S(2)}) collective-permute-start(f32[22528]{0:T(1024)S(1)} %concatenate.48), channel_id=1, source_target_pairs={{0,1},{1,0},{2,3},{3,2},{4,5},{5,4},{6,7},{7,6},{8,9},{9,8},{10,11... | collective-permute-start | bytes 270344 | tf_op jit(solution)/shard_map/ppermute | solution.py:14
  29.9 5.1 %collective-permute-start.3 = (f32[27648]{0:T(1024)S(1)}, f32[27648]{0:T(1024)S(1)}, u32[]{:S(2)}, u32[]{:S(2)}) collective-permute-start(f32[27648]{0:T(1024)S(1)} %concatenate.49), channel_id=1, source_target_pairs={{0,2},{1,3},{2,0},{3,1},{4,6},{5,7},{6,4},{7,5},{8,10},{9,11},{10,... | collective-permute-start | bytes 331784 | tf_op jit(solution)/shard_map/ppermute | solution.py:14
  37.2 9.3 %collective-permute-start.4 = (f32[37888]{0:T(1024)S(1)}, f32[37888]{0:T(1024)S(1)}, u32[]{:S(2)}, u32[]{:S(2)}) collective-permute-start(f32[37888]{0:T(1024)S(1)} %concatenate.50), channel_id=1, source_target_pairs={{0,4},{1,5},{2,6},{3,7},{4,0},{5,1},{6,2},{7,3},{8,12},{9,13},{10,... | collective-permute-start | bytes 454664 | tf_op jit(solution)/shard_map/ppermute | solution.py:14
  48.5 1.3 %collective-permute-start.5 = (f32[8,16,128]{2,1,0:T(8,128)S(1)}, f32[8,16,128]{2,1,0:T(8,128)S(1)}, u32[]{:S(2)}, u32[]{:S(2)}) collective-permute-start(f32[8,16,128]{2,1,0:T(8,128)S(1)} %add.203), channel_id=1, source_target_pairs={{0,1},{1,0},{2,3},{3,2},{4,5},{5,4},{6,7},{7,6},{8,9},{9,8},{10,11... | collective-permute-start | bytes 196616 | tf_op jit(solution)/shard_map/ppermute | solution.py:14
  51.7 3.5 %collective-permute-start.6 = (f32[32]{0:T(128)S(1)}, f32[32]{0:T(128)S(1)}, u32[]{:S(2)}, u32[]{:S(2)}) collective-permute-start(f32[32]{0:T(128)S(1)} %pad_maximum_fusion.5), channel_id=1, source_target_pairs={{0,8},{8,0},{16,24},{24,16},{1,9},{9,1},{17,25},{25,17},{2,10},{10... | collective-permute-start | bytes 392 | tf_op jit(solution)/shard_map/ppermute | solution.py:14
  55.4 3.5 %collective-permute-start.7 = (f32[32]{0:T(128)S(1)}, f32[32]{0:T(128)S(1)}, u32[]{:S(2)}, u32[]{:S(2)}) collective-permute-start(f32[32]{0:T(128)S(1)} %pad_maximum_fusion.6), channel_id=1, source_target_pairs={{0,16},{8,24},{16,0},{24,8},{1,17},{9,25},{17,1},{25,9},{2,18},{10... | collective-permute-start | bytes 392 | tf_op jit(solution)/shard_map/ppermute | solution.py:14
  59.0 1.3 %collective-permute-start.8 = (f32[16400]{0:T(1024)S(1)}, f32[16400]{0:T(1024)S(1)}, u32[]{:S(2)}, u32[]{:S(2)}) collective-permute-start(f32[16400]{0:T(1024)S(1)} %pad_maximum_fusion), channel_id=1, source_target_pairs={{0,1},{1,0},{2,3},{3,2},{4,5},{5,4},{6,7},{7,6},{8,9},{9,8},{10,11... | collective-permute-start | bytes 196808 | tf_op jit(solution)/shard_map/ppermute | solution.py:14
  60.3 4.4 %collective-permute-start.9 = (f32[16400]{0:T(1024)S(1)}, f32[16400]{0:T(1024)S(1)}, u32[]{:S(2)}, u32[]{:S(2)}) collective-permute-start(f32[16400]{0:T(1024)S(1)} %pad_maximum_fusion.1), channel_id=1, source_target_pairs={{0,2},{1,3},{2,0},{3,1},{4,6},{5,7},{6,4},{7,5},{8,10},{9,11},{10,... | collective-permute-start | bytes 196808 | tf_op jit(solution)/shard_map/ppermute | solution.py:14
  64.7 6.0 %collective-permute-start.10 = (f32[16400]{0:T(1024)S(1)}, f32[16400]{0:T(1024)S(1)}, u32[]{:S(2)}, u32[]{:S(2)}) collective-permute-start(f32[16400]{0:T(1024)S(1)} %pad_maximum_fusion.2), channel_id=1, source_target_pairs={{0,4},{1,5},{2,6},{3,7},{4,0},{5,1},{6,2},{7,3},{8,12},{9,13},{10,... | collective-permute-start | bytes 196808 | tf_op jit(solution)/shard_map/ppermute | solution.py:14
  70.8 1.3 %collective-permute-start.11 = (f32[8,16,128]{2,1,0:T(8,128)S(1)}, f32[8,16,128]{2,1,0:T(8,128)S(1)}, u32[]{:S(2)}, u32[]{:S(2)}) collective-permute-start(f32[8,16,128]{2,1,0:T(8,128)S(1)} %fusion.66), channel_id=1, source_target_pairs={{0,1},{1,0},{2,3},{3,2},{4,5},{5,4},{6,7},{7,6},{8,9},{9,8},{10,11... | collective-permute-start | bytes 196616 | tf_op jit(solution)/shard_map/ppermute | solution.py:14
  74.5 3.5 %collective-permute-start.12 = (f32[32]{0:T(128)S(1)}, f32[32]{0:T(128)S(1)}, u32[]{:S(2)}, u32[]{:S(2)}) collective-permute-start(f32[32]{0:T(128)S(1)} %pad_maximum_fusion.7), channel_id=1, source_target_pairs={{0,8},{8,0},{16,24},{24,16},{1,9},{9,1},{17,25},{25,17},{2,10},{10... | collective-permute-start | bytes 392 | tf_op jit(solution)/shard_map/ppermute | solution.py:14
  78.2 3.5 %collective-permute-start.13 = (f32[32]{0:T(128)S(1)}, f32[32]{0:T(128)S(1)}, u32[]{:S(2)}, u32[]{:S(2)}) collective-permute-start(f32[32]{0:T(128)S(1)} %pad_maximum_fusion.8), channel_id=1, source_target_pairs={{0,16},{8,24},{16,0},{24,8},{1,17},{9,25},{17,1},{25,9},{2,18},{10... | collective-permute-start | bytes 392 | tf_op jit(solution)/shard_map/ppermute | solution.py:14
  81.8 1.1 %collective-permute-start.14 = (f32[16]{0:T(128)S(1)}, f32[16]{0:T(128)S(1)}, u32[]{:S(2)}, u32[]{:S(2)}) collective-permute-start(f32[16]{0:T(128)S(1)} %slice_add_fusion.6), channel_id=1, source_target_pairs={{0,1},{1,0},{2,3},{3,2},{4,5},{5,4},{6,7},{7,6},{8,9},{9,8},{10,11... | collective-permute-start | bytes 200 | tf_op jit(solution)/shard_map/ppermute | solution.py:14
  82.9 3.5 %collective-permute-start.15 = (f32[16]{0:T(128)S(1)}, f32[16]{0:T(128)S(1)}, u32[]{:S(2)}, u32[]{:S(2)}) collective-permute-start(f32[16]{0:T(128)S(1)} %add.227), channel_id=1, source_target_pairs={{0,2},{1,3},{2,0},{3,1},{4,6},{5,7},{6,4},{7,5},{8,10},{9,11},{10,... | collective-permute-start | bytes 200 | tf_op jit(solution)/shard_map/ppermute | solution.py:14
  86.5 4.4 %collective-permute-start.16 = (f32[16]{0:T(128)S(1)}, f32[16]{0:T(128)S(1)}, u32[]{:S(2)}, u32[]{:S(2)}) collective-permute-start(f32[16]{0:T(128)S(1)} %add.228), channel_id=1, source_target_pairs={{0,4},{1,5},{2,6},{3,7},{4,0},{5,1},{6,2},{7,3},{8,12},{9,13},{10,... | collective-permute-start | bytes 200 | tf_op jit(solution)/shard_map/ppermute | solution.py:14

commit v14 on v11

--- a/solution.py
+++ b/solution.py
@@ -14,65 +14,84 @@
     return lax.ppermute(x, axis, [(i, i ^ (1 << bit)) for i in range(n)])
 
 
+def _gather_order(n):
+    bits = n.bit_length() - 1
+    return list(range(1, bits)) + [0] if bits > 1 else list(range(bits))
+
+
+def _slot(index, n):
+    out = 0
+    for m, bit in enumerate(_gather_order(n)):
+        out = out + (((index >> bit) & 1) << m)
+    return out
+
+
 def _rounds(axis, sums, own=None, split=None):
     n = lax.axis_size(axis)
-    if split is not None and (not _pow2(n) or n < 2 or split.shape[0] % 2):
-        sums = [split] + list(sums)
-        split = None
-        joined = True
-    else:
-        joined = False
-    if not _pow2(n):
+    if not _pow2(n) or n < 2:
         sums = [lax.psum(s, axis) for s in sums]
+        full = None if split is None else lax.psum(split, axis)
         if own is not None:
             own = lax.all_gather(own, axis, axis=0, tiled=False)
-        return (sums[0] if joined else None), sums[1:] if joined else sums, own
+        return full, sums, own
     shapes = [s.shape for s in sums]
     sizes = [s.size for s in sums]
     me = lax.axis_index(axis)
+    order = _gather_order(n)
+    bits = n.bit_length() - 1
     buf = None
     if own is not None:
+        assert split is not None
+        mine_slot = _slot(me, n)
         buf = jnp.zeros((n,) + own.shape, own.dtype)
-        buf = lax.dynamic_update_index_in_dim(buf, own, me, 0)
+        buf = lax.dynamic_update_index_in_dim(buf, own, mine_slot, 0)
     if split is not None:
         half = lax.rem(me, 2)
         halves = split.reshape((2, split.shape[0] // 2) + split.shape[1:])
         keep = lax.dynamic_index_in_dim(halves, half, 0, keepdims=False)
         give = lax.dynamic_index_in_dim(halves, 1 - half, 0, keepdims=False)
-    for bit in range(n.bit_length() - 1):
+    steps = list(range(bits)) + ([0] if split is not None else [])
+    m = 0
+    for step, bit in enumerate(steps):
+        last = split is not None and step == bits
         parts = []
         if split is not None:
-            parts.append((give if bit == 0 else keep).reshape(-1))
-        parts += [s.reshape(-1) for s in sums]
-        if buf is not None:
+            parts.append((give if step == 0 else keep).reshape(-1))
+        if not last:
+            parts += [s.reshape(-1) for s in sums]
+        carry = buf is not None and m < bits and order[m] == bit and (step > 0 or bits == 1)
+        if carry:
             used = sum(p.shape[0] for p in parts)
             if used % 1024:
                 parts.append(jnp.zeros((-used % 1024,), jnp.float32))
-            start = (me >> bit) << bit
-            parts.append(lax.dynamic_slice_in_dim(buf, start, 1 << bit, axis=0).reshape(-1))
+            start = (mine_slot >> m) << m
+            parts.append(lax.dynamic_slice_in_dim(buf, start, 1 << m, axis=0).reshape(-1))
         flat = jnp.concatenate(parts) if len(parts) > 1 else parts[0]
         got = _exchange(flat, axis, n, bit)
         off = 0
         if split is not None:
-            keep = keep + got[: keep.size].reshape(keep.shape)
+            piece = got[: keep.size].reshape(keep.shape)
+            if last:
+                other = piece
+            else:
+                keep = keep + piece
             off = keep.size
-        new_sums = []
-        for shape, size, s in zip(shapes, sizes, sums):
-            new_sums.append(s + got[off : off + size].reshape(shape))
-            off += size
-        sums = new_sums
-        if buf is not None:
+        if not last:
+            new_sums = []
+            for shape, size, s in zip(shapes, sizes, sums):
+                new_sums.append(s + got[off : off + size].reshape(shape))
+                off += size
+            sums = new_sums
+        if carry:
             off += -off % 1024
-            theirs = ((me ^ (1 << bit)) >> bit) << bit
-            chunk = got[off:].reshape((1 << bit,) + own.shape)
+            theirs = ((mine_slot ^ (1 << m)) >> m) << m
+            chunk = got[off:].reshape((1 << m,) + own.shape)
             buf = lax.dynamic_update_slice_in_dim(buf, chunk, theirs, axis=0)
+            m += 1
     full = None
     if split is not None:
-        other = _exchange(keep, axis, n, 0)
         both = jnp.concatenate([keep, other, keep], axis=0)
         full = lax.dynamic_slice_in_dim(both, half * keep.shape[0], 2 * keep.shape[0], axis=0)
-    elif joined:
-        full, sums = sums[0], sums[1:]
     return full, sums, buf
 
 
@@ -110,7 +129,8 @@
     local_b = jnp.sum(rhs * rhs)
     width = scenarios * lanes
 
-    place = tile_cols * row_blocks + tile_rows
+    slot_cols = _slot(tile_cols // own_blocks, ncol) * own_blocks + tile_cols % own_blocks
+    place = slot_cols * row_blocks + tile_rows
     place_live = (
         place[None, :] == jnp.arange(region_blocks * row_blocks, dtype=jnp.int32)[:, None]
     ).astype(jnp.float32) * live[None, :]
@@ -166,7 +186,9 @@
     _, (step_x, part_y), _ = _rounds("region", [local_x, local_y])
     _, (step_y,), _ = _rounds("col", [part_y])
     weight = jnp.sqrt(weight * jnp.sqrt((step_x + 1e-06) / (step_y + 1e-06)))
-    primal_out = lax.dynamic_slice_in_dim(primal_reg, me * own_blocks, own_blocks, axis=0)
+    primal_out = lax.dynamic_slice_in_dim(
+        primal_reg, _slot(me, ncol) * own_blocks, own_blocks, axis=0
+    )
     return (primal_out, dual, weight)
 
 

time: 91.5 us -> 89.3 us (0.976)
  waiting for transfers between devices: 39.5 us -> 37.4 us
    ppermute x17, waiting for transfers between devices: 39.5 us -> 37.4 us  [_exchange(): return lax.ppermute(x, axis, [(i, i ^ 1 << bit) for i in range(n)])]
  transfers between devices with their start and end apart: 17 -> 17, of which waited for: 16 -> 16; matrix products, arithmetic and copies ran while one was open for 9% -> 10% of each run, Pallas kernels for 0% -> 0%
where the time goes in v14:
time: 89.3 us; the launch traced here: 89 us
  waiting for transfers between devices  37.4 us (42%)
  starting transfers between devices  18.5 us (21%)
  matrix products  11.5 us (13%)
  between operations  9.55 us (11%)
  other arithmetic  8.03 us (9%)
  local copies, waits for them, and re-layouts  4.06 us (5%)
    ppermute x17, waiting for transfers between devices, _exchange(): return lax.ppermute(x, axis, [(i, i ^ 1 << bit) for i in range(n)])  37.4 us
    ppermute x17, starting transfers between devices, _exchange(): return lax.ppermute(x, axis, [(i, i ^ 1 << bit) for i in range(n)])  18.5 us
    dot_general x1, matrix products, local(): dense = jnp.dot(place_live, tiles.reshape(ntiles, -1), precision=hp)  5.57 us
    dot_general x2, matrix products, product_of(): jnp.einsum('ricj,csj->rsi', dense, point, precision=lax.Precision.HIGH)  3.64 us
    reduce_sum x2, other arithmetic, local(): local_a = jnp.sum(jnp.sum(tiles * tiles, axis=(1, 2)) * live)  2.94 us
    slice x5, local copies, waits for them, and re-layouts, _rounds(): new_sums.append(s + got[off:off + size].reshape(shape))  2.91 us
    dot_general x2, matrix products, transposed_product(): jnp.einsum('rsi,ricj->csj', dual, dense, precision=lax.Precision.HIGH)  2.13 us
    concatenate x10, other arithmetic, _rounds(): flat = jnp.concatenate(parts) if len(parts) > 1 else parts[0]  1.8 us
  transfers between devices with their start and end apart: 17, of which 16 were waited for; matrix products, arithmetic and copies ran while one was open for 10% of the time, Pallas kernels for 0%

profile of v14, /device:TPU:0, one launch (start us, length us, event | category | flops | bytes accessed | tf_op | source)
XLA Modules:
  0.0 89.0 jit_solution(4743987896721054421)
XLA Ops:
  1.4 1.3 %multiply_reduce_fusion.6 = f32[]{:T(128)} fusion(f32[2,128]{1,0:T(2,128)} %param.15), kind=kLoop, calls=%fused_computation.101 | loop fusion | flops 511 | bytes 1028 | tf_op jit(solution)/shard_map/reduce_sum | solution.py:129
  2.7 2.3 %multiply_reduce_fusion = f32[48]{0:T(128)S(1)} fusion(f32[48,128,128]{2,1,0:T(8,128)} %param.11), kind=kLoop, calls=%fused_computation.4 | loop fusion | flops 1572816 | bytes 3145920 | tf_op jit(solution)/shard_map/reduce_sum | solution.py:127
  5.0 0.6 fusion.84
  5.6 0.2 fusion.81
  5.8 0.1 multiply_reduce_fusion.5
  5.9 1.4 %pad_maximum_fusion.4 = f32[18]{0:T(128)S(1)} fusion(f32[1]{0:T(128)} %bitcast.18, f32[16]{0:T(128)S(1)} %multiply_reduce_fusion.5, f32[1]{0:T(128)} %bitcast.17), kind=kLoop, calls=%fused_computation.114 | loop fusion | flops 36 | bytes 144 | tf_op jit(solution)/shard_map/concatenate | solution.py:69
  7.3 2.9 %collective-permute-start = (f32[18]{0:T(128)S(1)}, f32[18]{0:T(128)S(1)}, u32[]{:S(2)}, u32[]{:S(2)}) collective-permute-start(f32[18]{0:T(128)S(1)} %pad_maximum_fusion.4), channel_id=1, source_target_pairs={{0,8},{8,0},{16,24},{24,16},{1,9},{9,1},{17,25},{25,17},{2,10},{10... | collective-permute-start | bytes 224 | tf_op jit(solution)/shard_map/ppermute | solution.py:14
  10.3 0.1 pad.31.clone
  10.4 5.6 %fusion.10 = f32[2,128,16,128]{3,2,1,0:T(8,128)S(1)} fusion(f32[48]{0:T(128)S(1)} %compare_convert_fusion, s32[16,2]{0,1:T(2,128)S(1)} %multiply_add_fusion, s32[48]{0:T(128)S(1)} %multiply_add_fusion.1, f32[6,8,128,128]{3,2,1,0:T(8,128)} %bitcast.143), kind=kOutput, calls=%fused_computation.13 | convolution fusion | flops 301992960 | bytes 5243392 | tf_op jit(solution)/shard_map/dot_general | solution.py:137
  16.0 1.1 %fusion.8 = f32[16,128,16,1]{1,2,3,0:T(8,128)S(1)} fusion(f32[2,128,16,128]{3,2,1,0:T(8,128)S(1)} %fusion.10, f32[2,16,128]{2,1,0:T(8,128)S(1)} %copy-done.1), kind=kOutput, calls=%fused_computation.11 | convolution fusion | flops 50331648 | bytes 2244608 | tf_op jit(solution)/shard_map/rsi,ricj->csj/dot_general | solution.py:142
  17.1 0.1 fusion.71
  17.2 0.6 fusion.101
  20.4 0.1 slice_add_fusion.13
  20.4 0.1 pad_maximum_fusion.5
  20.5 1.5 %collective-permute-start.1 = (f32[18]{0:T(128)S(1)}, f32[18]{0:T(128)S(1)}, u32[]{:S(2)}, u32[]{:S(2)}) collective-permute-start(f32[18]{0:T(128)S(1)} %pad_maximum_fusion.5), channel_id=1, source_target_pairs={{0,16},{8,24},{16,0},{24,8},{1,17},{9,25},{17,1},{25,9},{2,18},{10... | collective-permute-start | bytes 224 | tf_op jit(solution)/shard_map/ppermute | solution.py:14
  22.0 2.0 %collective-permute-done.1 = f32[18]{0:T(128)S(1)} collective-permute-done((f32[18]{0:T(128)S(1)}, f32[18]{0:T(128)S(1)}, u32[]{:S(2)}, u32[]{:S(2)}) %collective-permute-start.1) | collective-permute-done | bytes 104 | tf_op jit(solution)/shard_map/ppermute | solution.py:14
  24.1 0.6 fusion.100
  25.9 0.1 slice_add_fusion.12
  26.0 0.1 concatenate.51
  26.1 1.2 %collective-permute-done.2 = f32[16402]{0:T(1024)S(1)} collective-permute-done((f32[16402]{0:T(1024)S(1)}, f32[16402]{0:T(1024)S(1)}, u32[]{:S(2)}, u32[]{:S(2)}) %collective-permute-start.2) | collective-permute-done | bytes 65640 | tf_op jit(solution)/shard_map/ppermute | solution.py:14
  27.4 0.6 fusion.99
  29.2 0.1 slice_add_fusion.5
  29.3 0.1 concatenate.52
  29.4 1.6 %collective-permute-start.3 = (f32[22528]{0:T(1024)S(1)}, f32[22528]{0:T(1024)S(1)}, u32[]{:S(2)}, u32[]{:S(2)}) collective-permute-start(f32[22528]{0:T(1024)S(1)} %concatenate.52), channel_id=1, source_target_pairs={{0,2},{1,3},{2,0},{3,1},{4,6},{5,7},{6,4},{7,5},{8,10},{9,11},{10,... | collective-permute-start | bytes 270344 | tf_op jit(solution)/shard_map/ppermute | solution.py:14
  31.0 3.1 %collective-permute-done.3 = f32[22528]{0:T(1024)S(1)} collective-permute-done((f32[22528]{0:T(1024)S(1)}, f32[22528]{0:T(1024)S(1)}, u32[]{:S(2)}, u32[]{:S(2)}) %collective-permute-start.3) | collective-permute-done | bytes 90144 | tf_op jit(solution)/shard_map/ppermute | solution.py:14
  34.1 0.6 fusion.95
  36.1 0.1 slice_add_fusion.4
  36.2 0.1 concatenate.53
  36.2 2.6 %collective-permute-start.4 = (f32[27648]{0:T(1024)S(1)}, f32[27648]{0:T(1024)S(1)}, u32[]{:S(2)}, u32[]{:S(2)}) collective-permute-start(f32[27648]{0:T(1024)S(1)} %concatenate.53), channel_id=1, source_target_pairs={{0,4},{1,5},{2,6},{3,7},{4,0},{5,1},{6,2},{7,3},{8,12},{9,13},{10,... | collective-permute-start | bytes 331784 | tf_op jit(solution)/shard_map/ppermute | solution.py:14
  38.8 5.0 %collective-permute-done.4 = f32[27648]{0:T(1024)S(1)} collective-permute-done((f32[27648]{0:T(1024)S(1)}, f32[27648]{0:T(1024)S(1)}, u32[]{:S(2)}, u32[]{:S(2)}) %collective-permute-start.4) | collective-permute-done | bytes 110624 | tf_op jit(solution)/shard_map/ppermute | solution.py:14
  43.8 0.6 fusion.94
  46.0 0.1 broadcast_multiply_fusion.1
  46.0 1.3 %collective-permute-done.5 = f32[36864]{0:T(1024)S(1)} collective-permute-done((f32[36864]{0:T(1024)S(1)}, f32[36864]{0:T(1024)S(1)}, u32[]{:S(2)}, u32[]{:S(2)}) %collective-permute-start.5) | collective-permute-done | bytes 147488 | tf_op jit(solution)/shard_map/ppermute | solution.py:14
  47.4 0.2 multiply_reduce_fusion.2
  47.6 1.5 %multiply_reduce_fusion.4 = (f32[16]{0:T(128)S(1)}, f32[2,16,128]{2,1,0:T(8,128)S(1)}) fusion(f32[2,16,128]{2,1,0:T(8,128)S(1)} %copy-done.1, f32[2,128,16,128]{3,2,1,0:T(8,128)S(1)} %fusion.10, f32[16,16,128]{2,1,0:T(8,128)S(1)} %bitcast.145, f32[16,16,128]{2,1,0:T(8,128)S(1)} %get-tuple-element.8, f32[2,128]{1,0:T(2,128)S(1)} %copy-done.3, ...), kind=kOutput, calls=%fused_computation.74 | convolution fusion | flops 50425840 | bytes 2393216 | tf_op jit(solution)/shard_map/ricj,csj->rsi/dot_general | solution.py:145
  49.1 0.1 pad_maximum_fusion.6
  49.2 0.7 collective-permute-start.6
  49.9 1.1 %fusion.6 = f32[16,128,16,1]{1,2,3,0:T(8,128)S(1)} fusion(f32[2,128,16,128]{3,2,1,0:T(8,128)S(1)} %fusion.10, f32[2,16,128]{2,1,0:T(8,128)S(1)} %get-tuple-element.41), kind=kOutput, calls=%fused_computation.9 | convolution fusion | flops 50331648 | bytes 2244608 | tf_op jit(solution)/shard_map/rsi,ricj->csj/dot_general | solution.py:142
  51.0 1.8 %collective-permute-done.6 = f32[32]{0:T(128)S(1)} collective-permute-done((f32[32]{0:T(128)S(1)}, f32[32]{0:T(128)S(1)}, u32[]{:S(2)}, u32[]{:S(2)}) %collective-permute-start.6) | collective-permute-done | bytes 160 | tf_op jit(solution)/shard_map/ppermute | solution.py:14
  52.8 0.1 pad_maximum_fusion.7
  52.9 1.5 %collective-permute-start.7 = (f32[32]{0:T(128)S(1)}, f32[32]{0:T(128)S(1)}, u32[]{:S(2)}, u32[]{:S(2)}) collective-permute-start(f32[32]{0:T(128)S(1)} %pad_maximum_fusion.7), channel_id=1, source_target_pairs={{0,16},{8,24},{16,0},{24,8},{1,17},{9,25},{17,1},{25,9},{2,18},{10... | collective-permute-start | bytes 392 | tf_op jit(solution)/shard_map/ppermute | solution.py:14
  54.4 2.0 %collective-permute-done.7 = f32[32]{0:T(128)S(1)} collective-permute-done((f32[32]{0:T(128)S(1)}, f32[32]{0:T(128)S(1)}, u32[]{:S(2)}, u32[]{:S(2)}) %collective-permute-start.7) | collective-permute-done | bytes 160 | tf_op jit(solution)/shard_map/ppermute | solution.py:14
  56.6 1.2 %collective-permute-done.8 = f32[16400]{0:T(1024)S(1)} collective-permute-done((f32[16400]{0:T(1024)S(1)}, f32[16400]{0:T(1024)S(1)}, u32[]{:S(2)}, u32[]{:S(2)}) %collective-permute-start.8) | collective-permute-done | bytes 65632 | tf_op jit(solution)/shard_map/ppermute | solution.py:14
  57.8 0.7 collective-permute-start.9
  58.6 3.6 %collective-permute-done.9 = f32[16400]{0:T(1024)S(1)} collective-permute-done((f32[16400]{0:T(1024)S(1)}, f32[16400]{0:T(1024)S(1)}, u32[]{:S(2)}, u32[]{:S(2)}) %collective-permute-start.9) | collective-permute-done | bytes 65632 | tf_op jit(solution)/shard_map/ppermute | solution.py:14
  62.2 2.3 %collective-permute-start.10 = (f32[16400]{0:T(1024)S(1)}, f32[16400]{0:T(1024)S(1)}, u32[]{:S(2)}, u32[]{:S(2)}) collective-permute-start(f32[16400]{0:T(1024)S(1)} %pad_maximum_fusion.3), channel_id=1, source_target_pairs={{0,4},{1,5},{2,6},{3,7},{4,0},{5,1},{6,2},{7,3},{8,12},{9,13},{10,... | collective-permute-start | bytes 196808 | tf_op jit(solution)/shard_map/ppermute | solution.py:14
  64.6 3.7 %collective-permute-done.10 = f32[16400]{0:T(1024)S(1)} collective-permute-done((f32[16400]{0:T(1024)S(1)}, f32[16400]{0:T(1024)S(1)}, u32[]{:S(2)}, u32[]{:S(2)}) %collective-permute-start.10) | collective-permute-done | bytes 65632 | tf_op jit(solution)/shard_map/ppermute | solution.py:14
  68.4 1.2 %collective-permute-done.11 = f32[16384]{0:T(1024)S(1)} collective-permute-done((f32[16384]{0:T(1024)S(1)}, f32[16384]{0:T(1024)S(1)}, u32[]{:S(2)}, u32[]{:S(2)}) %collective-permute-start.11) | collective-permute-done | bytes 65568 | tf_op jit(solution)/shard_map/ppermute | solution.py:14
  69.6 0.2 multiply_reduce_fusion.1
  69.8 2.1 %multiply_reduce_fusion.3 = (f32[16]{0:T(128)S(1)}, f32[2,16,128]{2,1,0:T(8,128)}) fusion(f32[2,16,128]{2,1,0:T(8,128)S(1)} %get-tuple-element.41, f32[2,128,16,128]{3,2,1,0:T(8,128)S(1)} %fusion.10, f32[16,16,128]{2,1,0:T(8,128)S(1)} %get-tuple-element.8, f32[16,16,128]{2,1,0:T(8,128)S(1)} %get-tuple-element.4, f32[2,128]{1,0:T(2,128)S(1)} %copy-done.3, ...), kind=kOutput, calls=%fused_computation.73 | convolution fusion | flops 50425840 | bytes 2393216 | tf_op jit(solution)/shard_map/ricj,csj->rsi/dot_general | solution.py:145
  71.9 0.1 pad_maximum_fusion.8
  72.0 0.7 collective-permute-start.12
  72.7 2.9 %collective-permute-done.12 = f32[32]{0:T(128)S(1)} collective-permute-done((f32[32]{0:T(128)S(1)}, f32[32]{0:T(128)S(1)}, u32[]{:S(2)}, u32[]{:S(2)}) %collective-permute-start.12) | collective-permute-done | bytes 160 | tf_op jit(solution)/shard_map/ppermute | solution.py:14
  75.6 0.1 slice_add_fusion.8
  75.6 0.1 pad_maximum_fusion.9
  75.7 1.5 %collective-permute-start.13 = (f32[32]{0:T(128)S(1)}, f32[32]{0:T(128)S(1)}, u32[]{:S(2)}, u32[]{:S(2)}) collective-permute-start(f32[32]{0:T(128)S(1)} %pad_maximum_fusion.9), channel_id=1, source_target_pairs={{0,16},{8,24},{16,0},{24,8},{1,17},{9,25},{17,1},{25,9},{2,18},{10... | collective-permute-start | bytes 392 | tf_op jit(solution)/shard_map/ppermute | solution.py:14
  77.2 2.0 %collective-permute-done.13 = f32[32]{0:T(128)S(1)} collective-permute-done((f32[32]{0:T(128)S(1)}, f32[32]{0:T(128)S(1)}, u32[]{:S(2)}, u32[]{:S(2)}) %collective-permute-start.13) | collective-permute-done | bytes 160 | tf_op jit(solution)/shard_map/ppermute | solution.py:14
  79.3 1.1 %collective-permute-done.14 = f32[16]{0:T(128)S(1)} collective-permute-done((f32[16]{0:T(128)S(1)}, f32[16]{0:T(128)S(1)}, u32[]{:S(2)}, u32[]{:S(2)}) %collective-permute-start.14) | collective-permute-done | bytes 96 | tf_op jit(solution)/shard_map/ppermute | solution.py:14
  80.5 0.5 collective-permute-start.15
  80.9 3.1 %collective-permute-done.15 = f32[16]{0:T(128)S(1)} collective-permute-done((f32[16]{0:T(128)S(1)}, f32[16]{0:T(128)S(1)}, u32[]{:S(2)}, u32[]{:S(2)}) %collective-permute-start.15) | collective-permute-done | bytes 96 | tf_op jit(solution)/shard_map/ppermute | solution.py:14
  84.0 1.7 %collective-permute-start.16 = (f32[16]{0:T(128)S(1)}, f32[16]{0:T(128)S(1)}, u32[]{:S(2)}, u32[]{:S(2)}) collective-permute-start(f32[16]{0:T(128)S(1)} %add.268), channel_id=1, source_target_pairs={{0,4},{1,5},{2,6},{3,7},{4,0},{5,1},{6,2},{7,3},{8,12},{9,13},{10,... | collective-permute-start | bytes 200 | tf_op jit(solution)/shard_map/ppermute | solution.py:14
  85.7 0.6 constant_dynamic-slice_fusion
  86.3 2.1 %collective-permute-done.16 = f32[16]{0:T(128)S(1)} collective-permute-done((f32[16]{0:T(128)S(1)}, f32[16]{0:T(128)S(1)}, u32[]{:S(2)}, u32[]{:S(2)}) %collective-permute-start.16) | collective-permute-done | bytes 96 | tf_op jit(solution)/shard_map/ppermute | solution.py:14
  88.4 0.5 multiply_sqrt_fusion
  (65 shorter events, 0.8 us)
Async XLA Ops:
  0.6 5.0 %copy-start = (f32[32,128]{1,0:T(8,128)S(1)}, f32[32,128]{1,0:T(8,128)}, u32[]{:S(2)}) copy-start(f32[32,128]{1,0:T(8,128)} %param.20) | copy-start | bytes 49156
  0.6 5.0 %copy-start.6 = (s32[16]{0:T(128)S(1)}, s32[16]{0:T(128)}, u32[]{:S(2)}) copy-start(s32[16]{0:T(128)} %param.21) | copy-start | bytes 196
  0.7 5.1 %copy-start.4 = (f32[2,128]{1,0:T(2,128)S(1)}, f32[2,128]{1,0:T(2,128)}, u32[]{:S(2)}) copy-start(f32[2,128]{1,0:T(2,128)} %param.16) | copy-start | bytes 3076
  0.7 9.6 %copy-start.8 = (s32[48]{0:T(128)S(1)}, s32[48]{0:T(128)}, u32[]{:S(2)}) copy-start(s32[48]{0:T(128)} %param.13) | copy-start | bytes 580
  0.7 9.6 %copy-start.7 = (s32[48]{0:T(128)S(1)}, s32[48]{0:T(128)}, u32[]{:S(2)}) copy-start(s32[48]{0:T(128)} %param.12) | copy-start | bytes 580
  7.3 9.9 %collective-permute-start = (f32[18]{0:T(128)S(1)}, f32[18]{0:T(128)S(1)}, u32[]{:S(2)}, u32[]{:S(2)}) collective-permute-start(f32[18]{0:T(128)S(1)} %pad_maximum_fusion.4), channel_id=1, source_target_pairs={{0,8},{8,0},{16,24},{24,16},{1,9},{9,1},{17,25},{25,17},{2,10},{10... | collective-permute-start | bytes 224 | tf_op jit(solution)/shard_map/ppermute | solution.py:14
  10.4 5.6 %copy-start.1 = (f32[2,16,128]{2,1,0:T(8,128)S(1)}, f32[2,16,128]{2,1,0:T(8,128)}, u32[]{:S(2)}) copy-start(f32[2,16,128]{2,1,0:T(8,128)} %param.19) | copy-start | bytes 49156
  16.0 1.1 %copy-start.2 = (f32[2,16,128]{2,1,0:T(8,128)S(1)}, f32[2,16,128]{2,1,0:T(8,128)}, u32[]{:S(2)}) copy-start(f32[2,16,128]{2,1,0:T(8,128)} %param.18) | copy-start | bytes 49156
  16.0 1.1 %copy-start.5 = (f32[2,128]{1,0:T(2,128)S(1)}, f32[2,128]{1,0:T(2,128)}, u32[]{:S(2)}) copy-start(f32[2,128]{1,0:T(2,128)} %param.17) | copy-start | bytes 3076
  17.0 30.6 %copy-start.3 = (f32[2,128]{1,0:T(2,128)S(1)}, f32[2,128]{1,0:T(2,128)}, u32[]{:S(2)}) copy-start(f32[2,128]{1,0:T(2,128)} %param.15) | copy-start | bytes 3076
  20.5 3.5 %collective-permute-start.1 = (f32[18]{0:T(128)S(1)}, f32[18]{0:T(128)S(1)}, u32[]{:S(2)}, u32[]{:S(2)}) collective-permute-start(f32[18]{0:T(128)S(1)} %pad_maximum_fusion.5), channel_id=1, source_target_pairs={{0,16},{8,24},{16,0},{24,8},{1,17},{9,25},{17,1},{25,9},{2,18},{10... | collective-permute-start | bytes 224 | tf_op jit(solution)/shard_map/ppermute | solution.py:14
  26.1 1.3 %collective-permute-start.2 = (f32[16402]{0:T(1024)S(1)}, f32[16402]{0:T(1024)S(1)}, u32[]{:S(2)}, u32[]{:S(2)}) collective-permute-start(f32[16402]{0:T(1024)S(1)} %concatenate.51), channel_id=1, source_target_pairs={{0,1},{1,0},{2,3},{3,2},{4,5},{5,4},{6,7},{7,6},{8,9},{9,8},{10,11... | collective-permute-start | bytes 196832 | tf_op jit(solution)/shard_map/ppermute | solution.py:14
  29.4 4.7 %collective-permute-start.3 = (f32[22528]{0:T(1024)S(1)}, f32[22528]{0:T(1024)S(1)}, u32[]{:S(2)}, u32[]{:S(2)}) collective-permute-start(f32[22528]{0:T(1024)S(1)} %concatenate.52), channel_id=1, source_target_pairs={{0,2},{1,3},{2,0},{3,1},{4,6},{5,7},{6,4},{7,5},{8,10},{9,11},{10,... | collective-permute-start | bytes 270344 | tf_op jit(solution)/shard_map/ppermute | solution.py:14
  36.2 7.6 %collective-permute-start.4 = (f32[27648]{0:T(1024)S(1)}, f32[27648]{0:T(1024)S(1)}, u32[]{:S(2)}, u32[]{:S(2)}) collective-permute-start(f32[27648]{0:T(1024)S(1)} %concatenate.53), channel_id=1, source_target_pairs={{0,4},{1,5},{2,6},{3,7},{4,0},{5,1},{6,2},{7,3},{8,12},{9,13},{10,... | collective-permute-start | bytes 331784 | tf_op jit(solution)/shard_map/ppermute | solution.py:14
  45.9 1.4 %collective-permute-start.5 = (f32[36864]{0:T(1024)S(1)}, f32[36864]{0:T(1024)S(1)}, u32[]{:S(2)}, u32[]{:S(2)}) collective-permute-start(f32[36864]{0:T(1024)S(1)} %pad_maximum_fusion), channel_id=1, source_target_pairs={{0,1},{1,0},{2,3},{3,2},{4,5},{5,4},{6,7},{7,6},{8,9},{9,8},{10,11... | collective-permute-start | bytes 442376 | tf_op jit(solution)/shard_map/ppermute | solution.py:14
  49.2 3.5 %collective-permute-start.6 = (f32[32]{0:T(128)S(1)}, f32[32]{0:T(128)S(1)}, u32[]{:S(2)}, u32[]{:S(2)}) collective-permute-start(f32[32]{0:T(128)S(1)} %pad_maximum_fusion.6), channel_id=1, source_target_pairs={{0,8},{8,0},{16,24},{24,16},{1,9},{9,1},{17,25},{25,17},{2,10},{10... | collective-permute-start | bytes 392 | tf_op jit(solution)/shard_map/ppermute | solution.py:14
  52.9 3.5 %collective-permute-start.7 = (f32[32]{0:T(128)S(1)}, f32[32]{0:T(128)S(1)}, u32[]{:S(2)}, u32[]{:S(2)}) collective-permute-start(f32[32]{0:T(128)S(1)} %pad_maximum_fusion.7), channel_id=1, source_target_pairs={{0,16},{8,24},{16,0},{24,8},{1,17},{9,25},{17,1},{25,9},{2,18},{10... | collective-permute-start | bytes 392 | tf_op jit(solution)/shard_map/ppermute | solution.py:14
  56.5 1.3 %collective-permute-start.8 = (f32[16400]{0:T(1024)S(1)}, f32[16400]{0:T(1024)S(1)}, u32[]{:S(2)}, u32[]{:S(2)}) collective-permute-start(f32[16400]{0:T(1024)S(1)} %pad_maximum_fusion.1), channel_id=1, source_target_pairs={{0,1},{1,0},{2,3},{3,2},{4,5},{5,4},{6,7},{7,6},{8,9},{9,8},{10,11... | collective-permute-start | bytes 196808 | tf_op jit(solution)/shard_map/ppermute | solution.py:14
  57.8 4.4 %collective-permute-start.9 = (f32[16400]{0:T(1024)S(1)}, f32[16400]{0:T(1024)S(1)}, u32[]{:S(2)}, u32[]{:S(2)}) collective-permute-start(f32[16400]{0:T(1024)S(1)} %pad_maximum_fusion.2), channel_id=1, source_target_pairs={{0,2},{1,3},{2,0},{3,1},{4,6},{5,7},{6,4},{7,5},{8,10},{9,11},{10,... | collective-permute-start | bytes 196808 | tf_op jit(solution)/shard_map/ppermute | solution.py:14
  62.2 6.0 %collective-permute-start.10 = (f32[16400]{0:T(1024)S(1)}, f32[16400]{0:T(1024)S(1)}, u32[]{:S(2)}, u32[]{:S(2)}) collective-permute-start(f32[16400]{0:T(1024)S(1)} %pad_maximum_fusion.3), channel_id=1, source_target_pairs={{0,4},{1,5},{2,6},{3,7},{4,0},{5,1},{6,2},{7,3},{8,12},{9,13},{10,... | collective-permute-start | bytes 196808 | tf_op jit(solution)/shard_map/ppermute | solution.py:14
  68.3 1.3 %collective-permute-start.11 = (f32[16384]{0:T(1024)S(1)}, f32[16384]{0:T(1024)S(1)}, u32[]{:S(2)}, u32[]{:S(2)}) collective-permute-start(f32[16384]{0:T(1024)S(1)} %get-tuple-element.22), channel_id=1, source_target_pairs={{0,1},{1,0},{2,3},{3,2},{4,5},{5,4},{6,7},{7,6},{8,9},{9,8},{10,11... | collective-permute-start | bytes 196616 | tf_op jit(solution)/shard_map/ppermute | solution.py:14
  72.0 3.5 %collective-permute-start.12 = (f32[32]{0:T(128)S(1)}, f32[32]{0:T(128)S(1)}, u32[]{:S(2)}, u32[]{:S(2)}) collective-permute-start(f32[32]{0:T(128)S(1)} %pad_maximum_fusion.8), channel_id=1, source_target_pairs={{0,8},{8,0},{16,24},{24,16},{1,9},{9,1},{17,25},{25,17},{2,10},{10... | collective-permute-start | bytes 392 | tf_op jit(solution)/shard_map/ppermute | solution.py:14
  75.7 3.5 %collective-permute-start.13 = (f32[32]{0:T(128)S(1)}, f32[32]{0:T(128)S(1)}, u32[]{:S(2)}, u32[]{:S(2)}) collective-permute-start(f32[32]{0:T(128)S(1)} %pad_maximum_fusion.9), channel_id=1, source_target_pairs={{0,16},{8,24},{16,0},{24,8},{1,17},{9,25},{17,1},{25,9},{2,18},{10... | collective-permute-start | bytes 392 | tf_op jit(solution)/shard_map/ppermute | solution.py:14
  79.3 1.1 %collective-permute-start.14 = (f32[16]{0:T(128)S(1)}, f32[16]{0:T(128)S(1)}, u32[]{:S(2)}, u32[]{:S(2)}) collective-permute-start(f32[16]{0:T(128)S(1)} %slice_add_fusion.6), channel_id=1, source_target_pairs={{0,1},{1,0},{2,3},{3,2},{4,5},{5,4},{6,7},{7,6},{8,9},{9,8},{10,11... | collective-permute-start | bytes 200 | tf_op jit(solution)/shard_map/ppermute | solution.py:14
  80.5 3.5 %collective-permute-start.15 = (f32[16]{0:T(128)S(1)}, f32[16]{0:T(128)S(1)}, u32[]{:S(2)}, u32[]{:S(2)}) collective-permute-start(f32[16]{0:T(128)S(1)} %add.267), channel_id=1, source_target_pairs={{0,2},{1,3},{2,0},{3,1},{4,6},{5,7},{6,4},{7,5},{8,10},{9,11},{10,... | collective-permute-start | bytes 200 | tf_op jit(solution)/shard_map/ppermute | solution.py:14
  84.0 4.4 %collective-permute-start.16 = (f32[16]{0:T(128)S(1)}, f32[16]{0:T(128)S(1)}, u32[]{:S(2)}, u32[]{:S(2)}) collective-permute-start(f32[16]{0:T(128)S(1)} %add.268), channel_id=1, source_target_pairs={{0,4},{1,5},{2,6},{3,7},{4,0},{5,1},{6,2},{7,3},{8,12},{9,13},{10,... | collective-permute-start | bytes 200 | tf_op jit(solution)/shard_map/ppermute | solution.py:14

commit v15 on v14

--- a/solution.py
+++ b/solution.py
@@ -144,9 +144,8 @@
     def product_of(point):
         return jnp.einsum("ricj,csj->rsi", dense, point, precision=lax.Precision.HIGH)
 
-    _, (local_a, local_c, local_b), _ = _rounds(
-        "region", [local_a.reshape(1), local_c, local_b.reshape(1)]
-    )
+    norms = jnp.concatenate([local_a.reshape(1), local_c, local_b.reshape(1)])
+    _, (norms,), _ = _rounds("region", [norms])
     own_rows = own_blocks * (scenarios + 2)
     own = jnp.concatenate(
         [
@@ -158,16 +157,15 @@
         axis=0,
     )
     partial_value = transposed_product(dual)
-    grad, (sq_a, sq_c, sq_b), gathered = _rounds(
-        "col", [local_a, local_c, local_b], own, split=partial_value
-    )
+    grad, (norms,), gathered = _rounds("col", [norms], own, split=partial_value)
+    sq_a, sq_c, sq_b = norms[0], norms[1 : scenarios + 1], norms[scenarios + 1]
     primal_reg = gathered[:, : own_blocks * scenarios].reshape(region_blocks, scenarios, lanes)
     base_reg = gathered[:, own_blocks * scenarios : own_blocks * (scenarios + 1)]
     upper_reg = gathered[:, own_blocks * (scenarios + 1) : own_rows]
     cost_reg = base_reg.reshape(region_blocks, lanes)[:, None, :] * factor[None, :, :]
     upper_reg = upper_reg.reshape(region_blocks, lanes)[:, None, :]
-    eta = 0.5 / jnp.sqrt(sq_a[0] / (lanes * row_blocks * devices))
-    weight = jnp.sqrt(sq_c) / jnp.sqrt(sq_b[0])
+    eta = 0.5 / jnp.sqrt(sq_a / (lanes * row_blocks * devices))
+    weight = jnp.sqrt(sq_c) / jnp.sqrt(sq_b)
     for step in range(ITERS):
         if step > 0:
             _, (step_x, part_y), _ = _rounds("region", [local_x, local_y])

time: 89.3 us -> 81.5 us (0.913)
  between operations: 9.55 us -> 3.06 us
  local copies, waits for them, and re-layouts: 4.06 us -> 1.64 us
  other arithmetic: 8.03 us -> 9.04 us
    slice x5 -> x1, local copies, waits for them, and re-layouts: 2.91 us -> 0.59 us  [local(): sq_a, sq_c, sq_b = (norms[0], norms[1:scenarios + 1], norms[scenarios + 1])]
    concatenate x10 -> x9, other arithmetic: 1.8 us -> 0.35 us  [_rounds(): flat = jnp.concatenate(parts) if len(parts) > 1 else parts[0]]
    concatenate x0 -> x1, other arithmetic: none -> 1.37 us  [local(): norms = jnp.concatenate([local_a.reshape(1), local_c, local_b.reshape(1)])]
    add x12 -> x13, other arithmetic: 0.6 us -> 1.69 us  [_rounds(): new_sums.append(s + got[off:off + size].reshape(shape))]
  transfers between devices with their start and end apart: 17 -> 17, of which waited for: 16 -> 16; matrix products, arithmetic and copies ran while one was open for 10% -> 11% of each run, Pallas kernels for 0% -> 0%
where the time goes in v15:
time: 81.5 us; the launch traced here: 81.2 us
  waiting for transfers between devices  37.4 us (46%)
  starting transfers between devices  18.5 us (23%)
  matrix products  11.5 us (14%)
  other arithmetic  9.04 us (11%)
  between operations  3.06 us (4%)
  local copies, waits for them, and re-layouts  1.64 us (2%)
    ppermute x17, waiting for transfers between devices, _exchange(): return lax.ppermute(x, axis, [(i, i ^ 1 << bit) for i in range(n)])  37.4 us
    ppermute x17, starting transfers between devices, _exchange(): return lax.ppermute(x, axis, [(i, i ^ 1 << bit) for i in range(n)])  18.5 us
    dot_general x1, matrix products, local(): dense = jnp.dot(place_live, tiles.reshape(ntiles, -1), precision=hp)  5.57 us
    dot_general x2, matrix products, product_of(): jnp.einsum('ricj,csj->rsi', dense, point, precision=lax.Precision.HIGH)  3.64 us
    reduce_sum x2, other arithmetic, local(): local_a = jnp.sum(jnp.sum(tiles * tiles, axis=(1, 2)) * live)  2.94 us
    dot_general x2, matrix products, transposed_product(): jnp.einsum('rsi,ricj->csj', dual, dense, precision=lax.Precision.HIGH)  2.13 us
    add x13, other arithmetic, _rounds(): new_sums.append(s + got[off:off + size].reshape(shape))  1.69 us
  transfers between devices with their start and end apart: 17, of which 16 were waited for; matrix products, arithmetic and copies ran while one was open for 11% of the time, Pallas kernels for 0%

profile of v15, /device:TPU:0, one launch (start us, length us, event | category | flops | bytes accessed | tf_op | source)
XLA Modules:
  0.0 81.2 jit_solution(7024115424106134052)
XLA Ops:
  0.6 0.0 copy-start
  1.4 1.3 %multiply_reduce_fusion.6 = f32[]{:T(128)} fusion(f32[2,128]{1,0:T(2,128)} %param.15), kind=kLoop, calls=%fused_computation.102 | loop fusion | flops 511 | bytes 1028 | tf_op jit(solution)/shard_map/reduce_sum | solution.py:129
  2.7 2.3 %multiply_reduce_fusion = f32[48]{0:T(128)S(1)} fusion(f32[48,128,128]{2,1,0:T(8,128)} %param.11), kind=kLoop, calls=%fused_computation.4 | loop fusion | flops 1572816 | bytes 3145920 | tf_op jit(solution)/shard_map/reduce_sum | solution.py:127
  5.0 0.6 fusion.84
  5.6 0.2 fusion.81
  5.8 0.1 multiply_reduce_fusion.5
  5.9 1.4 %pad_maximum_fusion.5 = f32[18]{0:T(128)S(1)} fusion(f32[1]{0:T(128)} %bitcast.18, f32[16]{0:T(128)S(1)} %multiply_reduce_fusion.5, f32[1]{0:T(128)} %bitcast.17), kind=kLoop, calls=%fused_computation.114 | loop fusion | flops 36 | bytes 144 | tf_op jit(solution)/shard_map/concatenate | solution.py:147
  7.3 2.9 %collective-permute-start = (f32[18]{0:T(128)S(1)}, f32[18]{0:T(128)S(1)}, u32[]{:S(2)}, u32[]{:S(2)}) collective-permute-start(f32[18]{0:T(128)S(1)} %pad_maximum_fusion.5), channel_id=1, source_target_pairs={{0,8},{8,0},{16,24},{24,16},{1,9},{9,1},{17,25},{25,17},{2,10},{10... | collective-permute-start | bytes 224 | tf_op jit(solution)/shard_map/ppermute | solution.py:14
  10.3 0.1 pad.30.clone
  10.4 5.6 %fusion.10 = f32[2,128,16,128]{3,2,1,0:T(8,128)S(1)} fusion(f32[48]{0:T(128)S(1)} %compare_convert_fusion, s32[16,2]{0,1:T(2,128)S(1)} %multiply_add_fusion, s32[48]{0:T(128)S(1)} %multiply_add_fusion.1, f32[6,8,128,128]{3,2,1,0:T(8,128)} %bitcast.143), kind=kOutput, calls=%fused_computation.13 | convolution fusion | flops 301992960 | bytes 5243392 | tf_op jit(solution)/shard_map/dot_general | solution.py:137
  16.0 0.0 copy-start.2
  16.0 1.1 %fusion.8 = f32[16,128,16,1]{1,2,3,0:T(8,128)S(1)} fusion(f32[2,128,16,128]{3,2,1,0:T(8,128)S(1)} %fusion.10, f32[2,16,128]{2,1,0:T(8,128)S(1)} %copy-done.1), kind=kOutput, calls=%fused_computation.11 | convolution fusion | flops 50331648 | bytes 2244608 | tf_op jit(solution)/shard_map/rsi,ricj->csj/dot_general | solution.py:142
  17.1 0.1 fusion.71
  17.2 1.4 %fusion.98 = f32[18]{0:T(128)S(1)} fusion(f32[18]{0:T(128)S(1)} %collective-permute-done, f32[1]{0:T(128)} %bitcast.18, f32[16]{0:T(128)S(1)} %multiply_reduce_fusion.5, f32[1]{0:T(128)} %bitcast.17), kind=kLoop, calls=%fused_computation.147 | loop fusion | flops 54 | bytes 216 | tf_op jit(solution)/shard_map/add | solution.py:82
  18.6 1.5 %collective-permute-start.1 = (f32[18]{0:T(128)S(1)}, f32[18]{0:T(128)S(1)}, u32[]{:S(2)}, u32[]{:S(2)}) collective-permute-start(f32[18]{0:T(128)S(1)} %fusion.98), channel_id=1, source_target_pairs={{0,16},{8,24},{16,0},{24,8},{1,17},{9,25},{17,1},{25,9},{2,18},{10... | collective-permute-start | bytes 224 | tf_op jit(solution)/shard_map/ppermute | solution.py:14
  20.1 2.0 %collective-permute-done.1 = f32[18]{0:T(128)S(1)} collective-permute-done((f32[18]{0:T(128)S(1)}, f32[18]{0:T(128)S(1)}, u32[]{:S(2)}, u32[]{:S(2)}) %collective-permute-start.1) | collective-permute-done | bytes 104 | tf_op jit(solution)/shard_map/ppermute | solution.py:14
  22.1 0.1 collective-permute-start.2
  22.2 1.2 %collective-permute-done.2 = f32[16402]{0:T(1024)S(1)} collective-permute-done((f32[16402]{0:T(1024)S(1)}, f32[16402]{0:T(1024)S(1)}, u32[]{:S(2)}, u32[]{:S(2)}) %collective-permute-start.2) | collective-permute-done | bytes 65640 | tf_op jit(solution)/shard_map/ppermute | solution.py:14
  23.5 0.1 concatenate.48
  23.6 1.6 %collective-permute-start.3 = (f32[22528]{0:T(1024)S(1)}, f32[22528]{0:T(1024)S(1)}, u32[]{:S(2)}, u32[]{:S(2)}) collective-permute-start(f32[22528]{0:T(1024)S(1)} %concatenate.48), channel_id=1, source_target_pairs={{0,2},{1,3},{2,0},{3,1},{4,6},{5,7},{6,4},{7,5},{8,10},{9,11},{10,... | collective-permute-start | bytes 270344 | tf_op jit(solution)/shard_map/ppermute | solution.py:14
  25.1 3.1 %collective-permute-done.3 = f32[22528]{0:T(1024)S(1)} collective-permute-done((f32[22528]{0:T(1024)S(1)}, f32[22528]{0:T(1024)S(1)}, u32[]{:S(2)}, u32[]{:S(2)}) %collective-permute-start.3) | collective-permute-done | bytes 90144 | tf_op jit(solution)/shard_map/ppermute | solution.py:14
  28.3 0.1 concatenate.49
  28.4 2.6 %collective-permute-start.4 = (f32[27648]{0:T(1024)S(1)}, f32[27648]{0:T(1024)S(1)}, u32[]{:S(2)}, u32[]{:S(2)}) collective-permute-start(f32[27648]{0:T(1024)S(1)} %concatenate.49), channel_id=1, source_target_pairs={{0,4},{1,5},{2,6},{3,7},{4,0},{5,1},{6,2},{7,3},{8,12},{9,13},{10,... | collective-permute-start | bytes 331784 | tf_op jit(solution)/shard_map/ppermute | solution.py:14
  31.0 5.0 %collective-permute-done.4 = f32[27648]{0:T(1024)S(1)} collective-permute-done((f32[27648]{0:T(1024)S(1)}, f32[27648]{0:T(1024)S(1)}, u32[]{:S(2)}, u32[]{:S(2)}) %collective-permute-start.4) | collective-permute-done | bytes 110624 | tf_op jit(solution)/shard_map/ppermute | solution.py:14
  36.0 0.6 fusion.96
  38.0 0.1 collective-permute-start.5
  38.1 0.1 broadcast_multiply_fusion.1
  38.2 1.3 %collective-permute-done.5 = f32[36864]{0:T(1024)S(1)} collective-permute-done((f32[36864]{0:T(1024)S(1)}, f32[36864]{0:T(1024)S(1)}, u32[]{:S(2)}, u32[]{:S(2)}) %collective-permute-start.5) | collective-permute-done | bytes 147488 | tf_op jit(solution)/shard_map/ppermute | solution.py:14
  39.6 0.2 multiply_reduce_fusion.2
  39.8 1.5 %multiply_reduce_fusion.4 = (f32[16]{0:T(128)S(1)}, f32[2,16,128]{2,1,0:T(8,128)S(1)}) fusion(f32[2,16,128]{2,1,0:T(8,128)S(1)} %copy-done.1, f32[2,128,16,128]{3,2,1,0:T(8,128)S(1)} %fusion.10, f32[16,16,128]{2,1,0:T(8,128)S(1)} %bitcast.145, f32[16,16,128]{2,1,0:T(8,128)S(1)} %get-tuple-element.8, f32[2,128]{1,0:T(2,128)S(1)} %copy-done.3, ...), kind=kOutput, calls=%fused_computation.75 | convolution fusion | flops 50425840 | bytes 2393216 | tf_op jit(solution)/shard_map/ricj,csj->rsi/dot_general | solution.py:145
  41.3 0.1 pad_maximum_fusion.6
  41.4 0.7 collective-permute-start.6
  42.1 1.1 %fusion.6 = f32[16,128,16,1]{1,2,3,0:T(8,128)S(1)} fusion(f32[2,128,16,128]{3,2,1,0:T(8,128)S(1)} %fusion.10, f32[2,16,128]{2,1,0:T(8,128)S(1)} %get-tuple-element.33), kind=kOutput, calls=%fused_computation.9 | convolution fusion | flops 50331648 | bytes 2244608 | tf_op jit(solution)/shard_map/rsi,ricj->csj/dot_general | solution.py:142
  43.1 1.8 %collective-permute-done.6 = f32[32]{0:T(128)S(1)} collective-permute-done((f32[32]{0:T(128)S(1)}, f32[32]{0:T(128)S(1)}, u32[]{:S(2)}, u32[]{:S(2)}) %collective-permute-start.6) | collective-permute-done | bytes 160 | tf_op jit(solution)/shard_map/ppermute | solution.py:14
  44.9 0.1 slice_add_fusion.11
  45.0 0.1 pad_maximum_fusion.7
  45.1 1.5 %collective-permute-start.7 = (f32[32]{0:T(128)S(1)}, f32[32]{0:T(128)S(1)}, u32[]{:S(2)}, u32[]{:S(2)}) collective-permute-start(f32[32]{0:T(128)S(1)} %pad_maximum_fusion.7), channel_id=1, source_target_pairs={{0,16},{8,24},{16,0},{24,8},{1,17},{9,25},{17,1},{25,9},{2,18},{10... | collective-permute-start | bytes 392 | tf_op jit(solution)/shard_map/ppermute | solution.py:14
  46.6 2.0 %collective-permute-done.7 = f32[32]{0:T(128)S(1)} collective-permute-done((f32[32]{0:T(128)S(1)}, f32[32]{0:T(128)S(1)}, u32[]{:S(2)}, u32[]{:S(2)}) %collective-permute-start.7) | collective-permute-done | bytes 160 | tf_op jit(solution)/shard_map/ppermute | solution.py:14
  48.6 0.1 slice_add_fusion.9
  48.7 0.0 collective-permute-start.8
  48.7 1.2 %collective-permute-done.8 = f32[16400]{0:T(1024)S(1)} collective-permute-done((f32[16400]{0:T(1024)S(1)}, f32[16400]{0:T(1024)S(1)}, u32[]{:S(2)}, u32[]{:S(2)}) %collective-permute-start.8) | collective-permute-done | bytes 65632 | tf_op jit(solution)/shard_map/ppermute | solution.py:14
  50.0 0.7 collective-permute-start.9
  50.7 3.6 %collective-permute-done.9 = f32[16400]{0:T(1024)S(1)} collective-permute-done((f32[16400]{0:T(1024)S(1)}, f32[16400]{0:T(1024)S(1)}, u32[]{:S(2)}, u32[]{:S(2)}) %collective-permute-start.9) | collective-permute-done | bytes 65632 | tf_op jit(solution)/shard_map/ppermute | solution.py:14
  54.4 2.3 %collective-permute-start.10 = (f32[16400]{0:T(1024)S(1)}, f32[16400]{0:T(1024)S(1)}, u32[]{:S(2)}, u32[]{:S(2)}) collective-permute-start(f32[16400]{0:T(1024)S(1)} %pad_maximum_fusion.4), channel_id=1, source_target_pairs={{0,4},{1,5},{2,6},{3,7},{4,0},{5,1},{6,2},{7,3},{8,12},{9,13},{10,... | collective-permute-start | bytes 196808 | tf_op jit(solution)/shard_map/ppermute | solution.py:14
  56.7 3.7 %collective-permute-done.10 = f32[16400]{0:T(1024)S(1)} collective-permute-done((f32[16400]{0:T(1024)S(1)}, f32[16400]{0:T(1024)S(1)}, u32[]{:S(2)}, u32[]{:S(2)}) %collective-permute-start.10) | collective-permute-done | bytes 65632 | tf_op jit(solution)/shard_map/ppermute | solution.py:14
  60.5 0.1 collective-permute-start.11
  60.6 1.2 %collective-permute-done.11 = f32[16384]{0:T(1024)S(1)} collective-permute-done((f32[16384]{0:T(1024)S(1)}, f32[16384]{0:T(1024)S(1)}, u32[]{:S(2)}, u32[]{:S(2)}) %collective-permute-start.11) | collective-permute-done | bytes 65568 | tf_op jit(solution)/shard_map/ppermute | solution.py:14
  61.8 0.2 multiply_reduce_fusion.1
  62.0 2.1 %multiply_reduce_fusion.3 = (f32[16]{0:T(128)S(1)}, f32[2,16,128]{2,1,0:T(8,128)}) fusion(f32[2,16,128]{2,1,0:T(8,128)S(1)} %get-tuple-element.33, f32[2,128,16,128]{3,2,1,0:T(8,128)S(1)} %fusion.10, f32[16,16,128]{2,1,0:T(8,128)S(1)} %get-tuple-element.8, f32[16,16,128]{2,1,0:T(8,128)S(1)} %get-tuple-element.4, f32[2,128]{1,0:T(2,128)S(1)} %copy-done.3, ...), kind=kOutput, calls=%fused_computation.74 | convolution fusion | flops 50425840 | bytes 2393216 | tf_op jit(solution)/shard_map/ricj,csj->rsi/dot_general | solution.py:145
  64.1 0.1 pad_maximum_fusion.8
  64.2 0.7 collective-permute-start.12
  64.9 2.9 %collective-permute-done.12 = f32[32]{0:T(128)S(1)} collective-permute-done((f32[32]{0:T(128)S(1)}, f32[32]{0:T(128)S(1)}, u32[]{:S(2)}, u32[]{:S(2)}) %collective-permute-start.12) | collective-permute-done | bytes 160 | tf_op jit(solution)/shard_map/ppermute | solution.py:14
  67.7 0.1 slice_add_fusion.8
  67.8 0.1 pad_maximum_fusion.9
  67.9 1.5 %collective-permute-start.13 = (f32[32]{0:T(128)S(1)}, f32[32]{0:T(128)S(1)}, u32[]{:S(2)}, u32[]{:S(2)}) collective-permute-start(f32[32]{0:T(128)S(1)} %pad_maximum_fusion.9), channel_id=1, source_target_pairs={{0,16},{8,24},{16,0},{24,8},{1,17},{9,25},{17,1},{25,9},{2,18},{10... | collective-permute-start | bytes 392 | tf_op jit(solution)/shard_map/ppermute | solution.py:14
  69.4 2.0 %collective-permute-done.13 = f32[32]{0:T(128)S(1)} collective-permute-done((f32[32]{0:T(128)S(1)}, f32[32]{0:T(128)S(1)}, u32[]{:S(2)}, u32[]{:S(2)}) %collective-permute-start.13) | collective-permute-done | bytes 160 | tf_op jit(solution)/shard_map/ppermute | solution.py:14
  71.4 0.1 slice_add_fusion.6
  71.5 1.1 %collective-permute-done.14 = f32[16]{0:T(128)S(1)} collective-permute-done((f32[16]{0:T(128)S(1)}, f32[16]{0:T(128)S(1)}, u32[]{:S(2)}, u32[]{:S(2)}) %collective-permute-start.14) | collective-permute-done | bytes 96 | tf_op jit(solution)/shard_map/ppermute | solution.py:14
  72.6 0.5 collective-permute-start.15
  73.1 3.1 %collective-permute-done.15 = f32[16]{0:T(128)S(1)} collective-permute-done((f32[16]{0:T(128)S(1)}, f32[16]{0:T(128)S(1)}, u32[]{:S(2)}, u32[]{:S(2)}) %collective-permute-start.15) | collective-permute-done | bytes 96 | tf_op jit(solution)/shard_map/ppermute | solution.py:14
  76.2 1.7 %collective-permute-start.16 = (f32[16]{0:T(128)S(1)}, f32[16]{0:T(128)S(1)}, u32[]{:S(2)}, u32[]{:S(2)}) collective-permute-start(f32[16]{0:T(128)S(1)} %add.228), channel_id=1, source_target_pairs={{0,4},{1,5},{2,6},{3,7},{4,0},{5,1},{6,2},{7,3},{8,12},{9,13},{10,... | collective-permute-start | bytes 200 | tf_op jit(solution)/shard_map/ppermute | solution.py:14
  77.9 0.6 constant_dynamic-slice_fusion
  78.5 2.2 %collective-permute-done.16 = f32[16]{0:T(128)S(1)} collective-permute-done((f32[16]{0:T(128)S(1)}, f32[16]{0:T(128)S(1)}, u32[]{:S(2)}, u32[]{:S(2)}) %collective-permute-start.16) | collective-permute-done | bytes 96 | tf_op jit(solution)/shard_map/ppermute | solution.py:14
  80.6 0.5 multiply_sqrt_fusion
  (61 shorter events, 0.4 us)
Async XLA Ops:
  0.6 5.0 %copy-start = (f32[32,128]{1,0:T(8,128)S(1)}, f32[32,128]{1,0:T(8,128)}, u32[]{:S(2)}) copy-start(f32[32,128]{1,0:T(8,128)} %param.20) | copy-start | bytes 49156
  0.6 5.0 %copy-start.6 = (s32[16]{0:T(128)S(1)}, s32[16]{0:T(128)}, u32[]{:S(2)}) copy-start(s32[16]{0:T(128)} %param.21) | copy-start | bytes 196
  0.7 5.1 %copy-start.4 = (f32[2,128]{1,0:T(2,128)S(1)}, f32[2,128]{1,0:T(2,128)}, u32[]{:S(2)}) copy-start(f32[2,128]{1,0:T(2,128)} %param.16) | copy-start | bytes 3076
  0.7 9.6 %copy-start.8 = (s32[48]{0:T(128)S(1)}, s32[48]{0:T(128)}, u32[]{:S(2)}) copy-start(s32[48]{0:T(128)} %param.13) | copy-start | bytes 580
  0.7 9.6 %copy-start.7 = (s32[48]{0:T(128)S(1)}, s32[48]{0:T(128)}, u32[]{:S(2)}) copy-start(s32[48]{0:T(128)} %param.12) | copy-start | bytes 580
  7.3 9.9 %collective-permute-start = (f32[18]{0:T(128)S(1)}, f32[18]{0:T(128)S(1)}, u32[]{:S(2)}, u32[]{:S(2)}) collective-permute-start(f32[18]{0:T(128)S(1)} %pad_maximum_fusion.5), channel_id=1, source_target_pairs={{0,8},{8,0},{16,24},{24,16},{1,9},{9,1},{17,25},{25,17},{2,10},{10... | collective-permute-start | bytes 224 | tf_op jit(solution)/shard_map/ppermute | solution.py:14
  10.4 5.6 %copy-start.1 = (f32[2,16,128]{2,1,0:T(8,128)S(1)}, f32[2,16,128]{2,1,0:T(8,128)}, u32[]{:S(2)}) copy-start(f32[2,16,128]{2,1,0:T(8,128)} %param.19) | copy-start | bytes 49156
  16.0 1.1 %copy-start.2 = (f32[2,16,128]{2,1,0:T(8,128)S(1)}, f32[2,16,128]{2,1,0:T(8,128)}, u32[]{:S(2)}) copy-start(f32[2,16,128]{2,1,0:T(8,128)} %param.18) | copy-start | bytes 49156
  16.0 1.1 %copy-start.5 = (f32[2,128]{1,0:T(2,128)S(1)}, f32[2,128]{1,0:T(2,128)}, u32[]{:S(2)}) copy-start(f32[2,128]{1,0:T(2,128)} %param.17) | copy-start | bytes 3076
  17.0 22.7 %copy-start.3 = (f32[2,128]{1,0:T(2,128)S(1)}, f32[2,128]{1,0:T(2,128)}, u32[]{:S(2)}) copy-start(f32[2,128]{1,0:T(2,128)} %param.15) | copy-start | bytes 3076
  18.6 3.5 %collective-permute-start.1 = (f32[18]{0:T(128)S(1)}, f32[18]{0:T(128)S(1)}, u32[]{:S(2)}, u32[]{:S(2)}) collective-permute-start(f32[18]{0:T(128)S(1)} %fusion.98), channel_id=1, source_target_pairs={{0,16},{8,24},{16,0},{24,8},{1,17},{9,25},{17,1},{25,9},{2,18},{10... | collective-permute-start | bytes 224 | tf_op jit(solution)/shard_map/ppermute | solution.py:14
  22.1 1.3 %collective-permute-start.2 = (f32[16402]{0:T(1024)S(1)}, f32[16402]{0:T(1024)S(1)}, u32[]{:S(2)}, u32[]{:S(2)}) collective-permute-start(f32[16402]{0:T(1024)S(1)} %pad_maximum_fusion.1), channel_id=1, source_target_pairs={{0,1},{1,0},{2,3},{3,2},{4,5},{5,4},{6,7},{7,6},{8,9},{9,8},{10,11... | collective-permute-start | bytes 196832 | tf_op jit(solution)/shard_map/ppermute | solution.py:14
  23.6 4.7 %collective-permute-start.3 = (f32[22528]{0:T(1024)S(1)}, f32[22528]{0:T(1024)S(1)}, u32[]{:S(2)}, u32[]{:S(2)}) collective-permute-start(f32[22528]{0:T(1024)S(1)} %concatenate.48), channel_id=1, source_target_pairs={{0,2},{1,3},{2,0},{3,1},{4,6},{5,7},{6,4},{7,5},{8,10},{9,11},{10,... | collective-permute-start | bytes 270344 | tf_op jit(solution)/shard_map/ppermute | solution.py:14
  28.4 7.6 %collective-permute-start.4 = (f32[27648]{0:T(1024)S(1)}, f32[27648]{0:T(1024)S(1)}, u32[]{:S(2)}, u32[]{:S(2)}) collective-permute-start(f32[27648]{0:T(1024)S(1)} %concatenate.49), channel_id=1, source_target_pairs={{0,4},{1,5},{2,6},{3,7},{4,0},{5,1},{6,2},{7,3},{8,12},{9,13},{10,... | collective-permute-start | bytes 331784 | tf_op jit(solution)/shard_map/ppermute | solution.py:14
  38.0 1.4 %collective-permute-start.5 = (f32[36864]{0:T(1024)S(1)}, f32[36864]{0:T(1024)S(1)}, u32[]{:S(2)}, u32[]{:S(2)}) collective-permute-start(f32[36864]{0:T(1024)S(1)} %pad_maximum_fusion), channel_id=1, source_target_pairs={{0,1},{1,0},{2,3},{3,2},{4,5},{5,4},{6,7},{7,6},{8,9},{9,8},{10,11... | collective-permute-start | bytes 442376 | tf_op jit(solution)/shard_map/ppermute | solution.py:14
  41.4 3.5 %collective-permute-start.6 = (f32[32]{0:T(128)S(1)}, f32[32]{0:T(128)S(1)}, u32[]{:S(2)}, u32[]{:S(2)}) collective-permute-start(f32[32]{0:T(128)S(1)} %pad_maximum_fusion.6), channel_id=1, source_target_pairs={{0,8},{8,0},{16,24},{24,16},{1,9},{9,1},{17,25},{25,17},{2,10},{10... | collective-permute-start | bytes 392 | tf_op jit(solution)/shard_map/ppermute | solution.py:14
  45.1 3.5 %collective-permute-start.7 = (f32[32]{0:T(128)S(1)}, f32[32]{0:T(128)S(1)}, u32[]{:S(2)}, u32[]{:S(2)}) collective-permute-start(f32[32]{0:T(128)S(1)} %pad_maximum_fusion.7), channel_id=1, source_target_pairs={{0,16},{8,24},{16,0},{24,8},{1,17},{9,25},{17,1},{25,9},{2,18},{10... | collective-permute-start | bytes 392 | tf_op jit(solution)/shard_map/ppermute | solution.py:14
  48.7 1.3 %collective-permute-start.8 = (f32[16400]{0:T(1024)S(1)}, f32[16400]{0:T(1024)S(1)}, u32[]{:S(2)}, u32[]{:S(2)}) collective-permute-start(f32[16400]{0:T(1024)S(1)} %pad_maximum_fusion.2), channel_id=1, source_target_pairs={{0,1},{1,0},{2,3},{3,2},{4,5},{5,4},{6,7},{7,6},{8,9},{9,8},{10,11... | collective-permute-start | bytes 196808 | tf_op jit(solution)/shard_map/ppermute | solution.py:14
  50.0 4.4 %collective-permute-start.9 = (f32[16400]{0:T(1024)S(1)}, f32[16400]{0:T(1024)S(1)}, u32[]{:S(2)}, u32[]{:S(2)}) collective-permute-start(f32[16400]{0:T(1024)S(1)} %pad_maximum_fusion.3), channel_id=1, source_target_pairs={{0,2},{1,3},{2,0},{3,1},{4,6},{5,7},{6,4},{7,5},{8,10},{9,11},{10,... | collective-permute-start | bytes 196808 | tf_op jit(solution)/shard_map/ppermute | solution.py:14
  54.4 6.0 %collective-permute-start.10 = (f32[16400]{0:T(1024)S(1)}, f32[16400]{0:T(1024)S(1)}, u32[]{:S(2)}, u32[]{:S(2)}) collective-permute-start(f32[16400]{0:T(1024)S(1)} %pad_maximum_fusion.4), channel_id=1, source_target_pairs={{0,4},{1,5},{2,6},{3,7},{4,0},{5,1},{6,2},{7,3},{8,12},{9,13},{10,... | collective-permute-start | bytes 196808 | tf_op jit(solution)/shard_map/ppermute | solution.py:14
  60.5 1.3 %collective-permute-start.11 = (f32[16384]{0:T(1024)S(1)}, f32[16384]{0:T(1024)S(1)}, u32[]{:S(2)}, u32[]{:S(2)}) collective-permute-start(f32[16384]{0:T(1024)S(1)} %get-tuple-element.17), channel_id=1, source_target_pairs={{0,1},{1,0},{2,3},{3,2},{4,5},{5,4},{6,7},{7,6},{8,9},{9,8},{10,11... | collective-permute-start | bytes 196616 | tf_op jit(solution)/shard_map/ppermute | solution.py:14
  64.2 3.5 %collective-permute-start.12 = (f32[32]{0:T(128)S(1)}, f32[32]{0:T(128)S(1)}, u32[]{:S(2)}, u32[]{:S(2)}) collective-permute-start(f32[32]{0:T(128)S(1)} %pad_maximum_fusion.8), channel_id=1, source_target_pairs={{0,8},{8,0},{16,24},{24,16},{1,9},{9,1},{17,25},{25,17},{2,10},{10... | collective-permute-start | bytes 392 | tf_op jit(solution)/shard_map/ppermute | solution.py:14
  67.9 3.5 %collective-permute-start.13 = (f32[32]{0:T(128)S(1)}, f32[32]{0:T(128)S(1)}, u32[]{:S(2)}, u32[]{:S(2)}) collective-permute-start(f32[32]{0:T(128)S(1)} %pad_maximum_fusion.9), channel_id=1, source_target_pairs={{0,16},{8,24},{16,0},{24,8},{1,17},{9,25},{17,1},{25,9},{2,18},{10... | collective-permute-start | bytes 392 | tf_op jit(solution)/shard_map/ppermute | solution.py:14
  71.5 1.1 %collective-permute-start.14 = (f32[16]{0:T(128)S(1)}, f32[16]{0:T(128)S(1)}, u32[]{:S(2)}, u32[]{:S(2)}) collective-permute-start(f32[16]{0:T(128)S(1)} %slice_add_fusion.6), channel_id=1, source_target_pairs={{0,1},{1,0},{2,3},{3,2},{4,5},{5,4},{6,7},{7,6},{8,9},{9,8},{10,11... | collective-permute-start | bytes 200 | tf_op jit(solution)/shard_map/ppermute | solution.py:14
  72.6 3.5 %collective-permute-start.15 = (f32[16]{0:T(128)S(1)}, f32[16]{0:T(128)S(1)}, u32[]{:S(2)}, u32[]{:S(2)}) collective-permute-start(f32[16]{0:T(128)S(1)} %add.227), channel_id=1, source_target_pairs={{0,2},{1,3},{2,0},{3,1},{4,6},{5,7},{6,4},{7,5},{8,10},{9,11},{10,... | collective-permute-start | bytes 200 | tf_op jit(solution)/shard_map/ppermute | solution.py:14
  76.2 4.4 %collective-permute-start.16 = (f32[16]{0:T(128)S(1)}, f32[16]{0:T(128)S(1)}, u32[]{:S(2)}, u32[]{:S(2)}) collective-permute-start(f32[16]{0:T(128)S(1)} %add.228), channel_id=1, source_target_pairs={{0,4},{1,5},{2,6},{3,7},{4,0},{5,1},{6,2},{7,3},{8,12},{9,13},{10,... | collective-permute-start | bytes 200 | tf_op jit(solution)/shard_map/ppermute | solution.py:14

commit v16 on v15

--- a/solution.py
+++ b/solution.py
@@ -134,18 +134,25 @@
     place_live = (
         place[None, :] == jnp.arange(region_blocks * row_blocks, dtype=jnp.int32)[:, None]
     ).astype(jnp.float32) * live[None, :]
+
+    def transposed_product(dual):
+        return jnp.einsum("rsi,ricj->csj", dual, dense, precision=lax.Precision.HIGH)
+
+    def product_of(point):
+        return jnp.einsum("ricj,csj->rsi", dense, point, precision=lax.Precision.HIGH)
+
+    norms = jnp.concatenate([local_a.reshape(1), local_c, local_b.reshape(1)])
+    n_region = lax.axis_size("region")
+    if _pow2(n_region) and n_region >= 2:
+        norms = norms + _exchange(norms, "region", n_region, 0)
+        norms, place_live = lax.optimization_barrier((norms, place_live))
+        for bit in range(1, n_region.bit_length() - 1):
+            norms = norms + _exchange(norms, "region", n_region, bit)
+    else:
+        norms = lax.psum(norms, "region")
     dense = jnp.dot(place_live, tiles.reshape(ntiles, -1), precision=hp)
     dense = dense.reshape(region_blocks, row_blocks, tiles.shape[1], tiles.shape[2])
     dense = dense.transpose(1, 2, 0, 3)
-
-    def transposed_product(dual):
-        return jnp.einsum("rsi,ricj->csj", dual, dense, precision=lax.Precision.HIGH)
-
-    def product_of(point):
-        return jnp.einsum("ricj,csj->rsi", dense, point, precision=lax.Precision.HIGH)
-
-    norms = jnp.concatenate([local_a.reshape(1), local_c, local_b.reshape(1)])
-    _, (norms,), _ = _rounds("region", [norms])
     own_rows = own_blocks * (scenarios + 2)
     own = jnp.concatenate(
         [

time: 81.5 us -> 81.2 us (level)
    add x0 -> x2, other arithmetic: none -> 1.37 us  [the longest x1 1.37 us: local(): norms = norms + _exchange(norms, 'region', n_region, 0)]
    add x13 -> x11, other arithmetic: 1.69 us -> 0.31 us  [_rounds(): new_sums.append(s + got[off:off + size].reshape(shape))]
where the time goes in v16:
time: 81.2 us; the launch traced here: 80.9 us
  waiting for transfers between devices  36.7 us (45%)
  starting transfers between devices  19 us (23%)
  matrix products  11.5 us (14%)
  other arithmetic  9.04 us (11%)
  between operations  3.08 us (4%)
  local copies, waits for them, and re-layouts  1.64 us (2%)
    ppermute x17, waiting for transfers between devices, _exchange(): return lax.ppermute(x, axis, [(i, i ^ 1 << bit) for i in range(n)])  36.7 us
    ppermute x17, starting transfers between devices, _exchange(): return lax.ppermute(x, axis, [(i, i ^ 1 << bit) for i in range(n)])  19 us
    dot_general x1, matrix products, local(): dense = jnp.dot(place_live, tiles.reshape(ntiles, -1), precision=hp)  5.55 us
    dot_general x2, matrix products, product_of(): jnp.einsum('ricj,csj->rsi', dense, point, precision=lax.Precision.HIGH)  3.64 us
    reduce_sum x2, other arithmetic, local(): local_a = jnp.sum(jnp.sum(tiles * tiles, axis=(1, 2)) * live)  2.94 us
    dot_general x2, matrix products, transposed_product(): jnp.einsum('rsi,ricj->csj', dual, dense, precision=lax.Precision.HIGH)  2.13 us
  transfers between devices with their start and end apart: 17, of which 16 were waited for; matrix products, arithmetic and copies ran while one was open for 11% of the time, Pallas kernels for 0%

profile of v16, /device:TPU:0, one launch (start us, length us, event | category | flops | bytes accessed | tf_op | source)
XLA Modules:
  0.0 80.9 jit_solution(4964877682801822910)
XLA Ops:
  0.6 0.0 copy-start
  1.4 1.3 %multiply_reduce_fusion.6 = f32[]{:T(128)} fusion(f32[2,128]{1,0:T(2,128)} %param.15), kind=kLoop, calls=%fused_computation.98 | loop fusion | flops 511 | bytes 1028 | tf_op jit(solution)/shard_map/reduce_sum | solution.py:129
  2.7 2.3 %multiply_reduce_fusion = f32[48]{0:T(128)S(1)} fusion(f32[48,128,128]{2,1,0:T(8,128)} %param.11), kind=kLoop, calls=%fused_computation.4 | loop fusion | flops 1572816 | bytes 3145920 | tf_op jit(solution)/shard_map/reduce_sum | solution.py:127
  5.0 0.6 fusion.79
  5.6 0.2 fusion.76
  5.8 0.1 multiply_reduce_fusion.5
  5.9 1.4 %pad_maximum_fusion.5 = f32[18]{0:T(128)S(1)} fusion(f32[1]{0:T(128)} %bitcast.4, f32[16]{0:T(128)S(1)} %multiply_reduce_fusion.5, f32[1]{0:T(128)} %bitcast.3), kind=kLoop, calls=%fused_computation.109 | loop fusion | flops 36 | bytes 144 | tf_op jit(solution)/shard_map/concatenate | solution.py:144
  7.3 2.9 %collective-permute-start = (f32[18]{0:T(128)S(1)}, f32[18]{0:T(128)S(1)}, u32[]{:S(2)}, u32[]{:S(2)}) collective-permute-start(f32[18]{0:T(128)S(1)} %pad_maximum_fusion.5), channel_id=1, source_target_pairs={{0,8},{8,0},{16,24},{24,16},{1,9},{9,1},{17,25},{25,17},{2,10},{10... | collective-permute-start | bytes 224 | tf_op jit(solution)/shard_map/ppermute | solution.py:14
  10.3 0.1 pad.30.clone
  10.4 0.1 fusion.71
  10.5 1.3 %collective-permute-done = f32[18]{0:T(128)S(1)} collective-permute-done((f32[18]{0:T(128)S(1)}, f32[18]{0:T(128)S(1)}, u32[]{:S(2)}, u32[]{:S(2)}) %collective-permute-start) | collective-permute-done | bytes 104 | tf_op jit(solution)/shard_map/ppermute | solution.py:14
  11.8 1.4 %fusion.92 = f32[18]{0:T(128)S(1)} fusion(f32[18]{0:T(128)S(1)} %collective-permute-done, f32[1]{0:T(128)} %bitcast.4, f32[16]{0:T(128)S(1)} %multiply_reduce_fusion.5, f32[1]{0:T(128)} %bitcast.3), kind=kLoop, calls=%fused_computation.141 | loop fusion | flops 54 | bytes 216 | tf_op jit(solution)/shard_map/add | solution.py:147
  13.2 2.1 %collective-permute-start.1 = (f32[18]{0:T(128)S(1)}, f32[18]{0:T(128)S(1)}, u32[]{:S(2)}, u32[]{:S(2)}) collective-permute-start(f32[18]{0:T(128)S(1)} %fusion.92), channel_id=1, source_target_pairs={{0,16},{8,24},{16,0},{24,8},{1,17},{9,25},{17,1},{25,9},{2,18},{10... | collective-permute-start | bytes 224 | tf_op jit(solution)/shard_map/ppermute | solution.py:14
  15.2 5.5 %fusion.10 = f32[2,128,16,128]{3,2,1,0:T(8,128)S(1)} fusion(f32[16,2,48,1]{2,1,0,3:T(2,128)S(1)} %bitcast.167, f32[6,8,128,128]{3,2,1,0:T(8,128)} %bitcast.141), kind=kOutput, calls=%fused_computation.13 | convolution fusion | flops 301989888 | bytes 5249024 | tf_op jit(solution)/shard_map/dot_general | solution.py:153
  20.8 1.1 %fusion.8 = f32[16,128,16,1]{1,2,3,0:T(8,128)S(1)} fusion(f32[2,128,16,128]{3,2,1,0:T(8,128)S(1)} %fusion.10, f32[2,16,128]{2,1,0:T(8,128)S(1)} %copy-done.1), kind=kOutput, calls=%fused_computation.11 | convolution fusion | flops 50331648 | bytes 2244608 | tf_op jit(solution)/shard_map/rsi,ricj->csj/dot_general | solution.py:139
  21.9 0.1 collective-permute-start.2
  22.0 1.2 %collective-permute-done.2 = f32[16402]{0:T(1024)S(1)} collective-permute-done((f32[16402]{0:T(1024)S(1)}, f32[16402]{0:T(1024)S(1)}, u32[]{:S(2)}, u32[]{:S(2)}) %collective-permute-start.2) | collective-permute-done | bytes 65640 | tf_op jit(solution)/shard_map/ppermute | solution.py:14
  23.3 0.1 concatenate.48
  23.4 1.6 %collective-permute-start.3 = (f32[22528]{0:T(1024)S(1)}, f32[22528]{0:T(1024)S(1)}, u32[]{:S(2)}, u32[]{:S(2)}) collective-permute-start(f32[22528]{0:T(1024)S(1)} %concatenate.48), channel_id=1, source_target_pairs={{0,2},{1,3},{2,0},{3,1},{4,6},{5,7},{6,4},{7,5},{8,10},{9,11},{10,... | collective-permute-start | bytes 270344 | tf_op jit(solution)/shard_map/ppermute | solution.py:14
  24.9 3.1 %collective-permute-done.3 = f32[22528]{0:T(1024)S(1)} collective-permute-done((f32[22528]{0:T(1024)S(1)}, f32[22528]{0:T(1024)S(1)}, u32[]{:S(2)}, u32[]{:S(2)}) %collective-permute-start.3) | collective-permute-done | bytes 90144 | tf_op jit(solution)/shard_map/ppermute | solution.py:14
  28.1 0.1 concatenate.49
  28.2 2.6 %collective-permute-start.4 = (f32[27648]{0:T(1024)S(1)}, f32[27648]{0:T(1024)S(1)}, u32[]{:S(2)}, u32[]{:S(2)}) collective-permute-start(f32[27648]{0:T(1024)S(1)} %concatenate.49), channel_id=1, source_target_pairs={{0,4},{1,5},{2,6},{3,7},{4,0},{5,1},{6,2},{7,3},{8,12},{9,13},{10,... | collective-permute-start | bytes 331784 | tf_op jit(solution)/shard_map/ppermute | solution.py:14
  30.8 5.0 %collective-permute-done.4 = f32[27648]{0:T(1024)S(1)} collective-permute-done((f32[27648]{0:T(1024)S(1)}, f32[27648]{0:T(1024)S(1)}, u32[]{:S(2)}, u32[]{:S(2)}) %collective-permute-start.4) | collective-permute-done | bytes 110624 | tf_op jit(solution)/shard_map/ppermute | solution.py:14
  35.8 0.6 fusion.90
  37.8 0.1 collective-permute-start.5
  37.9 0.1 broadcast_multiply_fusion.1
  38.0 1.3 %collective-permute-done.5 = f32[36864]{0:T(1024)S(1)} collective-permute-done((f32[36864]{0:T(1024)S(1)}, f32[36864]{0:T(1024)S(1)}, u32[]{:S(2)}, u32[]{:S(2)}) %collective-permute-start.5) | collective-permute-done | bytes 147488 | tf_op jit(solution)/shard_map/ppermute | solution.py:14
  39.3 0.2 multiply_reduce_fusion.2
  39.6 1.5 %multiply_reduce_fusion.4 = (f32[16]{0:T(128)S(1)}, f32[2,16,128]{2,1,0:T(8,128)S(1)}) fusion(f32[2,16,128]{2,1,0:T(8,128)S(1)} %copy-done.1, f32[2,128,16,128]{3,2,1,0:T(8,128)S(1)} %fusion.10, f32[16,16,128]{2,1,0:T(8,128)S(1)} %bitcast.143, f32[16,16,128]{2,1,0:T(8,128)S(1)} %get-tuple-element.12, f32[2,128]{1,0:T(2,128)S(1)} %copy-done.3, ...), kind=kOutput, calls=%fused_computation.75 | convolution fusion | flops 50425840 | bytes 2393216 | tf_op jit(solution)/shard_map/ricj,csj->rsi/dot_general | solution.py:142
  41.1 0.1 pad_maximum_fusion.6
  41.2 1.5 %collective-permute-start.6 = (f32[32]{0:T(128)S(1)}, f32[32]{0:T(128)S(1)}, u32[]{:S(2)}, u32[]{:S(2)}) collective-permute-start(f32[32]{0:T(128)S(1)} %pad_maximum_fusion.6), channel_id=1, source_target_pairs={{0,8},{8,0},{16,24},{24,16},{1,9},{9,1},{17,25},{25,17},{2,10},{10... | collective-permute-start | bytes 392 | tf_op jit(solution)/shard_map/ppermute | solution.py:14
  42.7 1.1 %fusion.6 = f32[16,128,16,1]{1,2,3,0:T(8,128)S(1)} fusion(f32[2,128,16,128]{3,2,1,0:T(8,128)S(1)} %fusion.10, f32[2,16,128]{2,1,0:T(8,128)S(1)} %get-tuple-element.37), kind=kOutput, calls=%fused_computation.9 | convolution fusion | flops 50331648 | bytes 2244608 | tf_op jit(solution)/shard_map/rsi,ricj->csj/dot_general | solution.py:139
  43.7 1.0 %collective-permute-done.6 = f32[32]{0:T(128)S(1)} collective-permute-done((f32[32]{0:T(128)S(1)}, f32[32]{0:T(128)S(1)}, u32[]{:S(2)}, u32[]{:S(2)}) %collective-permute-start.6) | collective-permute-done | bytes 160 | tf_op jit(solution)/shard_map/ppermute | solution.py:14
  44.7 0.1 slice_add_fusion.11
  44.8 0.1 pad_maximum_fusion.7
  44.9 0.7 collective-permute-start.7
  45.5 2.9 %collective-permute-done.7 = f32[32]{0:T(128)S(1)} collective-permute-done((f32[32]{0:T(128)S(1)}, f32[32]{0:T(128)S(1)}, u32[]{:S(2)}, u32[]{:S(2)}) %collective-permute-start.7) | collective-permute-done | bytes 160 | tf_op jit(solution)/shard_map/ppermute | solution.py:14
  48.4 0.1 slice_add_fusion.9
  48.5 0.0 collective-permute-start.8
  48.5 1.2 %collective-permute-done.8 = f32[16400]{0:T(1024)S(1)} collective-permute-done((f32[16400]{0:T(1024)S(1)}, f32[16400]{0:T(1024)S(1)}, u32[]{:S(2)}, u32[]{:S(2)}) %collective-permute-start.8) | collective-permute-done | bytes 65632 | tf_op jit(solution)/shard_map/ppermute | solution.py:14
  49.8 0.7 collective-permute-start.9
  50.5 3.6 %collective-permute-done.9 = f32[16400]{0:T(1024)S(1)} collective-permute-done((f32[16400]{0:T(1024)S(1)}, f32[16400]{0:T(1024)S(1)}, u32[]{:S(2)}, u32[]{:S(2)}) %collective-permute-start.9) | collective-permute-done | bytes 65632 | tf_op jit(solution)/shard_map/ppermute | solution.py:14
  54.2 2.3 %collective-permute-start.10 = (f32[16400]{0:T(1024)S(1)}, f32[16400]{0:T(1024)S(1)}, u32[]{:S(2)}, u32[]{:S(2)}) collective-permute-start(f32[16400]{0:T(1024)S(1)} %pad_maximum_fusion.4), channel_id=1, source_target_pairs={{0,4},{1,5},{2,6},{3,7},{4,0},{5,1},{6,2},{7,3},{8,12},{9,13},{10,... | collective-permute-start | bytes 196808 | tf_op jit(solution)/shard_map/ppermute | solution.py:14
  56.5 3.7 %collective-permute-done.10 = f32[16400]{0:T(1024)S(1)} collective-permute-done((f32[16400]{0:T(1024)S(1)}, f32[16400]{0:T(1024)S(1)}, u32[]{:S(2)}, u32[]{:S(2)}) %collective-permute-start.10) | collective-permute-done | bytes 65632 | tf_op jit(solution)/shard_map/ppermute | solution.py:14
  60.2 0.1 collective-permute-start.11
  60.4 1.2 %collective-permute-done.11 = f32[16384]{0:T(1024)S(1)} collective-permute-done((f32[16384]{0:T(1024)S(1)}, f32[16384]{0:T(1024)S(1)}, u32[]{:S(2)}, u32[]{:S(2)}) %collective-permute-start.11) | collective-permute-done | bytes 65568 | tf_op jit(solution)/shard_map/ppermute | solution.py:14
  61.6 0.2 multiply_reduce_fusion.1
  61.8 2.1 %multiply_reduce_fusion.3 = (f32[16]{0:T(128)S(1)}, f32[2,16,128]{2,1,0:T(8,128)}) fusion(f32[2,16,128]{2,1,0:T(8,128)S(1)} %get-tuple-element.37, f32[2,128,16,128]{3,2,1,0:T(8,128)S(1)} %fusion.10, f32[16,16,128]{2,1,0:T(8,128)S(1)} %get-tuple-element.12, f32[16,16,128]{2,1,0:T(8,128)S(1)} %get-tuple-element.8, f32[2,128]{1,0:T(2,128)S(1)} %copy-done.3, ...), kind=kOutput, calls=%fused_computation.74 | convolution fusion | flops 50425840 | bytes 2393216 | tf_op jit(solution)/shard_map/ricj,csj->rsi/dot_general | solution.py:142
  63.9 0.1 pad_maximum_fusion.8
  64.0 1.5 %collective-permute-start.12 = (f32[32]{0:T(128)S(1)}, f32[32]{0:T(128)S(1)}, u32[]{:S(2)}, u32[]{:S(2)}) collective-permute-start(f32[32]{0:T(128)S(1)} %pad_maximum_fusion.8), channel_id=1, source_target_pairs={{0,8},{8,0},{16,24},{24,16},{1,9},{9,1},{17,25},{25,17},{2,10},{10... | collective-permute-start | bytes 392 | tf_op jit(solution)/shard_map/ppermute | solution.py:14
  65.5 2.0 %collective-permute-done.12 = f32[32]{0:T(128)S(1)} collective-permute-done((f32[32]{0:T(128)S(1)}, f32[32]{0:T(128)S(1)}, u32[]{:S(2)}, u32[]{:S(2)}) %collective-permute-start.12) | collective-permute-done | bytes 160 | tf_op jit(solution)/shard_map/ppermute | solution.py:14
  67.5 0.1 slice_add_fusion.8
  67.6 0.1 pad_maximum_fusion.9
  67.7 0.7 collective-permute-start.13
  68.3 2.9 %collective-permute-done.13 = f32[32]{0:T(128)S(1)} collective-permute-done((f32[32]{0:T(128)S(1)}, f32[32]{0:T(128)S(1)}, u32[]{:S(2)}, u32[]{:S(2)}) %collective-permute-start.13) | collective-permute-done | bytes 160 | tf_op jit(solution)/shard_map/ppermute | solution.py:14
  71.2 0.1 slice_add_fusion.6
  71.3 0.0 collective-permute-start.14
  71.3 1.1 %collective-permute-done.14 = f32[16]{0:T(128)S(1)} collective-permute-done((f32[16]{0:T(128)S(1)}, f32[16]{0:T(128)S(1)}, u32[]{:S(2)}, u32[]{:S(2)}) %collective-permute-start.14) | collective-permute-done | bytes 96 | tf_op jit(solution)/shard_map/ppermute | solution.py:14
  72.4 0.5 collective-permute-start.15
  72.9 3.0 %collective-permute-done.15 = f32[16]{0:T(128)S(1)} collective-permute-done((f32[16]{0:T(128)S(1)}, f32[16]{0:T(128)S(1)}, u32[]{:S(2)}, u32[]{:S(2)}) %collective-permute-start.15) | collective-permute-done | bytes 96 | tf_op jit(solution)/shard_map/ppermute | solution.py:14
  76.0 1.7 %collective-permute-start.16 = (f32[16]{0:T(128)S(1)}, f32[16]{0:T(128)S(1)}, u32[]{:S(2)}, u32[]{:S(2)}) collective-permute-start(f32[16]{0:T(128)S(1)} %add.224), channel_id=1, source_target_pairs={{0,4},{1,5},{2,6},{3,7},{4,0},{5,1},{6,2},{7,3},{8,12},{9,13},{10,... | collective-permute-start | bytes 200 | tf_op jit(solution)/shard_map/ppermute | solution.py:14
  77.7 0.6 constant_dynamic-slice_fusion
  78.3 2.1 %collective-permute-done.16 = f32[16]{0:T(128)S(1)} collective-permute-done((f32[16]{0:T(128)S(1)}, f32[16]{0:T(128)S(1)}, u32[]{:S(2)}, u32[]{:S(2)}) %collective-permute-start.16) | collective-permute-done | bytes 96 | tf_op jit(solution)/shard_map/ppermute | solution.py:14
  80.4 0.5 multiply_sqrt_fusion
  (61 shorter events, 0.4 us)
Async XLA Ops:
  0.6 5.0 %copy-start = (f32[32,128]{1,0:T(8,128)S(1)}, f32[32,128]{1,0:T(8,128)}, u32[]{:S(2)}) copy-start(f32[32,128]{1,0:T(8,128)} %param.20) | copy-start | bytes 49156
  0.6 5.0 %copy-start.6 = (s32[16]{0:T(128)S(1)}, s32[16]{0:T(128)}, u32[]{:S(2)}) copy-start(s32[16]{0:T(128)} %param.21) | copy-start | bytes 196
  0.7 5.2 %copy-start.4 = (f32[2,128]{1,0:T(2,128)S(1)}, f32[2,128]{1,0:T(2,128)}, u32[]{:S(2)}) copy-start(f32[2,128]{1,0:T(2,128)} %param.16) | copy-start | bytes 3076
  0.7 9.6 %copy-start.8 = (s32[48]{0:T(128)S(1)}, s32[48]{0:T(128)}, u32[]{:S(2)}) copy-start(s32[48]{0:T(128)} %param.13) | copy-start | bytes 580
  0.7 9.6 %copy-start.7 = (s32[48]{0:T(128)S(1)}, s32[48]{0:T(128)}, u32[]{:S(2)}) copy-start(s32[48]{0:T(128)} %param.12) | copy-start | bytes 580
  0.7 9.7 %copy-start.2 = (f32[2,16,128]{2,1,0:T(8,128)S(1)}, f32[2,16,128]{2,1,0:T(8,128)}, u32[]{:S(2)}) copy-start(f32[2,16,128]{2,1,0:T(8,128)} %param.18) | copy-start | bytes 49156
  0.7 9.7 %copy-start.5 = (f32[2,128]{1,0:T(2,128)S(1)}, f32[2,128]{1,0:T(2,128)}, u32[]{:S(2)}) copy-start(f32[2,128]{1,0:T(2,128)} %param.17) | copy-start | bytes 3076
  7.3 4.5 %collective-permute-start = (f32[18]{0:T(128)S(1)}, f32[18]{0:T(128)S(1)}, u32[]{:S(2)}, u32[]{:S(2)}) collective-permute-start(f32[18]{0:T(128)S(1)} %pad_maximum_fusion.5), channel_id=1, source_target_pairs={{0,8},{8,0},{16,24},{24,16},{1,9},{9,1},{17,25},{25,17},{2,10},{10... | collective-permute-start | bytes 224 | tf_op jit(solution)/shard_map/ppermute | solution.py:14
  13.2 8.7 %collective-permute-start.1 = (f32[18]{0:T(128)S(1)}, f32[18]{0:T(128)S(1)}, u32[]{:S(2)}, u32[]{:S(2)}) collective-permute-start(f32[18]{0:T(128)S(1)} %fusion.92), channel_id=1, source_target_pairs={{0,16},{8,24},{16,0},{24,8},{1,17},{9,25},{17,1},{25,9},{2,18},{10... | collective-permute-start | bytes 224 | tf_op jit(solution)/shard_map/ppermute | solution.py:14
  15.2 5.6 %copy-start.1 = (f32[2,16,128]{2,1,0:T(8,128)S(1)}, f32[2,16,128]{2,1,0:T(8,128)}, u32[]{:S(2)}) copy-start(f32[2,16,128]{2,1,0:T(8,128)} %param.19) | copy-start | bytes 49156
  21.8 17.7 %copy-start.3 = (f32[2,128]{1,0:T(2,128)S(1)}, f32[2,128]{1,0:T(2,128)}, u32[]{:S(2)}) copy-start(f32[2,128]{1,0:T(2,128)} %param.15) | copy-start | bytes 3076
  21.9 1.3 %collective-permute-start.2 = (f32[16402]{0:T(1024)S(1)}, f32[16402]{0:T(1024)S(1)}, u32[]{:S(2)}, u32[]{:S(2)}) collective-permute-start(f32[16402]{0:T(1024)S(1)} %pad_maximum_fusion.1), channel_id=1, source_target_pairs={{0,1},{1,0},{2,3},{3,2},{4,5},{5,4},{6,7},{7,6},{8,9},{9,8},{10,11... | collective-permute-start | bytes 196832 | tf_op jit(solution)/shard_map/ppermute | solution.py:14
  23.4 4.7 %collective-permute-start.3 = (f32[22528]{0:T(1024)S(1)}, f32[22528]{0:T(1024)S(1)}, u32[]{:S(2)}, u32[]{:S(2)}) collective-permute-start(f32[22528]{0:T(1024)S(1)} %concatenate.48), channel_id=1, source_target_pairs={{0,2},{1,3},{2,0},{3,1},{4,6},{5,7},{6,4},{7,5},{8,10},{9,11},{10,... | collective-permute-start | bytes 270344 | tf_op jit(solution)/shard_map/ppermute | solution.py:14
  28.2 7.6 %collective-permute-start.4 = (f32[27648]{0:T(1024)S(1)}, f32[27648]{0:T(1024)S(1)}, u32[]{:S(2)}, u32[]{:S(2)}) collective-permute-start(f32[27648]{0:T(1024)S(1)} %concatenate.49), channel_id=1, source_target_pairs={{0,4},{1,5},{2,6},{3,7},{4,0},{5,1},{6,2},{7,3},{8,12},{9,13},{10,... | collective-permute-start | bytes 331784 | tf_op jit(solution)/shard_map/ppermute | solution.py:14
  37.8 1.4 %collective-permute-start.5 = (f32[36864]{0:T(1024)S(1)}, f32[36864]{0:T(1024)S(1)}, u32[]{:S(2)}, u32[]{:S(2)}) collective-permute-start(f32[36864]{0:T(1024)S(1)} %pad_maximum_fusion), channel_id=1, source_target_pairs={{0,1},{1,0},{2,3},{3,2},{4,5},{5,4},{6,7},{7,6},{8,9},{9,8},{10,11... | collective-permute-start | bytes 442376 | tf_op jit(solution)/shard_map/ppermute | solution.py:14
  41.2 3.5 %collective-permute-start.6 = (f32[32]{0:T(128)S(1)}, f32[32]{0:T(128)S(1)}, u32[]{:S(2)}, u32[]{:S(2)}) collective-permute-start(f32[32]{0:T(128)S(1)} %pad_maximum_fusion.6), channel_id=1, source_target_pairs={{0,8},{8,0},{16,24},{24,16},{1,9},{9,1},{17,25},{25,17},{2,10},{10... | collective-permute-start | bytes 392 | tf_op jit(solution)/shard_map/ppermute | solution.py:14
  44.9 3.5 %collective-permute-start.7 = (f32[32]{0:T(128)S(1)}, f32[32]{0:T(128)S(1)}, u32[]{:S(2)}, u32[]{:S(2)}) collective-permute-start(f32[32]{0:T(128)S(1)} %pad_maximum_fusion.7), channel_id=1, source_target_pairs={{0,16},{8,24},{16,0},{24,8},{1,17},{9,25},{17,1},{25,9},{2,18},{10... | collective-permute-start | bytes 392 | tf_op jit(solution)/shard_map/ppermute | solution.py:14
  48.5 1.3 %collective-permute-start.8 = (f32[16400]{0:T(1024)S(1)}, f32[16400]{0:T(1024)S(1)}, u32[]{:S(2)}, u32[]{:S(2)}) collective-permute-start(f32[16400]{0:T(1024)S(1)} %pad_maximum_fusion.2), channel_id=1, source_target_pairs={{0,1},{1,0},{2,3},{3,2},{4,5},{5,4},{6,7},{7,6},{8,9},{9,8},{10,11... | collective-permute-start | bytes 196808 | tf_op jit(solution)/shard_map/ppermute | solution.py:14
  49.8 4.4 %collective-permute-start.9 = (f32[16400]{0:T(1024)S(1)}, f32[16400]{0:T(1024)S(1)}, u32[]{:S(2)}, u32[]{:S(2)}) collective-permute-start(f32[16400]{0:T(1024)S(1)} %pad_maximum_fusion.3), channel_id=1, source_target_pairs={{0,2},{1,3},{2,0},{3,1},{4,6},{5,7},{6,4},{7,5},{8,10},{9,11},{10,... | collective-permute-start | bytes 196808 | tf_op jit(solution)/shard_map/ppermute | solution.py:14
  54.2 6.0 %collective-permute-start.10 = (f32[16400]{0:T(1024)S(1)}, f32[16400]{0:T(1024)S(1)}, u32[]{:S(2)}, u32[]{:S(2)}) collective-permute-start(f32[16400]{0:T(1024)S(1)} %pad_maximum_fusion.4), channel_id=1, source_target_pairs={{0,4},{1,5},{2,6},{3,7},{4,0},{5,1},{6,2},{7,3},{8,12},{9,13},{10,... | collective-permute-start | bytes 196808 | tf_op jit(solution)/shard_map/ppermute | solution.py:14
  60.2 1.3 %collective-permute-start.11 = (f32[16384]{0:T(1024)S(1)}, f32[16384]{0:T(1024)S(1)}, u32[]{:S(2)}, u32[]{:S(2)}) collective-permute-start(f32[16384]{0:T(1024)S(1)} %get-tuple-element.21), channel_id=1, source_target_pairs={{0,1},{1,0},{2,3},{3,2},{4,5},{5,4},{6,7},{7,6},{8,9},{9,8},{10,11... | collective-permute-start | bytes 196616 | tf_op jit(solution)/shard_map/ppermute | solution.py:14
  64.0 3.5 %collective-permute-start.12 = (f32[32]{0:T(128)S(1)}, f32[32]{0:T(128)S(1)}, u32[]{:S(2)}, u32[]{:S(2)}) collective-permute-start(f32[32]{0:T(128)S(1)} %pad_maximum_fusion.8), channel_id=1, source_target_pairs={{0,8},{8,0},{16,24},{24,16},{1,9},{9,1},{17,25},{25,17},{2,10},{10... | collective-permute-start | bytes 392 | tf_op jit(solution)/shard_map/ppermute | solution.py:14
  67.7 3.5 %collective-permute-start.13 = (f32[32]{0:T(128)S(1)}, f32[32]{0:T(128)S(1)}, u32[]{:S(2)}, u32[]{:S(2)}) collective-permute-start(f32[32]{0:T(128)S(1)} %pad_maximum_fusion.9), channel_id=1, source_target_pairs={{0,16},{8,24},{16,0},{24,8},{1,17},{9,25},{17,1},{25,9},{2,18},{10... | collective-permute-start | bytes 392 | tf_op jit(solution)/shard_map/ppermute | solution.py:14
  71.3 1.1 %collective-permute-start.14 = (f32[16]{0:T(128)S(1)}, f32[16]{0:T(128)S(1)}, u32[]{:S(2)}, u32[]{:S(2)}) collective-permute-start(f32[16]{0:T(128)S(1)} %slice_add_fusion.6), channel_id=1, source_target_pairs={{0,1},{1,0},{2,3},{3,2},{4,5},{5,4},{6,7},{7,6},{8,9},{9,8},{10,11... | collective-permute-start | bytes 200 | tf_op jit(solution)/shard_map/ppermute | solution.py:14
  72.4 3.5 %collective-permute-start.15 = (f32[16]{0:T(128)S(1)}, f32[16]{0:T(128)S(1)}, u32[]{:S(2)}, u32[]{:S(2)}) collective-permute-start(f32[16]{0:T(128)S(1)} %add.223), channel_id=1, source_target_pairs={{0,2},{1,3},{2,0},{3,1},{4,6},{5,7},{6,4},{7,5},{8,10},{9,11},{10,... | collective-permute-start | bytes 200 | tf_op jit(solution)/shard_map/ppermute | solution.py:14
  76.0 4.4 %collective-permute-start.16 = (f32[16]{0:T(128)S(1)}, f32[16]{0:T(128)S(1)}, u32[]{:S(2)}, u32[]{:S(2)}) collective-permute-start(f32[16]{0:T(128)S(1)} %add.224), channel_id=1, source_target_pairs={{0,4},{1,5},{2,6},{3,7},{4,0},{5,1},{6,2},{7,3},{8,12},{9,13},{10,... | collective-permute-start | bytes 200 | tf_op jit(solution)/shard_map/ppermute | solution.py:14

commit v17 on v16

--- a/solution.py
+++ b/solution.py
@@ -143,16 +143,22 @@
 
     norms = jnp.concatenate([local_a.reshape(1), local_c, local_b.reshape(1)])
     n_region = lax.axis_size("region")
+    by_row = place_live.reshape(region_blocks, row_blocks, ntiles).transpose(1, 0, 2)
+
+    def build(r, by_row):
+        return jnp.dot(by_row[r], tiles.reshape(ntiles, -1), precision=hp)
+
+    first = build(0, by_row)
     if _pow2(n_region) and n_region >= 2:
         norms = norms + _exchange(norms, "region", n_region, 0)
-        norms, place_live = lax.optimization_barrier((norms, place_live))
+        norms, by_row = lax.optimization_barrier((norms, by_row))
         for bit in range(1, n_region.bit_length() - 1):
             norms = norms + _exchange(norms, "region", n_region, bit)
     else:
         norms = lax.psum(norms, "region")
-    dense = jnp.dot(place_live, tiles.reshape(ntiles, -1), precision=hp)
-    dense = dense.reshape(region_blocks, row_blocks, tiles.shape[1], tiles.shape[2])
-    dense = dense.transpose(1, 2, 0, 3)
+    dense = jnp.stack([first] + [build(r, by_row) for r in range(1, row_blocks)])
+    dense = dense.reshape(row_blocks, region_blocks, tiles.shape[1], tiles.shape[2])
+    dense = dense.transpose(0, 2, 1, 3)
     own_rows = own_blocks * (scenarios + 2)
     own = jnp.concatenate(
         [

time: 81.2 us -> 82 us (level)
  matrix products: 11.5 us -> 13.8 us
    dot_general x1 -> x2, matrix products: 5.55 us -> 7.62 us  [build(): return jnp.dot(by_row[r], tiles.reshape(ntiles, -1), precision=hp)]
  transfers between devices with their start and end apart: 17 -> 17, of which waited for: 16 -> 16; matrix products, arithmetic and copies ran while one was open for 11% -> 10% of each run, Pallas kernels for 0% -> 0%
where the time goes in v17:
time: 82 us; the launch traced here: 81.8 us
  waiting for transfers between devices  35.9 us (44%)
  starting transfers between devices  18.6 us (23%)
  matrix products  13.8 us (17%)
  other arithmetic  8.72 us (11%)
  between operations  3.18 us (4%)
  local copies, waits for them, and re-layouts  1.64 us (2%)
    ppermute x17, waiting for transfers between devices, _exchange(): return lax.ppermute(x, axis, [(i, i ^ 1 << bit) for i in range(n)])  35.9 us
    ppermute x17, starting transfers between devices, _exchange(): return lax.ppermute(x, axis, [(i, i ^ 1 << bit) for i in range(n)])  18.6 us
    dot_general x2, matrix products, build(): return jnp.dot(by_row[r], tiles.reshape(ntiles, -1), precision=hp)  7.62 us
    dot_general x2, matrix products, product_of(): jnp.einsum('ricj,csj->rsi', dense, point, precision=lax.Precision.HIGH)  3.64 us
    reduce_sum x2, other arithmetic, local(): local_a = jnp.sum(jnp.sum(tiles * tiles, axis=(1, 2)) * live)  3.11 us
    dot_general x2, matrix products, transposed_product(): jnp.einsum('rsi,ricj->csj', dual, dense, precision=lax.Precision.HIGH)  2.31 us
  transfers between devices with their start and end apart: 17, of which 16 were waited for; matrix products, arithmetic and copies ran while one was open for 10% of the time, Pallas kernels for 0%

profile of v17, /device:TPU:0, one launch (start us, length us, event | category | flops | bytes accessed | tf_op | source)
XLA Modules:
  0.0 81.8 jit_solution(1092906537860274056)
XLA Ops:
  1.5 2.5 %multiply_reduce_fusion = f32[48]{0:T(128)S(1)} fusion(f32[48,128,128]{2,1,0:T(8,128)} %param.11), kind=kLoop, calls=%fused_computation.5 | loop fusion | flops 1572816 | bytes 3145920 | tf_op jit(solution)/shard_map/reduce_sum | solution.py:127
  4.0 0.6 multiply_reduce_fusion.6
  4.6 0.2 fusion.85
  4.8 0.1 multiply_reduce_fusion.5
  4.9 0.6 fusion.88
  5.5 1.4 %pad_maximum_fusion.5 = f32[18]{0:T(128)S(1)} fusion(f32[1]{0:T(128)} %bitcast.8, f32[16]{0:T(128)S(1)} %multiply_reduce_fusion.5, f32[1]{0:T(128)} %bitcast.7), kind=kLoop, calls=%fused_computation.116 | loop fusion | flops 36 | bytes 144 | tf_op jit(solution)/shard_map/concatenate | solution.py:144
  6.9 2.9 %collective-permute-start = (f32[18]{0:T(128)S(1)}, f32[18]{0:T(128)S(1)}, u32[]{:S(2)}, u32[]{:S(2)}) collective-permute-start(f32[18]{0:T(128)S(1)} %pad_maximum_fusion.5), channel_id=1, source_target_pairs={{0,8},{8,0},{16,24},{24,16},{1,9},{9,1},{17,25},{25,17},{2,10},{10... | collective-permute-start | bytes 224 | tf_op jit(solution)/shard_map/ppermute | solution.py:14
  9.9 0.1 compare_select_fusion
  10.0 4.3 %fusion.14 = f32[1,16,128,128]{3,1,2,0:T(8,128)} fusion(f32[2,16,48]{2,1,0:T(8,128)S(1)} %compare_select_fusion, f32[6,8,128,128]{3,2,1,0:T(8,128)S(1)} %bitcast.153), kind=kOutput, calls=%fused_computation.17 | convolution fusion | flops 150994944 | bytes 4202496 | tf_op jit(solution)/shard_map/dot_general | solution.py:149
  14.3 0.1 pad.32.clone
  14.4 0.1 fusion.80
  14.5 1.4 %fusion.101 = f32[18]{0:T(128)S(1)} fusion(f32[18]{0:T(128)S(1)} %collective-permute-done, f32[1]{0:T(128)} %bitcast.8, f32[16]{0:T(128)S(1)} %multiply_reduce_fusion.5, f32[1]{0:T(128)} %bitcast.7), kind=kLoop, calls=%fused_computation.148 | loop fusion | flops 54 | bytes 216 | tf_op jit(solution)/shard_map/add | solution.py:153
  15.8 3.3 %fusion.17 = f32[1,16,128,128]{3,1,2,0:T(8,128)S(1)} fusion(f32[2,16,48]{2,1,0:T(8,128)S(1)} %compare_select_fusion, f32[6,8,128,128]{3,2,1,0:T(8,128)S(1)} %bitcast.154), kind=kOutput, calls=%fused_computation.18 | convolution fusion | flops 150994944 | bytes 4202496 | tf_op jit(solution)/shard_map/dot_general | solution.py:149
  19.2 1.6 %collective-permute-start.1 = (f32[18]{0:T(128)S(1)}, f32[18]{0:T(128)S(1)}, u32[]{:S(2)}, u32[]{:S(2)}) collective-permute-start(f32[18]{0:T(128)S(1)} %fusion.101), channel_id=1, source_target_pairs={{0,16},{8,24},{16,0},{24,8},{1,17},{9,25},{17,1},{25,9},{2,18},{10... | collective-permute-start | bytes 224 | tf_op jit(solution)/shard_map/ppermute | solution.py:14
  20.8 0.1 maximum_bitcast_fusion
  20.9 1.1 %fusion.12 = f32[16,128,16,1]{1,2,3,0:T(8,128)S(1)} fusion(f32[2,128,16,128]{3,2,1,0:T(8,128)S(1)} %maximum_bitcast_fusion, f32[2,16,128]{2,1,0:T(8,128)S(1)} %copy-done.3), kind=kOutput, calls=%fused_computation.15 | convolution fusion | flops 50331648 | bytes 2244608 | tf_op jit(solution)/shard_map/rsi,ricj->csj/dot_general | solution.py:139
  22.0 0.8 collective-permute-done.1
  22.8 0.1 collective-permute-start.2
  22.9 1.2 %collective-permute-done.2 = f32[16402]{0:T(1024)S(1)} collective-permute-done((f32[16402]{0:T(1024)S(1)}, f32[16402]{0:T(1024)S(1)}, u32[]{:S(2)}, u32[]{:S(2)}) %collective-permute-start.2) | collective-permute-done | bytes 65640 | tf_op jit(solution)/shard_map/ppermute | solution.py:14
  24.2 0.1 concatenate.49
  24.2 1.6 %collective-permute-start.3 = (f32[22528]{0:T(1024)S(1)}, f32[22528]{0:T(1024)S(1)}, u32[]{:S(2)}, u32[]{:S(2)}) collective-permute-start(f32[22528]{0:T(1024)S(1)} %concatenate.49), channel_id=1, source_target_pairs={{0,2},{1,3},{2,0},{3,1},{4,6},{5,7},{6,4},{7,5},{8,10},{9,11},{10,... | collective-permute-start | bytes 270344 | tf_op jit(solution)/shard_map/ppermute | solution.py:14
  25.8 3.1 %collective-permute-done.3 = f32[22528]{0:T(1024)S(1)} collective-permute-done((f32[22528]{0:T(1024)S(1)}, f32[22528]{0:T(1024)S(1)}, u32[]{:S(2)}, u32[]{:S(2)}) %collective-permute-start.3) | collective-permute-done | bytes 90144 | tf_op jit(solution)/shard_map/ppermute | solution.py:14
  29.0 0.1 concatenate.50
  29.1 2.6 %collective-permute-start.4 = (f32[27648]{0:T(1024)S(1)}, f32[27648]{0:T(1024)S(1)}, u32[]{:S(2)}, u32[]{:S(2)}) collective-permute-start(f32[27648]{0:T(1024)S(1)} %concatenate.50), channel_id=1, source_target_pairs={{0,4},{1,5},{2,6},{3,7},{4,0},{5,1},{6,2},{7,3},{8,12},{9,13},{10,... | collective-permute-start | bytes 331784 | tf_op jit(solution)/shard_map/ppermute | solution.py:14
  31.7 5.0 %collective-permute-done.4 = f32[27648]{0:T(1024)S(1)} collective-permute-done((f32[27648]{0:T(1024)S(1)}, f32[27648]{0:T(1024)S(1)}, u32[]{:S(2)}, u32[]{:S(2)}) %collective-permute-start.4) | collective-permute-done | bytes 110624 | tf_op jit(solution)/shard_map/ppermute | solution.py:14
  36.6 0.6 fusion.99
  38.7 0.1 collective-permute-start.5
  38.8 0.1 broadcast_multiply_fusion.1
  38.9 1.3 %collective-permute-done.5 = f32[36864]{0:T(1024)S(1)} collective-permute-done((f32[36864]{0:T(1024)S(1)}, f32[36864]{0:T(1024)S(1)}, u32[]{:S(2)}, u32[]{:S(2)}) %collective-permute-start.5) | collective-permute-done | bytes 147488 | tf_op jit(solution)/shard_map/ppermute | solution.py:14
  40.2 0.2 multiply_reduce_fusion.2
  40.4 1.5 %multiply_reduce_fusion.4 = (f32[16]{0:T(128)S(1)}, f32[2,16,128]{2,1,0:T(8,128)S(1)}) fusion(f32[2,16,128]{2,1,0:T(8,128)S(1)} %copy-done.3, f32[2,128,16,128]{3,2,1,0:T(8,128)S(1)} %maximum_bitcast_fusion, f32[16,16,128]{2,1,0:T(8,128)S(1)} %bitcast.156, f32[16,16,128]{2,1,0:T(8,128)S(1)} %get-tuple-element.12, f32[2,128]{1,0:T(2,128)S(1)} %copy-done.5, ...), kind=kOutput, calls=%fused_computation.79 | convolution fusion | flops 50425840 | bytes 2393216 | tf_op jit(solution)/shard_map/ricj,csj->rsi/dot_general | solution.py:142
  42.0 0.1 pad_maximum_fusion.6
  42.0 0.7 collective-permute-start.6
  42.7 1.2 %fusion.10 = f32[16,128,16,1]{1,2,3,0:T(8,128)S(1)} fusion(f32[2,128,16,128]{3,2,1,0:T(8,128)S(1)} %maximum_bitcast_fusion, f32[2,16,128]{2,1,0:T(8,128)S(1)} %get-tuple-element.37), kind=kOutput, calls=%fused_computation.13 | convolution fusion | flops 50331648 | bytes 2244608 | tf_op jit(solution)/shard_map/rsi,ricj->csj/dot_general | solution.py:139
  44.0 1.6 %collective-permute-done.6 = f32[32]{0:T(128)S(1)} collective-permute-done((f32[32]{0:T(128)S(1)}, f32[32]{0:T(128)S(1)}, u32[]{:S(2)}, u32[]{:S(2)}) %collective-permute-start.6) | collective-permute-done | bytes 160 | tf_op jit(solution)/shard_map/ppermute | solution.py:14
  45.6 0.1 slice_add_fusion.11
  45.7 0.1 pad_maximum_fusion.7
  45.7 1.5 %collective-permute-start.7 = (f32[32]{0:T(128)S(1)}, f32[32]{0:T(128)S(1)}, u32[]{:S(2)}, u32[]{:S(2)}) collective-permute-start(f32[32]{0:T(128)S(1)} %pad_maximum_fusion.7), channel_id=1, source_target_pairs={{0,16},{8,24},{16,0},{24,8},{1,17},{9,25},{17,1},{25,9},{2,18},{10... | collective-permute-start | bytes 392 | tf_op jit(solution)/shard_map/ppermute | solution.py:14
  47.3 2.0 %collective-permute-done.7 = f32[32]{0:T(128)S(1)} collective-permute-done((f32[32]{0:T(128)S(1)}, f32[32]{0:T(128)S(1)}, u32[]{:S(2)}, u32[]{:S(2)}) %collective-permute-start.7) | collective-permute-done | bytes 160 | tf_op jit(solution)/shard_map/ppermute | solution.py:14
  49.3 0.1 slice_add_fusion.9
  49.4 1.2 %collective-permute-done.8 = f32[16400]{0:T(1024)S(1)} collective-permute-done((f32[16400]{0:T(1024)S(1)}, f32[16400]{0:T(1024)S(1)}, u32[]{:S(2)}, u32[]{:S(2)}) %collective-permute-start.8) | collective-permute-done | bytes 65632 | tf_op jit(solution)/shard_map/ppermute | solution.py:14
  50.7 0.7 collective-permute-start.9
  51.4 3.6 %collective-permute-done.9 = f32[16400]{0:T(1024)S(1)} collective-permute-done((f32[16400]{0:T(1024)S(1)}, f32[16400]{0:T(1024)S(1)}, u32[]{:S(2)}, u32[]{:S(2)}) %collective-permute-start.9) | collective-permute-done | bytes 65632 | tf_op jit(solution)/shard_map/ppermute | solution.py:14
  55.1 2.3 %collective-permute-start.10 = (f32[16400]{0:T(1024)S(1)}, f32[16400]{0:T(1024)S(1)}, u32[]{:S(2)}, u32[]{:S(2)}) collective-permute-start(f32[16400]{0:T(1024)S(1)} %pad_maximum_fusion.4), channel_id=1, source_target_pairs={{0,4},{1,5},{2,6},{3,7},{4,0},{5,1},{6,2},{7,3},{8,12},{9,13},{10,... | collective-permute-start | bytes 196808 | tf_op jit(solution)/shard_map/ppermute | solution.py:14
  57.4 3.7 %collective-permute-done.10 = f32[16400]{0:T(1024)S(1)} collective-permute-done((f32[16400]{0:T(1024)S(1)}, f32[16400]{0:T(1024)S(1)}, u32[]{:S(2)}, u32[]{:S(2)}) %collective-permute-start.10) | collective-permute-done | bytes 65632 | tf_op jit(solution)/shard_map/ppermute | solution.py:14
  61.1 0.1 collective-permute-start.11
  61.3 1.2 %collective-permute-done.11 = f32[16384]{0:T(1024)S(1)} collective-permute-done((f32[16384]{0:T(1024)S(1)}, f32[16384]{0:T(1024)S(1)}, u32[]{:S(2)}, u32[]{:S(2)}) %collective-permute-start.11) | collective-permute-done | bytes 65568 | tf_op jit(solution)/shard_map/ppermute | solution.py:14
  62.4 0.2 multiply_reduce_fusion.1
  62.7 2.1 %multiply_reduce_fusion.3 = (f32[16]{0:T(128)S(1)}, f32[2,16,128]{2,1,0:T(8,128)}) fusion(f32[2,16,128]{2,1,0:T(8,128)S(1)} %get-tuple-element.37, f32[2,128,16,128]{3,2,1,0:T(8,128)S(1)} %maximum_bitcast_fusion, f32[16,16,128]{2,1,0:T(8,128)S(1)} %get-tuple-element.12, f32[16,16,128]{2,1,0:T(8,128)S(1)} %get-tuple-element.8, f32[2,128]{1,0:T(2,128)S(1)} %copy-done.5, ...), kind=kOutput, calls=%fused_computation.78 | convolution fusion | flops 50425840 | bytes 2393216 | tf_op jit(solution)/shard_map/ricj,csj->rsi/dot_general | solution.py:142
  64.8 0.1 pad_maximum_fusion.8
  64.9 0.7 collective-permute-start.12
  65.6 2.9 %collective-permute-done.12 = f32[32]{0:T(128)S(1)} collective-permute-done((f32[32]{0:T(128)S(1)}, f32[32]{0:T(128)S(1)}, u32[]{:S(2)}, u32[]{:S(2)}) %collective-permute-start.12) | collective-permute-done | bytes 160 | tf_op jit(solution)/shard_map/ppermute | solution.py:14
  68.4 0.1 slice_add_fusion.8
  68.5 0.1 pad_maximum_fusion.9
  68.6 1.5 %collective-permute-start.13 = (f32[32]{0:T(128)S(1)}, f32[32]{0:T(128)S(1)}, u32[]{:S(2)}, u32[]{:S(2)}) collective-permute-start(f32[32]{0:T(128)S(1)} %pad_maximum_fusion.9), channel_id=1, source_target_pairs={{0,16},{8,24},{16,0},{24,8},{1,17},{9,25},{17,1},{25,9},{2,18},{10... | collective-permute-start | bytes 392 | tf_op jit(solution)/shard_map/ppermute | solution.py:14
  70.1 2.0 %collective-permute-done.13 = f32[32]{0:T(128)S(1)} collective-permute-done((f32[32]{0:T(128)S(1)}, f32[32]{0:T(128)S(1)}, u32[]{:S(2)}, u32[]{:S(2)}) %collective-permute-start.13) | collective-permute-done | bytes 160 | tf_op jit(solution)/shard_map/ppermute | solution.py:14
  72.1 0.1 slice_add_fusion.6
  72.2 1.1 %collective-permute-done.14 = f32[16]{0:T(128)S(1)} collective-permute-done((f32[16]{0:T(128)S(1)}, f32[16]{0:T(128)S(1)}, u32[]{:S(2)}, u32[]{:S(2)}) %collective-permute-start.14) | collective-permute-done | bytes 96 | tf_op jit(solution)/shard_map/ppermute | solution.py:14
  73.3 0.5 collective-permute-start.15
  73.8 3.1 %collective-permute-done.15 = f32[16]{0:T(128)S(1)} collective-permute-done((f32[16]{0:T(128)S(1)}, f32[16]{0:T(128)S(1)}, u32[]{:S(2)}, u32[]{:S(2)}) %collective-permute-start.15) | collective-permute-done | bytes 96 | tf_op jit(solution)/shard_map/ppermute | solution.py:14
  76.8 1.7 %collective-permute-start.16 = (f32[16]{0:T(128)S(1)}, f32[16]{0:T(128)S(1)}, u32[]{:S(2)}, u32[]{:S(2)}) collective-permute-start(f32[16]{0:T(128)S(1)} %add.229), channel_id=1, source_target_pairs={{0,4},{1,5},{2,6},{3,7},{4,0},{5,1},{6,2},{7,3},{8,12},{9,13},{10,... | collective-permute-start | bytes 200 | tf_op jit(solution)/shard_map/ppermute | solution.py:14
  78.5 0.6 constant_dynamic-slice_fusion
  79.1 2.1 %collective-permute-done.16 = f32[16]{0:T(128)S(1)} collective-permute-done((f32[16]{0:T(128)S(1)}, f32[16]{0:T(128)S(1)}, u32[]{:S(2)}, u32[]{:S(2)}) %collective-permute-start.16) | collective-permute-done | bytes 96 | tf_op jit(solution)/shard_map/ppermute | solution.py:14
  81.3 0.5 multiply_sqrt_fusion
  (68 shorter events, 0.5 us)
Async XLA Ops:
  0.6 4.0 %copy-start = (f32[32,128]{1,0:T(8,128)S(1)}, f32[32,128]{1,0:T(8,128)}, u32[]{:S(2)}) copy-start(f32[32,128]{1,0:T(8,128)} %param.20) | copy-start | bytes 49156
  0.6 9.3 %copy-start.1 = (f32[48,128,128]{2,1,0:T(8,128)S(1)}, f32[48,128,128]{2,1,0:T(8,128)}, u32[]{:S(2)}) copy-start(f32[48,128,128]{2,1,0:T(8,128)} %param.11) | copy-start | bytes 9437188
  0.7 3.3 %copy-start.5 = (f32[2,128]{1,0:T(2,128)S(1)}, f32[2,128]{1,0:T(2,128)}, u32[]{:S(2)}) copy-start(f32[2,128]{1,0:T(2,128)} %param.15) | copy-start | bytes 3076
  0.7 3.9 %copy-start.8 = (s32[16]{0:T(128)S(1)}, s32[16]{0:T(128)}, u32[]{:S(2)}) copy-start(s32[16]{0:T(128)} %param.21) | copy-start | bytes 196
  0.7 4.1 %copy-start.6 = (f32[2,128]{1,0:T(2,128)S(1)}, f32[2,128]{1,0:T(2,128)}, u32[]{:S(2)}) copy-start(f32[2,128]{1,0:T(2,128)} %param.16) | copy-start | bytes 3076
  0.7 9.2 %copy-start.9 = (s32[48]{0:T(128)S(1)}, s32[48]{0:T(128)}, u32[]{:S(2)}) copy-start(s32[48]{0:T(128)} %param.12) | copy-start | bytes 580
  0.7 9.2 %copy-start.10 = (s32[48]{0:T(128)S(1)}, s32[48]{0:T(128)}, u32[]{:S(2)}) copy-start(s32[48]{0:T(128)} %param.13) | copy-start | bytes 580
  6.9 7.6 %collective-permute-start = (f32[18]{0:T(128)S(1)}, f32[18]{0:T(128)S(1)}, u32[]{:S(2)}, u32[]{:S(2)}) collective-permute-start(f32[18]{0:T(128)S(1)} %pad_maximum_fusion.5), channel_id=1, source_target_pairs={{0,8},{8,0},{16,24},{24,16},{1,9},{9,1},{17,25},{25,17},{2,10},{10... | collective-permute-start | bytes 224 | tf_op jit(solution)/shard_map/ppermute | solution.py:14
  10.0 4.4 %copy-start.4 = (f32[2,16,128]{2,1,0:T(8,128)S(1)}, f32[2,16,128]{2,1,0:T(8,128)}, u32[]{:S(2)}) copy-start(f32[2,16,128]{2,1,0:T(8,128)} %param.18) | copy-start | bytes 49156
  10.0 4.4 %copy-start.7 = (f32[2,128]{1,0:T(2,128)S(1)}, f32[2,128]{1,0:T(2,128)}, u32[]{:S(2)}) copy-start(f32[2,128]{1,0:T(2,128)} %param.17) | copy-start | bytes 3076
  15.8 4.9 %copy-start.2 = (f32[1,16,128,128]{3,1,2,0:T(8,128)S(1)}, f32[1,16,128,128]{3,1,2,0:T(8,128)}, u32[]{:S(2)}) copy-start(f32[1,16,128,128]{3,1,2,0:T(8,128)} %fusion.14) | copy-start | bytes 3145732
  19.2 1.7 %copy-start.3 = (f32[2,16,128]{2,1,0:T(8,128)S(1)}, f32[2,16,128]{2,1,0:T(8,128)}, u32[]{:S(2)}) copy-start(f32[2,16,128]{2,1,0:T(8,128)} %param.19) | copy-start | bytes 49156
  19.2 3.6 %collective-permute-start.1 = (f32[18]{0:T(128)S(1)}, f32[18]{0:T(128)S(1)}, u32[]{:S(2)}, u32[]{:S(2)}) collective-permute-start(f32[18]{0:T(128)S(1)} %fusion.101), channel_id=1, source_target_pairs={{0,16},{8,24},{16,0},{24,8},{1,17},{9,25},{17,1},{25,9},{2,18},{10... | collective-permute-start | bytes 224 | tf_op jit(solution)/shard_map/ppermute | solution.py:14
  22.8 1.3 %collective-permute-start.2 = (f32[16402]{0:T(1024)S(1)}, f32[16402]{0:T(1024)S(1)}, u32[]{:S(2)}, u32[]{:S(2)}) collective-permute-start(f32[16402]{0:T(1024)S(1)} %pad_maximum_fusion.1), channel_id=1, source_target_pairs={{0,1},{1,0},{2,3},{3,2},{4,5},{5,4},{6,7},{7,6},{8,9},{9,8},{10,11... | collective-permute-start | bytes 196832 | tf_op jit(solution)/shard_map/ppermute | solution.py:14
  24.2 4.7 %collective-permute-start.3 = (f32[22528]{0:T(1024)S(1)}, f32[22528]{0:T(1024)S(1)}, u32[]{:S(2)}, u32[]{:S(2)}) collective-permute-start(f32[22528]{0:T(1024)S(1)} %concatenate.49), channel_id=1, source_target_pairs={{0,2},{1,3},{2,0},{3,1},{4,6},{5,7},{6,4},{7,5},{8,10},{9,11},{10,... | collective-permute-start | bytes 270344 | tf_op jit(solution)/shard_map/ppermute | solution.py:14
  29.1 7.6 %collective-permute-start.4 = (f32[27648]{0:T(1024)S(1)}, f32[27648]{0:T(1024)S(1)}, u32[]{:S(2)}, u32[]{:S(2)}) collective-permute-start(f32[27648]{0:T(1024)S(1)} %concatenate.50), channel_id=1, source_target_pairs={{0,4},{1,5},{2,6},{3,7},{4,0},{5,1},{6,2},{7,3},{8,12},{9,13},{10,... | collective-permute-start | bytes 331784 | tf_op jit(solution)/shard_map/ppermute | solution.py:14
  38.7 1.4 %collective-permute-start.5 = (f32[36864]{0:T(1024)S(1)}, f32[36864]{0:T(1024)S(1)}, u32[]{:S(2)}, u32[]{:S(2)}) collective-permute-start(f32[36864]{0:T(1024)S(1)} %pad_maximum_fusion), channel_id=1, source_target_pairs={{0,1},{1,0},{2,3},{3,2},{4,5},{5,4},{6,7},{7,6},{8,9},{9,8},{10,11... | collective-permute-start | bytes 442376 | tf_op jit(solution)/shard_map/ppermute | solution.py:14
  42.0 3.5 %collective-permute-start.6 = (f32[32]{0:T(128)S(1)}, f32[32]{0:T(128)S(1)}, u32[]{:S(2)}, u32[]{:S(2)}) collective-permute-start(f32[32]{0:T(128)S(1)} %pad_maximum_fusion.6), channel_id=1, source_target_pairs={{0,8},{8,0},{16,24},{24,16},{1,9},{9,1},{17,25},{25,17},{2,10},{10... | collective-permute-start | bytes 392 | tf_op jit(solution)/shard_map/ppermute | solution.py:14
  45.7 3.5 %collective-permute-start.7 = (f32[32]{0:T(128)S(1)}, f32[32]{0:T(128)S(1)}, u32[]{:S(2)}, u32[]{:S(2)}) collective-permute-start(f32[32]{0:T(128)S(1)} %pad_maximum_fusion.7), channel_id=1, source_target_pairs={{0,16},{8,24},{16,0},{24,8},{1,17},{9,25},{17,1},{25,9},{2,18},{10... | collective-permute-start | bytes 392 | tf_op jit(solution)/shard_map/ppermute | solution.py:14
  49.4 1.3 %collective-permute-start.8 = (f32[16400]{0:T(1024)S(1)}, f32[16400]{0:T(1024)S(1)}, u32[]{:S(2)}, u32[]{:S(2)}) collective-permute-start(f32[16400]{0:T(1024)S(1)} %pad_maximum_fusion.2), channel_id=1, source_target_pairs={{0,1},{1,0},{2,3},{3,2},{4,5},{5,4},{6,7},{7,6},{8,9},{9,8},{10,11... | collective-permute-start | bytes 196808 | tf_op jit(solution)/shard_map/ppermute | solution.py:14
  50.7 4.4 %collective-permute-start.9 = (f32[16400]{0:T(1024)S(1)}, f32[16400]{0:T(1024)S(1)}, u32[]{:S(2)}, u32[]{:S(2)}) collective-permute-start(f32[16400]{0:T(1024)S(1)} %pad_maximum_fusion.3), channel_id=1, source_target_pairs={{0,2},{1,3},{2,0},{3,1},{4,6},{5,7},{6,4},{7,5},{8,10},{9,11},{10,... | collective-permute-start | bytes 196808 | tf_op jit(solution)/shard_map/ppermute | solution.py:14
  55.1 6.0 %collective-permute-start.10 = (f32[16400]{0:T(1024)S(1)}, f32[16400]{0:T(1024)S(1)}, u32[]{:S(2)}, u32[]{:S(2)}) collective-permute-start(f32[16400]{0:T(1024)S(1)} %pad_maximum_fusion.4), channel_id=1, source_target_pairs={{0,4},{1,5},{2,6},{3,7},{4,0},{5,1},{6,2},{7,3},{8,12},{9,13},{10,... | collective-permute-start | bytes 196808 | tf_op jit(solution)/shard_map/ppermute | solution.py:14
  61.1 1.3 %collective-permute-start.11 = (f32[16384]{0:T(1024)S(1)}, f32[16384]{0:T(1024)S(1)}, u32[]{:S(2)}, u32[]{:S(2)}) collective-permute-start(f32[16384]{0:T(1024)S(1)} %get-tuple-element.21), channel_id=1, source_target_pairs={{0,1},{1,0},{2,3},{3,2},{4,5},{5,4},{6,7},{7,6},{8,9},{9,8},{10,11... | collective-permute-start | bytes 196616 | tf_op jit(solution)/shard_map/ppermute | solution.py:14
  64.9 3.5 %collective-permute-start.12 = (f32[32]{0:T(128)S(1)}, f32[32]{0:T(128)S(1)}, u32[]{:S(2)}, u32[]{:S(2)}) collective-permute-start(f32[32]{0:T(128)S(1)} %pad_maximum_fusion.8), channel_id=1, source_target_pairs={{0,8},{8,0},{16,24},{24,16},{1,9},{9,1},{17,25},{25,17},{2,10},{10... | collective-permute-start | bytes 392 | tf_op jit(solution)/shard_map/ppermute | solution.py:14
  68.6 3.5 %collective-permute-start.13 = (f32[32]{0:T(128)S(1)}, f32[32]{0:T(128)S(1)}, u32[]{:S(2)}, u32[]{:S(2)}) collective-permute-start(f32[32]{0:T(128)S(1)} %pad_maximum_fusion.9), channel_id=1, source_target_pairs={{0,16},{8,24},{16,0},{24,8},{1,17},{9,25},{17,1},{25,9},{2,18},{10... | collective-permute-start | bytes 392 | tf_op jit(solution)/shard_map/ppermute | solution.py:14
  72.2 1.1 %collective-permute-start.14 = (f32[16]{0:T(128)S(1)}, f32[16]{0:T(128)S(1)}, u32[]{:S(2)}, u32[]{:S(2)}) collective-permute-start(f32[16]{0:T(128)S(1)} %slice_add_fusion.6), channel_id=1, source_target_pairs={{0,1},{1,0},{2,3},{3,2},{4,5},{5,4},{6,7},{7,6},{8,9},{9,8},{10,11... | collective-permute-start | bytes 200 | tf_op jit(solution)/shard_map/ppermute | solution.py:14
  73.3 3.5 %collective-permute-start.15 = (f32[16]{0:T(128)S(1)}, f32[16]{0:T(128)S(1)}, u32[]{:S(2)}, u32[]{:S(2)}) collective-permute-start(f32[16]{0:T(128)S(1)} %add.228), channel_id=1, source_target_pairs={{0,2},{1,3},{2,0},{3,1},{4,6},{5,7},{6,4},{7,5},{8,10},{9,11},{10,... | collective-permute-start | bytes 200 | tf_op jit(solution)/shard_map/ppermute | solution.py:14
  76.8 4.4 %collective-permute-start.16 = (f32[16]{0:T(128)S(1)}, f32[16]{0:T(128)S(1)}, u32[]{:S(2)}, u32[]{:S(2)}) collective-permute-start(f32[16]{0:T(128)S(1)} %add.229), channel_id=1, source_target_pairs={{0,4},{1,5},{2,6},{3,7},{4,0},{5,1},{6,2},{7,3},{8,12},{9,13},{10,... | collective-permute-start | bytes 200 | tf_op jit(solution)/shard_map/ppermute | solution.py:14

commit v18 on v15

--- a/solution.py
+++ b/solution.py
@@ -124,9 +124,9 @@
     ).astype(jnp.float32)
     factor = jnp.dot(choose, price_levels, precision=hp)
     cost = base_cost[:, None, :] * factor[None, :, :]
-    local_a = jnp.sum(jnp.sum(tiles * tiles, axis=(1, 2)) * live)
+    local_a = jnp.sum(tiles * tiles * live[:, None, None], axis=(0, 1))
     local_c = jnp.sum(cost * cost, axis=(0, 2))
-    local_b = jnp.sum(rhs * rhs)
+    local_b = jnp.sum(rhs * rhs, axis=0)
     width = scenarios * lanes
 
     slot_cols = _slot(tile_cols // own_blocks, ncol) * own_blocks + tile_cols % own_blocks
@@ -144,7 +144,7 @@
     def product_of(point):
         return jnp.einsum("ricj,csj->rsi", dense, point, precision=lax.Precision.HIGH)
 
-    norms = jnp.concatenate([local_a.reshape(1), local_c, local_b.reshape(1)])
+    norms = jnp.concatenate([local_a, local_b, local_c])
     _, (norms,), _ = _rounds("region", [norms])
     own_rows = own_blocks * (scenarios + 2)
     own = jnp.concatenate(
@@ -158,7 +158,9 @@
     )
     partial_value = transposed_product(dual)
     grad, (norms,), gathered = _rounds("col", [norms], own, split=partial_value)
-    sq_a, sq_c, sq_b = norms[0], norms[1 : scenarios + 1], norms[scenarios + 1]
+    sq_a = jnp.sum(norms[:lanes])
+    sq_b = jnp.sum(norms[lanes : 2 * lanes])
+    sq_c = norms[2 * lanes :]
     primal_reg = gathered[:, : own_blocks * scenarios].reshape(region_blocks, scenarios, lanes)
     base_reg = gathered[:, own_blocks * scenarios : own_blocks * (scenarios + 1)]
     upper_reg = gathered[:, own_blocks * (scenarios + 1) : own_rows]

time: 81.5 us -> 78.1 us (0.958)
  other arithmetic: 9.04 us -> 6.1 us
    concatenate x1, other arithmetic: 1.37 us -> 0.01 us  [local(): norms = jnp.concatenate([local_a, local_b, local_c])]
    add x13, other arithmetic: 1.69 us -> 0.33 us  [_rounds(): new_sums.append(s + got[off:off + size].reshape(shape))]
where the time goes in v18:
time: 78.1 us; the launch traced here: 77.8 us
  waiting for transfers between devices  37.4 us (48%)
  starting transfers between devices  18.7 us (24%)
  matrix products  11.5 us (15%)
  other arithmetic  6.1 us (8%)
  between operations  3.07 us (4%)
  local copies, waits for them, and re-layouts  1.05 us (1%)
    ppermute x17, waiting for transfers between devices, _exchange(): return lax.ppermute(x, axis, [(i, i ^ 1 << bit) for i in range(n)])  37.4 us
    ppermute x17, starting transfers between devices, _exchange(): return lax.ppermute(x, axis, [(i, i ^ 1 << bit) for i in range(n)])  18.7 us
    dot_general x1, matrix products, local(): dense = jnp.dot(place_live, tiles.reshape(ntiles, -1), precision=hp)  5.56 us
    dot_general x2, matrix products, product_of(): jnp.einsum('ricj,csj->rsi', dense, point, precision=lax.Precision.HIGH)  3.64 us
    reduce_sum x1, other arithmetic, local(): local_a = jnp.sum(tiles * tiles * live[:, None, None], axis=(0, 1))  2.78 us
    dot_general x2, matrix products, transposed_product(): jnp.einsum('rsi,ricj->csj', dual, dense, precision=lax.Precision.HIGH)  2.13 us
  transfers between devices with their start and end apart: 17, of which 16 were waited for; matrix products, arithmetic and copies ran while one was open for 11% of the time, Pallas kernels for 0%

profile of v18, /device:TPU:0, one launch (start us, length us, event | category | flops | bytes accessed | tf_op | source)
XLA Modules:
  0.0 77.8 jit_solution(13571297350753689949)
XLA Ops:
  0.6 0.0 copy-start
  1.4 0.7 multiply_reduce_fusion.6
  2.1 2.8 %multiply_reduce_fusion = f32[128]{0:T(128)S(1)} fusion(f32[48,128,128]{2,1,0:T(8,128)} %param.11, f32[48]{0:T(128)S(1)} %compare_convert_fusion), kind=kLoop, calls=%fused_computation.4 | loop fusion | flops 2359168 | bytes 3146432 | tf_op jit(solution)/shard_map/reduce_sum | solution.py:127
  4.9 0.2 fusion.81
  5.1 0.0 copy-done.4
  5.1 0.1 multiply_reduce_fusion.5
  5.2 3.0 %collective-permute-start = (f32[272]{0:T(512)S(1)}, f32[272]{0:T(512)S(1)}, u32[]{:S(2)}, u32[]{:S(2)}) collective-permute-start(f32[272]{0:T(512)S(1)} %pad_maximum_fusion.5), channel_id=1, source_target_pairs={{0,8},{8,0},{16,24},{24,16},{1,9},{9,1},{17,25},{25,17},{2,10},{10... | collective-permute-start | bytes 3272 | tf_op jit(solution)/shard_map/ppermute | solution.py:14
  8.2 0.1 pad.30.clone
  8.3 5.6 %fusion.10 = f32[2,128,16,128]{3,2,1,0:T(8,128)S(1)} fusion(f32[48]{0:T(128)S(1)} %compare_convert_fusion, s32[16,2]{0,1:T(2,128)S(1)} %multiply_add_fusion, s32[48]{0:T(128)S(1)} %multiply_add_fusion.1, f32[6,8,128,128]{3,2,1,0:T(8,128)} %bitcast.138), kind=kOutput, calls=%fused_computation.13 | convolution fusion | flops 301992960 | bytes 5243392 | tf_op jit(solution)/shard_map/dot_general | solution.py:137
  13.9 0.0 copy-start.2
  13.9 0.0 copy-start.5
  13.9 1.1 %fusion.8 = f32[16,128,16,1]{1,2,3,0:T(8,128)S(1)} fusion(f32[2,128,16,128]{3,2,1,0:T(8,128)S(1)} %fusion.10, f32[2,16,128]{2,1,0:T(8,128)S(1)} %copy-done.1), kind=kOutput, calls=%fused_computation.11 | convolution fusion | flops 50331648 | bytes 2244608 | tf_op jit(solution)/shard_map/rsi,ricj->csj/dot_general | solution.py:142
  15.0 0.1 fusion.71
  15.1 0.0 collective-permute-done
  15.1 1.6 %collective-permute-start.1 = (f32[272]{0:T(512)S(1)}, f32[272]{0:T(512)S(1)}, u32[]{:S(2)}, u32[]{:S(2)}) collective-permute-start(f32[272]{0:T(512)S(1)} %fusion.89), channel_id=1, source_target_pairs={{0,16},{8,24},{16,0},{24,8},{1,17},{9,25},{17,1},{25,9},{2,18},{10... | collective-permute-start | bytes 3272 | tf_op jit(solution)/shard_map/ppermute | solution.py:14
  16.7 2.1 %collective-permute-done.1 = f32[272]{0:T(512)S(1)} collective-permute-done((f32[272]{0:T(512)S(1)}, f32[272]{0:T(512)S(1)}, u32[]{:S(2)}, u32[]{:S(2)}) %collective-permute-start.1) | collective-permute-done | bytes 1120 | tf_op jit(solution)/shard_map/ppermute | solution.py:14
  18.8 0.1 collective-permute-start.2
  18.9 1.2 %collective-permute-done.2 = f32[16656]{0:T(1024)S(1)} collective-permute-done((f32[16656]{0:T(1024)S(1)}, f32[16656]{0:T(1024)S(1)}, u32[]{:S(2)}, u32[]{:S(2)}) %collective-permute-start.2) | collective-permute-done | bytes 66656 | tf_op jit(solution)/shard_map/ppermute | solution.py:14
  20.2 0.1 concatenate.48
  20.2 1.6 %collective-permute-start.3 = (f32[22528]{0:T(1024)S(1)}, f32[22528]{0:T(1024)S(1)}, u32[]{:S(2)}, u32[]{:S(2)}) collective-permute-start(f32[22528]{0:T(1024)S(1)} %concatenate.48), channel_id=1, source_target_pairs={{0,2},{1,3},{2,0},{3,1},{4,6},{5,7},{6,4},{7,5},{8,10},{9,11},{10,... | collective-permute-start | bytes 270344 | tf_op jit(solution)/shard_map/ppermute | solution.py:14
  21.8 3.1 %collective-permute-done.3 = f32[22528]{0:T(1024)S(1)} collective-permute-done((f32[22528]{0:T(1024)S(1)}, f32[22528]{0:T(1024)S(1)}, u32[]{:S(2)}, u32[]{:S(2)}) %collective-permute-start.3) | collective-permute-done | bytes 90144 | tf_op jit(solution)/shard_map/ppermute | solution.py:14
  25.0 0.1 concatenate.49
  25.1 2.6 %collective-permute-start.4 = (f32[27648]{0:T(1024)S(1)}, f32[27648]{0:T(1024)S(1)}, u32[]{:S(2)}, u32[]{:S(2)}) collective-permute-start(f32[27648]{0:T(1024)S(1)} %concatenate.49), channel_id=1, source_target_pairs={{0,4},{1,5},{2,6},{3,7},{4,0},{5,1},{6,2},{7,3},{8,12},{9,13},{10,... | collective-permute-start | bytes 331784 | tf_op jit(solution)/shard_map/ppermute | solution.py:14
  27.7 5.0 %collective-permute-done.4 = f32[27648]{0:T(1024)S(1)} collective-permute-done((f32[27648]{0:T(1024)S(1)}, f32[27648]{0:T(1024)S(1)}, u32[]{:S(2)}, u32[]{:S(2)}) %collective-permute-start.4) | collective-permute-done | bytes 110624 | tf_op jit(solution)/shard_map/ppermute | solution.py:14
  32.6 0.6 slice_reduce_fusion
  34.7 0.1 collective-permute-start.5
  34.8 1.3 %collective-permute-done.5 = f32[36864]{0:T(1024)S(1)} collective-permute-done((f32[36864]{0:T(1024)S(1)}, f32[36864]{0:T(1024)S(1)}, u32[]{:S(2)}, u32[]{:S(2)}) %collective-permute-start.5) | collective-permute-done | bytes 147488 | tf_op jit(solution)/shard_map/ppermute | solution.py:14
  36.2 0.2 multiply_reduce_fusion.2
  36.5 1.5 %multiply_reduce_fusion.4 = (f32[16]{0:T(128)S(1)}, f32[2,16,128]{2,1,0:T(8,128)S(1)}) fusion(f32[2,16,128]{2,1,0:T(8,128)S(1)} %copy-done.1, f32[2,128,16,128]{3,2,1,0:T(8,128)S(1)} %fusion.10, f32[16,16,128]{2,1,0:T(8,128)S(1)} %bitcast.140, f32[16,16,128]{2,1,0:T(8,128)S(1)} %get-tuple-element.10, f32[2,128]{1,0:T(2,128)S(1)} %copy-done.3, ...), kind=kOutput, calls=%fused_computation.75 | convolution fusion | flops 50425840 | bytes 2393216 | tf_op jit(solution)/shard_map/ricj,csj->rsi/dot_general | solution.py:145
  38.0 0.1 pad_maximum_fusion.6
  38.1 0.7 collective-permute-start.6
  38.8 1.1 %fusion.6 = f32[16,128,16,1]{1,2,3,0:T(8,128)S(1)} fusion(f32[2,128,16,128]{3,2,1,0:T(8,128)S(1)} %fusion.10, f32[2,16,128]{2,1,0:T(8,128)S(1)} %get-tuple-element.33), kind=kOutput, calls=%fused_computation.9 | convolution fusion | flops 50331648 | bytes 2244608 | tf_op jit(solution)/shard_map/rsi,ricj->csj/dot_general | solution.py:142
  39.8 1.8 %collective-permute-done.6 = f32[32]{0:T(128)S(1)} collective-permute-done((f32[32]{0:T(128)S(1)}, f32[32]{0:T(128)S(1)}, u32[]{:S(2)}, u32[]{:S(2)}) %collective-permute-start.6) | collective-permute-done | bytes 160 | tf_op jit(solution)/shard_map/ppermute | solution.py:14
  41.6 0.1 slice_add_fusion.11
  41.7 0.1 pad_maximum_fusion.7
  41.8 1.5 %collective-permute-start.7 = (f32[32]{0:T(128)S(1)}, f32[32]{0:T(128)S(1)}, u32[]{:S(2)}, u32[]{:S(2)}) collective-permute-start(f32[32]{0:T(128)S(1)} %pad_maximum_fusion.7), channel_id=1, source_target_pairs={{0,16},{8,24},{16,0},{24,8},{1,17},{9,25},{17,1},{25,9},{2,18},{10... | collective-permute-start | bytes 392 | tf_op jit(solution)/shard_map/ppermute | solution.py:14
  43.3 2.0 %collective-permute-done.7 = f32[32]{0:T(128)S(1)} collective-permute-done((f32[32]{0:T(128)S(1)}, f32[32]{0:T(128)S(1)}, u32[]{:S(2)}, u32[]{:S(2)}) %collective-permute-start.7) | collective-permute-done | bytes 160 | tf_op jit(solution)/shard_map/ppermute | solution.py:14
  45.3 0.1 slice_add_fusion.9
  45.4 0.0 collective-permute-start.8
  45.4 1.2 %collective-permute-done.8 = f32[16400]{0:T(1024)S(1)} collective-permute-done((f32[16400]{0:T(1024)S(1)}, f32[16400]{0:T(1024)S(1)}, u32[]{:S(2)}, u32[]{:S(2)}) %collective-permute-start.8) | collective-permute-done | bytes 65632 | tf_op jit(solution)/shard_map/ppermute | solution.py:14
  46.7 0.7 collective-permute-start.9
  47.4 3.6 %collective-permute-done.9 = f32[16400]{0:T(1024)S(1)} collective-permute-done((f32[16400]{0:T(1024)S(1)}, f32[16400]{0:T(1024)S(1)}, u32[]{:S(2)}, u32[]{:S(2)}) %collective-permute-start.9) | collective-permute-done | bytes 65632 | tf_op jit(solution)/shard_map/ppermute | solution.py:14
  51.1 2.3 %collective-permute-start.10 = (f32[16400]{0:T(1024)S(1)}, f32[16400]{0:T(1024)S(1)}, u32[]{:S(2)}, u32[]{:S(2)}) collective-permute-start(f32[16400]{0:T(1024)S(1)} %pad_maximum_fusion.4), channel_id=1, source_target_pairs={{0,4},{1,5},{2,6},{3,7},{4,0},{5,1},{6,2},{7,3},{8,12},{9,13},{10,... | collective-permute-start | bytes 196808 | tf_op jit(solution)/shard_map/ppermute | solution.py:14
  53.4 3.7 %collective-permute-done.10 = f32[16400]{0:T(1024)S(1)} collective-permute-done((f32[16400]{0:T(1024)S(1)}, f32[16400]{0:T(1024)S(1)}, u32[]{:S(2)}, u32[]{:S(2)}) %collective-permute-start.10) | collective-permute-done | bytes 65632 | tf_op jit(solution)/shard_map/ppermute | solution.py:14
  57.1 0.1 collective-permute-start.11
  57.3 1.2 %collective-permute-done.11 = f32[16384]{0:T(1024)S(1)} collective-permute-done((f32[16384]{0:T(1024)S(1)}, f32[16384]{0:T(1024)S(1)}, u32[]{:S(2)}, u32[]{:S(2)}) %collective-permute-start.11) | collective-permute-done | bytes 65568 | tf_op jit(solution)/shard_map/ppermute | solution.py:14
  58.5 0.2 multiply_reduce_fusion.1
  58.7 2.1 %multiply_reduce_fusion.3 = (f32[16]{0:T(128)S(1)}, f32[2,16,128]{2,1,0:T(8,128)}) fusion(f32[2,16,128]{2,1,0:T(8,128)S(1)} %get-tuple-element.33, f32[2,128,16,128]{3,2,1,0:T(8,128)S(1)} %fusion.10, f32[16,16,128]{2,1,0:T(8,128)S(1)} %get-tuple-element.10, f32[16,16,128]{2,1,0:T(8,128)S(1)} %get-tuple-element.6, f32[2,128]{1,0:T(2,128)S(1)} %copy-done.3, ...), kind=kOutput, calls=%fused_computation.74 | convolution fusion | flops 50425840 | bytes 2393216 | tf_op jit(solution)/shard_map/ricj,csj->rsi/dot_general | solution.py:145
  60.8 0.1 pad_maximum_fusion.8
  60.9 0.7 collective-permute-start.12
  61.6 2.8 %collective-permute-done.12 = f32[32]{0:T(128)S(1)} collective-permute-done((f32[32]{0:T(128)S(1)}, f32[32]{0:T(128)S(1)}, u32[]{:S(2)}, u32[]{:S(2)}) %collective-permute-start.12) | collective-permute-done | bytes 160 | tf_op jit(solution)/shard_map/ppermute | solution.py:14
  64.4 0.1 slice_add_fusion.8
  64.5 0.1 pad_maximum_fusion.9
  64.6 1.5 %collective-permute-start.13 = (f32[32]{0:T(128)S(1)}, f32[32]{0:T(128)S(1)}, u32[]{:S(2)}, u32[]{:S(2)}) collective-permute-start(f32[32]{0:T(128)S(1)} %pad_maximum_fusion.9), channel_id=1, source_target_pairs={{0,16},{8,24},{16,0},{24,8},{1,17},{9,25},{17,1},{25,9},{2,18},{10... | collective-permute-start | bytes 392 | tf_op jit(solution)/shard_map/ppermute | solution.py:14
  66.1 2.0 %collective-permute-done.13 = f32[32]{0:T(128)S(1)} collective-permute-done((f32[32]{0:T(128)S(1)}, f32[32]{0:T(128)S(1)}, u32[]{:S(2)}, u32[]{:S(2)}) %collective-permute-start.13) | collective-permute-done | bytes 160 | tf_op jit(solution)/shard_map/ppermute | solution.py:14
  68.1 0.1 slice_add_fusion.6
  68.2 0.0 collective-permute-start.14
  68.2 1.1 %collective-permute-done.14 = f32[16]{0:T(128)S(1)} collective-permute-done((f32[16]{0:T(128)S(1)}, f32[16]{0:T(128)S(1)}, u32[]{:S(2)}, u32[]{:S(2)}) %collective-permute-start.14) | collective-permute-done | bytes 96 | tf_op jit(solution)/shard_map/ppermute | solution.py:14
  69.3 0.5 collective-permute-start.15
  69.8 3.1 %collective-permute-done.15 = f32[16]{0:T(128)S(1)} collective-permute-done((f32[16]{0:T(128)S(1)}, f32[16]{0:T(128)S(1)}, u32[]{:S(2)}, u32[]{:S(2)}) %collective-permute-start.15) | collective-permute-done | bytes 96 | tf_op jit(solution)/shard_map/ppermute | solution.py:14
  72.9 1.7 %collective-permute-start.16 = (f32[16]{0:T(128)S(1)}, f32[16]{0:T(128)S(1)}, u32[]{:S(2)}, u32[]{:S(2)}) collective-permute-start(f32[16]{0:T(128)S(1)} %add.228), channel_id=1, source_target_pairs={{0,4},{1,5},{2,6},{3,7},{4,0},{5,1},{6,2},{7,3},{8,12},{9,13},{10,... | collective-permute-start | bytes 200 | tf_op jit(solution)/shard_map/ppermute | solution.py:14
  74.5 0.6 constant_dynamic-slice_fusion
  75.2 2.1 %collective-permute-done.16 = f32[16]{0:T(128)S(1)} collective-permute-done((f32[16]{0:T(128)S(1)}, f32[16]{0:T(128)S(1)}, u32[]{:S(2)}, u32[]{:S(2)}) %collective-permute-start.16) | collective-permute-done | bytes 96 | tf_op jit(solution)/shard_map/ppermute | solution.py:14
  77.3 0.5 multiply_sqrt_fusion
  (60 shorter events, 0.4 us)
Async XLA Ops:
  0.6 4.2 %copy-start = (f32[32,128]{1,0:T(8,128)S(1)}, f32[32,128]{1,0:T(8,128)}, u32[]{:S(2)}) copy-start(f32[32,128]{1,0:T(8,128)} %param.20) | copy-start | bytes 49156
  0.6 4.2 %copy-start.6 = (s32[16]{0:T(128)S(1)}, s32[16]{0:T(128)}, u32[]{:S(2)}) copy-start(s32[16]{0:T(128)} %param.21) | copy-start | bytes 196
  0.7 4.4 %copy-start.4 = (f32[2,128]{1,0:T(2,128)S(1)}, f32[2,128]{1,0:T(2,128)}, u32[]{:S(2)}) copy-start(f32[2,128]{1,0:T(2,128)} %param.16) | copy-start | bytes 3076
  0.7 7.5 %copy-start.8 = (s32[48]{0:T(128)S(1)}, s32[48]{0:T(128)}, u32[]{:S(2)}) copy-start(s32[48]{0:T(128)} %param.13) | copy-start | bytes 580
  0.7 7.5 %copy-start.7 = (s32[48]{0:T(128)S(1)}, s32[48]{0:T(128)}, u32[]{:S(2)}) copy-start(s32[48]{0:T(128)} %param.12) | copy-start | bytes 580
  5.2 9.9 %collective-permute-start = (f32[272]{0:T(512)S(1)}, f32[272]{0:T(512)S(1)}, u32[]{:S(2)}, u32[]{:S(2)}) collective-permute-start(f32[272]{0:T(512)S(1)} %pad_maximum_fusion.5), channel_id=1, source_target_pairs={{0,8},{8,0},{16,24},{24,16},{1,9},{9,1},{17,25},{25,17},{2,10},{10... | collective-permute-start | bytes 3272 | tf_op jit(solution)/shard_map/ppermute | solution.py:14
  8.3 5.6 %copy-start.1 = (f32[2,16,128]{2,1,0:T(8,128)S(1)}, f32[2,16,128]{2,1,0:T(8,128)}, u32[]{:S(2)}) copy-start(f32[2,16,128]{2,1,0:T(8,128)} %param.19) | copy-start | bytes 49156
  13.9 1.1 %copy-start.2 = (f32[2,16,128]{2,1,0:T(8,128)S(1)}, f32[2,16,128]{2,1,0:T(8,128)}, u32[]{:S(2)}) copy-start(f32[2,16,128]{2,1,0:T(8,128)} %param.18) | copy-start | bytes 49156
  13.9 1.1 %copy-start.5 = (f32[2,128]{1,0:T(2,128)S(1)}, f32[2,128]{1,0:T(2,128)}, u32[]{:S(2)}) copy-start(f32[2,128]{1,0:T(2,128)} %param.17) | copy-start | bytes 3076
  15.0 21.5 %copy-start.3 = (f32[2,128]{1,0:T(2,128)S(1)}, f32[2,128]{1,0:T(2,128)}, u32[]{:S(2)}) copy-start(f32[2,128]{1,0:T(2,128)} %param.15) | copy-start | bytes 3076
  15.1 3.7 %collective-permute-start.1 = (f32[272]{0:T(512)S(1)}, f32[272]{0:T(512)S(1)}, u32[]{:S(2)}, u32[]{:S(2)}) collective-permute-start(f32[272]{0:T(512)S(1)} %fusion.89), channel_id=1, source_target_pairs={{0,16},{8,24},{16,0},{24,8},{1,17},{9,25},{17,1},{25,9},{2,18},{10... | collective-permute-start | bytes 3272 | tf_op jit(solution)/shard_map/ppermute | solution.py:14
  18.8 1.3 %collective-permute-start.2 = (f32[16656]{0:T(1024)S(1)}, f32[16656]{0:T(1024)S(1)}, u32[]{:S(2)}, u32[]{:S(2)}) collective-permute-start(f32[16656]{0:T(1024)S(1)} %pad_maximum_fusion.1), channel_id=1, source_target_pairs={{0,1},{1,0},{2,3},{3,2},{4,5},{5,4},{6,7},{7,6},{8,9},{9,8},{10,11... | collective-permute-start | bytes 199880 | tf_op jit(solution)/shard_map/ppermute | solution.py:14
  20.2 4.7 %collective-permute-start.3 = (f32[22528]{0:T(1024)S(1)}, f32[22528]{0:T(1024)S(1)}, u32[]{:S(2)}, u32[]{:S(2)}) collective-permute-start(f32[22528]{0:T(1024)S(1)} %concatenate.48), channel_id=1, source_target_pairs={{0,2},{1,3},{2,0},{3,1},{4,6},{5,7},{6,4},{7,5},{8,10},{9,11},{10,... | collective-permute-start | bytes 270344 | tf_op jit(solution)/shard_map/ppermute | solution.py:14
  25.1 7.6 %collective-permute-start.4 = (f32[27648]{0:T(1024)S(1)}, f32[27648]{0:T(1024)S(1)}, u32[]{:S(2)}, u32[]{:S(2)}) collective-permute-start(f32[27648]{0:T(1024)S(1)} %concatenate.49), channel_id=1, source_target_pairs={{0,4},{1,5},{2,6},{3,7},{4,0},{5,1},{6,2},{7,3},{8,12},{9,13},{10,... | collective-permute-start | bytes 331784 | tf_op jit(solution)/shard_map/ppermute | solution.py:14
  34.7 1.4 %collective-permute-start.5 = (f32[36864]{0:T(1024)S(1)}, f32[36864]{0:T(1024)S(1)}, u32[]{:S(2)}, u32[]{:S(2)}) collective-permute-start(f32[36864]{0:T(1024)S(1)} %pad_maximum_fusion), channel_id=1, source_target_pairs={{0,1},{1,0},{2,3},{3,2},{4,5},{5,4},{6,7},{7,6},{8,9},{9,8},{10,11... | collective-permute-start | bytes 442376 | tf_op jit(solution)/shard_map/ppermute | solution.py:14
  38.1 3.5 %collective-permute-start.6 = (f32[32]{0:T(128)S(1)}, f32[32]{0:T(128)S(1)}, u32[]{:S(2)}, u32[]{:S(2)}) collective-permute-start(f32[32]{0:T(128)S(1)} %pad_maximum_fusion.6), channel_id=1, source_target_pairs={{0,8},{8,0},{16,24},{24,16},{1,9},{9,1},{17,25},{25,17},{2,10},{10... | collective-permute-start | bytes 392 | tf_op jit(solution)/shard_map/ppermute | solution.py:14
  41.8 3.5 %collective-permute-start.7 = (f32[32]{0:T(128)S(1)}, f32[32]{0:T(128)S(1)}, u32[]{:S(2)}, u32[]{:S(2)}) collective-permute-start(f32[32]{0:T(128)S(1)} %pad_maximum_fusion.7), channel_id=1, source_target_pairs={{0,16},{8,24},{16,0},{24,8},{1,17},{9,25},{17,1},{25,9},{2,18},{10... | collective-permute-start | bytes 392 | tf_op jit(solution)/shard_map/ppermute | solution.py:14
  45.4 1.3 %collective-permute-start.8 = (f32[16400]{0:T(1024)S(1)}, f32[16400]{0:T(1024)S(1)}, u32[]{:S(2)}, u32[]{:S(2)}) collective-permute-start(f32[16400]{0:T(1024)S(1)} %pad_maximum_fusion.2), channel_id=1, source_target_pairs={{0,1},{1,0},{2,3},{3,2},{4,5},{5,4},{6,7},{7,6},{8,9},{9,8},{10,11... | collective-permute-start | bytes 196808 | tf_op jit(solution)/shard_map/ppermute | solution.py:14
  46.7 4.4 %collective-permute-start.9 = (f32[16400]{0:T(1024)S(1)}, f32[16400]{0:T(1024)S(1)}, u32[]{:S(2)}, u32[]{:S(2)}) collective-permute-start(f32[16400]{0:T(1024)S(1)} %pad_maximum_fusion.3), channel_id=1, source_target_pairs={{0,2},{1,3},{2,0},{3,1},{4,6},{5,7},{6,4},{7,5},{8,10},{9,11},{10,... | collective-permute-start | bytes 196808 | tf_op jit(solution)/shard_map/ppermute | solution.py:14
  51.1 6.0 %collective-permute-start.10 = (f32[16400]{0:T(1024)S(1)}, f32[16400]{0:T(1024)S(1)}, u32[]{:S(2)}, u32[]{:S(2)}) collective-permute-start(f32[16400]{0:T(1024)S(1)} %pad_maximum_fusion.4), channel_id=1, source_target_pairs={{0,4},{1,5},{2,6},{3,7},{4,0},{5,1},{6,2},{7,3},{8,12},{9,13},{10,... | collective-permute-start | bytes 196808 | tf_op jit(solution)/shard_map/ppermute | solution.py:14
  57.1 1.3 %collective-permute-start.11 = (f32[16384]{0:T(1024)S(1)}, f32[16384]{0:T(1024)S(1)}, u32[]{:S(2)}, u32[]{:S(2)}) collective-permute-start(f32[16384]{0:T(1024)S(1)} %get-tuple-element.19), channel_id=1, source_target_pairs={{0,1},{1,0},{2,3},{3,2},{4,5},{5,4},{6,7},{7,6},{8,9},{9,8},{10,11... | collective-permute-start | bytes 196616 | tf_op jit(solution)/shard_map/ppermute | solution.py:14
  60.9 3.5 %collective-permute-start.12 = (f32[32]{0:T(128)S(1)}, f32[32]{0:T(128)S(1)}, u32[]{:S(2)}, u32[]{:S(2)}) collective-permute-start(f32[32]{0:T(128)S(1)} %pad_maximum_fusion.8), channel_id=1, source_target_pairs={{0,8},{8,0},{16,24},{24,16},{1,9},{9,1},{17,25},{25,17},{2,10},{10... | collective-permute-start | bytes 392 | tf_op jit(solution)/shard_map/ppermute | solution.py:14
  64.6 3.5 %collective-permute-start.13 = (f32[32]{0:T(128)S(1)}, f32[32]{0:T(128)S(1)}, u32[]{:S(2)}, u32[]{:S(2)}) collective-permute-start(f32[32]{0:T(128)S(1)} %pad_maximum_fusion.9), channel_id=1, source_target_pairs={{0,16},{8,24},{16,0},{24,8},{1,17},{9,25},{17,1},{25,9},{2,18},{10... | collective-permute-start | bytes 392 | tf_op jit(solution)/shard_map/ppermute | solution.py:14
  68.2 1.1 %collective-permute-start.14 = (f32[16]{0:T(128)S(1)}, f32[16]{0:T(128)S(1)}, u32[]{:S(2)}, u32[]{:S(2)}) collective-permute-start(f32[16]{0:T(128)S(1)} %slice_add_fusion.6), channel_id=1, source_target_pairs={{0,1},{1,0},{2,3},{3,2},{4,5},{5,4},{6,7},{7,6},{8,9},{9,8},{10,11... | collective-permute-start | bytes 200 | tf_op jit(solution)/shard_map/ppermute | solution.py:14
  69.3 3.5 %collective-permute-start.15 = (f32[16]{0:T(128)S(1)}, f32[16]{0:T(128)S(1)}, u32[]{:S(2)}, u32[]{:S(2)}) collective-permute-start(f32[16]{0:T(128)S(1)} %add.227), channel_id=1, source_target_pairs={{0,2},{1,3},{2,0},{3,1},{4,6},{5,7},{6,4},{7,5},{8,10},{9,11},{10,... | collective-permute-start | bytes 200 | tf_op jit(solution)/shard_map/ppermute | solution.py:14
  72.9 4.4 %collective-permute-start.16 = (f32[16]{0:T(128)S(1)}, f32[16]{0:T(128)S(1)}, u32[]{:S(2)}, u32[]{:S(2)}) collective-permute-start(f32[16]{0:T(128)S(1)} %add.228), channel_id=1, source_target_pairs={{0,4},{1,5},{2,6},{3,7},{4,0},{5,1},{6,2},{7,3},{8,12},{9,13},{10,... | collective-permute-start | bytes 200 | tf_op jit(solution)/shard_map/ppermute | solution.py:14

commit v19 on v18

--- a/solution.py
+++ b/solution.py
@@ -158,8 +158,8 @@
     )
     partial_value = transposed_product(dual)
     grad, (norms,), gathered = _rounds("col", [norms], own, split=partial_value)
-    sq_a = jnp.sum(norms[:lanes])
-    sq_b = jnp.sum(norms[lanes : 2 * lanes])
+    sq_a = jnp.sum(jnp.broadcast_to(norms[:lanes], (scenarios, lanes)), axis=1)
+    sq_b = jnp.sum(jnp.broadcast_to(norms[lanes : 2 * lanes], (scenarios, lanes)), axis=1)
     sq_c = norms[2 * lanes :]
     primal_reg = gathered[:, : own_blocks * scenarios].reshape(region_blocks, scenarios, lanes)
     base_reg = gathered[:, own_blocks * scenarios : own_blocks * (scenarios + 1)]

time: 78.1 us -> 78.1 us (level)
  no operation moved by 1% of the time
where the time goes in v19:
time: 78.1 us; the launch traced here: 77.8 us
  waiting for transfers between devices  37.4 us (48%)
  starting transfers between devices  18.7 us (24%)
  matrix products  11.5 us (15%)
  other arithmetic  6.1 us (8%)
  between operations  3.07 us (4%)
  local copies, waits for them, and re-layouts  1.05 us (1%)
    ppermute x17, waiting for transfers between devices, _exchange(): return lax.ppermute(x, axis, [(i, i ^ 1 << bit) for i in range(n)])  37.4 us
    ppermute x17, starting transfers between devices, _exchange(): return lax.ppermute(x, axis, [(i, i ^ 1 << bit) for i in range(n)])  18.7 us
    dot_general x1, matrix products, local(): dense = jnp.dot(place_live, tiles.reshape(ntiles, -1), precision=hp)  5.56 us
    dot_general x2, matrix products, product_of(): jnp.einsum('ricj,csj->rsi', dense, point, precision=lax.Precision.HIGH)  3.64 us
    reduce_sum x1, other arithmetic, local(): local_a = jnp.sum(tiles * tiles * live[:, None, None], axis=(0, 1))  2.78 us
    dot_general x2, matrix products, transposed_product(): jnp.einsum('rsi,ricj->csj', dual, dense, precision=lax.Precision.HIGH)  2.13 us
  transfers between devices with their start and end apart: 17, of which 16 were waited for; matrix products, arithmetic and copies ran while one was open for 11% of the time, Pallas kernels for 0%

profile of v19, /device:TPU:0, one launch (start us, length us, event | category | flops | bytes accessed | tf_op | source)
XLA Modules:
  0.0 77.8 jit_solution(5134956902560779473)
XLA Ops:
  0.6 0.0 copy-start
  1.4 0.7 multiply_reduce_fusion.6
  2.1 2.8 %multiply_reduce_fusion = f32[128]{0:T(128)S(1)} fusion(f32[48,128,128]{2,1,0:T(8,128)} %param.11, f32[48]{0:T(128)S(1)} %compare_convert_fusion), kind=kLoop, calls=%fused_computation.4 | loop fusion | flops 2359168 | bytes 3146432 | tf_op jit(solution)/shard_map/reduce_sum | solution.py:127
  4.9 0.2 fusion.81
  5.1 0.0 copy-done.4
  5.1 0.1 multiply_reduce_fusion.5
  5.2 3.0 %collective-permute-start = (f32[272]{0:T(512)S(1)}, f32[272]{0:T(512)S(1)}, u32[]{:S(2)}, u32[]{:S(2)}) collective-permute-start(f32[272]{0:T(512)S(1)} %pad_maximum_fusion.5), channel_id=1, source_target_pairs={{0,8},{8,0},{16,24},{24,16},{1,9},{9,1},{17,25},{25,17},{2,10},{10... | collective-permute-start | bytes 3272 | tf_op jit(solution)/shard_map/ppermute | solution.py:14
  8.2 0.1 pad.30.clone
  8.3 5.6 %fusion.10 = f32[2,128,16,128]{3,2,1,0:T(8,128)S(1)} fusion(f32[48]{0:T(128)S(1)} %compare_convert_fusion, s32[16,2]{0,1:T(2,128)S(1)} %multiply_add_fusion, s32[48]{0:T(128)S(1)} %multiply_add_fusion.1, f32[6,8,128,128]{3,2,1,0:T(8,128)} %bitcast.138), kind=kOutput, calls=%fused_computation.13 | convolution fusion | flops 301992960 | bytes 5243392 | tf_op jit(solution)/shard_map/dot_general | solution.py:137
  13.9 0.0 copy-start.2
  13.9 0.0 copy-start.5
  13.9 1.1 %fusion.8 = f32[16,128,16,1]{1,2,3,0:T(8,128)S(1)} fusion(f32[2,128,16,128]{3,2,1,0:T(8,128)S(1)} %fusion.10, f32[2,16,128]{2,1,0:T(8,128)S(1)} %copy-done.1), kind=kOutput, calls=%fused_computation.11 | convolution fusion | flops 50331648 | bytes 2244608 | tf_op jit(solution)/shard_map/rsi,ricj->csj/dot_general | solution.py:142
  15.0 0.1 fusion.71
  15.1 0.0 collective-permute-done
  15.1 1.6 %collective-permute-start.1 = (f32[272]{0:T(512)S(1)}, f32[272]{0:T(512)S(1)}, u32[]{:S(2)}, u32[]{:S(2)}) collective-permute-start(f32[272]{0:T(512)S(1)} %fusion.89), channel_id=1, source_target_pairs={{0,16},{8,24},{16,0},{24,8},{1,17},{9,25},{17,1},{25,9},{2,18},{10... | collective-permute-start | bytes 3272 | tf_op jit(solution)/shard_map/ppermute | solution.py:14
  16.7 2.1 %collective-permute-done.1 = f32[272]{0:T(512)S(1)} collective-permute-done((f32[272]{0:T(512)S(1)}, f32[272]{0:T(512)S(1)}, u32[]{:S(2)}, u32[]{:S(2)}) %collective-permute-start.1) | collective-permute-done | bytes 1120 | tf_op jit(solution)/shard_map/ppermute | solution.py:14
  18.8 0.1 collective-permute-start.2
  18.9 1.2 %collective-permute-done.2 = f32[16656]{0:T(1024)S(1)} collective-permute-done((f32[16656]{0:T(1024)S(1)}, f32[16656]{0:T(1024)S(1)}, u32[]{:S(2)}, u32[]{:S(2)}) %collective-permute-start.2) | collective-permute-done | bytes 66656 | tf_op jit(solution)/shard_map/ppermute | solution.py:14
  20.2 0.1 concatenate.48
  20.2 1.6 %collective-permute-start.3 = (f32[22528]{0:T(1024)S(1)}, f32[22528]{0:T(1024)S(1)}, u32[]{:S(2)}, u32[]{:S(2)}) collective-permute-start(f32[22528]{0:T(1024)S(1)} %concatenate.48), channel_id=1, source_target_pairs={{0,2},{1,3},{2,0},{3,1},{4,6},{5,7},{6,4},{7,5},{8,10},{9,11},{10,... | collective-permute-start | bytes 270344 | tf_op jit(solution)/shard_map/ppermute | solution.py:14
  21.8 3.1 %collective-permute-done.3 = f32[22528]{0:T(1024)S(1)} collective-permute-done((f32[22528]{0:T(1024)S(1)}, f32[22528]{0:T(1024)S(1)}, u32[]{:S(2)}, u32[]{:S(2)}) %collective-permute-start.3) | collective-permute-done | bytes 90144 | tf_op jit(solution)/shard_map/ppermute | solution.py:14
  25.0 0.1 concatenate.49
  25.1 2.6 %collective-permute-start.4 = (f32[27648]{0:T(1024)S(1)}, f32[27648]{0:T(1024)S(1)}, u32[]{:S(2)}, u32[]{:S(2)}) collective-permute-start(f32[27648]{0:T(1024)S(1)} %concatenate.49), channel_id=1, source_target_pairs={{0,4},{1,5},{2,6},{3,7},{4,0},{5,1},{6,2},{7,3},{8,12},{9,13},{10,... | collective-permute-start | bytes 331784 | tf_op jit(solution)/shard_map/ppermute | solution.py:14
  27.7 5.0 %collective-permute-done.4 = f32[27648]{0:T(1024)S(1)} collective-permute-done((f32[27648]{0:T(1024)S(1)}, f32[27648]{0:T(1024)S(1)}, u32[]{:S(2)}, u32[]{:S(2)}) %collective-permute-start.4) | collective-permute-done | bytes 110624 | tf_op jit(solution)/shard_map/ppermute | solution.py:14
  32.6 0.6 slice_reduce_fusion.1
  34.7 0.1 collective-permute-start.5
  34.8 1.3 %collective-permute-done.5 = f32[36864]{0:T(1024)S(1)} collective-permute-done((f32[36864]{0:T(1024)S(1)}, f32[36864]{0:T(1024)S(1)}, u32[]{:S(2)}, u32[]{:S(2)}) %collective-permute-start.5) | collective-permute-done | bytes 147488 | tf_op jit(solution)/shard_map/ppermute | solution.py:14
  36.2 0.2 multiply_reduce_fusion.2
  36.5 1.5 %multiply_reduce_fusion.4 = (f32[16]{0:T(128)S(1)}, f32[2,16,128]{2,1,0:T(8,128)S(1)}) fusion(f32[2,16,128]{2,1,0:T(8,128)S(1)} %copy-done.1, f32[2,128,16,128]{3,2,1,0:T(8,128)S(1)} %fusion.10, f32[16,16,128]{2,1,0:T(8,128)S(1)} %bitcast.140, f32[16,16,128]{2,1,0:T(8,128)S(1)} %get-tuple-element.10, f32[2,128]{1,0:T(2,128)S(1)} %copy-done.3, ...), kind=kOutput, calls=%fused_computation.75 | convolution fusion | flops 50425840 | bytes 2393216 | tf_op jit(solution)/shard_map/ricj,csj->rsi/dot_general | solution.py:145
  38.0 0.1 pad_maximum_fusion.6
  38.1 0.7 collective-permute-start.6
  38.8 1.1 %fusion.6 = f32[16,128,16,1]{1,2,3,0:T(8,128)S(1)} fusion(f32[2,128,16,128]{3,2,1,0:T(8,128)S(1)} %fusion.10, f32[2,16,128]{2,1,0:T(8,128)S(1)} %get-tuple-element.32), kind=kOutput, calls=%fused_computation.9 | convolution fusion | flops 50331648 | bytes 2244608 | tf_op jit(solution)/shard_map/rsi,ricj->csj/dot_general | solution.py:142
  39.8 1.8 %collective-permute-done.6 = f32[32]{0:T(128)S(1)} collective-permute-done((f32[32]{0:T(128)S(1)}, f32[32]{0:T(128)S(1)}, u32[]{:S(2)}, u32[]{:S(2)}) %collective-permute-start.6) | collective-permute-done | bytes 160 | tf_op jit(solution)/shard_map/ppermute | solution.py:14
  41.6 0.1 slice_add_fusion.11
  41.7 0.1 pad_maximum_fusion.7
  41.8 1.5 %collective-permute-start.7 = (f32[32]{0:T(128)S(1)}, f32[32]{0:T(128)S(1)}, u32[]{:S(2)}, u32[]{:S(2)}) collective-permute-start(f32[32]{0:T(128)S(1)} %pad_maximum_fusion.7), channel_id=1, source_target_pairs={{0,16},{8,24},{16,0},{24,8},{1,17},{9,25},{17,1},{25,9},{2,18},{10... | collective-permute-start | bytes 392 | tf_op jit(solution)/shard_map/ppermute | solution.py:14
  43.3 2.0 %collective-permute-done.7 = f32[32]{0:T(128)S(1)} collective-permute-done((f32[32]{0:T(128)S(1)}, f32[32]{0:T(128)S(1)}, u32[]{:S(2)}, u32[]{:S(2)}) %collective-permute-start.7) | collective-permute-done | bytes 160 | tf_op jit(solution)/shard_map/ppermute | solution.py:14
  45.3 0.1 slice_add_fusion.9
  45.4 0.0 collective-permute-start.8
  45.4 1.2 %collective-permute-done.8 = f32[16400]{0:T(1024)S(1)} collective-permute-done((f32[16400]{0:T(1024)S(1)}, f32[16400]{0:T(1024)S(1)}, u32[]{:S(2)}, u32[]{:S(2)}) %collective-permute-start.8) | collective-permute-done | bytes 65632 | tf_op jit(solution)/shard_map/ppermute | solution.py:14
  46.7 0.7 collective-permute-start.9
  47.4 3.6 %collective-permute-done.9 = f32[16400]{0:T(1024)S(1)} collective-permute-done((f32[16400]{0:T(1024)S(1)}, f32[16400]{0:T(1024)S(1)}, u32[]{:S(2)}, u32[]{:S(2)}) %collective-permute-start.9) | collective-permute-done | bytes 65632 | tf_op jit(solution)/shard_map/ppermute | solution.py:14
  51.1 2.3 %collective-permute-start.10 = (f32[16400]{0:T(1024)S(1)}, f32[16400]{0:T(1024)S(1)}, u32[]{:S(2)}, u32[]{:S(2)}) collective-permute-start(f32[16400]{0:T(1024)S(1)} %pad_maximum_fusion.4), channel_id=1, source_target_pairs={{0,4},{1,5},{2,6},{3,7},{4,0},{5,1},{6,2},{7,3},{8,12},{9,13},{10,... | collective-permute-start | bytes 196808 | tf_op jit(solution)/shard_map/ppermute | solution.py:14
  53.4 3.7 %collective-permute-done.10 = f32[16400]{0:T(1024)S(1)} collective-permute-done((f32[16400]{0:T(1024)S(1)}, f32[16400]{0:T(1024)S(1)}, u32[]{:S(2)}, u32[]{:S(2)}) %collective-permute-start.10) | collective-permute-done | bytes 65632 | tf_op jit(solution)/shard_map/ppermute | solution.py:14
  57.1 0.1 collective-permute-start.11
  57.3 1.2 %collective-permute-done.11 = f32[16384]{0:T(1024)S(1)} collective-permute-done((f32[16384]{0:T(1024)S(1)}, f32[16384]{0:T(1024)S(1)}, u32[]{:S(2)}, u32[]{:S(2)}) %collective-permute-start.11) | collective-permute-done | bytes 65568 | tf_op jit(solution)/shard_map/ppermute | solution.py:14
  58.5 0.2 multiply_reduce_fusion.1
  58.7 2.1 %multiply_reduce_fusion.3 = (f32[16]{0:T(128)S(1)}, f32[2,16,128]{2,1,0:T(8,128)}) fusion(f32[2,16,128]{2,1,0:T(8,128)S(1)} %get-tuple-element.32, f32[2,128,16,128]{3,2,1,0:T(8,128)S(1)} %fusion.10, f32[16,16,128]{2,1,0:T(8,128)S(1)} %get-tuple-element.10, f32[16,16,128]{2,1,0:T(8,128)S(1)} %get-tuple-element.6, f32[2,128]{1,0:T(2,128)S(1)} %copy-done.3, ...), kind=kOutput, calls=%fused_computation.74 | convolution fusion | flops 50425840 | bytes 2393216 | tf_op jit(solution)/shard_map/ricj,csj->rsi/dot_general | solution.py:145
  60.8 0.1 pad_maximum_fusion.8
  60.9 0.7 collective-permute-start.12
  61.6 2.8 %collective-permute-done.12 = f32[32]{0:T(128)S(1)} collective-permute-done((f32[32]{0:T(128)S(1)}, f32[32]{0:T(128)S(1)}, u32[]{:S(2)}, u32[]{:S(2)}) %collective-permute-start.12) | collective-permute-done | bytes 160 | tf_op jit(solution)/shard_map/ppermute | solution.py:14
  64.4 0.1 slice_add_fusion.8
  64.5 0.1 pad_maximum_fusion.9
  64.6 1.5 %collective-permute-start.13 = (f32[32]{0:T(128)S(1)}, f32[32]{0:T(128)S(1)}, u32[]{:S(2)}, u32[]{:S(2)}) collective-permute-start(f32[32]{0:T(128)S(1)} %pad_maximum_fusion.9), channel_id=1, source_target_pairs={{0,16},{8,24},{16,0},{24,8},{1,17},{9,25},{17,1},{25,9},{2,18},{10... | collective-permute-start | bytes 392 | tf_op jit(solution)/shard_map/ppermute | solution.py:14
  66.1 2.0 %collective-permute-done.13 = f32[32]{0:T(128)S(1)} collective-permute-done((f32[32]{0:T(128)S(1)}, f32[32]{0:T(128)S(1)}, u32[]{:S(2)}, u32[]{:S(2)}) %collective-permute-start.13) | collective-permute-done | bytes 160 | tf_op jit(solution)/shard_map/ppermute | solution.py:14
  68.1 0.1 slice_add_fusion.6
  68.2 0.0 collective-permute-start.14
  68.2 1.1 %collective-permute-done.14 = f32[16]{0:T(128)S(1)} collective-permute-done((f32[16]{0:T(128)S(1)}, f32[16]{0:T(128)S(1)}, u32[]{:S(2)}, u32[]{:S(2)}) %collective-permute-start.14) | collective-permute-done | bytes 96 | tf_op jit(solution)/shard_map/ppermute | solution.py:14
  69.3 0.5 collective-permute-start.15
  69.8 3.1 %collective-permute-done.15 = f32[16]{0:T(128)S(1)} collective-permute-done((f32[16]{0:T(128)S(1)}, f32[16]{0:T(128)S(1)}, u32[]{:S(2)}, u32[]{:S(2)}) %collective-permute-start.15) | collective-permute-done | bytes 96 | tf_op jit(solution)/shard_map/ppermute | solution.py:14
  72.9 1.7 %collective-permute-start.16 = (f32[16]{0:T(128)S(1)}, f32[16]{0:T(128)S(1)}, u32[]{:S(2)}, u32[]{:S(2)}) collective-permute-start(f32[16]{0:T(128)S(1)} %add.228), channel_id=1, source_target_pairs={{0,4},{1,5},{2,6},{3,7},{4,0},{5,1},{6,2},{7,3},{8,12},{9,13},{10,... | collective-permute-start | bytes 200 | tf_op jit(solution)/shard_map/ppermute | solution.py:14
  74.5 0.6 constant_dynamic-slice_fusion
  75.2 2.1 %collective-permute-done.16 = f32[16]{0:T(128)S(1)} collective-permute-done((f32[16]{0:T(128)S(1)}, f32[16]{0:T(128)S(1)}, u32[]{:S(2)}, u32[]{:S(2)}) %collective-permute-start.16) | collective-permute-done | bytes 96 | tf_op jit(solution)/shard_map/ppermute | solution.py:14
  77.3 0.5 multiply_sqrt_fusion
  (61 shorter events, 0.4 us)
Async XLA Ops:
  0.6 4.2 %copy-start = (f32[32,128]{1,0:T(8,128)S(1)}, f32[32,128]{1,0:T(8,128)}, u32[]{:S(2)}) copy-start(f32[32,128]{1,0:T(8,128)} %param.20) | copy-start | bytes 49156
  0.6 4.2 %copy-start.6 = (s32[16]{0:T(128)S(1)}, s32[16]{0:T(128)}, u32[]{:S(2)}) copy-start(s32[16]{0:T(128)} %param.21) | copy-start | bytes 196
  0.7 4.4 %copy-start.4 = (f32[2,128]{1,0:T(2,128)S(1)}, f32[2,128]{1,0:T(2,128)}, u32[]{:S(2)}) copy-start(f32[2,128]{1,0:T(2,128)} %param.16) | copy-start | bytes 3076
  0.7 7.5 %copy-start.8 = (s32[48]{0:T(128)S(1)}, s32[48]{0:T(128)}, u32[]{:S(2)}) copy-start(s32[48]{0:T(128)} %param.13) | copy-start | bytes 580
  0.7 7.5 %copy-start.7 = (s32[48]{0:T(128)S(1)}, s32[48]{0:T(128)}, u32[]{:S(2)}) copy-start(s32[48]{0:T(128)} %param.12) | copy-start | bytes 580
  5.2 9.9 %collective-permute-start = (f32[272]{0:T(512)S(1)}, f32[272]{0:T(512)S(1)}, u32[]{:S(2)}, u32[]{:S(2)}) collective-permute-start(f32[272]{0:T(512)S(1)} %pad_maximum_fusion.5), channel_id=1, source_target_pairs={{0,8},{8,0},{16,24},{24,16},{1,9},{9,1},{17,25},{25,17},{2,10},{10... | collective-permute-start | bytes 3272 | tf_op jit(solution)/shard_map/ppermute | solution.py:14
  8.3 5.6 %copy-start.1 = (f32[2,16,128]{2,1,0:T(8,128)S(1)}, f32[2,16,128]{2,1,0:T(8,128)}, u32[]{:S(2)}) copy-start(f32[2,16,128]{2,1,0:T(8,128)} %param.19) | copy-start | bytes 49156
  13.9 1.1 %copy-start.2 = (f32[2,16,128]{2,1,0:T(8,128)S(1)}, f32[2,16,128]{2,1,0:T(8,128)}, u32[]{:S(2)}) copy-start(f32[2,16,128]{2,1,0:T(8,128)} %param.18) | copy-start | bytes 49156
  13.9 1.1 %copy-start.5 = (f32[2,128]{1,0:T(2,128)S(1)}, f32[2,128]{1,0:T(2,128)}, u32[]{:S(2)}) copy-start(f32[2,128]{1,0:T(2,128)} %param.17) | copy-start | bytes 3076
  15.0 21.5 %copy-start.3 = (f32[2,128]{1,0:T(2,128)S(1)}, f32[2,128]{1,0:T(2,128)}, u32[]{:S(2)}) copy-start(f32[2,128]{1,0:T(2,128)} %param.15) | copy-start | bytes 3076
  15.1 3.7 %collective-permute-start.1 = (f32[272]{0:T(512)S(1)}, f32[272]{0:T(512)S(1)}, u32[]{:S(2)}, u32[]{:S(2)}) collective-permute-start(f32[272]{0:T(512)S(1)} %fusion.89), channel_id=1, source_target_pairs={{0,16},{8,24},{16,0},{24,8},{1,17},{9,25},{17,1},{25,9},{2,18},{10... | collective-permute-start | bytes 3272 | tf_op jit(solution)/shard_map/ppermute | solution.py:14
  18.8 1.3 %collective-permute-start.2 = (f32[16656]{0:T(1024)S(1)}, f32[16656]{0:T(1024)S(1)}, u32[]{:S(2)}, u32[]{:S(2)}) collective-permute-start(f32[16656]{0:T(1024)S(1)} %pad_maximum_fusion.1), channel_id=1, source_target_pairs={{0,1},{1,0},{2,3},{3,2},{4,5},{5,4},{6,7},{7,6},{8,9},{9,8},{10,11... | collective-permute-start | bytes 199880 | tf_op jit(solution)/shard_map/ppermute | solution.py:14
  20.2 4.7 %collective-permute-start.3 = (f32[22528]{0:T(1024)S(1)}, f32[22528]{0:T(1024)S(1)}, u32[]{:S(2)}, u32[]{:S(2)}) collective-permute-start(f32[22528]{0:T(1024)S(1)} %concatenate.48), channel_id=1, source_target_pairs={{0,2},{1,3},{2,0},{3,1},{4,6},{5,7},{6,4},{7,5},{8,10},{9,11},{10,... | collective-permute-start | bytes 270344 | tf_op jit(solution)/shard_map/ppermute | solution.py:14
  25.1 7.6 %collective-permute-start.4 = (f32[27648]{0:T(1024)S(1)}, f32[27648]{0:T(1024)S(1)}, u32[]{:S(2)}, u32[]{:S(2)}) collective-permute-start(f32[27648]{0:T(1024)S(1)} %concatenate.49), channel_id=1, source_target_pairs={{0,4},{1,5},{2,6},{3,7},{4,0},{5,1},{6,2},{7,3},{8,12},{9,13},{10,... | collective-permute-start | bytes 331784 | tf_op jit(solution)/shard_map/ppermute | solution.py:14
  34.7 1.4 %collective-permute-start.5 = (f32[36864]{0:T(1024)S(1)}, f32[36864]{0:T(1024)S(1)}, u32[]{:S(2)}, u32[]{:S(2)}) collective-permute-start(f32[36864]{0:T(1024)S(1)} %pad_maximum_fusion), channel_id=1, source_target_pairs={{0,1},{1,0},{2,3},{3,2},{4,5},{5,4},{6,7},{7,6},{8,9},{9,8},{10,11... | collective-permute-start | bytes 442376 | tf_op jit(solution)/shard_map/ppermute | solution.py:14
  38.1 3.5 %collective-permute-start.6 = (f32[32]{0:T(128)S(1)}, f32[32]{0:T(128)S(1)}, u32[]{:S(2)}, u32[]{:S(2)}) collective-permute-start(f32[32]{0:T(128)S(1)} %pad_maximum_fusion.6), channel_id=1, source_target_pairs={{0,8},{8,0},{16,24},{24,16},{1,9},{9,1},{17,25},{25,17},{2,10},{10... | collective-permute-start | bytes 392 | tf_op jit(solution)/shard_map/ppermute | solution.py:14
  41.8 3.5 %collective-permute-start.7 = (f32[32]{0:T(128)S(1)}, f32[32]{0:T(128)S(1)}, u32[]{:S(2)}, u32[]{:S(2)}) collective-permute-start(f32[32]{0:T(128)S(1)} %pad_maximum_fusion.7), channel_id=1, source_target_pairs={{0,16},{8,24},{16,0},{24,8},{1,17},{9,25},{17,1},{25,9},{2,18},{10... | collective-permute-start | bytes 392 | tf_op jit(solution)/shard_map/ppermute | solution.py:14
  45.4 1.3 %collective-permute-start.8 = (f32[16400]{0:T(1024)S(1)}, f32[16400]{0:T(1024)S(1)}, u32[]{:S(2)}, u32[]{:S(2)}) collective-permute-start(f32[16400]{0:T(1024)S(1)} %pad_maximum_fusion.2), channel_id=1, source_target_pairs={{0,1},{1,0},{2,3},{3,2},{4,5},{5,4},{6,7},{7,6},{8,9},{9,8},{10,11... | collective-permute-start | bytes 196808 | tf_op jit(solution)/shard_map/ppermute | solution.py:14
  46.7 4.4 %collective-permute-start.9 = (f32[16400]{0:T(1024)S(1)}, f32[16400]{0:T(1024)S(1)}, u32[]{:S(2)}, u32[]{:S(2)}) collective-permute-start(f32[16400]{0:T(1024)S(1)} %pad_maximum_fusion.3), channel_id=1, source_target_pairs={{0,2},{1,3},{2,0},{3,1},{4,6},{5,7},{6,4},{7,5},{8,10},{9,11},{10,... | collective-permute-start | bytes 196808 | tf_op jit(solution)/shard_map/ppermute | solution.py:14
  51.1 6.0 %collective-permute-start.10 = (f32[16400]{0:T(1024)S(1)}, f32[16400]{0:T(1024)S(1)}, u32[]{:S(2)}, u32[]{:S(2)}) collective-permute-start(f32[16400]{0:T(1024)S(1)} %pad_maximum_fusion.4), channel_id=1, source_target_pairs={{0,4},{1,5},{2,6},{3,7},{4,0},{5,1},{6,2},{7,3},{8,12},{9,13},{10,... | collective-permute-start | bytes 196808 | tf_op jit(solution)/shard_map/ppermute | solution.py:14
  57.1 1.3 %collective-permute-start.11 = (f32[16384]{0:T(1024)S(1)}, f32[16384]{0:T(1024)S(1)}, u32[]{:S(2)}, u32[]{:S(2)}) collective-permute-start(f32[16384]{0:T(1024)S(1)} %get-tuple-element.19), channel_id=1, source_target_pairs={{0,1},{1,0},{2,3},{3,2},{4,5},{5,4},{6,7},{7,6},{8,9},{9,8},{10,11... | collective-permute-start | bytes 196616 | tf_op jit(solution)/shard_map/ppermute | solution.py:14
  60.9 3.5 %collective-permute-start.12 = (f32[32]{0:T(128)S(1)}, f32[32]{0:T(128)S(1)}, u32[]{:S(2)}, u32[]{:S(2)}) collective-permute-start(f32[32]{0:T(128)S(1)} %pad_maximum_fusion.8), channel_id=1, source_target_pairs={{0,8},{8,0},{16,24},{24,16},{1,9},{9,1},{17,25},{25,17},{2,10},{10... | collective-permute-start | bytes 392 | tf_op jit(solution)/shard_map/ppermute | solution.py:14
  64.6 3.5 %collective-permute-start.13 = (f32[32]{0:T(128)S(1)}, f32[32]{0:T(128)S(1)}, u32[]{:S(2)}, u32[]{:S(2)}) collective-permute-start(f32[32]{0:T(128)S(1)} %pad_maximum_fusion.9), channel_id=1, source_target_pairs={{0,16},{8,24},{16,0},{24,8},{1,17},{9,25},{17,1},{25,9},{2,18},{10... | collective-permute-start | bytes 392 | tf_op jit(solution)/shard_map/ppermute | solution.py:14
  68.2 1.1 %collective-permute-start.14 = (f32[16]{0:T(128)S(1)}, f32[16]{0:T(128)S(1)}, u32[]{:S(2)}, u32[]{:S(2)}) collective-permute-start(f32[16]{0:T(128)S(1)} %slice_add_fusion.6), channel_id=1, source_target_pairs={{0,1},{1,0},{2,3},{3,2},{4,5},{5,4},{6,7},{7,6},{8,9},{9,8},{10,11... | collective-permute-start | bytes 200 | tf_op jit(solution)/shard_map/ppermute | solution.py:14
  69.3 3.5 %collective-permute-start.15 = (f32[16]{0:T(128)S(1)}, f32[16]{0:T(128)S(1)}, u32[]{:S(2)}, u32[]{:S(2)}) collective-permute-start(f32[16]{0:T(128)S(1)} %add.227), channel_id=1, source_target_pairs={{0,2},{1,3},{2,0},{3,1},{4,6},{5,7},{6,4},{7,5},{8,10},{9,11},{10,... | collective-permute-start | bytes 200 | tf_op jit(solution)/shard_map/ppermute | solution.py:14
  72.9 4.4 %collective-permute-start.16 = (f32[16]{0:T(128)S(1)}, f32[16]{0:T(128)S(1)}, u32[]{:S(2)}, u32[]{:S(2)}) collective-permute-start(f32[16]{0:T(128)S(1)} %add.228), channel_id=1, source_target_pairs={{0,4},{1,5},{2,6},{3,7},{4,0},{5,1},{6,2},{7,3},{8,12},{9,13},{10,... | collective-permute-start | bytes 200 | tf_op jit(solution)/shard_map/ppermute | solution.py:14

commit v20 on v18

--- a/solution.py
+++ b/solution.py
@@ -145,7 +145,14 @@
         return jnp.einsum("ricj,csj->rsi", dense, point, precision=lax.Precision.HIGH)
 
     norms = jnp.concatenate([local_a, local_b, local_c])
-    _, (norms,), _ = _rounds("region", [norms])
+    n_region = lax.axis_size("region")
+    if _pow2(n_region) and n_region >= 2:
+        norms = norms + _exchange(norms, "region", n_region, 0)
+        norms, dense = lax.optimization_barrier((norms, dense))
+        for bit in range(1, n_region.bit_length() - 1):
+            norms = norms + _exchange(norms, "region", n_region, bit)
+    else:
+        norms = lax.psum(norms, "region")
     own_rows = own_blocks * (scenarios + 2)
     own = jnp.concatenate(
         [

time: 78.1 us -> 77 us (0.986)
  waiting for transfers between devices: 37.4 us -> 36.4 us
    ppermute x17, waiting for transfers between devices: 37.4 us -> 36.4 us  [_exchange(): return lax.ppermute(x, axis, [(i, i ^ 1 << bit) for i in range(n)])]
where the time goes in v20:
time: 77 us; the launch traced here: 76.8 us
  waiting for transfers between devices  36.4 us (47%)
  starting transfers between devices  18.6 us (24%)
  matrix products  11.5 us (15%)
  other arithmetic  6.1 us (8%)
  between operations  3.05 us (4%)
  local copies, waits for them, and re-layouts  1.05 us (1%)
    ppermute x17, waiting for transfers between devices, _exchange(): return lax.ppermute(x, axis, [(i, i ^ 1 << bit) for i in range(n)])  36.4 us
    ppermute x17, starting transfers between devices, _exchange(): return lax.ppermute(x, axis, [(i, i ^ 1 << bit) for i in range(n)])  18.6 us
    dot_general x1, matrix products, local(): dense = jnp.dot(place_live, tiles.reshape(ntiles, -1), precision=hp)  5.59 us
    dot_general x2, matrix products, product_of(): jnp.einsum('ricj,csj->rsi', dense, point, precision=lax.Precision.HIGH)  3.64 us
    reduce_sum x1, other arithmetic, local(): local_a = jnp.sum(tiles * tiles * live[:, None, None], axis=(0, 1))  2.78 us
    dot_general x2, matrix products, transposed_product(): jnp.einsum('rsi,ricj->csj', dual, dense, precision=lax.Precision.HIGH)  2.13 us
  transfers between devices with their start and end apart: 17, of which 16 were waited for; matrix products, arithmetic and copies ran while one was open for 11% of the time, Pallas kernels for 0%

profile of v20, /device:TPU:0, one launch (start us, length us, event | category | flops | bytes accessed | tf_op | source)
XLA Modules:
  0.0 76.8 jit_solution(11510483250518161405)
XLA Ops:
  0.6 0.0 copy-start
  1.4 0.7 multiply_reduce_fusion.6
  2.1 2.8 %multiply_reduce_fusion = f32[128]{0:T(128)S(1)} fusion(f32[48,128,128]{2,1,0:T(8,128)} %param.11, f32[48]{0:T(128)S(1)} %compare_convert_fusion), kind=kLoop, calls=%fused_computation.4 | loop fusion | flops 2359168 | bytes 3146432 | tf_op jit(solution)/shard_map/reduce_sum | solution.py:127
  4.9 0.0 copy-done
  4.9 0.2 fusion.81
  5.1 0.1 multiply_reduce_fusion.5
  5.2 3.0 %collective-permute-start = (f32[272]{0:T(512)S(1)}, f32[272]{0:T(512)S(1)}, u32[]{:S(2)}, u32[]{:S(2)}) collective-permute-start(f32[272]{0:T(512)S(1)} %pad_maximum_fusion.5), channel_id=1, source_target_pairs={{0,8},{8,0},{16,24},{24,16},{1,9},{9,1},{17,25},{25,17},{2,10},{10... | collective-permute-start | bytes 3272 | tf_op jit(solution)/shard_map/ppermute | solution.py:14
  8.2 0.1 pad.30.clone
  8.3 5.6 %fusion.10 = f32[2,128,16,128]{3,2,1,0:T(8,128)S(1)} fusion(f32[48]{0:T(128)S(1)} %compare_convert_fusion, s32[16,2]{0,1:T(2,128)S(1)} %multiply_add_fusion, s32[48]{0:T(128)S(1)} %multiply_add_fusion.1, f32[6,8,128,128]{3,2,1,0:T(8,128)} %bitcast.138), kind=kOutput, calls=%fused_computation.13 | convolution fusion | flops 301992960 | bytes 5243392 | tf_op jit(solution)/shard_map/dot_general | solution.py:137
  13.9 0.0 copy-done.2
  14.0 0.0 copy-done.5
  14.0 0.1 fusion.71
  14.0 0.0 collective-permute-done
  14.1 1.6 %collective-permute-start.1 = (f32[272]{0:T(512)S(1)}, f32[272]{0:T(512)S(1)}, u32[]{:S(2)}, u32[]{:S(2)}) collective-permute-start(f32[272]{0:T(512)S(1)} %fusion.89), channel_id=1, source_target_pairs={{0,16},{8,24},{16,0},{24,8},{1,17},{9,25},{17,1},{25,9},{2,18},{10... | collective-permute-start | bytes 3272 | tf_op jit(solution)/shard_map/ppermute | solution.py:14
  15.6 1.1 %fusion.8 = f32[16,128,16,1]{1,2,3,0:T(8,128)S(1)} fusion(f32[2,128,16,128]{3,2,1,0:T(8,128)S(1)} %fusion.10, f32[2,16,128]{2,1,0:T(8,128)S(1)} %copy-done.1), kind=kOutput, calls=%fused_computation.11 | convolution fusion | flops 50331648 | bytes 2244608 | tf_op jit(solution)/shard_map/rsi,ricj->csj/dot_general | solution.py:142
  16.7 1.0 %collective-permute-done.1 = f32[272]{0:T(512)S(1)} collective-permute-done((f32[272]{0:T(512)S(1)}, f32[272]{0:T(512)S(1)}, u32[]{:S(2)}, u32[]{:S(2)}) %collective-permute-start.1) | collective-permute-done | bytes 1120 | tf_op jit(solution)/shard_map/ppermute | solution.py:14
  17.7 0.1 collective-permute-start.2
  17.8 1.2 %collective-permute-done.2 = f32[16656]{0:T(1024)S(1)} collective-permute-done((f32[16656]{0:T(1024)S(1)}, f32[16656]{0:T(1024)S(1)}, u32[]{:S(2)}, u32[]{:S(2)}) %collective-permute-start.2) | collective-permute-done | bytes 66656 | tf_op jit(solution)/shard_map/ppermute | solution.py:14
  19.1 0.1 concatenate.48
  19.2 1.6 %collective-permute-start.3 = (f32[22528]{0:T(1024)S(1)}, f32[22528]{0:T(1024)S(1)}, u32[]{:S(2)}, u32[]{:S(2)}) collective-permute-start(f32[22528]{0:T(1024)S(1)} %concatenate.48), channel_id=1, source_target_pairs={{0,2},{1,3},{2,0},{3,1},{4,6},{5,7},{6,4},{7,5},{8,10},{9,11},{10,... | collective-permute-start | bytes 270344 | tf_op jit(solution)/shard_map/ppermute | solution.py:14
  20.7 3.1 %collective-permute-done.3 = f32[22528]{0:T(1024)S(1)} collective-permute-done((f32[22528]{0:T(1024)S(1)}, f32[22528]{0:T(1024)S(1)}, u32[]{:S(2)}, u32[]{:S(2)}) %collective-permute-start.3) | collective-permute-done | bytes 90144 | tf_op jit(solution)/shard_map/ppermute | solution.py:14
  23.9 0.1 concatenate.49
  24.0 2.6 %collective-permute-start.4 = (f32[27648]{0:T(1024)S(1)}, f32[27648]{0:T(1024)S(1)}, u32[]{:S(2)}, u32[]{:S(2)}) collective-permute-start(f32[27648]{0:T(1024)S(1)} %concatenate.49), channel_id=1, source_target_pairs={{0,4},{1,5},{2,6},{3,7},{4,0},{5,1},{6,2},{7,3},{8,12},{9,13},{10,... | collective-permute-start | bytes 331784 | tf_op jit(solution)/shard_map/ppermute | solution.py:14
  26.6 5.0 %collective-permute-done.4 = f32[27648]{0:T(1024)S(1)} collective-permute-done((f32[27648]{0:T(1024)S(1)}, f32[27648]{0:T(1024)S(1)}, u32[]{:S(2)}, u32[]{:S(2)}) %collective-permute-start.4) | collective-permute-done | bytes 110624 | tf_op jit(solution)/shard_map/ppermute | solution.py:14
  31.6 0.6 slice_reduce_fusion
  33.7 0.1 collective-permute-start.5
  33.8 1.3 %collective-permute-done.5 = f32[36864]{0:T(1024)S(1)} collective-permute-done((f32[36864]{0:T(1024)S(1)}, f32[36864]{0:T(1024)S(1)}, u32[]{:S(2)}, u32[]{:S(2)}) %collective-permute-start.5) | collective-permute-done | bytes 147488 | tf_op jit(solution)/shard_map/ppermute | solution.py:14
  35.2 0.2 multiply_reduce_fusion.2
  35.4 1.5 %multiply_reduce_fusion.4 = (f32[16]{0:T(128)S(1)}, f32[2,16,128]{2,1,0:T(8,128)S(1)}) fusion(f32[2,16,128]{2,1,0:T(8,128)S(1)} %copy-done.1, f32[2,128,16,128]{3,2,1,0:T(8,128)S(1)} %fusion.10, f32[16,16,128]{2,1,0:T(8,128)S(1)} %bitcast.140, f32[16,16,128]{2,1,0:T(8,128)S(1)} %get-tuple-element.14, f32[2,128]{1,0:T(2,128)S(1)} %copy-done.3, ...), kind=kOutput, calls=%fused_computation.75 | convolution fusion | flops 50425840 | bytes 2393216 | tf_op jit(solution)/shard_map/ricj,csj->rsi/dot_general | solution.py:145
  36.9 0.1 pad_maximum_fusion.6
  37.0 0.7 collective-permute-start.6
  37.7 1.1 %fusion.6 = f32[16,128,16,1]{1,2,3,0:T(8,128)S(1)} fusion(f32[2,128,16,128]{3,2,1,0:T(8,128)S(1)} %fusion.10, f32[2,16,128]{2,1,0:T(8,128)S(1)} %get-tuple-element.37), kind=kOutput, calls=%fused_computation.9 | convolution fusion | flops 50331648 | bytes 2244608 | tf_op jit(solution)/shard_map/rsi,ricj->csj/dot_general | solution.py:142
  38.7 1.8 %collective-permute-done.6 = f32[32]{0:T(128)S(1)} collective-permute-done((f32[32]{0:T(128)S(1)}, f32[32]{0:T(128)S(1)}, u32[]{:S(2)}, u32[]{:S(2)}) %collective-permute-start.6) | collective-permute-done | bytes 160 | tf_op jit(solution)/shard_map/ppermute | solution.py:14
  40.5 0.1 slice_add_fusion.11
  40.6 0.1 pad_maximum_fusion.7
  40.7 1.5 %collective-permute-start.7 = (f32[32]{0:T(128)S(1)}, f32[32]{0:T(128)S(1)}, u32[]{:S(2)}, u32[]{:S(2)}) collective-permute-start(f32[32]{0:T(128)S(1)} %pad_maximum_fusion.7), channel_id=1, source_target_pairs={{0,16},{8,24},{16,0},{24,8},{1,17},{9,25},{17,1},{25,9},{2,18},{10... | collective-permute-start | bytes 392 | tf_op jit(solution)/shard_map/ppermute | solution.py:14
  42.2 2.0 %collective-permute-done.7 = f32[32]{0:T(128)S(1)} collective-permute-done((f32[32]{0:T(128)S(1)}, f32[32]{0:T(128)S(1)}, u32[]{:S(2)}, u32[]{:S(2)}) %collective-permute-start.7) | collective-permute-done | bytes 160 | tf_op jit(solution)/shard_map/ppermute | solution.py:14
  44.2 0.1 slice_add_fusion.9
  44.3 0.0 collective-permute-start.8
  44.3 1.2 %collective-permute-done.8 = f32[16400]{0:T(1024)S(1)} collective-permute-done((f32[16400]{0:T(1024)S(1)}, f32[16400]{0:T(1024)S(1)}, u32[]{:S(2)}, u32[]{:S(2)}) %collective-permute-start.8) | collective-permute-done | bytes 65632 | tf_op jit(solution)/shard_map/ppermute | solution.py:14
  45.6 0.7 collective-permute-start.9
  46.4 3.6 %collective-permute-done.9 = f32[16400]{0:T(1024)S(1)} collective-permute-done((f32[16400]{0:T(1024)S(1)}, f32[16400]{0:T(1024)S(1)}, u32[]{:S(2)}, u32[]{:S(2)}) %collective-permute-start.9) | collective-permute-done | bytes 65632 | tf_op jit(solution)/shard_map/ppermute | solution.py:14
  50.0 2.3 %collective-permute-start.10 = (f32[16400]{0:T(1024)S(1)}, f32[16400]{0:T(1024)S(1)}, u32[]{:S(2)}, u32[]{:S(2)}) collective-permute-start(f32[16400]{0:T(1024)S(1)} %pad_maximum_fusion.4), channel_id=1, source_target_pairs={{0,4},{1,5},{2,6},{3,7},{4,0},{5,1},{6,2},{7,3},{8,12},{9,13},{10,... | collective-permute-start | bytes 196808 | tf_op jit(solution)/shard_map/ppermute | solution.py:14
  52.3 3.7 %collective-permute-done.10 = f32[16400]{0:T(1024)S(1)} collective-permute-done((f32[16400]{0:T(1024)S(1)}, f32[16400]{0:T(1024)S(1)}, u32[]{:S(2)}, u32[]{:S(2)}) %collective-permute-start.10) | collective-permute-done | bytes 65632 | tf_op jit(solution)/shard_map/ppermute | solution.py:14
  56.1 0.1 collective-permute-start.11
  56.2 1.2 %collective-permute-done.11 = f32[16384]{0:T(1024)S(1)} collective-permute-done((f32[16384]{0:T(1024)S(1)}, f32[16384]{0:T(1024)S(1)}, u32[]{:S(2)}, u32[]{:S(2)}) %collective-permute-start.11) | collective-permute-done | bytes 65568 | tf_op jit(solution)/shard_map/ppermute | solution.py:14
  57.4 0.2 multiply_reduce_fusion.1
  57.6 2.1 %multiply_reduce_fusion.3 = (f32[16]{0:T(128)S(1)}, f32[2,16,128]{2,1,0:T(8,128)}) fusion(f32[2,16,128]{2,1,0:T(8,128)S(1)} %get-tuple-element.37, f32[2,128,16,128]{3,2,1,0:T(8,128)S(1)} %fusion.10, f32[16,16,128]{2,1,0:T(8,128)S(1)} %get-tuple-element.14, f32[16,16,128]{2,1,0:T(8,128)S(1)} %get-tuple-element.10, f32[2,128]{1,0:T(2,128)S(1)} %copy-done.3, ...), kind=kOutput, calls=%fused_computation.74 | convolution fusion | flops 50425840 | bytes 2393216 | tf_op jit(solution)/shard_map/ricj,csj->rsi/dot_general | solution.py:145
  59.7 0.1 pad_maximum_fusion.8
  59.8 0.7 collective-permute-start.12
  60.5 2.9 %collective-permute-done.12 = f32[32]{0:T(128)S(1)} collective-permute-done((f32[32]{0:T(128)S(1)}, f32[32]{0:T(128)S(1)}, u32[]{:S(2)}, u32[]{:S(2)}) %collective-permute-start.12) | collective-permute-done | bytes 160 | tf_op jit(solution)/shard_map/ppermute | solution.py:14
  63.3 0.1 slice_add_fusion.8
  63.4 0.1 pad_maximum_fusion.9
  63.5 1.5 %collective-permute-start.13 = (f32[32]{0:T(128)S(1)}, f32[32]{0:T(128)S(1)}, u32[]{:S(2)}, u32[]{:S(2)}) collective-permute-start(f32[32]{0:T(128)S(1)} %pad_maximum_fusion.9), channel_id=1, source_target_pairs={{0,16},{8,24},{16,0},{24,8},{1,17},{9,25},{17,1},{25,9},{2,18},{10... | collective-permute-start | bytes 392 | tf_op jit(solution)/shard_map/ppermute | solution.py:14
  65.0 2.0 %collective-permute-done.13 = f32[32]{0:T(128)S(1)} collective-permute-done((f32[32]{0:T(128)S(1)}, f32[32]{0:T(128)S(1)}, u32[]{:S(2)}, u32[]{:S(2)}) %collective-permute-start.13) | collective-permute-done | bytes 160 | tf_op jit(solution)/shard_map/ppermute | solution.py:14
  67.0 0.1 slice_add_fusion.6
  67.1 0.0 collective-permute-start.14
  67.1 1.1 %collective-permute-done.14 = f32[16]{0:T(128)S(1)} collective-permute-done((f32[16]{0:T(128)S(1)}, f32[16]{0:T(128)S(1)}, u32[]{:S(2)}, u32[]{:S(2)}) %collective-permute-start.14) | collective-permute-done | bytes 96 | tf_op jit(solution)/shard_map/ppermute | solution.py:14
  68.2 0.5 collective-permute-start.15
  68.7 3.1 %collective-permute-done.15 = f32[16]{0:T(128)S(1)} collective-permute-done((f32[16]{0:T(128)S(1)}, f32[16]{0:T(128)S(1)}, u32[]{:S(2)}, u32[]{:S(2)}) %collective-permute-start.15) | collective-permute-done | bytes 96 | tf_op jit(solution)/shard_map/ppermute | solution.py:14
  71.8 1.7 %collective-permute-start.16 = (f32[16]{0:T(128)S(1)}, f32[16]{0:T(128)S(1)}, u32[]{:S(2)}, u32[]{:S(2)}) collective-permute-start(f32[16]{0:T(128)S(1)} %add.228), channel_id=1, source_target_pairs={{0,4},{1,5},{2,6},{3,7},{4,0},{5,1},{6,2},{7,3},{8,12},{9,13},{10,... | collective-permute-start | bytes 200 | tf_op jit(solution)/shard_map/ppermute | solution.py:14
  73.5 0.6 constant_dynamic-slice_fusion
  74.1 2.2 %collective-permute-done.16 = f32[16]{0:T(128)S(1)} collective-permute-done((f32[16]{0:T(128)S(1)}, f32[16]{0:T(128)S(1)}, u32[]{:S(2)}, u32[]{:S(2)}) %collective-permute-start.16) | collective-permute-done | bytes 96 | tf_op jit(solution)/shard_map/ppermute | solution.py:14
  76.2 0.5 multiply_sqrt_fusion
  (60 shorter events, 0.4 us)
Async XLA Ops:
  0.6 4.2 %copy-start = (f32[32,128]{1,0:T(8,128)S(1)}, f32[32,128]{1,0:T(8,128)}, u32[]{:S(2)}) copy-start(f32[32,128]{1,0:T(8,128)} %param.20) | copy-start | bytes 49156
  0.6 4.2 %copy-start.6 = (s32[16]{0:T(128)S(1)}, s32[16]{0:T(128)}, u32[]{:S(2)}) copy-start(s32[16]{0:T(128)} %param.21) | copy-start | bytes 196
  0.7 4.4 %copy-start.4 = (f32[2,128]{1,0:T(2,128)S(1)}, f32[2,128]{1,0:T(2,128)}, u32[]{:S(2)}) copy-start(f32[2,128]{1,0:T(2,128)} %param.16) | copy-start | bytes 3076
  0.7 7.5 %copy-start.8 = (s32[48]{0:T(128)S(1)}, s32[48]{0:T(128)}, u32[]{:S(2)}) copy-start(s32[48]{0:T(128)} %param.13) | copy-start | bytes 580
  0.7 7.5 %copy-start.7 = (s32[48]{0:T(128)S(1)}, s32[48]{0:T(128)}, u32[]{:S(2)}) copy-start(s32[48]{0:T(128)} %param.12) | copy-start | bytes 580
  5.2 8.8 %collective-permute-start = (f32[272]{0:T(512)S(1)}, f32[272]{0:T(512)S(1)}, u32[]{:S(2)}, u32[]{:S(2)}) collective-permute-start(f32[272]{0:T(512)S(1)} %pad_maximum_fusion.5), channel_id=1, source_target_pairs={{0,8},{8,0},{16,24},{24,16},{1,9},{9,1},{17,25},{25,17},{2,10},{10... | collective-permute-start | bytes 3272 | tf_op jit(solution)/shard_map/ppermute | solution.py:14
  8.3 5.6 %copy-start.2 = (f32[2,16,128]{2,1,0:T(8,128)S(1)}, f32[2,16,128]{2,1,0:T(8,128)}, u32[]{:S(2)}) copy-start(f32[2,16,128]{2,1,0:T(8,128)} %param.18) | copy-start | bytes 49156
  8.3 5.6 %copy-start.5 = (f32[2,128]{1,0:T(2,128)S(1)}, f32[2,128]{1,0:T(2,128)}, u32[]{:S(2)}) copy-start(f32[2,128]{1,0:T(2,128)} %param.17) | copy-start | bytes 3076
  8.3 7.3 %copy-start.1 = (f32[2,16,128]{2,1,0:T(8,128)S(1)}, f32[2,16,128]{2,1,0:T(8,128)}, u32[]{:S(2)}) copy-start(f32[2,16,128]{2,1,0:T(8,128)} %param.19) | copy-start | bytes 49156
  14.1 3.7 %collective-permute-start.1 = (f32[272]{0:T(512)S(1)}, f32[272]{0:T(512)S(1)}, u32[]{:S(2)}, u32[]{:S(2)}) collective-permute-start(f32[272]{0:T(512)S(1)} %fusion.89), channel_id=1, source_target_pairs={{0,16},{8,24},{16,0},{24,8},{1,17},{9,25},{17,1},{25,9},{2,18},{10... | collective-permute-start | bytes 3272 | tf_op jit(solution)/shard_map/ppermute | solution.py:14
  16.7 18.7 %copy-start.3 = (f32[2,128]{1,0:T(2,128)S(1)}, f32[2,128]{1,0:T(2,128)}, u32[]{:S(2)}) copy-start(f32[2,128]{1,0:T(2,128)} %param.15) | copy-start | bytes 3076
  17.7 1.3 %collective-permute-start.2 = (f32[16656]{0:T(1024)S(1)}, f32[16656]{0:T(1024)S(1)}, u32[]{:S(2)}, u32[]{:S(2)}) collective-permute-start(f32[16656]{0:T(1024)S(1)} %pad_maximum_fusion.1), channel_id=1, source_target_pairs={{0,1},{1,0},{2,3},{3,2},{4,5},{5,4},{6,7},{7,6},{8,9},{9,8},{10,11... | collective-permute-start | bytes 199880 | tf_op jit(solution)/shard_map/ppermute | solution.py:14
  19.2 4.7 %collective-permute-start.3 = (f32[22528]{0:T(1024)S(1)}, f32[22528]{0:T(1024)S(1)}, u32[]{:S(2)}, u32[]{:S(2)}) collective-permute-start(f32[22528]{0:T(1024)S(1)} %concatenate.48), channel_id=1, source_target_pairs={{0,2},{1,3},{2,0},{3,1},{4,6},{5,7},{6,4},{7,5},{8,10},{9,11},{10,... | collective-permute-start | bytes 270344 | tf_op jit(solution)/shard_map/ppermute | solution.py:14
  24.0 7.6 %collective-permute-start.4 = (f32[27648]{0:T(1024)S(1)}, f32[27648]{0:T(1024)S(1)}, u32[]{:S(2)}, u32[]{:S(2)}) collective-permute-start(f32[27648]{0:T(1024)S(1)} %concatenate.49), channel_id=1, source_target_pairs={{0,4},{1,5},{2,6},{3,7},{4,0},{5,1},{6,2},{7,3},{8,12},{9,13},{10,... | collective-permute-start | bytes 331784 | tf_op jit(solution)/shard_map/ppermute | solution.py:14
  33.7 1.4 %collective-permute-start.5 = (f32[36864]{0:T(1024)S(1)}, f32[36864]{0:T(1024)S(1)}, u32[]{:S(2)}, u32[]{:S(2)}) collective-permute-start(f32[36864]{0:T(1024)S(1)} %pad_maximum_fusion), channel_id=1, source_target_pairs={{0,1},{1,0},{2,3},{3,2},{4,5},{5,4},{6,7},{7,6},{8,9},{9,8},{10,11... | collective-permute-start | bytes 442376 | tf_op jit(solution)/shard_map/ppermute | solution.py:14
  37.0 3.5 %collective-permute-start.6 = (f32[32]{0:T(128)S(1)}, f32[32]{0:T(128)S(1)}, u32[]{:S(2)}, u32[]{:S(2)}) collective-permute-start(f32[32]{0:T(128)S(1)} %pad_maximum_fusion.6), channel_id=1, source_target_pairs={{0,8},{8,0},{16,24},{24,16},{1,9},{9,1},{17,25},{25,17},{2,10},{10... | collective-permute-start | bytes 392 | tf_op jit(solution)/shard_map/ppermute | solution.py:14
  40.7 3.5 %collective-permute-start.7 = (f32[32]{0:T(128)S(1)}, f32[32]{0:T(128)S(1)}, u32[]{:S(2)}, u32[]{:S(2)}) collective-permute-start(f32[32]{0:T(128)S(1)} %pad_maximum_fusion.7), channel_id=1, source_target_pairs={{0,16},{8,24},{16,0},{24,8},{1,17},{9,25},{17,1},{25,9},{2,18},{10... | collective-permute-start | bytes 392 | tf_op jit(solution)/shard_map/ppermute | solution.py:14
  44.3 1.3 %collective-permute-start.8 = (f32[16400]{0:T(1024)S(1)}, f32[16400]{0:T(1024)S(1)}, u32[]{:S(2)}, u32[]{:S(2)}) collective-permute-start(f32[16400]{0:T(1024)S(1)} %pad_maximum_fusion.2), channel_id=1, source_target_pairs={{0,1},{1,0},{2,3},{3,2},{4,5},{5,4},{6,7},{7,6},{8,9},{9,8},{10,11... | collective-permute-start | bytes 196808 | tf_op jit(solution)/shard_map/ppermute | solution.py:14
  45.6 4.4 %collective-permute-start.9 = (f32[16400]{0:T(1024)S(1)}, f32[16400]{0:T(1024)S(1)}, u32[]{:S(2)}, u32[]{:S(2)}) collective-permute-start(f32[16400]{0:T(1024)S(1)} %pad_maximum_fusion.3), channel_id=1, source_target_pairs={{0,2},{1,3},{2,0},{3,1},{4,6},{5,7},{6,4},{7,5},{8,10},{9,11},{10,... | collective-permute-start | bytes 196808 | tf_op jit(solution)/shard_map/ppermute | solution.py:14
  50.0 6.0 %collective-permute-start.10 = (f32[16400]{0:T(1024)S(1)}, f32[16400]{0:T(1024)S(1)}, u32[]{:S(2)}, u32[]{:S(2)}) collective-permute-start(f32[16400]{0:T(1024)S(1)} %pad_maximum_fusion.4), channel_id=1, source_target_pairs={{0,4},{1,5},{2,6},{3,7},{4,0},{5,1},{6,2},{7,3},{8,12},{9,13},{10,... | collective-permute-start | bytes 196808 | tf_op jit(solution)/shard_map/ppermute | solution.py:14
  56.1 1.3 %collective-permute-start.11 = (f32[16384]{0:T(1024)S(1)}, f32[16384]{0:T(1024)S(1)}, u32[]{:S(2)}, u32[]{:S(2)}) collective-permute-start(f32[16384]{0:T(1024)S(1)} %get-tuple-element.23), channel_id=1, source_target_pairs={{0,1},{1,0},{2,3},{3,2},{4,5},{5,4},{6,7},{7,6},{8,9},{9,8},{10,11... | collective-permute-start | bytes 196616 | tf_op jit(solution)/shard_map/ppermute | solution.py:14
  59.8 3.5 %collective-permute-start.12 = (f32[32]{0:T(128)S(1)}, f32[32]{0:T(128)S(1)}, u32[]{:S(2)}, u32[]{:S(2)}) collective-permute-start(f32[32]{0:T(128)S(1)} %pad_maximum_fusion.8), channel_id=1, source_target_pairs={{0,8},{8,0},{16,24},{24,16},{1,9},{9,1},{17,25},{25,17},{2,10},{10... | collective-permute-start | bytes 392 | tf_op jit(solution)/shard_map/ppermute | solution.py:14
  63.5 3.5 %collective-permute-start.13 = (f32[32]{0:T(128)S(1)}, f32[32]{0:T(128)S(1)}, u32[]{:S(2)}, u32[]{:S(2)}) collective-permute-start(f32[32]{0:T(128)S(1)} %pad_maximum_fusion.9), channel_id=1, source_target_pairs={{0,16},{8,24},{16,0},{24,8},{1,17},{9,25},{17,1},{25,9},{2,18},{10... | collective-permute-start | bytes 392 | tf_op jit(solution)/shard_map/ppermute | solution.py:14
  67.1 1.1 %collective-permute-start.14 = (f32[16]{0:T(128)S(1)}, f32[16]{0:T(128)S(1)}, u32[]{:S(2)}, u32[]{:S(2)}) collective-permute-start(f32[16]{0:T(128)S(1)} %slice_add_fusion.6), channel_id=1, source_target_pairs={{0,1},{1,0},{2,3},{3,2},{4,5},{5,4},{6,7},{7,6},{8,9},{9,8},{10,11... | collective-permute-start | bytes 200 | tf_op jit(solution)/shard_map/ppermute | solution.py:14
  68.2 3.5 %collective-permute-start.15 = (f32[16]{0:T(128)S(1)}, f32[16]{0:T(128)S(1)}, u32[]{:S(2)}, u32[]{:S(2)}) collective-permute-start(f32[16]{0:T(128)S(1)} %add.227), channel_id=1, source_target_pairs={{0,2},{1,3},{2,0},{3,1},{4,6},{5,7},{6,4},{7,5},{8,10},{9,11},{10,... | collective-permute-start | bytes 200 | tf_op jit(solution)/shard_map/ppermute | solution.py:14
  71.8 4.4 %collective-permute-start.16 = (f32[16]{0:T(128)S(1)}, f32[16]{0:T(128)S(1)}, u32[]{:S(2)}, u32[]{:S(2)}) collective-permute-start(f32[16]{0:T(128)S(1)} %add.228), channel_id=1, source_target_pairs={{0,4},{1,5},{2,6},{3,7},{4,0},{5,1},{6,2},{7,3},{8,12},{9,13},{10,... | collective-permute-start | bytes 200 | tf_op jit(solution)/shard_map/ppermute | solution.py:14

commit v21 on v20

--- a/solution.py
+++ b/solution.py
@@ -165,6 +165,7 @@
     )
     partial_value = transposed_product(dual)
     grad, (norms,), gathered = _rounds("col", [norms], own, split=partial_value)
+    norms, grad = lax.optimization_barrier((norms, grad))
     sq_a = jnp.sum(norms[:lanes])
     sq_b = jnp.sum(norms[lanes : 2 * lanes])
     sq_c = norms[2 * lanes :]

time: 77 us -> 77.1 us (level)
  no operation moved by 1% of the time
where the time goes in v21:
time: 77.1 us; the launch traced here: 76.8 us
  waiting for transfers between devices  36.4 us (47%)
  starting transfers between devices  18.6 us (24%)
  matrix products  11.5 us (15%)
  other arithmetic  6.16 us (8%)
  between operations  3.06 us (4%)
  local copies, waits for them, and re-layouts  1.05 us (1%)
    ppermute x17, waiting for transfers between devices, _exchange(): return lax.ppermute(x, axis, [(i, i ^ 1 << bit) for i in range(n)])  36.4 us
    ppermute x17, starting transfers between devices, _exchange(): return lax.ppermute(x, axis, [(i, i ^ 1 << bit) for i in range(n)])  18.6 us
    dot_general x1, matrix products, local(): dense = jnp.dot(place_live, tiles.reshape(ntiles, -1), precision=hp)  5.59 us
    dot_general x2, matrix products, product_of(): jnp.einsum('ricj,csj->rsi', dense, point, precision=lax.Precision.HIGH)  3.64 us
    reduce_sum x1, other arithmetic, local(): local_a = jnp.sum(tiles * tiles * live[:, None, None], axis=(0, 1))  2.78 us
    dot_general x2, matrix products, transposed_product(): jnp.einsum('rsi,ricj->csj', dual, dense, precision=lax.Precision.HIGH)  2.13 us
  transfers between devices with their start and end apart: 17, of which 16 were waited for; matrix products, arithmetic and copies ran while one was open for 11% of the time, Pallas kernels for 0%

profile of v21, /device:TPU:0, one launch (start us, length us, event | category | flops | bytes accessed | tf_op | source)
XLA Modules:
  0.0 76.8 jit_solution(5327831198834084519)
XLA Ops:
  0.6 0.0 copy-start
  1.4 0.7 multiply_reduce_fusion.6
  2.1 2.8 %multiply_reduce_fusion = f32[128]{0:T(128)S(1)} fusion(f32[48,128,128]{2,1,0:T(8,128)} %param.11, f32[48]{0:T(128)S(1)} %compare_convert_fusion), kind=kLoop, calls=%fused_computation.4 | loop fusion | flops 2359168 | bytes 3146432 | tf_op jit(solution)/shard_map/reduce_sum | solution.py:127
  4.9 0.0 copy-done.6
  4.9 0.2 fusion.81
  5.1 0.1 multiply_reduce_fusion.5
  5.2 3.0 %collective-permute-start = (f32[272]{0:T(512)S(1)}, f32[272]{0:T(512)S(1)}, u32[]{:S(2)}, u32[]{:S(2)}) collective-permute-start(f32[272]{0:T(512)S(1)} %pad_maximum_fusion.5), channel_id=1, source_target_pairs={{0,8},{8,0},{16,24},{24,16},{1,9},{9,1},{17,25},{25,17},{2,10},{10... | collective-permute-start | bytes 3272 | tf_op jit(solution)/shard_map/ppermute | solution.py:14
  8.2 0.1 pad.30.clone
  8.3 5.6 %fusion.10 = f32[2,128,16,128]{3,2,1,0:T(8,128)S(1)} fusion(f32[48]{0:T(128)S(1)} %compare_convert_fusion, s32[16,2]{0,1:T(2,128)S(1)} %multiply_add_fusion, s32[48]{0:T(128)S(1)} %multiply_add_fusion.1, f32[6,8,128,128]{3,2,1,0:T(8,128)} %bitcast.138), kind=kOutput, calls=%fused_computation.13 | convolution fusion | flops 301992960 | bytes 5243392 | tf_op jit(solution)/shard_map/dot_general | solution.py:137
  13.9 0.0 copy-done.2
  14.0 0.1 fusion.71
  14.0 0.0 collective-permute-done
  14.1 1.6 %collective-permute-start.1 = (f32[272]{0:T(512)S(1)}, f32[272]{0:T(512)S(1)}, u32[]{:S(2)}, u32[]{:S(2)}) collective-permute-start(f32[272]{0:T(512)S(1)} %fusion.89), channel_id=1, source_target_pairs={{0,16},{8,24},{16,0},{24,8},{1,17},{9,25},{17,1},{25,9},{2,18},{10... | collective-permute-start | bytes 3272 | tf_op jit(solution)/shard_map/ppermute | solution.py:14
  15.6 1.1 %fusion.8 = f32[16,128,16,1]{1,2,3,0:T(8,128)S(1)} fusion(f32[2,128,16,128]{3,2,1,0:T(8,128)S(1)} %fusion.10, f32[2,16,128]{2,1,0:T(8,128)S(1)} %copy-done.1), kind=kOutput, calls=%fused_computation.11 | convolution fusion | flops 50331648 | bytes 2244608 | tf_op jit(solution)/shard_map/rsi,ricj->csj/dot_general | solution.py:142
  16.7 1.0 %collective-permute-done.1 = f32[272]{0:T(512)S(1)} collective-permute-done((f32[272]{0:T(512)S(1)}, f32[272]{0:T(512)S(1)}, u32[]{:S(2)}, u32[]{:S(2)}) %collective-permute-start.1) | collective-permute-done | bytes 1120 | tf_op jit(solution)/shard_map/ppermute | solution.py:14
  17.7 0.1 collective-permute-start.2
  17.8 1.2 %collective-permute-done.2 = f32[16656]{0:T(1024)S(1)} collective-permute-done((f32[16656]{0:T(1024)S(1)}, f32[16656]{0:T(1024)S(1)}, u32[]{:S(2)}, u32[]{:S(2)}) %collective-permute-start.2) | collective-permute-done | bytes 66656 | tf_op jit(solution)/shard_map/ppermute | solution.py:14
  19.1 0.1 concatenate.48
  19.2 1.6 %collective-permute-start.3 = (f32[22528]{0:T(1024)S(1)}, f32[22528]{0:T(1024)S(1)}, u32[]{:S(2)}, u32[]{:S(2)}) collective-permute-start(f32[22528]{0:T(1024)S(1)} %concatenate.48), channel_id=1, source_target_pairs={{0,2},{1,3},{2,0},{3,1},{4,6},{5,7},{6,4},{7,5},{8,10},{9,11},{10,... | collective-permute-start | bytes 270344 | tf_op jit(solution)/shard_map/ppermute | solution.py:14
  20.7 3.1 %collective-permute-done.3 = f32[22528]{0:T(1024)S(1)} collective-permute-done((f32[22528]{0:T(1024)S(1)}, f32[22528]{0:T(1024)S(1)}, u32[]{:S(2)}, u32[]{:S(2)}) %collective-permute-start.3) | collective-permute-done | bytes 90144 | tf_op jit(solution)/shard_map/ppermute | solution.py:14
  23.9 0.1 concatenate.49
  24.0 2.6 %collective-permute-start.4 = (f32[27648]{0:T(1024)S(1)}, f32[27648]{0:T(1024)S(1)}, u32[]{:S(2)}, u32[]{:S(2)}) collective-permute-start(f32[27648]{0:T(1024)S(1)} %concatenate.49), channel_id=1, source_target_pairs={{0,4},{1,5},{2,6},{3,7},{4,0},{5,1},{6,2},{7,3},{8,12},{9,13},{10,... | collective-permute-start | bytes 331784 | tf_op jit(solution)/shard_map/ppermute | solution.py:14
  26.6 5.0 %collective-permute-done.4 = f32[27648]{0:T(1024)S(1)} collective-permute-done((f32[27648]{0:T(1024)S(1)}, f32[27648]{0:T(1024)S(1)}, u32[]{:S(2)}, u32[]{:S(2)}) %collective-permute-start.4) | collective-permute-done | bytes 110624 | tf_op jit(solution)/shard_map/ppermute | solution.py:14
  31.6 0.1 collective-permute-start.5
  31.7 1.3 %collective-permute-done.5 = f32[36864]{0:T(1024)S(1)} collective-permute-done((f32[36864]{0:T(1024)S(1)}, f32[36864]{0:T(1024)S(1)}, u32[]{:S(2)}, u32[]{:S(2)}) %collective-permute-start.5) | collective-permute-done | bytes 147488 | tf_op jit(solution)/shard_map/ppermute | solution.py:14
  33.2 0.1 fusion.58
  33.2 0.6 slice_reduce_fusion
  35.2 0.2 multiply_reduce_fusion.2
  35.5 1.5 %multiply_reduce_fusion.4 = (f32[16]{0:T(128)S(1)}, f32[2,16,128]{2,1,0:T(8,128)S(1)}) fusion(f32[2,16,128]{2,1,0:T(8,128)S(1)} %copy-done.1, f32[2,128,16,128]{3,2,1,0:T(8,128)S(1)} %fusion.10, f32[16,16,128]{2,1,0:T(8,128)S(1)} %bitcast.140, f32[16,16,128]{2,1,0:T(8,128)S(1)} %get-tuple-element.18, f32[2,128]{1,0:T(2,128)S(1)} %copy-done.3, ...), kind=kOutput, calls=%fused_computation.75 | convolution fusion | flops 50425840 | bytes 2393216 | tf_op jit(solution)/shard_map/ricj,csj->rsi/dot_general | solution.py:145
  37.0 0.1 pad_maximum_fusion.6
  37.1 0.7 collective-permute-start.6
  37.8 1.1 %fusion.6 = f32[16,128,16,1]{1,2,3,0:T(8,128)S(1)} fusion(f32[2,128,16,128]{3,2,1,0:T(8,128)S(1)} %fusion.10, f32[2,16,128]{2,1,0:T(8,128)S(1)} %get-tuple-element.41), kind=kOutput, calls=%fused_computation.9 | convolution fusion | flops 50331648 | bytes 2244608 | tf_op jit(solution)/shard_map/rsi,ricj->csj/dot_general | solution.py:142
  38.8 1.8 %collective-permute-done.6 = f32[32]{0:T(128)S(1)} collective-permute-done((f32[32]{0:T(128)S(1)}, f32[32]{0:T(128)S(1)}, u32[]{:S(2)}, u32[]{:S(2)}) %collective-permute-start.6) | collective-permute-done | bytes 160 | tf_op jit(solution)/shard_map/ppermute | solution.py:14
  40.6 0.1 slice_add_fusion.11
  40.7 0.1 pad_maximum_fusion.7
  40.8 1.5 %collective-permute-start.7 = (f32[32]{0:T(128)S(1)}, f32[32]{0:T(128)S(1)}, u32[]{:S(2)}, u32[]{:S(2)}) collective-permute-start(f32[32]{0:T(128)S(1)} %pad_maximum_fusion.7), channel_id=1, source_target_pairs={{0,16},{8,24},{16,0},{24,8},{1,17},{9,25},{17,1},{25,9},{2,18},{10... | collective-permute-start | bytes 392 | tf_op jit(solution)/shard_map/ppermute | solution.py:14
  42.3 2.0 %collective-permute-done.7 = f32[32]{0:T(128)S(1)} collective-permute-done((f32[32]{0:T(128)S(1)}, f32[32]{0:T(128)S(1)}, u32[]{:S(2)}, u32[]{:S(2)}) %collective-permute-start.7) | collective-permute-done | bytes 160 | tf_op jit(solution)/shard_map/ppermute | solution.py:14
  44.3 0.1 slice_add_fusion.9
  44.4 0.0 collective-permute-start.8
  44.4 1.2 %collective-permute-done.8 = f32[16400]{0:T(1024)S(1)} collective-permute-done((f32[16400]{0:T(1024)S(1)}, f32[16400]{0:T(1024)S(1)}, u32[]{:S(2)}, u32[]{:S(2)}) %collective-permute-start.8) | collective-permute-done | bytes 65632 | tf_op jit(solution)/shard_map/ppermute | solution.py:14
  45.7 0.7 collective-permute-start.9
  46.4 3.6 %collective-permute-done.9 = f32[16400]{0:T(1024)S(1)} collective-permute-done((f32[16400]{0:T(1024)S(1)}, f32[16400]{0:T(1024)S(1)}, u32[]{:S(2)}, u32[]{:S(2)}) %collective-permute-start.9) | collective-permute-done | bytes 65632 | tf_op jit(solution)/shard_map/ppermute | solution.py:14
  50.1 2.3 %collective-permute-start.10 = (f32[16400]{0:T(1024)S(1)}, f32[16400]{0:T(1024)S(1)}, u32[]{:S(2)}, u32[]{:S(2)}) collective-permute-start(f32[16400]{0:T(1024)S(1)} %pad_maximum_fusion.4), channel_id=1, source_target_pairs={{0,4},{1,5},{2,6},{3,7},{4,0},{5,1},{6,2},{7,3},{8,12},{9,13},{10,... | collective-permute-start | bytes 196808 | tf_op jit(solution)/shard_map/ppermute | solution.py:14
  52.4 3.7 %collective-permute-done.10 = f32[16400]{0:T(1024)S(1)} collective-permute-done((f32[16400]{0:T(1024)S(1)}, f32[16400]{0:T(1024)S(1)}, u32[]{:S(2)}, u32[]{:S(2)}) %collective-permute-start.10) | collective-permute-done | bytes 65632 | tf_op jit(solution)/shard_map/ppermute | solution.py:14
  56.1 0.1 collective-permute-start.11
  56.3 1.2 %collective-permute-done.11 = f32[16384]{0:T(1024)S(1)} collective-permute-done((f32[16384]{0:T(1024)S(1)}, f32[16384]{0:T(1024)S(1)}, u32[]{:S(2)}, u32[]{:S(2)}) %collective-permute-start.11) | collective-permute-done | bytes 65568 | tf_op jit(solution)/shard_map/ppermute | solution.py:14
  57.5 0.2 multiply_reduce_fusion.1
  57.7 2.1 %multiply_reduce_fusion.3 = (f32[16]{0:T(128)S(1)}, f32[2,16,128]{2,1,0:T(8,128)}) fusion(f32[2,16,128]{2,1,0:T(8,128)S(1)} %get-tuple-element.41, f32[2,128,16,128]{3,2,1,0:T(8,128)S(1)} %fusion.10, f32[16,16,128]{2,1,0:T(8,128)S(1)} %get-tuple-element.18, f32[16,16,128]{2,1,0:T(8,128)S(1)} %get-tuple-element.14, f32[2,128]{1,0:T(2,128)S(1)} %copy-done.3, ...), kind=kOutput, calls=%fused_computation.74 | convolution fusion | flops 50425840 | bytes 2393216 | tf_op jit(solution)/shard_map/ricj,csj->rsi/dot_general | solution.py:145
  59.8 0.1 pad_maximum_fusion.8
  59.9 0.7 collective-permute-start.12
  60.6 2.9 %collective-permute-done.12 = f32[32]{0:T(128)S(1)} collective-permute-done((f32[32]{0:T(128)S(1)}, f32[32]{0:T(128)S(1)}, u32[]{:S(2)}, u32[]{:S(2)}) %collective-permute-start.12) | collective-permute-done | bytes 160 | tf_op jit(solution)/shard_map/ppermute | solution.py:14
  63.4 0.1 slice_add_fusion.8
  63.5 0.1 pad_maximum_fusion.9
  63.6 1.5 %collective-permute-start.13 = (f32[32]{0:T(128)S(1)}, f32[32]{0:T(128)S(1)}, u32[]{:S(2)}, u32[]{:S(2)}) collective-permute-start(f32[32]{0:T(128)S(1)} %pad_maximum_fusion.9), channel_id=1, source_target_pairs={{0,16},{8,24},{16,0},{24,8},{1,17},{9,25},{17,1},{25,9},{2,18},{10... | collective-permute-start | bytes 392 | tf_op jit(solution)/shard_map/ppermute | solution.py:14
  65.1 2.0 %collective-permute-done.13 = f32[32]{0:T(128)S(1)} collective-permute-done((f32[32]{0:T(128)S(1)}, f32[32]{0:T(128)S(1)}, u32[]{:S(2)}, u32[]{:S(2)}) %collective-permute-start.13) | collective-permute-done | bytes 160 | tf_op jit(solution)/shard_map/ppermute | solution.py:14
  67.1 0.1 slice_add_fusion.6
  67.2 0.0 collective-permute-start.14
  67.2 1.1 %collective-permute-done.14 = f32[16]{0:T(128)S(1)} collective-permute-done((f32[16]{0:T(128)S(1)}, f32[16]{0:T(128)S(1)}, u32[]{:S(2)}, u32[]{:S(2)}) %collective-permute-start.14) | collective-permute-done | bytes 96 | tf_op jit(solution)/shard_map/ppermute | solution.py:14
  68.3 0.5 collective-permute-start.15
  68.8 3.1 %collective-permute-done.15 = f32[16]{0:T(128)S(1)} collective-permute-done((f32[16]{0:T(128)S(1)}, f32[16]{0:T(128)S(1)}, u32[]{:S(2)}, u32[]{:S(2)}) %collective-permute-start.15) | collective-permute-done | bytes 96 | tf_op jit(solution)/shard_map/ppermute | solution.py:14
  71.9 1.7 %collective-permute-start.16 = (f32[16]{0:T(128)S(1)}, f32[16]{0:T(128)S(1)}, u32[]{:S(2)}, u32[]{:S(2)}) collective-permute-start(f32[16]{0:T(128)S(1)} %add.228), channel_id=1, source_target_pairs={{0,4},{1,5},{2,6},{3,7},{4,0},{5,1},{6,2},{7,3},{8,12},{9,13},{10,... | collective-permute-start | bytes 200 | tf_op jit(solution)/shard_map/ppermute | solution.py:14
  73.5 0.6 constant_dynamic-slice_fusion
  74.2 2.2 %collective-permute-done.16 = f32[16]{0:T(128)S(1)} collective-permute-done((f32[16]{0:T(128)S(1)}, f32[16]{0:T(128)S(1)}, u32[]{:S(2)}, u32[]{:S(2)}) %collective-permute-start.16) | collective-permute-done | bytes 96 | tf_op jit(solution)/shard_map/ppermute | solution.py:14
  76.3 0.5 multiply_sqrt_fusion
  (61 shorter events, 0.4 us)
Async XLA Ops:
  0.6 4.2 %copy-start = (f32[32,128]{1,0:T(8,128)S(1)}, f32[32,128]{1,0:T(8,128)}, u32[]{:S(2)}) copy-start(f32[32,128]{1,0:T(8,128)} %param.20) | copy-start | bytes 49156
  0.6 4.2 %copy-start.6 = (s32[16]{0:T(128)S(1)}, s32[16]{0:T(128)}, u32[]{:S(2)}) copy-start(s32[16]{0:T(128)} %param.21) | copy-start | bytes 196
  0.7 4.4 %copy-start.4 = (f32[2,128]{1,0:T(2,128)S(1)}, f32[2,128]{1,0:T(2,128)}, u32[]{:S(2)}) copy-start(f32[2,128]{1,0:T(2,128)} %param.16) | copy-start | bytes 3076
  0.7 7.5 %copy-start.8 = (s32[48]{0:T(128)S(1)}, s32[48]{0:T(128)}, u32[]{:S(2)}) copy-start(s32[48]{0:T(128)} %param.13) | copy-start | bytes 580
  0.7 7.5 %copy-start.7 = (s32[48]{0:T(128)S(1)}, s32[48]{0:T(128)}, u32[]{:S(2)}) copy-start(s32[48]{0:T(128)} %param.12) | copy-start | bytes 580
  5.2 8.8 %collective-permute-start = (f32[272]{0:T(512)S(1)}, f32[272]{0:T(512)S(1)}, u32[]{:S(2)}, u32[]{:S(2)}) collective-permute-start(f32[272]{0:T(512)S(1)} %pad_maximum_fusion.5), channel_id=1, source_target_pairs={{0,8},{8,0},{16,24},{24,16},{1,9},{9,1},{17,25},{25,17},{2,10},{10... | collective-permute-start | bytes 3272 | tf_op jit(solution)/shard_map/ppermute | solution.py:14
  8.3 5.6 %copy-start.2 = (f32[2,16,128]{2,1,0:T(8,128)S(1)}, f32[2,16,128]{2,1,0:T(8,128)}, u32[]{:S(2)}) copy-start(f32[2,16,128]{2,1,0:T(8,128)} %param.18) | copy-start | bytes 49156
  8.3 5.6 %copy-start.5 = (f32[2,128]{1,0:T(2,128)S(1)}, f32[2,128]{1,0:T(2,128)}, u32[]{:S(2)}) copy-start(f32[2,128]{1,0:T(2,128)} %param.17) | copy-start | bytes 3076
  8.3 7.3 %copy-start.1 = (f32[2,16,128]{2,1,0:T(8,128)S(1)}, f32[2,16,128]{2,1,0:T(8,128)}, u32[]{:S(2)}) copy-start(f32[2,16,128]{2,1,0:T(8,128)} %param.19) | copy-start | bytes 49156
  14.1 3.7 %collective-permute-start.1 = (f32[272]{0:T(512)S(1)}, f32[272]{0:T(512)S(1)}, u32[]{:S(2)}, u32[]{:S(2)}) collective-permute-start(f32[272]{0:T(512)S(1)} %fusion.89), channel_id=1, source_target_pairs={{0,16},{8,24},{16,0},{24,8},{1,17},{9,25},{17,1},{25,9},{2,18},{10... | collective-permute-start | bytes 3272 | tf_op jit(solution)/shard_map/ppermute | solution.py:14
  16.7 18.8 %copy-start.3 = (f32[2,128]{1,0:T(2,128)S(1)}, f32[2,128]{1,0:T(2,128)}, u32[]{:S(2)}) copy-start(f32[2,128]{1,0:T(2,128)} %param.15) | copy-start | bytes 3076
  17.7 1.3 %collective-permute-start.2 = (f32[16656]{0:T(1024)S(1)}, f32[16656]{0:T(1024)S(1)}, u32[]{:S(2)}, u32[]{:S(2)}) collective-permute-start(f32[16656]{0:T(1024)S(1)} %pad_maximum_fusion.1), channel_id=1, source_target_pairs={{0,1},{1,0},{2,3},{3,2},{4,5},{5,4},{6,7},{7,6},{8,9},{9,8},{10,11... | collective-permute-start | bytes 199880 | tf_op jit(solution)/shard_map/ppermute | solution.py:14
  19.2 4.7 %collective-permute-start.3 = (f32[22528]{0:T(1024)S(1)}, f32[22528]{0:T(1024)S(1)}, u32[]{:S(2)}, u32[]{:S(2)}) collective-permute-start(f32[22528]{0:T(1024)S(1)} %concatenate.48), channel_id=1, source_target_pairs={{0,2},{1,3},{2,0},{3,1},{4,6},{5,7},{6,4},{7,5},{8,10},{9,11},{10,... | collective-permute-start | bytes 270344 | tf_op jit(solution)/shard_map/ppermute | solution.py:14
  24.0 7.6 %collective-permute-start.4 = (f32[27648]{0:T(1024)S(1)}, f32[27648]{0:T(1024)S(1)}, u32[]{:S(2)}, u32[]{:S(2)}) collective-permute-start(f32[27648]{0:T(1024)S(1)} %concatenate.49), channel_id=1, source_target_pairs={{0,4},{1,5},{2,6},{3,7},{4,0},{5,1},{6,2},{7,3},{8,12},{9,13},{10,... | collective-permute-start | bytes 331784 | tf_op jit(solution)/shard_map/ppermute | solution.py:14
  31.6 1.4 %collective-permute-start.5 = (f32[36864]{0:T(1024)S(1)}, f32[36864]{0:T(1024)S(1)}, u32[]{:S(2)}, u32[]{:S(2)}) collective-permute-start(f32[36864]{0:T(1024)S(1)} %pad_maximum_fusion), channel_id=1, source_target_pairs={{0,1},{1,0},{2,3},{3,2},{4,5},{5,4},{6,7},{7,6},{8,9},{9,8},{10,11... | collective-permute-start | bytes 442376 | tf_op jit(solution)/shard_map/ppermute | solution.py:14
  37.1 3.5 %collective-permute-start.6 = (f32[32]{0:T(128)S(1)}, f32[32]{0:T(128)S(1)}, u32[]{:S(2)}, u32[]{:S(2)}) collective-permute-start(f32[32]{0:T(128)S(1)} %pad_maximum_fusion.6), channel_id=1, source_target_pairs={{0,8},{8,0},{16,24},{24,16},{1,9},{9,1},{17,25},{25,17},{2,10},{10... | collective-permute-start | bytes 392 | tf_op jit(solution)/shard_map/ppermute | solution.py:14
  40.8 3.5 %collective-permute-start.7 = (f32[32]{0:T(128)S(1)}, f32[32]{0:T(128)S(1)}, u32[]{:S(2)}, u32[]{:S(2)}) collective-permute-start(f32[32]{0:T(128)S(1)} %pad_maximum_fusion.7), channel_id=1, source_target_pairs={{0,16},{8,24},{16,0},{24,8},{1,17},{9,25},{17,1},{25,9},{2,18},{10... | collective-permute-start | bytes 392 | tf_op jit(solution)/shard_map/ppermute | solution.py:14
  44.4 1.3 %collective-permute-start.8 = (f32[16400]{0:T(1024)S(1)}, f32[16400]{0:T(1024)S(1)}, u32[]{:S(2)}, u32[]{:S(2)}) collective-permute-start(f32[16400]{0:T(1024)S(1)} %pad_maximum_fusion.2), channel_id=1, source_target_pairs={{0,1},{1,0},{2,3},{3,2},{4,5},{5,4},{6,7},{7,6},{8,9},{9,8},{10,11... | collective-permute-start | bytes 196808 | tf_op jit(solution)/shard_map/ppermute | solution.py:14
  45.7 4.4 %collective-permute-start.9 = (f32[16400]{0:T(1024)S(1)}, f32[16400]{0:T(1024)S(1)}, u32[]{:S(2)}, u32[]{:S(2)}) collective-permute-start(f32[16400]{0:T(1024)S(1)} %pad_maximum_fusion.3), channel_id=1, source_target_pairs={{0,2},{1,3},{2,0},{3,1},{4,6},{5,7},{6,4},{7,5},{8,10},{9,11},{10,... | collective-permute-start | bytes 196808 | tf_op jit(solution)/shard_map/ppermute | solution.py:14
  50.1 6.0 %collective-permute-start.10 = (f32[16400]{0:T(1024)S(1)}, f32[16400]{0:T(1024)S(1)}, u32[]{:S(2)}, u32[]{:S(2)}) collective-permute-start(f32[16400]{0:T(1024)S(1)} %pad_maximum_fusion.4), channel_id=1, source_target_pairs={{0,4},{1,5},{2,6},{3,7},{4,0},{5,1},{6,2},{7,3},{8,12},{9,13},{10,... | collective-permute-start | bytes 196808 | tf_op jit(solution)/shard_map/ppermute | solution.py:14
  56.1 1.3 %collective-permute-start.11 = (f32[16384]{0:T(1024)S(1)}, f32[16384]{0:T(1024)S(1)}, u32[]{:S(2)}, u32[]{:S(2)}) collective-permute-start(f32[16384]{0:T(1024)S(1)} %get-tuple-element.27), channel_id=1, source_target_pairs={{0,1},{1,0},{2,3},{3,2},{4,5},{5,4},{6,7},{7,6},{8,9},{9,8},{10,11... | collective-permute-start | bytes 196616 | tf_op jit(solution)/shard_map/ppermute | solution.py:14
  59.9 3.5 %collective-permute-start.12 = (f32[32]{0:T(128)S(1)}, f32[32]{0:T(128)S(1)}, u32[]{:S(2)}, u32[]{:S(2)}) collective-permute-start(f32[32]{0:T(128)S(1)} %pad_maximum_fusion.8), channel_id=1, source_target_pairs={{0,8},{8,0},{16,24},{24,16},{1,9},{9,1},{17,25},{25,17},{2,10},{10... | collective-permute-start | bytes 392 | tf_op jit(solution)/shard_map/ppermute | solution.py:14
  63.6 3.5 %collective-permute-start.13 = (f32[32]{0:T(128)S(1)}, f32[32]{0:T(128)S(1)}, u32[]{:S(2)}, u32[]{:S(2)}) collective-permute-start(f32[32]{0:T(128)S(1)} %pad_maximum_fusion.9), channel_id=1, source_target_pairs={{0,16},{8,24},{16,0},{24,8},{1,17},{9,25},{17,1},{25,9},{2,18},{10... | collective-permute-start | bytes 392 | tf_op jit(solution)/shard_map/ppermute | solution.py:14
  67.2 1.1 %collective-permute-start.14 = (f32[16]{0:T(128)S(1)}, f32[16]{0:T(128)S(1)}, u32[]{:S(2)}, u32[]{:S(2)}) collective-permute-start(f32[16]{0:T(128)S(1)} %slice_add_fusion.6), channel_id=1, source_target_pairs={{0,1},{1,0},{2,3},{3,2},{4,5},{5,4},{6,7},{7,6},{8,9},{9,8},{10,11... | collective-permute-start | bytes 200 | tf_op jit(solution)/shard_map/ppermute | solution.py:14
  68.3 3.5 %collective-permute-start.15 = (f32[16]{0:T(128)S(1)}, f32[16]{0:T(128)S(1)}, u32[]{:S(2)}, u32[]{:S(2)}) collective-permute-start(f32[16]{0:T(128)S(1)} %add.227), channel_id=1, source_target_pairs={{0,2},{1,3},{2,0},{3,1},{4,6},{5,7},{6,4},{7,5},{8,10},{9,11},{10,... | collective-permute-start | bytes 200 | tf_op jit(solution)/shard_map/ppermute | solution.py:14
  71.9 4.4 %collective-permute-start.16 = (f32[16]{0:T(128)S(1)}, f32[16]{0:T(128)S(1)}, u32[]{:S(2)}, u32[]{:S(2)}) collective-permute-start(f32[16]{0:T(128)S(1)} %add.228), channel_id=1, source_target_pairs={{0,4},{1,5},{2,6},{3,7},{4,0},{5,1},{6,2},{7,3},{8,12},{9,13},{10,... | collective-permute-start | bytes 200 | tf_op jit(solution)/shard_map/ppermute | solution.py:14

commit v22 on v20

--- a/solution.py
+++ b/solution.py
@@ -190,8 +190,8 @@
         local_x = jnp.sum((new_primal - primal_reg) ** 2, axis=(0, 2))
         local_y = jnp.sum((new_dual - dual) ** 2, axis=(0, 2))
         primal_reg, dual = (new_primal, new_dual)
-    _, (step_x, part_y), _ = _rounds("region", [local_x, local_y])
-    _, (step_y,), _ = _rounds("col", [part_y])
+    _, (part_y,), _ = _rounds("col", [local_y])
+    _, (step_x, step_y), _ = _rounds("region", [local_x, part_y])
     weight = jnp.sqrt(weight * jnp.sqrt((step_x + 1e-06) / (step_y + 1e-06)))
     primal_out = lax.dynamic_slice_in_dim(
         primal_reg, _slot(me, ncol) * own_blocks, own_blocks, axis=0

time: 77 us -> 77.1 us (level)
  no operation moved by 1% of the time
where the time goes in v22:
time: 77.1 us; the launch traced here: 76.8 us
  waiting for transfers between devices  36.2 us (47%)
  starting transfers between devices  18.8 us (24%)
  matrix products  11.5 us (15%)
  other arithmetic  6.1 us (8%)
  between operations  3.05 us (4%)
  local copies, waits for them, and re-layouts  1.05 us (1%)
    ppermute x17, waiting for transfers between devices, _exchange(): return lax.ppermute(x, axis, [(i, i ^ 1 << bit) for i in range(n)])  36.2 us
    ppermute x17, starting transfers between devices, _exchange(): return lax.ppermute(x, axis, [(i, i ^ 1 << bit) for i in range(n)])  18.8 us
    dot_general x1, matrix products, local(): dense = jnp.dot(place_live, tiles.reshape(ntiles, -1), precision=hp)  5.59 us
    dot_general x2, matrix products, product_of(): jnp.einsum('ricj,csj->rsi', dense, point, precision=lax.Precision.HIGH)  3.64 us
    reduce_sum x1, other arithmetic, local(): local_a = jnp.sum(tiles * tiles * live[:, None, None], axis=(0, 1))  2.78 us
    dot_general x2, matrix products, transposed_product(): jnp.einsum('rsi,ricj->csj', dual, dense, precision=lax.Precision.HIGH)  2.13 us
  transfers between devices with their start and end apart: 17, of which 16 were waited for; matrix products, arithmetic and copies ran while one was open for 11% of the time, Pallas kernels for 0%

profile of v22, /device:TPU:0, one launch (start us, length us, event | category | flops | bytes accessed | tf_op | source)
XLA Modules:
  0.0 76.8 jit_solution(16019441516456337222)
XLA Ops:
  0.6 0.0 copy-start
  1.4 0.7 multiply_reduce_fusion.6
  2.1 2.8 %multiply_reduce_fusion = f32[128]{0:T(128)S(1)} fusion(f32[48,128,128]{2,1,0:T(8,128)} %param.11, f32[48]{0:T(128)S(1)} %compare_convert_fusion), kind=kLoop, calls=%fused_computation.4 | loop fusion | flops 2359168 | bytes 3146432 | tf_op jit(solution)/shard_map/reduce_sum | solution.py:127
  4.9 0.0 copy-done
  4.9 0.2 fusion.81
  5.1 0.1 multiply_reduce_fusion.5
  5.2 3.0 %collective-permute-start = (f32[272]{0:T(512)S(1)}, f32[272]{0:T(512)S(1)}, u32[]{:S(2)}, u32[]{:S(2)}) collective-permute-start(f32[272]{0:T(512)S(1)} %pad_maximum_fusion.5), channel_id=1, source_target_pairs={{0,8},{8,0},{16,24},{24,16},{1,9},{9,1},{17,25},{25,17},{2,10},{10... | collective-permute-start | bytes 3272 | tf_op jit(solution)/shard_map/ppermute | solution.py:14
  8.2 0.1 pad.30.clone
  8.3 5.6 %fusion.10 = f32[2,128,16,128]{3,2,1,0:T(8,128)S(1)} fusion(f32[48]{0:T(128)S(1)} %compare_convert_fusion, s32[16,2]{0,1:T(2,128)S(1)} %multiply_add_fusion, s32[48]{0:T(128)S(1)} %multiply_add_fusion.1, f32[6,8,128,128]{3,2,1,0:T(8,128)} %bitcast.138), kind=kOutput, calls=%fused_computation.13 | convolution fusion | flops 301992960 | bytes 5243392 | tf_op jit(solution)/shard_map/dot_general | solution.py:137
  13.9 0.0 copy-done.2
  14.0 0.0 copy-done.5
  14.0 0.1 fusion.71
  14.0 0.0 collective-permute-done
  14.1 1.6 %collective-permute-start.1 = (f32[272]{0:T(512)S(1)}, f32[272]{0:T(512)S(1)}, u32[]{:S(2)}, u32[]{:S(2)}) collective-permute-start(f32[272]{0:T(512)S(1)} %fusion.89), channel_id=1, source_target_pairs={{0,16},{8,24},{16,0},{24,8},{1,17},{9,25},{17,1},{25,9},{2,18},{10... | collective-permute-start | bytes 3272 | tf_op jit(solution)/shard_map/ppermute | solution.py:14
  15.6 0.0 copy-done.1
  15.6 1.1 %fusion.8 = f32[16,128,16,1]{1,2,3,0:T(8,128)S(1)} fusion(f32[2,128,16,128]{3,2,1,0:T(8,128)S(1)} %fusion.10, f32[2,16,128]{2,1,0:T(8,128)S(1)} %copy-done.1), kind=kOutput, calls=%fused_computation.11 | convolution fusion | flops 50331648 | bytes 2244608 | tf_op jit(solution)/shard_map/rsi,ricj->csj/dot_general | solution.py:142
  16.7 1.0 %collective-permute-done.1 = f32[272]{0:T(512)S(1)} collective-permute-done((f32[272]{0:T(512)S(1)}, f32[272]{0:T(512)S(1)}, u32[]{:S(2)}, u32[]{:S(2)}) %collective-permute-start.1) | collective-permute-done | bytes 1120 | tf_op jit(solution)/shard_map/ppermute | solution.py:14
  17.7 0.1 collective-permute-start.2
  17.8 1.2 %collective-permute-done.2 = f32[16656]{0:T(1024)S(1)} collective-permute-done((f32[16656]{0:T(1024)S(1)}, f32[16656]{0:T(1024)S(1)}, u32[]{:S(2)}, u32[]{:S(2)}) %collective-permute-start.2) | collective-permute-done | bytes 66656 | tf_op jit(solution)/shard_map/ppermute | solution.py:14
  19.1 0.1 concatenate.48
  19.2 1.6 %collective-permute-start.3 = (f32[22528]{0:T(1024)S(1)}, f32[22528]{0:T(1024)S(1)}, u32[]{:S(2)}, u32[]{:S(2)}) collective-permute-start(f32[22528]{0:T(1024)S(1)} %concatenate.48), channel_id=1, source_target_pairs={{0,2},{1,3},{2,0},{3,1},{4,6},{5,7},{6,4},{7,5},{8,10},{9,11},{10,... | collective-permute-start | bytes 270344 | tf_op jit(solution)/shard_map/ppermute | solution.py:14
  20.7 3.1 %collective-permute-done.3 = f32[22528]{0:T(1024)S(1)} collective-permute-done((f32[22528]{0:T(1024)S(1)}, f32[22528]{0:T(1024)S(1)}, u32[]{:S(2)}, u32[]{:S(2)}) %collective-permute-start.3) | collective-permute-done | bytes 90144 | tf_op jit(solution)/shard_map/ppermute | solution.py:14
  23.9 0.1 concatenate.49
  24.0 2.6 %collective-permute-start.4 = (f32[27648]{0:T(1024)S(1)}, f32[27648]{0:T(1024)S(1)}, u32[]{:S(2)}, u32[]{:S(2)}) collective-permute-start(f32[27648]{0:T(1024)S(1)} %concatenate.49), channel_id=1, source_target_pairs={{0,4},{1,5},{2,6},{3,7},{4,0},{5,1},{6,2},{7,3},{8,12},{9,13},{10,... | collective-permute-start | bytes 331784 | tf_op jit(solution)/shard_map/ppermute | solution.py:14
  26.6 5.0 %collective-permute-done.4 = f32[27648]{0:T(1024)S(1)} collective-permute-done((f32[27648]{0:T(1024)S(1)}, f32[27648]{0:T(1024)S(1)}, u32[]{:S(2)}, u32[]{:S(2)}) %collective-permute-start.4) | collective-permute-done | bytes 110624 | tf_op jit(solution)/shard_map/ppermute | solution.py:14
  31.6 0.6 slice_reduce_fusion
  33.7 0.1 collective-permute-start.5
  33.8 1.3 %collective-permute-done.5 = f32[36864]{0:T(1024)S(1)} collective-permute-done((f32[36864]{0:T(1024)S(1)}, f32[36864]{0:T(1024)S(1)}, u32[]{:S(2)}, u32[]{:S(2)}) %collective-permute-start.5) | collective-permute-done | bytes 147488 | tf_op jit(solution)/shard_map/ppermute | solution.py:14
  35.2 0.2 multiply_reduce_fusion.2
  35.4 1.5 %multiply_reduce_fusion.4 = (f32[16]{0:T(128)S(1)}, f32[2,16,128]{2,1,0:T(8,128)S(1)}) fusion(f32[2,16,128]{2,1,0:T(8,128)S(1)} %copy-done.1, f32[2,128,16,128]{3,2,1,0:T(8,128)S(1)} %fusion.10, f32[16,16,128]{2,1,0:T(8,128)S(1)} %bitcast.140, f32[16,16,128]{2,1,0:T(8,128)S(1)} %get-tuple-element.14, f32[2,128]{1,0:T(2,128)S(1)} %copy-done.3, ...), kind=kOutput, calls=%fused_computation.75 | convolution fusion | flops 50425840 | bytes 2393216 | tf_op jit(solution)/shard_map/ricj,csj->rsi/dot_general | solution.py:145
  36.9 0.1 pad_maximum_fusion.6
  37.0 0.7 collective-permute-start.6
  37.7 1.1 %fusion.6 = f32[16,128,16,1]{1,2,3,0:T(8,128)S(1)} fusion(f32[2,128,16,128]{3,2,1,0:T(8,128)S(1)} %fusion.10, f32[2,16,128]{2,1,0:T(8,128)S(1)} %get-tuple-element.37), kind=kOutput, calls=%fused_computation.9 | convolution fusion | flops 50331648 | bytes 2244608 | tf_op jit(solution)/shard_map/rsi,ricj->csj/dot_general | solution.py:142
  38.7 1.8 %collective-permute-done.6 = f32[32]{0:T(128)S(1)} collective-permute-done((f32[32]{0:T(128)S(1)}, f32[32]{0:T(128)S(1)}, u32[]{:S(2)}, u32[]{:S(2)}) %collective-permute-start.6) | collective-permute-done | bytes 160 | tf_op jit(solution)/shard_map/ppermute | solution.py:14
  40.5 0.1 slice_add_fusion.10
  40.6 0.1 pad_maximum_fusion.7
  40.7 1.5 %collective-permute-start.7 = (f32[32]{0:T(128)S(1)}, f32[32]{0:T(128)S(1)}, u32[]{:S(2)}, u32[]{:S(2)}) collective-permute-start(f32[32]{0:T(128)S(1)} %pad_maximum_fusion.7), channel_id=1, source_target_pairs={{0,16},{8,24},{16,0},{24,8},{1,17},{9,25},{17,1},{25,9},{2,18},{10... | collective-permute-start | bytes 392 | tf_op jit(solution)/shard_map/ppermute | solution.py:14
  42.2 2.0 %collective-permute-done.7 = f32[32]{0:T(128)S(1)} collective-permute-done((f32[32]{0:T(128)S(1)}, f32[32]{0:T(128)S(1)}, u32[]{:S(2)}, u32[]{:S(2)}) %collective-permute-start.7) | collective-permute-done | bytes 160 | tf_op jit(solution)/shard_map/ppermute | solution.py:14
  44.2 0.1 slice_add_fusion.8
  44.3 0.0 collective-permute-start.8
  44.3 1.2 %collective-permute-done.8 = f32[16400]{0:T(1024)S(1)} collective-permute-done((f32[16400]{0:T(1024)S(1)}, f32[16400]{0:T(1024)S(1)}, u32[]{:S(2)}, u32[]{:S(2)}) %collective-permute-start.8) | collective-permute-done | bytes 65632 | tf_op jit(solution)/shard_map/ppermute | solution.py:14
  45.6 0.7 collective-permute-start.9
  46.4 3.6 %collective-permute-done.9 = f32[16400]{0:T(1024)S(1)} collective-permute-done((f32[16400]{0:T(1024)S(1)}, f32[16400]{0:T(1024)S(1)}, u32[]{:S(2)}, u32[]{:S(2)}) %collective-permute-start.9) | collective-permute-done | bytes 65632 | tf_op jit(solution)/shard_map/ppermute | solution.py:14
  50.0 2.3 %collective-permute-start.10 = (f32[16400]{0:T(1024)S(1)}, f32[16400]{0:T(1024)S(1)}, u32[]{:S(2)}, u32[]{:S(2)}) collective-permute-start(f32[16400]{0:T(1024)S(1)} %pad_maximum_fusion.4), channel_id=1, source_target_pairs={{0,4},{1,5},{2,6},{3,7},{4,0},{5,1},{6,2},{7,3},{8,12},{9,13},{10,... | collective-permute-start | bytes 196808 | tf_op jit(solution)/shard_map/ppermute | solution.py:14
  52.3 3.7 %collective-permute-done.10 = f32[16400]{0:T(1024)S(1)} collective-permute-done((f32[16400]{0:T(1024)S(1)}, f32[16400]{0:T(1024)S(1)}, u32[]{:S(2)}, u32[]{:S(2)}) %collective-permute-start.10) | collective-permute-done | bytes 65632 | tf_op jit(solution)/shard_map/ppermute | solution.py:14
  56.1 0.1 collective-permute-start.11
  56.2 1.2 %collective-permute-done.11 = f32[16384]{0:T(1024)S(1)} collective-permute-done((f32[16384]{0:T(1024)S(1)}, f32[16384]{0:T(1024)S(1)}, u32[]{:S(2)}, u32[]{:S(2)}) %collective-permute-start.11) | collective-permute-done | bytes 65568 | tf_op jit(solution)/shard_map/ppermute | solution.py:14
  57.4 0.2 multiply_reduce_fusion.1
  57.6 2.1 %multiply_reduce_fusion.3 = (f32[16]{0:T(128)S(1)}, f32[2,16,128]{2,1,0:T(8,128)}) fusion(f32[2,16,128]{2,1,0:T(8,128)S(1)} %get-tuple-element.37, f32[2,128,16,128]{3,2,1,0:T(8,128)S(1)} %fusion.10, f32[16,16,128]{2,1,0:T(8,128)S(1)} %get-tuple-element.14, f32[16,16,128]{2,1,0:T(8,128)S(1)} %get-tuple-element.10, f32[2,128]{1,0:T(2,128)S(1)} %copy-done.3, ...), kind=kOutput, calls=%fused_computation.74 | convolution fusion | flops 50425840 | bytes 2393216 | tf_op jit(solution)/shard_map/ricj,csj->rsi/dot_general | solution.py:145
  59.7 0.2 collective-permute-start.12
  59.9 1.0 %collective-permute-done.12 = f32[16]{0:T(128)S(1)} collective-permute-done((f32[16]{0:T(128)S(1)}, f32[16]{0:T(128)S(1)}, u32[]{:S(2)}, u32[]{:S(2)}) %collective-permute-start.12) | collective-permute-done | bytes 96 | tf_op jit(solution)/shard_map/ppermute | solution.py:14
  60.9 0.5 collective-permute-start.13
  61.4 3.1 %collective-permute-done.13 = f32[16]{0:T(128)S(1)} collective-permute-done((f32[16]{0:T(128)S(1)}, f32[16]{0:T(128)S(1)}, u32[]{:S(2)}, u32[]{:S(2)}) %collective-permute-start.13) | collective-permute-done | bytes 96 | tf_op jit(solution)/shard_map/ppermute | solution.py:14
  64.5 1.7 %collective-permute-start.14 = (f32[16]{0:T(128)S(1)}, f32[16]{0:T(128)S(1)}, u32[]{:S(2)}, u32[]{:S(2)}) collective-permute-start(f32[16]{0:T(128)S(1)} %add.223), channel_id=1, source_target_pairs={{0,4},{1,5},{2,6},{3,7},{4,0},{5,1},{6,2},{7,3},{8,12},{9,13},{10,... | collective-permute-start | bytes 200 | tf_op jit(solution)/shard_map/ppermute | solution.py:14
  66.1 2.8 %collective-permute-done.14 = f32[16]{0:T(128)S(1)} collective-permute-done((f32[16]{0:T(128)S(1)}, f32[16]{0:T(128)S(1)}, u32[]{:S(2)}, u32[]{:S(2)}) %collective-permute-start.14) | collective-permute-done | bytes 96 | tf_op jit(solution)/shard_map/ppermute | solution.py:14
  68.9 0.1 pad_maximum_fusion.8
  69.0 0.7 collective-permute-start.15
  69.7 2.9 %collective-permute-done.15 = f32[32]{0:T(128)S(1)} collective-permute-done((f32[32]{0:T(128)S(1)}, f32[32]{0:T(128)S(1)}, u32[]{:S(2)}, u32[]{:S(2)}) %collective-permute-start.15) | collective-permute-done | bytes 160 | tf_op jit(solution)/shard_map/ppermute | solution.py:14
  72.5 0.1 slice_add_fusion.7
  72.6 0.1 pad_maximum_fusion.9
  72.7 1.5 %collective-permute-start.16 = (f32[32]{0:T(128)S(1)}, f32[32]{0:T(128)S(1)}, u32[]{:S(2)}, u32[]{:S(2)}) collective-permute-start(f32[32]{0:T(128)S(1)} %pad_maximum_fusion.9), channel_id=1, source_target_pairs={{0,16},{8,24},{16,0},{24,8},{1,17},{9,25},{17,1},{25,9},{2,18},{10... | collective-permute-start | bytes 392 | tf_op jit(solution)/shard_map/ppermute | solution.py:14
  74.2 0.6 constant_dynamic-slice_fusion
  74.8 1.4 %collective-permute-done.16 = f32[32]{0:T(128)S(1)} collective-permute-done((f32[32]{0:T(128)S(1)}, f32[32]{0:T(128)S(1)}, u32[]{:S(2)}, u32[]{:S(2)}) %collective-permute-start.16) | collective-permute-done | bytes 160 | tf_op jit(solution)/shard_map/ppermute | solution.py:14
  76.2 0.6 multiply_sqrt_fusion
  (60 shorter events, 0.4 us)
Async XLA Ops:
  0.6 4.2 %copy-start = (f32[32,128]{1,0:T(8,128)S(1)}, f32[32,128]{1,0:T(8,128)}, u32[]{:S(2)}) copy-start(f32[32,128]{1,0:T(8,128)} %param.20) | copy-start | bytes 49156
  0.6 4.2 %copy-start.6 = (s32[16]{0:T(128)S(1)}, s32[16]{0:T(128)}, u32[]{:S(2)}) copy-start(s32[16]{0:T(128)} %param.21) | copy-start | bytes 196
  0.7 4.4 %copy-start.4 = (f32[2,128]{1,0:T(2,128)S(1)}, f32[2,128]{1,0:T(2,128)}, u32[]{:S(2)}) copy-start(f32[2,128]{1,0:T(2,128)} %param.16) | copy-start | bytes 3076
  0.7 7.5 %copy-start.8 = (s32[48]{0:T(128)S(1)}, s32[48]{0:T(128)}, u32[]{:S(2)}) copy-start(s32[48]{0:T(128)} %param.13) | copy-start | bytes 580
  0.7 7.5 %copy-start.7 = (s32[48]{0:T(128)S(1)}, s32[48]{0:T(128)}, u32[]{:S(2)}) copy-start(s32[48]{0:T(128)} %param.12) | copy-start | bytes 580
  5.2 8.8 %collective-permute-start = (f32[272]{0:T(512)S(1)}, f32[272]{0:T(512)S(1)}, u32[]{:S(2)}, u32[]{:S(2)}) collective-permute-start(f32[272]{0:T(512)S(1)} %pad_maximum_fusion.5), channel_id=1, source_target_pairs={{0,8},{8,0},{16,24},{24,16},{1,9},{9,1},{17,25},{25,17},{2,10},{10... | collective-permute-start | bytes 3272 | tf_op jit(solution)/shard_map/ppermute | solution.py:14
  8.3 5.6 %copy-start.2 = (f32[2,16,128]{2,1,0:T(8,128)S(1)}, f32[2,16,128]{2,1,0:T(8,128)}, u32[]{:S(2)}) copy-start(f32[2,16,128]{2,1,0:T(8,128)} %param.18) | copy-start | bytes 49156
  8.3 5.6 %copy-start.5 = (f32[2,128]{1,0:T(2,128)S(1)}, f32[2,128]{1,0:T(2,128)}, u32[]{:S(2)}) copy-start(f32[2,128]{1,0:T(2,128)} %param.17) | copy-start | bytes 3076
  8.3 7.3 %copy-start.1 = (f32[2,16,128]{2,1,0:T(8,128)S(1)}, f32[2,16,128]{2,1,0:T(8,128)}, u32[]{:S(2)}) copy-start(f32[2,16,128]{2,1,0:T(8,128)} %param.19) | copy-start | bytes 49156
  14.1 3.7 %collective-permute-start.1 = (f32[272]{0:T(512)S(1)}, f32[272]{0:T(512)S(1)}, u32[]{:S(2)}, u32[]{:S(2)}) collective-permute-start(f32[272]{0:T(512)S(1)} %fusion.89), channel_id=1, source_target_pairs={{0,16},{8,24},{16,0},{24,8},{1,17},{9,25},{17,1},{25,9},{2,18},{10... | collective-permute-start | bytes 3272 | tf_op jit(solution)/shard_map/ppermute | solution.py:14
  16.7 18.7 %copy-start.3 = (f32[2,128]{1,0:T(2,128)S(1)}, f32[2,128]{1,0:T(2,128)}, u32[]{:S(2)}) copy-start(f32[2,128]{1,0:T(2,128)} %param.15) | copy-start | bytes 3076
  17.7 1.3 %collective-permute-start.2 = (f32[16656]{0:T(1024)S(1)}, f32[16656]{0:T(1024)S(1)}, u32[]{:S(2)}, u32[]{:S(2)}) collective-permute-start(f32[16656]{0:T(1024)S(1)} %pad_maximum_fusion.1), channel_id=1, source_target_pairs={{0,1},{1,0},{2,3},{3,2},{4,5},{5,4},{6,7},{7,6},{8,9},{9,8},{10,11... | collective-permute-start | bytes 199880 | tf_op jit(solution)/shard_map/ppermute | solution.py:14
  19.2 4.7 %collective-permute-start.3 = (f32[22528]{0:T(1024)S(1)}, f32[22528]{0:T(1024)S(1)}, u32[]{:S(2)}, u32[]{:S(2)}) collective-permute-start(f32[22528]{0:T(1024)S(1)} %concatenate.48), channel_id=1, source_target_pairs={{0,2},{1,3},{2,0},{3,1},{4,6},{5,7},{6,4},{7,5},{8,10},{9,11},{10,... | collective-permute-start | bytes 270344 | tf_op jit(solution)/shard_map/ppermute | solution.py:14
  24.0 7.6 %collective-permute-start.4 = (f32[27648]{0:T(1024)S(1)}, f32[27648]{0:T(1024)S(1)}, u32[]{:S(2)}, u32[]{:S(2)}) collective-permute-start(f32[27648]{0:T(1024)S(1)} %concatenate.49), channel_id=1, source_target_pairs={{0,4},{1,5},{2,6},{3,7},{4,0},{5,1},{6,2},{7,3},{8,12},{9,13},{10,... | collective-permute-start | bytes 331784 | tf_op jit(solution)/shard_map/ppermute | solution.py:14
  33.7 1.4 %collective-permute-start.5 = (f32[36864]{0:T(1024)S(1)}, f32[36864]{0:T(1024)S(1)}, u32[]{:S(2)}, u32[]{:S(2)}) collective-permute-start(f32[36864]{0:T(1024)S(1)} %pad_maximum_fusion), channel_id=1, source_target_pairs={{0,1},{1,0},{2,3},{3,2},{4,5},{5,4},{6,7},{7,6},{8,9},{9,8},{10,11... | collective-permute-start | bytes 442376 | tf_op jit(solution)/shard_map/ppermute | solution.py:14
  37.0 3.5 %collective-permute-start.6 = (f32[32]{0:T(128)S(1)}, f32[32]{0:T(128)S(1)}, u32[]{:S(2)}, u32[]{:S(2)}) collective-permute-start(f32[32]{0:T(128)S(1)} %pad_maximum_fusion.6), channel_id=1, source_target_pairs={{0,8},{8,0},{16,24},{24,16},{1,9},{9,1},{17,25},{25,17},{2,10},{10... | collective-permute-start | bytes 392 | tf_op jit(solution)/shard_map/ppermute | solution.py:14
  40.7 3.5 %collective-permute-start.7 = (f32[32]{0:T(128)S(1)}, f32[32]{0:T(128)S(1)}, u32[]{:S(2)}, u32[]{:S(2)}) collective-permute-start(f32[32]{0:T(128)S(1)} %pad_maximum_fusion.7), channel_id=1, source_target_pairs={{0,16},{8,24},{16,0},{24,8},{1,17},{9,25},{17,1},{25,9},{2,18},{10... | collective-permute-start | bytes 392 | tf_op jit(solution)/shard_map/ppermute | solution.py:14
  44.3 1.3 %collective-permute-start.8 = (f32[16400]{0:T(1024)S(1)}, f32[16400]{0:T(1024)S(1)}, u32[]{:S(2)}, u32[]{:S(2)}) collective-permute-start(f32[16400]{0:T(1024)S(1)} %pad_maximum_fusion.2), channel_id=1, source_target_pairs={{0,1},{1,0},{2,3},{3,2},{4,5},{5,4},{6,7},{7,6},{8,9},{9,8},{10,11... | collective-permute-start | bytes 196808 | tf_op jit(solution)/shard_map/ppermute | solution.py:14
  45.6 4.4 %collective-permute-start.9 = (f32[16400]{0:T(1024)S(1)}, f32[16400]{0:T(1024)S(1)}, u32[]{:S(2)}, u32[]{:S(2)}) collective-permute-start(f32[16400]{0:T(1024)S(1)} %pad_maximum_fusion.3), channel_id=1, source_target_pairs={{0,2},{1,3},{2,0},{3,1},{4,6},{5,7},{6,4},{7,5},{8,10},{9,11},{10,... | collective-permute-start | bytes 196808 | tf_op jit(solution)/shard_map/ppermute | solution.py:14
  50.0 6.0 %collective-permute-start.10 = (f32[16400]{0:T(1024)S(1)}, f32[16400]{0:T(1024)S(1)}, u32[]{:S(2)}, u32[]{:S(2)}) collective-permute-start(f32[16400]{0:T(1024)S(1)} %pad_maximum_fusion.4), channel_id=1, source_target_pairs={{0,4},{1,5},{2,6},{3,7},{4,0},{5,1},{6,2},{7,3},{8,12},{9,13},{10,... | collective-permute-start | bytes 196808 | tf_op jit(solution)/shard_map/ppermute | solution.py:14
  56.1 1.3 %collective-permute-start.11 = (f32[16384]{0:T(1024)S(1)}, f32[16384]{0:T(1024)S(1)}, u32[]{:S(2)}, u32[]{:S(2)}) collective-permute-start(f32[16384]{0:T(1024)S(1)} %get-tuple-element.23), channel_id=1, source_target_pairs={{0,1},{1,0},{2,3},{3,2},{4,5},{5,4},{6,7},{7,6},{8,9},{9,8},{10,11... | collective-permute-start | bytes 196616 | tf_op jit(solution)/shard_map/ppermute | solution.py:14
  59.7 1.2 %collective-permute-start.12 = (f32[16]{0:T(128)S(1)}, f32[16]{0:T(128)S(1)}, u32[]{:S(2)}, u32[]{:S(2)}) collective-permute-start(f32[16]{0:T(128)S(1)} %get-tuple-element.38), channel_id=1, source_target_pairs={{0,1},{1,0},{2,3},{3,2},{4,5},{5,4},{6,7},{7,6},{8,9},{9,8},{10,11... | collective-permute-start | bytes 200 | tf_op jit(solution)/shard_map/ppermute | solution.py:14
  60.9 3.5 %collective-permute-start.13 = (f32[16]{0:T(128)S(1)}, f32[16]{0:T(128)S(1)}, u32[]{:S(2)}, u32[]{:S(2)}) collective-permute-start(f32[16]{0:T(128)S(1)} %add.222), channel_id=1, source_target_pairs={{0,2},{1,3},{2,0},{3,1},{4,6},{5,7},{6,4},{7,5},{8,10},{9,11},{10,... | collective-permute-start | bytes 200 | tf_op jit(solution)/shard_map/ppermute | solution.py:14
  64.5 4.4 %collective-permute-start.14 = (f32[16]{0:T(128)S(1)}, f32[16]{0:T(128)S(1)}, u32[]{:S(2)}, u32[]{:S(2)}) collective-permute-start(f32[16]{0:T(128)S(1)} %add.223), channel_id=1, source_target_pairs={{0,4},{1,5},{2,6},{3,7},{4,0},{5,1},{6,2},{7,3},{8,12},{9,13},{10,... | collective-permute-start | bytes 200 | tf_op jit(solution)/shard_map/ppermute | solution.py:14
  69.0 3.5 %collective-permute-start.15 = (f32[32]{0:T(128)S(1)}, f32[32]{0:T(128)S(1)}, u32[]{:S(2)}, u32[]{:S(2)}) collective-permute-start(f32[32]{0:T(128)S(1)} %pad_maximum_fusion.8), channel_id=1, source_target_pairs={{0,8},{8,0},{16,24},{24,16},{1,9},{9,1},{17,25},{25,17},{2,10},{10... | collective-permute-start | bytes 392 | tf_op jit(solution)/shard_map/ppermute | solution.py:14
  72.7 3.5 %collective-permute-start.16 = (f32[32]{0:T(128)S(1)}, f32[32]{0:T(128)S(1)}, u32[]{:S(2)}, u32[]{:S(2)}) collective-permute-start(f32[32]{0:T(128)S(1)} %pad_maximum_fusion.9), channel_id=1, source_target_pairs={{0,16},{8,24},{16,0},{24,8},{1,17},{9,25},{17,1},{25,9},{2,18},{10... | collective-permute-start | bytes 392 | tf_op jit(solution)/shard_map/ppermute | solution.py:14
